TPU v7x, 32 devices: a whole 2x2x4 slice. The times are simulated.
32 devices in a mesh: groups: 2 (over y), ctx: 4 (over z), dp: 2 (over x), sub: 2 (over core).
Axes of the slice: x: 2, y: 2, z: 4, core: 2. Of those that a mesh axis runs over, the one named last changes fastest.
Arguments:
- hidden: bfloat16 [8, 768, 2304], P(('groups', 'dp', 'sub'), 'ctx'), parts along dimension 0, may hold values from -16 to 16
- queries: bfloat16 [8, 768, 2048], P(('groups', 'dp', 'sub'), 'ctx'), parts along dimension 0, may hold values from -16 to 16
- kv_weight: bfloat16 [2, 2304, 1024], P(None, 'ctx', ('dp', 'sub')), may hold values from -0.125 to 0.125
- adapter_down: bfloat16 [2, 16, 2304], P(None, None, ('ctx', 'dp', 'sub')), may hold values from -0.125 to 0.125
- adapter_up: bfloat16 [2, 16, 1024], P(None, None, ('ctx', 'dp', 'sub')), may hold values from -1.5 to 1.5
- out_grad: bfloat16 [8, 768, 2048], P(('groups', 'dp', 'sub'), 'ctx'), parts along dimension 0, may hold values from -6 to 6
Outputs:
- attended: bfloat16 [8, 768, 2048], P(('groups', 'dp', 'sub'), 'ctx'), parts along dimension 0
- query_grad: bfloat16 [8, 768, 2048], P(('groups', 'dp', 'sub'), 'ctx'), parts along dimension 0
- down_grad: float32 [4, 16, 2304], P('groups', None, ('ctx', 'dp', 'sub')), parts along dimension 0
- up_grad: float32 [4, 16, 1024], P('groups', None, ('ctx', 'dp', 'sub')), parts along dimension 0
There are 2 independent parts, one for each index of `groups`. A program takes and returns all parts, laid end to end along the dimension named above; an argument that names none is the same for every part. Nothing has to cross between parts.
All inputs are finite; a program needn't handle non-finite values.
Results may differ from a plain program's by a relative error of at most 0.015.
The roundings to bfloat16 on the way count: a program that leaves them out, or rounds other values in their place, can miss the bound.
Values may be sent and summed in bfloat16 or wider, within the bound.
No kernel may reach another device: no remote copies, remote signals or barrier semaphores. Data moves between devices by JAX's collectives and lax.ppermute only.
A program may use at most 64 MiB of HBM per device.

v0:
```python
import jax
import jax.numpy as jnp
from jax import lax
from jax.sharding import PartitionSpec as P

HEADS = 16
KV_HEADS = 8
HEAD_DIM = 128


query_scale = 1.0 / 12.0
logit_cap = 50.0
adapter_scale = 0.5


def shifted(value, axis, by):
    length = lax.axis_size(axis)
    pairs = [(i, i + by) for i in range(length) if 0 <= i + by < length]
    return lax.ppermute(value, axis, pairs)


def attend(query_rows, key_rows, value_rows, grad_rows, is_first):
    length = query_rows.shape[0]
    group_size = HEADS // KV_HEADS
    head_query = query_rows.reshape(length, KV_HEADS, group_size, HEAD_DIM).transpose(1, 2, 0, 3)
    head_grad = grad_rows.reshape(length, KV_HEADS, group_size, HEAD_DIM).transpose(1, 2, 0, 3)
    head_key = key_rows.reshape(2 * length, KV_HEADS, HEAD_DIM).transpose(1, 0, 2)
    head_value = value_rows.reshape(2 * length, KV_HEADS, HEAD_DIM).transpose(1, 0, 2)
    query_pos = lax.broadcasted_iota(jnp.int32, (length, 2 * length), 0)
    key_pos = lax.broadcasted_iota(jnp.int32, (length, 2 * length), 1)
    visible = (
        (key_pos > query_pos)
        & (key_pos <= query_pos + length)
        & (jnp.logical_not(is_first) | (key_pos >= length))
    )

    def one_head(operands):
        queries_g, grads_g, keys_g, values_g = operands
        raw_score = (
            jnp.einsum("grd,kd->grk", queries_g, keys_g, preferred_element_type=jnp.float32)
            * query_scale
        )
        bent_score = jnp.tanh(raw_score / logit_cap)
        expo_terms = jnp.where(visible, jnp.exp(logit_cap * bent_score), 0.0)
        denominator = jnp.sum(expo_terms, axis=-1, keepdims=True)
        attn_prob = (expo_terms / denominator).astype(jnp.bfloat16)
        head_out = jnp.einsum(
            "grk,kd->grd", attn_prob, values_g, preferred_element_type=jnp.float32
        )
        prob_grad = jnp.einsum("grd,kd->grk", grads_g, values_g, preferred_element_type=jnp.float32)
        prob_wide = attn_prob.astype(jnp.float32)
        row_delta = jnp.sum(prob_wide * prob_grad, axis=-1, keepdims=True)
        score_grad = (
            prob_wide * (prob_grad - row_delta) * (1.0 - bent_score * bent_score) * query_scale
        ).astype(jnp.bfloat16)
        head_qgrad = jnp.einsum(
            "grk,kd->grd", score_grad, keys_g, preferred_element_type=jnp.float32
        )
        key_part = jnp.einsum(
            "grk,grd->kd", score_grad, queries_g, preferred_element_type=jnp.float32
        )
        value_part = jnp.einsum(
            "grk,grd->kd", attn_prob, grads_g, preferred_element_type=jnp.float32
        )
        return (head_out, head_qgrad, key_part, value_part)

    head_out, head_qgrad, key_part, value_part = lax.map(
        one_head, (head_query, head_grad, head_key, head_value)
    )
    attended = head_out.transpose(2, 0, 1, 3).reshape(length, HEADS * HEAD_DIM).astype(jnp.bfloat16)
    query_grad = (
        head_qgrad.transpose(2, 0, 1, 3).reshape(length, HEADS * HEAD_DIM).astype(jnp.bfloat16)
    )
    key_grad = key_part.transpose(1, 0, 2).reshape(2 * length, KV_HEADS * HEAD_DIM)
    value_grad = value_part.transpose(1, 0, 2).reshape(2 * length, KV_HEADS * HEAD_DIM)
    return (attended, query_grad, jnp.stack([key_grad, value_grad]))


def project_rows(row_block, kv_weight, down_full, up_full):
    low_rank = jnp.einsum(
        "rd,mkd->mrk", row_block, down_full, preferred_element_type=jnp.float32
    ).astype(jnp.bfloat16)
    partial_weight = lax.all_gather(kv_weight, "ctx", axis=1, tiled=True)
    base_part = jnp.einsum(
        "rd,mdc->mrc",
        row_block,
        lax.all_gather(partial_weight, ("dp", "sub"), axis=2, tiled=True),
        preferred_element_type=jnp.float32,
    )
    extra_part = jnp.einsum("mrk,mkc->mrc", low_rank, up_full, preferred_element_type=jnp.float32)
    key_value = (base_part + adapter_scale * extra_part).astype(jnp.bfloat16)
    return (low_rank, key_value)


def on_device(hidden, queries, kv_weight, adapter_down, adapter_up, out_grad):
    rows_own = hidden[0]
    query_rows = queries[0]
    grad_rows = out_grad[0]
    length = rows_own.shape[0]
    down_full, up_full = (
        lax.all_gather(adapter_down, ("ctx", "dp", "sub"), axis=2, tiled=True),
        lax.all_gather(adapter_up, ("ctx", "dp", "sub"), axis=2, tiled=True),
    )
    is_first = lax.axis_index("ctx") == 0
    low_rank, key_value = project_rows(rows_own, kv_weight, down_full, up_full)
    previous = shifted(key_value, "ctx", 1)
    key_rows = jnp.concatenate([previous[0], key_value[0]], axis=0)
    value_rows = jnp.concatenate([previous[1], key_value[1]], axis=0)
    attended, query_grad, kv_grads = attend(query_rows, key_rows, value_rows, grad_rows, is_first)
    kv_rounded = kv_grads.astype(jnp.bfloat16)
    far_part = kv_rounded[:, :length]
    near_part = kv_rounded[:, length:]
    returned = shifted(far_part, "ctx", -1)
    sources = (rows_own, rows_own)
    low_parts = (low_rank, low_rank)
    pieces = (near_part, returned)
    down_terms = jnp.zeros(down_full.shape, jnp.float32)
    up_terms = jnp.zeros(up_full.shape, jnp.float32)
    for source, low_piece, piece_rows in zip(sources, low_parts, pieces):
        projected = jnp.einsum(
            "mrc,mkc->mrk", piece_rows, up_full, preferred_element_type=jnp.float32
        ).astype(jnp.bfloat16)
        down_terms = down_terms + jnp.einsum(
            "mrk,rd->mkd", projected, source, preferred_element_type=jnp.float32
        )
        up_terms = up_terms + jnp.einsum(
            "mrk,mrc->mkc", low_piece, piece_rows, preferred_element_type=jnp.float32
        )
    factor = adapter_scale / (lax.axis_size("dp") * lax.axis_size("sub"))
    down_part, up_part = (
        lax.psum_scatter(
            down_terms * factor, ("ctx", "dp", "sub"), scatter_dimension=2, tiled=True
        ),
        lax.psum_scatter(up_terms * factor, ("ctx", "dp", "sub"), scatter_dimension=2, tiled=True),
    )
    return (attended[None], query_grad[None], down_part, up_part)


def solution(mesh):
    placed = (
        P(("groups", "dp", "sub"), "ctx", None),
        P(("groups", "dp", "sub"), "ctx", None),
        P(None, "ctx", ("dp", "sub")),
        P(None, None, ("ctx", "dp", "sub")),
        P(None, None, ("ctx", "dp", "sub")),
        P(("groups", "dp", "sub"), "ctx", None),
    )
    return jax.shard_map(
        on_device,
        mesh=mesh,
        in_specs=placed,
        out_specs=(
            P(("groups", "dp", "sub"), "ctx", None),
            P(("groups", "dp", "sub"), "ctx", None),
            P("groups", None, ("ctx", "dp", "sub")),
            P("groups", None, ("ctx", "dp", "sub")),
        ),
        check_vma=False,
    )
```

profile of v0, /device:TPU:0, one launch (start us, length us, event | category | flops | bytes accessed | tf_op | source)
XLA Modules:
  0.0 439.3 jit_solution(14295966328359549575)
XLA Ops:
  8.0 54.8 %all-gather.3.cloned.1.call-done = bf16[2,2304,256]{2,1,0:T(8,128)(2,1)} async-done(((bf16[2,576,256]{2,1,0:T(8,128)(2,1)}), bf16[2,2304,256]{2,1,0:T(8,128)(2,1)}) %all-gather.3.cloned.1.call-update) | async-done | bytes 2359312 | tf_op jit(solution)/shard_map/all_gather | solution.py:83
  63.1 20.8 %all_gather.15 = bf16[2,16,1024]{1,0,2:T(2,128)(2,1)S(1)} all-gather(bf16[2,16,64]{1,0,2:T(2,128)(2,1)S(1)} %copy.30), channel_id=1, replica_groups=mesh['groups'=2,'ctx'=4,'dp'=2,'sub'=2] {'ctx','dp','sub'}, dimensions={2}, use_global_device_ids=true | all-gather | bytes 69632 | tf_op jit(solution)/shard_map/all_gather | solution.py:102
  84.2 26.2 %all_gather.14 = bf16[2,16,2304]{1,0,2:T(2,128)(2,1)S(1)} all-gather(bf16[2,16,144]{1,0,2:T(2,128)(2,1)S(1)} %copy.28), channel_id=1, replica_groups=mesh['groups'=2,'ctx'=4,'dp'=2,'sub'=2] {'ctx','dp','sub'}, dimensions={2}, use_global_device_ids=true | all-gather | bytes 156672 | tf_op jit(solution)/shard_map/all_gather | solution.py:101
  110.8 30.7 %all-gather.5.cloned.1.call-done = bf16[2,2304,1024]{2,1,0:T(8,128)(2,1)} async-done(((bf16[2,2304,256]{2,1,0:T(8,128)(2,1)}), bf16[2,2304,1024]{2,1,0:T(8,128)(2,1)}) %all-gather.5.cloned.1.call-update) | async-done | bytes 9437200 | tf_op jit(solution)/shard_map/all_gather | solution.py:87
  141.5 5.7 %fusion.59 = f32[2,1024,192]{1,2,0:T(8,128)S(1)} fusion(bf16[2,2304,1024]{2,1,0:T(8,128)(2,1)} %all-gather.5.cloned.1.call-done, bf16[1,192,2304]{2,1,0:T(8,128)(2,1)S(1)} %copy-done), kind=kOutput, calls=%fused_computation.72 | convolution fusion | flops 1811939328 | bytes 11894784 | tf_op jit(solution)/shard_map/rd,mdc->mrc/dot_general | solution.py:84
  147.6 3.6 collective-permute-start
  151.8 2.6 reshape_squeeze.7
  154.7 12.8 %collective-permute-done = bf16[2,192,1024]{2,1,0:T(8,128)(2,1)} collective-permute-done((bf16[2,192,1024]{2,1,0:T(8,128)(2,1)S(1)}, bf16[2,192,1024]{2,1,0:T(8,128)(2,1)}, u32[]{:S(2)}, u32[]{:S(2)}) %collective-permute-start) | collective-permute-done | bytes 786464 | tf_op jit(solution)/shard_map/ppermute | solution.py:19
  167.5 1.2 slice_bitcast_fusion.1
  169.0 1.3 maximum_bitcast_fusion
  170.3 113.1 %while.19 = (s32[]{:T(128)}, bf16[8,2,192,128]{3,2,1,0:T(8,128)(2,1)}, bf16[8,2,192,128]{3,2,1,0:T(8,128)(2,1)}, bf16[8,384,128]{2,1,0:T(8,128)(2,1)}, bf16[8,38...) while((s32[]{:T(128)}, ...), condition=%wide.region_3.4_spmd.clone, body=%wide.region_0.3_spmd.clone.sunk | while | flops 233866368 | bytes 12009261 | solution.py:67
  170.6 1.2 fusion.95
  171.7 1.3 fusion.93
  174.9 3.9 fusion.97
  178.8 3.6 fusion.96
  182.4 2.0 fusion.94
  184.7 1.2 fusion.95
  185.9 1.3 fusion.93
  189.0 3.9 fusion.97
  192.9 3.6 fusion.96
  196.5 2.0 fusion.94
  198.8 1.2 fusion.95
  200.0 1.3 fusion.93
  203.2 3.9 fusion.97
  207.0 3.6 fusion.96
  210.7 2.0 fusion.94
  214.1 1.3 fusion.93
  217.3 3.9 fusion.97
  221.2 3.6 fusion.96
  224.8 2.0 fusion.94
  227.1 1.2 fusion.95
  228.3 1.3 fusion.93
  231.5 3.9 fusion.97
  235.3 3.6 fusion.96
  239.0 2.0 fusion.94
  241.3 1.2 fusion.95
  242.4 1.3 fusion.93
  245.6 3.9 fusion.97
  249.5 3.6 fusion.96
  253.1 2.0 fusion.94
  255.4 1.2 fusion.95
  256.6 1.3 fusion.93
  259.7 3.9 fusion.97
  263.6 3.6 fusion.96
  267.2 2.0 fusion.94
  269.5 1.2 fusion.95
  270.7 1.3 fusion.93
  273.9 3.9 fusion.97
  277.8 3.6 fusion.96
  281.4 2.0 fusion.94
  283.4 1.7 copy.41
  286.0 1.2 stack_reshape.8
  287.2 1.2 constant_dynamic-update-slice_fusion.1
  289.4 1.5 collective-permute-start.1
  291.7 1.4 fusion.55
  293.1 18.1 %collective-permute-done.1 = bf16[2,192,1024]{2,1,0:T(8,128)(2,1)S(1)} collective-permute-done((bf16[2,192,1024]{2,1,0:T(8,128)(2,1)}, bf16[2,192,1024]{2,1,0:T(8,128)(2,1)S(1)}, u32[]{:S(2)}, u32[]{:S(2)}) %collective-permute-start.1) | collective-permute-done | bytes 786464 | tf_op jit(solution)/shard_map/ppermute | solution.py:19
  313.8 1.4 reshape.51
  315.3 1.3 fusion.47
  316.6 3.3 copy.44
  319.8 2.3 reshape.49
  324.1 1.5 convert_element_type.68
  326.4 1.5 convert_element_type.71
  327.9 42.2 %reduce-scatter.9.cloned.1.call-done = f32[64,32]{1,0:T(8,128)} async-done(((f32[1024,32]{1,0:T(8,128)}), f32[64,32]{1,0:T(8,128)}) %reduce-scatter.9.cloned.1.call-update) | async-done | bytes 8208
  371.6 59.4 %reduce-scatter.7.cloned.1.call-done = f32[144,32]{1,0:T(8,128)} async-done(((f32[2304,32]{1,0:T(8,128)}), f32[144,32]{1,0:T(8,128)}) %reduce-scatter.7.cloned.1.call-update) | async-done | bytes 18448
  (105 shorter events, 32.6 us)
Async XLA Ops:
  7.2 103.2 %copy-start = (bf16[1,192,2304]{2,1,0:T(8,128)(2,1)S(1)}, bf16[1,192,2304]{2,1,0:T(8,128)(2,1)}, u32[]{:S(2)}) copy-start(bf16[1,192,2304]{2,1,0:T(8,128)(2,1)} %param.8) | copy-start | bytes 2654212
  7.2 55.7 %copy-start.10 = (bf16[2,16,64]{2,1,0:T(8,128)(2,1)S(1)}, bf16[2,16,64]{2,1,0:T(8,128)(2,1)}, u32[]{:S(2)}) copy-start(bf16[2,16,64]{2,1,0:T(8,128)(2,1)} %param.12) | copy-start | bytes 12292
  7.2 55.8 %copy-start.9 = (bf16[2,16,144]{2,1,0:T(8,128)(2,1)S(1)}, bf16[2,16,144]{2,1,0:T(8,128)(2,1)}, u32[]{:S(2)}) copy-start(bf16[2,16,144]{2,1,0:T(8,128)(2,1)} %param.11) | copy-start | bytes 27652
  7.2 55.6 %all-gather.3.cloned.1.call-start = ((), (), s32[]{:S(2)}) async-start(), calls=%async_computation.2 | async-start | bytes 2949120 | tf_op jit(solution)/shard_map/all_gather | solution.py:83
  7.9 133.6 %all-gather.5.cloned.1.call-start = ((), (), s32[]{:S(2)}) async-start(), calls=%async_computation.3 | async-start | bytes 11796480 | tf_op jit(solution)/shard_map/all_gather | solution.py:87
  62.8 307.3 %reduce-scatter.9.cloned.1.call-start = ((), (), s32[]{:S(2)}) async-start(), calls=%async_computation.5 | async-start | bytes 557056
  84.2 63.0 %copy-start.3 = (bf16[2,16,1024]{2,1,0:T(8,128)(2,1)}, bf16[2,16,1024]{2,1,0:T(8,128)(2,1)S(1)}, u32[]{:S(2)}) copy-start(bf16[2,16,1024]{2,1,0:T(8,128)(2,1)S(1)} %copy.31) | copy-start | bytes 196612
  147.2 4.0 copy-start.5
  147.6 19.9 %collective-permute-start = (bf16[2,192,1024]{2,1,0:T(8,128)(2,1)S(1)}, bf16[2,192,1024]{2,1,0:T(8,128)(2,1)}, u32[]{:S(2)}, u32[]{:S(2)}) collective-permute-start(bf16[2,192,1024]{2,1,0:T(8,128)(2,1)S(1)} %fusion.48), channel_id=1, source_target_pairs={{0,4},{4,8},{8,12},{1,5},{5,9},{9,13},{2,6},{6,10},{10,14},{3,7},{... | collective-permute-start | bytes 2359304 | tf_op jit(solution)/shard_map/ppermute | solution.py:19
  173.1 0.8 copy-start.11
  187.2 0.8 copy-start.11
  201.3 0.8 copy-start.11
  215.5 0.8 copy-start.11
  229.6 0.8 copy-start.11
  243.8 0.8 copy-start.11
  257.9 0.8 copy-start.11
  272.0 0.8 copy-start.11
  283.4 2.1 copy-start.6
  289.4 21.8 %collective-permute-start.1 = (bf16[2,192,1024]{2,1,0:T(8,128)(2,1)}, bf16[2,192,1024]{2,1,0:T(8,128)(2,1)S(1)}, u32[]{:S(2)}, u32[]{:S(2)}) collective-permute-start(bf16[2,192,1024]{2,1,0:T(8,128)(2,1)} %slice.29), channel_id=1, source_target_pairs={{4,0},{8,4},{12,8},{5,1},{9,5},{13,9},{6,2},{10,6},{14,10},{7,3},{... | collective-permute-start | bytes 2359304 | tf_op jit(solution)/shard_map/ppermute | solution.py:19
  311.2 0.9 copy-start.1
  313.2 2.0 copy-start.2
  313.2 2.0 copy-start.4
  315.2 115.8 %reduce-scatter.7.cloned.1.call-start = ((), (), s32[]{:S(2)}) async-start(), calls=%async_computation.4 | async-start | bytes 1253376
  322.2 1.1 copy-start.8
  323.3 2.3 copy-start.7
Sparse Core Ops, SparseCore 0:
  9.6 53.1 all-gather.2
  64.4 77.1 all-gather.4
  315.3 54.7 reduce-scatter.8
  374.0 56.9 reduce-scatter.6
where the time goes:
time: 441 us; the launch traced here: 439 us
  waiting for transfers between devices  219 us (50%)
  matrix products  115 us (26%)
  blocking collectives  46.9 us (11%)
  local copies, waits for them, and re-layouts  36.4 us (8%)
  between operations  14.1 us (3%)
  starting transfers between devices  5.21 us (1%)
    unnamed x6, waiting for transfers between devices  102 us
    all_gather x1, waiting for transfers between devices, project_rows(): partial_weight = lax.all_gather(kv_weight, 'ctx', axis=1, tiled=True)  54.8 us
    dot_general x8, matrix products, one_head(): jnp.einsum('grk,grd->kd', score_grad, queries_g, preferred_element_type=j...  31 us
    ppermute x2, waiting for transfers between devices, shifted(): return lax.ppermute(value, axis, pairs)  30.9 us
    all_gather x1, waiting for transfers between devices, project_rows(): lax.all_gather(partial_weight, ('dp', 'sub'), axis=2, tiled=True)  30.7 us
    dot_general x8, matrix products, one_head(): jnp.einsum('grk,kd->grd', score_grad, keys_g, preferred_element_type=jnp....  29 us
    all_gather x1, blocking collectives, on_device(): lax.all_gather(adapter_down, ('ctx', 'dp', 'sub'), axis=2, tiled=True)  26.2 us
    all_gather x1, blocking collectives, on_device(): lax.all_gather(adapter_up, ('ctx', 'dp', 'sub'), axis=2, tiled=True)  20.8 us
  transfers between devices with their start and end apart: 6, of which 6 were waited for; matrix products, arithmetic and copies ran while one was open for 4% of the time, Pallas kernels for 0%

commit v1 on v0

v1 whole, which is shorter than its diff:
```python
import jax
import jax.numpy as jnp
from jax import lax
from jax.sharding import PartitionSpec as P

HEADS = 16
KV_HEADS = 8
HEAD_DIM = 128


query_scale = 1.0 / 12.0
logit_cap = 50.0
adapter_scale = 0.5


def shifted(value, axis, by):
    length = lax.axis_size(axis)
    pairs = [(i, i + by) for i in range(length) if 0 <= i + by < length]
    return lax.ppermute(value, axis, pairs)


def attend(query_rows, key_rows, value_rows, grad_rows, is_first):
    length = query_rows.shape[0]
    group_size = HEADS // KV_HEADS
    queries_g = query_rows.reshape(length, KV_HEADS, group_size, HEAD_DIM)
    grads_g = grad_rows.reshape(length, KV_HEADS, group_size, HEAD_DIM)
    keys_g = key_rows.reshape(2 * length, KV_HEADS, HEAD_DIM)
    values_g = value_rows.reshape(2 * length, KV_HEADS, HEAD_DIM)
    query_pos = lax.broadcasted_iota(jnp.int32, (length, 2 * length), 0)
    key_pos = lax.broadcasted_iota(jnp.int32, (length, 2 * length), 1)
    visible = (
        (key_pos > query_pos)
        & (key_pos <= query_pos + length)
        & (jnp.logical_not(is_first) | (key_pos >= length))
    )
    raw_score = (
        jnp.einsum("rgjd,kgd->gjrk", queries_g, keys_g, preferred_element_type=jnp.float32)
        * query_scale
    )
    bent_score = jnp.tanh(raw_score / logit_cap)
    expo_terms = jnp.where(visible, jnp.exp(logit_cap * bent_score), 0.0)
    denominator = jnp.sum(expo_terms, axis=-1, keepdims=True)
    attn_prob = (expo_terms / denominator).astype(jnp.bfloat16)
    head_out = jnp.einsum(
        "gjrk,kgd->rgjd", attn_prob, values_g, preferred_element_type=jnp.float32
    )
    prob_grad = jnp.einsum(
        "rgjd,kgd->gjrk", grads_g, values_g, preferred_element_type=jnp.float32
    )
    prob_wide = attn_prob.astype(jnp.float32)
    row_delta = jnp.sum(prob_wide * prob_grad, axis=-1, keepdims=True)
    score_grad = (
        prob_wide * (prob_grad - row_delta) * (1.0 - bent_score * bent_score) * query_scale
    ).astype(jnp.bfloat16)
    head_qgrad = jnp.einsum(
        "gjrk,kgd->rgjd", score_grad, keys_g, preferred_element_type=jnp.float32
    )
    key_part = jnp.einsum(
        "gjrk,rgjd->kgd", score_grad, queries_g, preferred_element_type=jnp.float32
    )
    value_part = jnp.einsum(
        "gjrk,rgjd->kgd", attn_prob, grads_g, preferred_element_type=jnp.float32
    )
    attended = head_out.reshape(length, HEADS * HEAD_DIM).astype(jnp.bfloat16)
    query_grad = head_qgrad.reshape(length, HEADS * HEAD_DIM).astype(jnp.bfloat16)
    key_grad = key_part.reshape(2 * length, KV_HEADS * HEAD_DIM)
    value_grad = value_part.reshape(2 * length, KV_HEADS * HEAD_DIM)
    return (attended, query_grad, jnp.stack([key_grad, value_grad]))


def project_rows(row_block, kv_weight, down_full, up_full):
    low_rank = jnp.einsum(
        "rd,mkd->mrk", row_block, down_full, preferred_element_type=jnp.float32
    ).astype(jnp.bfloat16)
    partial_weight = lax.all_gather(kv_weight, "ctx", axis=1, tiled=True)
    base_part = jnp.einsum(
        "rd,mdc->mrc",
        row_block,
        lax.all_gather(partial_weight, ("dp", "sub"), axis=2, tiled=True),
        preferred_element_type=jnp.float32,
    )
    extra_part = jnp.einsum("mrk,mkc->mrc", low_rank, up_full, preferred_element_type=jnp.float32)
    key_value = (base_part + adapter_scale * extra_part).astype(jnp.bfloat16)
    return (low_rank, key_value)


def gather_adapters(adapter_down, adapter_up):
    axes = ("ctx", "dp", "sub")
    down_cols = adapter_down.shape[2]
    joined = jnp.concatenate([adapter_down, adapter_up], axis=2)
    gathered = lax.all_gather(joined, axes, axis=0, tiled=False)
    shards = gathered.shape[0]

    def unshard(piece):
        return piece.transpose(1, 2, 0, 3).reshape(2, piece.shape[2], shards * piece.shape[3])

    return unshard(gathered[..., :down_cols]), unshard(gathered[..., down_cols:])


def scatter_adapter_grads(down_terms, up_terms):
    axes = ("ctx", "dp", "sub")
    shards = lax.axis_size(axes)
    members, rank = down_terms.shape[0], down_terms.shape[1]

    def shard_major(terms):
        cols = terms.shape[2]
        return terms.transpose(2, 0, 1).reshape(shards, cols // shards, members * rank)

    down_cols = down_terms.shape[2] // shards
    joined = jnp.concatenate([shard_major(down_terms), shard_major(up_terms)], axis=1)
    mine = lax.psum_scatter(
        joined.reshape(-1, members * rank), axes, scatter_dimension=0, tiled=True
    )

    def unshard(piece):
        return piece.reshape(-1, members, rank).transpose(1, 2, 0)

    return unshard(mine[:down_cols]), unshard(mine[down_cols:])


def on_device(hidden, queries, kv_weight, adapter_down, adapter_up, out_grad):
    rows_own = hidden[0]
    query_rows = queries[0]
    grad_rows = out_grad[0]
    length = rows_own.shape[0]
    down_full, up_full = gather_adapters(adapter_down, adapter_up)
    is_first = lax.axis_index("ctx") == 0
    low_rank, key_value = project_rows(rows_own, kv_weight, down_full, up_full)
    previous = shifted(key_value, "ctx", 1)
    key_rows = jnp.concatenate([previous[0], key_value[0]], axis=0)
    value_rows = jnp.concatenate([previous[1], key_value[1]], axis=0)
    attended, query_grad, kv_grads = attend(query_rows, key_rows, value_rows, grad_rows, is_first)
    kv_rounded = kv_grads.astype(jnp.bfloat16)
    far_part = kv_rounded[:, :length]
    near_part = kv_rounded[:, length:]
    returned = shifted(far_part, "ctx", -1)
    sources = (rows_own, rows_own)
    low_parts = (low_rank, low_rank)
    pieces = (near_part, returned)
    down_terms = jnp.zeros(down_full.shape, jnp.float32)
    up_terms = jnp.zeros(up_full.shape, jnp.float32)
    for source, low_piece, piece_rows in zip(sources, low_parts, pieces):
        projected = jnp.einsum(
            "mrc,mkc->mrk", piece_rows, up_full, preferred_element_type=jnp.float32
        ).astype(jnp.bfloat16)
        down_terms = down_terms + jnp.einsum(
            "mrk,rd->mkd", projected, source, preferred_element_type=jnp.float32
        )
        up_terms = up_terms + jnp.einsum(
            "mrk,mrc->mkc", low_piece, piece_rows, preferred_element_type=jnp.float32
        )
    factor = adapter_scale / (lax.axis_size("dp") * lax.axis_size("sub"))
    down_part, up_part = scatter_adapter_grads(down_terms * factor, up_terms * factor)
    return (attended[None], query_grad[None], down_part, up_part)


def solution(mesh):
    placed = (
        P(("groups", "dp", "sub"), "ctx", None),
        P(("groups", "dp", "sub"), "ctx", None),
        P(None, "ctx", ("dp", "sub")),
        P(None, None, ("ctx", "dp", "sub")),
        P(None, None, ("ctx", "dp", "sub")),
        P(("groups", "dp", "sub"), "ctx", None),
    )
    return jax.shard_map(
        on_device,
        mesh=mesh,
        in_specs=placed,
        out_specs=(
            P(("groups", "dp", "sub"), "ctx", None),
            P(("groups", "dp", "sub"), "ctx", None),
            P("groups", None, ("ctx", "dp", "sub")),
            P("groups", None, ("ctx", "dp", "sub")),
        ),
        check_vma=False,
    )
```

time: 441 us -> 283 us (0.64)
  matrix products: 115 us -> 38.6 us
  waiting for transfers between devices: 219 us -> 171 us
  blocking collectives: 46.9 us -> 20 us
  local copies, waits for them, and re-layouts: 36.4 us -> 26.2 us
    dot_general x48 -> x6, matrix products: 104 us -> 25.2 us  [the longest x1 8.63 us: attend(): jnp.einsum('gjrk,rgjd->kgd', score_grad, queries_g, preferred_element_typ...]
    unnamed x6 -> x4, waiting for transfers between devices: 102 us -> 41.6 us
    all_gather x2 -> x1, blocking collectives: 46.9 us -> 20 us  [gather_adapters(): gathered = lax.all_gather(joined, axes, axis=0, tiled=False)]
    all_gather x1, waiting for transfers between devices: 30.7 us -> 44.6 us  [project_rows(): lax.all_gather(partial_weight, ('dp', 'sub'), axis=2, tiled=True)]
    unnamed x39 -> x33, local copies, waits for them, and re-layouts: 15.7 us -> 6.06 us
    while x16 -> x0, local copies, waits for them, and re-layouts: 6.48 us -> none
  transfers between devices with their start and end apart: 6 -> 5, of which waited for: 6 -> 5; matrix products, arithmetic and copies ran while one was open for 4% -> 10% of each run, Pallas kernels for 0% -> 0%
where the time goes in v1:
time: 283 us; the launch traced here: 282 us
  waiting for transfers between devices  171 us (60%)
  matrix products  38.6 us (14%)
  local copies, waits for them, and re-layouts  26.2 us (9%)
  blocking collectives  20 us (7%)
  between operations  14.1 us (5%)
  other arithmetic  6.63 us (2%)
  starting transfers between devices  5.55 us (2%)
    all_gather x1, waiting for transfers between devices, project_rows(): partial_weight = lax.all_gather(kv_weight, 'ctx', axis=1, tiled=True)  54.8 us
    all_gather x1, waiting for transfers between devices, project_rows(): lax.all_gather(partial_weight, ('dp', 'sub'), axis=2, tiled=True)  44.6 us
    unnamed x4, waiting for transfers between devices  41.6 us
    ppermute x2, waiting for transfers between devices, shifted(): return lax.ppermute(value, axis, pairs)  29.6 us
    all_gather x1, blocking collectives, gather_adapters(): gathered = lax.all_gather(joined, axes, axis=0, tiled=False)  20 us
    dot_general x1, matrix products, attend(): jnp.einsum('gjrk,rgjd->kgd', score_grad, queries_g, preferred_element_typ...  8.63 us
    dot_general x1, matrix products, attend(): jnp.einsum('gjrk,kgd->rgjd', score_grad, keys_g, preferred_element_type=j...  8.31 us
    unnamed x33, local copies, waits for them, and re-layouts  6.06 us
  transfers between devices with their start and end apart: 5, of which 5 were waited for; matrix products, arithmetic and copies ran while one was open for 10% of the time, Pallas kernels for 0%

profile of v1, /device:TPU:0, one launch (start us, length us, event | category | flops | bytes accessed | tf_op | source)
XLA Modules:
  0.0 281.8 jit_solution(10912318485950922118)
XLA Ops:
  7.2 0.0 copy-start
  7.2 0.0 all-gather.4.cloned.1.call-start
  7.2 0.7 all-gather.4.cloned.1.call-update
  7.9 0.0 all-gather.6.cloned.1.call-start
  8.0 54.8 %all-gather.4.cloned.1.call-done = bf16[2,2304,256]{2,1,0:T(8,128)(2,1)} async-done(((bf16[2,576,256]{2,1,0:T(8,128)(2,1)}), bf16[2,2304,256]{2,1,0:T(8,128)(2,1)}) %all-gather.4.cloned.1.call-update) | async-done | bytes 2359312 | tf_op jit(solution)/shard_map/all_gather | solution.py:75
  62.8 0.0 all-gather.6.cloned.1.call-update
  62.8 0.0 reduce-scatter.4.cloned.1.call-start
  62.9 0.8 pad_maximum_fusion.2
  63.7 20.0 %all-gather = bf16[32,16,208]{2,1,0:T(8,128)(2,1)S(1)} all-gather(bf16[2,16,208]{2,1,0:T(8,128)(2,1)S(1)} %pad_maximum_fusion.2), channel_id=2, replica_groups=mesh['groups'=2,'ctx'=4,'dp'=2,'sub'=2] {'ctx','dp','sub'}, dimensions={0}, use_global_device_ids=true | all-gather | bytes 226304 | tf_op jit(solution)/shard_map/all_gather | solution.py:91
  83.7 0.1 slice.41
  83.8 0.1 copy.78
  83.9 0.1 reshape.66
  84.0 0.2 copy.77
  84.2 0.3 reshape.65
  84.5 0.3 convolution_convert_fusion.3
  84.9 44.6 %all-gather.6.cloned.1.call-done = bf16[2,2304,1024]{2,1,0:T(8,128)(2,1)} async-done(((bf16[2,2304,256]{2,1,0:T(8,128)(2,1)}), bf16[2,2304,1024]{2,1,0:T(8,128)(2,1)}) %all-gather.6.cloned.1.call-update) | async-done | bytes 9437200 | tf_op jit(solution)/shard_map/all_gather | solution.py:79
  129.6 5.7 %fusion.20 = f32[2,1024,192]{1,2,0:T(8,128)S(1)} fusion(bf16[2,2304,1024]{2,1,0:T(8,128)(2,1)} %all-gather.6.cloned.1.call-done, bf16[1,192,2304]{2,1,0:T(8,128)(2,1)S(1)} %copy-done), kind=kOutput, calls=%fused_computation.37 | convolution fusion | flops 1811939328 | bytes 11894784 | tf_op jit(solution)/shard_map/rd,mdc->mrc/dot_general | solution.py:76
  135.3 0.4 fusion.10
  135.7 3.9 %collective-permute-start = (bf16[2,192,1024]{2,1,0:T(8,128)(2,1)S(1)}, bf16[2,192,1024]{2,1,0:T(8,128)(2,1)}, u32[]{:S(2)}, u32[]{:S(2)}) collective-permute-start(bf16[2,192,1024]{2,1,0:T(8,128)(2,1)S(1)} %fusion.10), channel_id=1, source_target_pairs={{0,4},{4,8},{8,12},{1,5},{5,9},{9,13},{2,6},{6,10},{10,14},{3,7},{... | collective-permute-start | bytes 2359304 | tf_op jit(solution)/shard_map/ppermute | solution.py:19
  139.6 1.4 reshape_squeeze.6
  141.1 1.4 reshape_squeeze.7
  142.5 0.1 fusion.30
  142.6 0.1 slice_bitcast_fusion.2
  142.7 0.1 copy.62
  142.8 0.1 copy.39
  142.9 0.1 copy.64
  142.9 0.1 copy.41
  143.0 12.9 %collective-permute-done = bf16[2,192,1024]{2,1,0:T(8,128)(2,1)} collective-permute-done((bf16[2,192,1024]{2,1,0:T(8,128)(2,1)S(1)}, bf16[2,192,1024]{2,1,0:T(8,128)(2,1)}, u32[]{:S(2)}, u32[]{:S(2)}) %collective-permute-start) | collective-permute-done | bytes 786464 | tf_op jit(solution)/shard_map/ppermute | solution.py:19
  155.9 1.2 slice_bitcast_fusion.3
  157.1 0.1 copy.61
  157.2 0.1 copy.38
  157.2 0.1 copy.63
  157.3 0.1 copy.40
  157.4 1.8 fusion.6
  159.2 1.6 divide_convert_fusion
  160.8 0.1 copy-done.1
  160.9 1.6 bitcast_convert_fusion
  162.5 3.0 %fusion.24 = f32[8,384,192,2]{1,2,3,0:T(8,128)} fusion(bf16[192,8,2,128]{3,2,1,0:T(2,128)(2,1)S(1)} %copy-done.1, bf16[192,8,128]{2,0,1:T(8,128)(2,1)S(1)} %copy.39, bf16[192,8,128]{2,0,1:T(8,128)(2,1)S(1)} %copy.38), kind=kOutput, calls=%fused_computation.44 | convolution fusion | flops 303562752 | bytes 6291456 | tf_op jit(solution)/shard_map/rgjd,kgd->gjrk/dot_general | solution.py:47
  165.5 8.6 %bitcast_convert_fusion.1 = bf16[8,384,128]{1,2,0:T(8,128)(2,1)} fusion(bf16[8,2,192,384]{3,2,1,0:T(8,128)(2,1)S(1)} %divide_convert_fusion, f32[8,384,192,2]{1,2,3,0:T(8,128)} %fusion.24, f32[8,384,192,2]{1,2,3,0:T(8,128)} %copy-done.2, bf16[192,8,2,128]{3,2,1,0:T(2,128)(2,1)} %reshape_squeeze.6), kind=kOutput, calls=%fused_computation.20 | convolution fusion | flops 315362688 | bytes 13369344 | tf_op jit(solution)/shard_map/gjrk,rgjd->kgd/dot_general | solution.py:58
  174.2 2.3 copy.48
  176.5 2.3 copy.49
  178.7 2.1 pad_maximum_fusion
  180.8 1.5 collective-permute-start.1
  182.3 1.3 fusion.44
  183.7 2.4 fusion.16
  186.1 16.7 %collective-permute-done.1 = bf16[2,192,1024]{2,1,0:T(8,128)(2,1)} collective-permute-done((bf16[2,192,1024]{2,1,0:T(8,128)(2,1)}, bf16[2,192,1024]{2,1,0:T(8,128)(2,1)}, u32[]{:S(2)}, u32[]{:S(2)}) %collective-permute-start.1) | collective-permute-done | bytes 786464 | tf_op jit(solution)/shard_map/ppermute | solution.py:19
  202.8 1.4 fusion.15
  204.1 0.8 reshape.68
  204.9 1.8 fusion.5
  206.7 1.2 reshape.67
  207.9 2.1 pad_maximum_fusion.1
  210.0 2.8 %copy.56 = f32[16,208,32]{2,1,0:T(8,128)} copy(f32[16,208,32]{1,0,2:T(8,128)} %pad_maximum_fusion.1) | data formatting | bytes 851968
  212.8 0.0 reduce-scatter.4.cloned.1.call-update
  212.8 8.3 %fusion.13 = bf16[192,8,2,128]{3,0,2,1:T(8,128)(2,1)} fusion(bf16[8,2,192,384]{3,2,1,0:T(8,128)(2,1)S(1)} %divide_convert_fusion, f32[8,384,192,2]{1,2,3,0:T(8,128)} %fusion.24, f32[8,384,192,2]{1,2,3,0:T(8,128)} %copy-done.2, bf16[192,8,128]{2,0,1:T(8,128)(2,1)} %copy-done.9, bf16[192,8,128]{2,0,1:T(8,128)(2,1)} %copy-done.10), kind=kOutput, calls=%fused_computation.26 | convolution fusion | flops 316935552 | bytes 13369344 | tf_op jit(solution)/shard_map/gjrk,kgd->rgjd/dot_general | solution.py:55
  221.1 2.8 %copy.45 = bf16[192,8,2,128]{3,2,1,0:T(2,128)(2,1)} copy(bf16[192,8,2,128]{3,0,2,1:T(8,128)(2,1)} %fusion.13) | data formatting | bytes 1572864 | tf_op jit(solution)/shard_map/convert_element_type | solution.py:65
  224.0 3.2 %convert_element_type.65 = bf16[1,192,2048]{2,1,0:T(8,128)(2,1)} reshape(bf16[192,8,2,128]{3,2,1,0:T(2,128)(2,1)} %copy.45) | data formatting | bytes 1572864 | tf_op jit(solution)/shard_map/convert_element_type | solution.py:65
  227.1 1.9 fusion.12
  229.0 0.8 copy.43
  229.8 1.5 convert_element_type.60
  231.3 40.9 %reduce-scatter.4.cloned.1.call-done = f32[208,32]{1,0:T(8,128)} async-done(((f32[3328,32]{1,0:T(8,128)}), f32[208,32]{1,0:T(8,128)}) %reduce-scatter.4.cloned.1.call-update) | async-done | bytes 26640
  272.2 0.9 slice.48
  273.1 0.7 copy.59
  273.8 0.8 slice.49
  274.6 0.7 copy.60
  (22 shorter events, 0.1 us)
Async XLA Ops:
  7.2 77.4 %copy-start = (bf16[1,192,2304]{2,1,0:T(8,128)(2,1)S(1)}, bf16[1,192,2304]{2,1,0:T(8,128)(2,1)}, u32[]{:S(2)}) copy-start(bf16[1,192,2304]{2,1,0:T(8,128)(2,1)} %param.6) | copy-start | bytes 2654212
  7.2 55.6 %all-gather.4.cloned.1.call-start = ((), (), s32[]{:S(2)}) async-start(), calls=%async_computation.1 | async-start | bytes 2949120 | tf_op jit(solution)/shard_map/all_gather | solution.py:75
  7.9 121.7 %all-gather.6.cloned.1.call-start = ((), (), s32[]{:S(2)}) async-start(), calls=%async_computation.2 | async-start | bytes 11796480 | tf_op jit(solution)/shard_map/all_gather | solution.py:79
  62.8 209.4 %reduce-scatter.4.cloned.1.call-start = ((), (), s32[]{:S(2)}) async-start(), calls=%async_computation.3 | async-start | bytes 1810432
  84.0 99.6 %copy-start.5 = (bf16[2,16,1024]{2,1,0:T(8,128)(2,1)}, bf16[2,16,1024]{2,1,0:T(8,128)(2,1)S(1)}, u32[]{:S(2)}) copy-start(bf16[2,16,1024]{2,1,0:T(8,128)(2,1)S(1)} %reshape.66) | copy-start | bytes 196612
  84.9 54.7 %copy-start.6 = (bf16[1,192,2048]{2,1,0:T(8,128)(2,1)S(1)}, bf16[1,192,2048]{2,1,0:T(8,128)(2,1)}, u32[]{:S(2)}) copy-start(bf16[1,192,2048]{2,1,0:T(8,128)(2,1)} %param.7) | copy-start | bytes 2359300
  84.9 56.2 %copy-start.7 = (bf16[1,192,2048]{2,1,0:T(8,128)(2,1)S(1)}, bf16[1,192,2048]{2,1,0:T(8,128)(2,1)}, u32[]{:S(2)}) copy-start(bf16[1,192,2048]{2,1,0:T(8,128)(2,1)} %param.11) | copy-start | bytes 2359300
  135.7 20.2 %collective-permute-start = (bf16[2,192,1024]{2,1,0:T(8,128)(2,1)S(1)}, bf16[2,192,1024]{2,1,0:T(8,128)(2,1)}, u32[]{:S(2)}, u32[]{:S(2)}) collective-permute-start(bf16[2,192,1024]{2,1,0:T(8,128)(2,1)S(1)} %fusion.10), channel_id=1, source_target_pairs={{0,4},{4,8},{8,12},{1,5},{5,9},{9,13},{2,6},{6,10},{10,14},{3,7},{... | collective-permute-start | bytes 2359304 | tf_op jit(solution)/shard_map/ppermute | solution.py:19
  142.6 14.7 %copy-start.8 = (bf16[192,8,2,128]{3,2,1,0:T(2,128)(2,1)S(1)}, bf16[192,8,2,128]{3,2,1,0:T(2,128)(2,1)}, u32[]{:S(2)}) copy-start(bf16[192,8,2,128]{3,2,1,0:T(2,128)(2,1)} %reshape_squeeze.6) | copy-start | bytes 2359300
  142.8 19.7 %copy-start.3 = (bf16[192,8,128]{2,0,1:T(8,128)(2,1)}, bf16[192,8,128]{2,0,1:T(8,128)(2,1)S(1)}, u32[]{:S(2)}) copy-start(bf16[192,8,128]{2,0,1:T(8,128)(2,1)S(1)} %copy.39) | copy-start | bytes 1179652
  143.0 16.2 %copy-start.9 = (bf16[192,8,128]{2,0,1:T(8,128)(2,1)}, bf16[192,8,128]{2,0,1:T(8,128)(2,1)S(1)}, u32[]{:S(2)}) copy-start(bf16[192,8,128]{2,0,1:T(8,128)(2,1)S(1)} %copy.41) | copy-start | bytes 1179652
  157.2 5.3 %copy-start.4 = (bf16[192,8,128]{2,0,1:T(8,128)(2,1)}, bf16[192,8,128]{2,0,1:T(8,128)(2,1)S(1)}, u32[]{:S(2)}) copy-start(bf16[192,8,128]{2,0,1:T(8,128)(2,1)S(1)} %copy.38) | copy-start | bytes 1179652
  157.4 1.8 copy-start.10
  159.2 3.3 %copy-start.2 = (f32[8,384,192,2]{1,2,3,0:T(8,128)}, f32[8,384,192,2]{1,2,3,0:T(8,128)S(1)}, u32[]{:S(2)}) copy-start(f32[8,384,192,2]{1,2,3,0:T(8,128)S(1)} %get-tuple-element.9) | copy-start | bytes 14155780
  159.2 1.7 copy-start.1
  180.8 21.9 %collective-permute-start.1 = (bf16[2,192,1024]{2,1,0:T(8,128)(2,1)}, bf16[2,192,1024]{2,1,0:T(8,128)(2,1)}, u32[]{:S(2)}, u32[]{:S(2)}) collective-permute-start(bf16[2,192,1024]{2,1,0:T(8,128)(2,1)} %pad_maximum_fusion), channel_id=1, source_target_pairs={{4,0},{8,4},{12,8},{5,1},{9,5},{13,9},{6,2},{10,6},{14,10},{7,3},{... | collective-permute-start | bytes 2359304 | tf_op jit(solution)/shard_map/ppermute | solution.py:19
Sparse Core Ops, SparseCore 0:
  9.6 53.1 all-gather.3
  64.4 65.1 all-gather.5
  212.9 59.2 reduce-scatter.3

commit v2 on v1

--- a/solution.py
+++ b/solution.py
@@ -72,13 +72,15 @@
     low_rank = jnp.einsum(
         "rd,mkd->mrk", row_block, down_full, preferred_element_type=jnp.float32
     ).astype(jnp.bfloat16)
-    partial_weight = lax.all_gather(kv_weight, "ctx", axis=1, tiled=True)
+    row_shards, col_shards = lax.axis_size("ctx"), lax.axis_size(("dp", "sub"))
+    gathered = lax.all_gather(kv_weight, ("ctx", "dp", "sub"), axis=0, tiled=False)
+    gathered = gathered.reshape((row_shards, col_shards) + kv_weight.shape)
     base_part = jnp.einsum(
-        "rd,mdc->mrc",
-        row_block,
-        lax.all_gather(partial_weight, ("dp", "sub"), axis=2, tiled=True),
+        "rcd,cimdn->mrin",
+        row_block.reshape(row_block.shape[0], row_shards, kv_weight.shape[1]),
+        gathered,
         preferred_element_type=jnp.float32,
-    )
+    ).reshape(2, row_block.shape[0], col_shards * kv_weight.shape[2])
     extra_part = jnp.einsum("mrk,mkc->mrc", low_rank, up_full, preferred_element_type=jnp.float32)
     key_value = (base_part + adapter_scale * extra_part).astype(jnp.bfloat16)
     return (low_rank, key_value)
@@ -100,6 +102,7 @@
 def scatter_adapter_grads(down_terms, up_terms):
     axes = ("ctx", "dp", "sub")
     shards = lax.axis_size(axes)
+    row_shards, col_shards = lax.axis_size("ctx"), lax.axis_size(("dp", "sub"))
     members, rank = down_terms.shape[0], down_terms.shape[1]
 
     def shard_major(terms):
@@ -108,9 +111,11 @@
 
     down_cols = down_terms.shape[2] // shards
     joined = jnp.concatenate([shard_major(down_terms), shard_major(up_terms)], axis=1)
-    mine = lax.psum_scatter(
-        joined.reshape(-1, members * rank), axes, scatter_dimension=0, tiled=True
+    joined = joined.reshape((row_shards, col_shards) + joined.shape[1:]).swapaxes(0, 1)
+    partial = lax.psum_scatter(
+        joined.reshape(-1, members * rank), ("dp", "sub"), scatter_dimension=0, tiled=True
     )
+    mine = lax.psum_scatter(partial, "ctx", scatter_dimension=0, tiled=True)
 
     def unshard(piece):
         return piece.reshape(-1, members, rank).transpose(1, 2, 0)
@@ -126,29 +131,32 @@
     down_full, up_full = gather_adapters(adapter_down, adapter_up)
     is_first = lax.axis_index("ctx") == 0
     low_rank, key_value = project_rows(rows_own, kv_weight, down_full, up_full)
-    previous = shifted(key_value, "ctx", 1)
-    key_rows = jnp.concatenate([previous[0], key_value[0]], axis=0)
-    value_rows = jnp.concatenate([previous[1], key_value[1]], axis=0)
+    width = key_value.shape[2]
+    previous = shifted(jnp.concatenate([key_value, low_rank], axis=2), "ctx", 1)
+    low_previous = previous[:, :, width:]
+    key_rows = jnp.concatenate([previous[0, :, :width], key_value[0]], axis=0)
+    value_rows = jnp.concatenate([previous[1, :, :width], key_value[1]], axis=0)
     attended, query_grad, kv_grads = attend(query_rows, key_rows, value_rows, grad_rows, is_first)
     kv_rounded = kv_grads.astype(jnp.bfloat16)
     far_part = kv_rounded[:, :length]
     near_part = kv_rounded[:, length:]
-    returned = shifted(far_part, "ctx", -1)
-    sources = (rows_own, rows_own)
-    low_parts = (low_rank, low_rank)
-    pieces = (near_part, returned)
-    down_terms = jnp.zeros(down_full.shape, jnp.float32)
-    up_terms = jnp.zeros(up_full.shape, jnp.float32)
-    for source, low_piece, piece_rows in zip(sources, low_parts, pieces):
-        projected = jnp.einsum(
-            "mrc,mkc->mrk", piece_rows, up_full, preferred_element_type=jnp.float32
-        ).astype(jnp.bfloat16)
-        down_terms = down_terms + jnp.einsum(
-            "mrk,rd->mkd", projected, source, preferred_element_type=jnp.float32
-        )
-        up_terms = up_terms + jnp.einsum(
-            "mrk,mrc->mkc", low_piece, piece_rows, preferred_element_type=jnp.float32
-        )
+    projected_far = jnp.einsum(
+        "mrc,mkc->mrk", far_part, up_full, preferred_element_type=jnp.float32
+    ).astype(jnp.bfloat16)
+    projected_returned = shifted(projected_far, "ctx", -1)
+    projected_near = jnp.einsum(
+        "mrc,mkc->mrk", near_part, up_full, preferred_element_type=jnp.float32
+    ).astype(jnp.bfloat16)
+    up_terms = jnp.einsum(
+        "mrk,mrc->mkc", low_rank, near_part, preferred_element_type=jnp.float32
+    ) + jnp.einsum(
+        "mrk,mrc->mkc", low_previous, far_part, preferred_element_type=jnp.float32
+    )
+    down_terms = jnp.einsum(
+        "mrk,rd->mkd", projected_near, rows_own, preferred_element_type=jnp.float32
+    ) + jnp.einsum(
+        "mrk,rd->mkd", projected_returned, rows_own, preferred_element_type=jnp.float32
+    )
     factor = adapter_scale / (lax.axis_size("dp") * lax.axis_size("sub"))
     down_part, up_part = scatter_adapter_grads(down_terms * factor, up_terms * factor)
     return (attended[None], query_grad[None], down_part, up_part)

time: 283 us -> 228 us (0.81)
  waiting for transfers between devices: 171 us -> 109 us
  blocking collectives: 20 us -> 24.5 us
  local copies, waits for them, and re-layouts: 26.2 us -> 29.4 us
    all_gather x2 -> x1, waiting for transfers between devices: 99.5 us -> 56.4 us  [project_rows(): lax.all_gather(kv_weight, ('ctx', 'dp', 'sub'), axis=0, tiled=False)]
    ppermute x2, waiting for transfers between devices: 29.6 us -> 15.4 us  [shifted(): return lax.ppermute(value, axis, pairs)]
    all_gather x1, blocking collectives: 20 us -> 24.5 us  [gather_adapters(): gathered = lax.all_gather(joined, axes, axis=0, tiled=False)]
    unnamed x4 -> x5, waiting for transfers between devices: 41.6 us -> 37.2 us
    dot_general x5 -> x6, matrix products: 12.6 us -> 14.2 us  [the longest x1 5.67 us: project_rows(): jnp.einsum('rcd,cimdn->mrin', row_block.reshape(row_block.shape[0], row_s...]
  transfers between devices with their start and end apart: 5 -> 5, of which waited for: 5 -> 5; matrix products, arithmetic and copies ran while one was open for 10% -> 14% of each run, Pallas kernels for 0% -> 0%
where the time goes in v2:
time: 228 us; the launch traced here: 227 us
  waiting for transfers between devices  109 us (48%)
  matrix products  40 us (18%)
  local copies, waits for them, and re-layouts  29.4 us (13%)
  blocking collectives  24.5 us (11%)
  between operations  14.1 us (6%)
  starting transfers between devices  5.05 us (2%)
  other arithmetic  4.67 us (2%)
    all_gather x1, waiting for transfers between devices, project_rows(): lax.all_gather(kv_weight, ('ctx', 'dp', 'sub'), axis=0, tiled=False)  56.4 us
    unnamed x5, waiting for transfers between devices  37.2 us
    all_gather x1, blocking collectives, gather_adapters(): gathered = lax.all_gather(joined, axes, axis=0, tiled=False)  24.5 us
    ppermute x2, waiting for transfers between devices, shifted(): return lax.ppermute(value, axis, pairs)  15.4 us
    dot_general x1, matrix products, attend(): jnp.einsum('gjrk,rgjd->kgd', score_grad, queries_g, preferred_element_typ...  8.55 us
    dot_general x1, matrix products, attend(): jnp.einsum('gjrk,kgd->rgjd', score_grad, keys_g, preferred_element_type=j...  8.15 us
    convert_element_type x2, local copies, waits for them, and re-layouts, attend(): head_qgrad.reshape(length, HEADS * HEAD_DIM).astype(jnp.bfloat16)  6.06 us
    dot_general x1, matrix products, project_rows(): jnp.einsum('rcd,cimdn->mrin', row_block.reshape(row_block.shape[0], row_s...  5.67 us
  transfers between devices with their start and end apart: 5, of which 5 were waited for; matrix products, arithmetic and copies ran while one was open for 14% of the time, Pallas kernels for 0%

profile of v2, /device:TPU:0, one launch (start us, length us, event | category | flops | bytes accessed | tf_op | source)
XLA Modules:
  0.0 226.8 jit_solution(4559958009668613254)
XLA Ops:
  7.2 0.7 all-gather.4.cloned.1.call-update
  7.9 0.8 pad_maximum_fusion.4
  8.8 24.5 %all-gather.1 = bf16[32,16,208]{2,1,0:T(8,128)(2,1)S(1)} all-gather(bf16[2,16,208]{2,1,0:T(8,128)(2,1)S(1)} %pad_maximum_fusion.4), channel_id=3, replica_groups=mesh['groups'=2,'ctx'=4,'dp'=2,'sub'=2] {'ctx','dp','sub'}, dimensions={0}, use_global_device_ids=true | all-gather | bytes 226304 | tf_op jit(solution)/shard_map/all_gather | solution.py:93
  33.3 0.1 slice.45
  33.4 0.1 copy.107
  33.4 0.1 reshape.75
  33.6 0.2 copy.106
  33.7 0.3 reshape.74
  34.1 2.6 %reshape_squeeze.9 = bf16[192,4,576]{2,1,0:T(4,128)(2,1)S(1)} reshape(bf16[1,192,2304]{2,1,0:T(8,128)(2,1)} %param.6) | data formatting | bytes 1769472 | tf_op jit(solution)/shard_map/reshape;squeeze | solution.py:80
  36.7 1.5 convolution_convert_fusion.3
  38.2 0.2 copy.51
  38.4 56.4 %all-gather.4.cloned.1.call-done = bf16[32,576,256]{2,1,0:T(8,128)(2,1)} async-done(((bf16[2,576,256]{2,1,0:T(8,128)(2,1)}), bf16[32,576,256]{2,1,0:T(8,128)(2,1)}) %all-gather.4.cloned.1.call-update) | async-done | bytes 9437200 | tf_op jit(solution)/shard_map/all_gather | solution.py:76
  94.8 5.7 %convolution_bitcast_fusion = f32[4,2,24,8,256]{4,3,2,1,0:T(8,128)S(1)} fusion(bf16[4,4,2,576,256]{4,3,2,1,0:T(8,128)(2,1)} %bitcast.168, bf16[192,4,576,1,1]{2,1,0,4,3:T(4,128)(2,1)S(1)} %bitcast.162), kind=kOutput, calls=%fused_computation.22 | convolution fusion | flops 1811939328 | bytes 11894784 | tf_op jit(solution)/shard_map/rcd,cimdn->mrin/dot_general | solution.py:78
  100.5 0.2 copy.87
  100.7 0.4 add_convert_fusion
  101.1 1.0 pad_maximum_fusion
  102.1 3.4 %collective-permute-start = (bf16[2,192,1040]{2,1,0:T(8,128)(2,1)}, bf16[2,192,1040]{2,1,0:T(8,128)(2,1)}, u32[]{:S(2)}, u32[]{:S(2)}) collective-permute-start(bf16[2,192,1040]{2,1,0:T(8,128)(2,1)} %pad_maximum_fusion), channel_id=1, source_target_pairs={{0,4},{4,8},{8,12},{1,5},{5,9},{9,13},{2,6},{6,10},{10,14},{3,7},{... | collective-permute-start | bytes 2396168 | tf_op jit(solution)/shard_map/ppermute | solution.py:19
  105.5 0.6 reshape_squeeze.10
  106.1 2.8 %reshape_squeeze.11 = bf16[192,8,2,128]{3,2,1,0:T(2,128)(2,1)S(1)} reshape(bf16[1,192,2048]{2,1,0:T(8,128)(2,1)} %param.11) | data formatting | bytes 1572864 | tf_op jit(solution)/shard_map/reshape;squeeze | solution.py:26
  109.0 0.1 fusion.28
  109.1 0.1 slice_bitcast_fusion.2
  109.2 0.1 copy.89
  109.3 0.1 copy.53
  109.3 0.1 copy.91
  109.4 0.1 copy.55
  109.5 14.8 %collective-permute-done = bf16[2,192,1040]{2,1,0:T(8,128)(2,1)} collective-permute-done((bf16[2,192,1040]{2,1,0:T(8,128)(2,1)}, bf16[2,192,1040]{2,1,0:T(8,128)(2,1)}, u32[]{:S(2)}, u32[]{:S(2)}) %collective-permute-start) | collective-permute-done | bytes 798752 | tf_op jit(solution)/shard_map/ppermute | solution.py:19
  124.2 1.2 slice_bitcast_fusion.3
  125.4 0.1 copy.88
  125.5 0.1 copy.52
  125.6 0.1 copy.90
  125.6 0.1 copy.54
  125.7 1.8 fusion.6
  127.6 1.6 divide_convert_fusion
  129.1 1.6 bitcast_convert_fusion
  130.7 3.0 %fusion.22 = f32[8,384,192,2]{1,2,3,0:T(8,128)} fusion(bf16[192,8,2,128]{3,2,1,0:T(2,128)(2,1)S(1)} %reshape_squeeze.11, bf16[192,8,128]{2,0,1:T(8,128)(2,1)S(1)} %copy.53, bf16[192,8,128]{2,0,1:T(8,128)(2,1)S(1)} %copy.52), kind=kOutput, calls=%fused_computation.44 | convolution fusion | flops 303562752 | bytes 6291456 | tf_op jit(solution)/shard_map/rgjd,kgd->gjrk/dot_general | solution.py:47
  133.7 8.5 %bitcast_convert_fusion.1 = bf16[8,384,128]{1,2,0:T(8,128)(2,1)} fusion(bf16[8,2,192,384]{3,2,1,0:T(8,128)(2,1)S(1)} %divide_convert_fusion, f32[8,384,192,2]{1,2,3,0:T(8,128)} %fusion.22, f32[8,384,192,2]{1,2,3,0:T(8,128)} %copy-done.1, bf16[192,8,2,128]{3,2,1,0:T(2,128)(2,1)} %copy-done.7), kind=kOutput, calls=%fused_computation.20 | convolution fusion | flops 315362688 | bytes 13369344 | tf_op jit(solution)/shard_map/gjrk,rgjd->kgd/dot_general | solution.py:58
  142.3 2.4 %copy.62 = bf16[1,384,1024]{2,1,0:T(8,128)(2,1)} copy(bf16[1,384,1024]{1,2,0:T(8,128)(2,1)} %bitcast.163) | data formatting | bytes 1572864 | tf_op jit(solution)/shard_map/stack;reshape | solution.py:68
  144.6 2.3 %copy.63 = bf16[1,384,1024]{2,1,0:T(8,128)(2,1)} copy(bf16[1,384,1024]{1,2,0:T(8,128)(2,1)} %bitcast.154) | data formatting | bytes 1572864 | tf_op jit(solution)/shard_map/stack;reshape | solution.py:68
  146.9 1.4 convolution_convert_fusion.1
  148.3 1.3 fusion.45
  149.7 2.4 %fusion.15 = f32[2,16,2304]{2,1,0:T(8,128)} fusion(bf16[2,16,1024]{2,1,0:T(8,128)(2,1)S(1)} %reshape.75, bf16[1,192,2304]{2,1,0:T(8,128)(2,1)S(1)} %copy-done, bf16[1,384,1024]{2,1,0:T(8,128)(2,1)} %copy.62, bf16[1,384,1024]{2,1,0:T(8,128)(2,1)} %copy.63), kind=kOutput, calls=%fused_computation.33 | convolution fusion | flops 41293824 | bytes 2818048 | tf_op jit(solution)/shard_map/mrk,rd->mkd/dot_general | solution.py:155
  152.1 1.5 collective-permute-start.1
  153.6 2.1 fusion.14
  155.7 1.1 concatenate.39
  156.8 0.8 copy.66
  157.6 0.6 collective-permute-done.1
  158.2 1.2 fusion.5
  159.4 0.8 concatenate.38
  160.2 0.1 copy.65
  160.4 1.2 maximum_bitcast_fusion.2
  161.5 1.8 copy.82
  163.3 0.0 reduce-scatter.9.cloned.1.call-start
  163.4 8.2 %fusion.12 = bf16[192,8,2,128]{3,0,2,1:T(8,128)(2,1)} fusion(bf16[8,2,192,384]{3,2,1,0:T(8,128)(2,1)S(1)} %divide_convert_fusion, f32[8,384,192,2]{1,2,3,0:T(8,128)} %fusion.22, f32[8,384,192,2]{1,2,3,0:T(8,128)} %copy-done.1, bf16[192,8,128]{2,0,1:T(8,128)(2,1)S(1)} %copy-done.9, bf16[192,8,128]{2,0,1:T(8,128)(2,1)} %copy-done.10), kind=kOutput, calls=%fused_computation.26 | convolution fusion | flops 316935552 | bytes 13369344 | tf_op jit(solution)/shard_map/gjrk,kgd->rgjd/dot_general | solution.py:55
  171.6 2.9 %copy.59 = bf16[192,8,2,128]{3,2,1,0:T(2,128)(2,1)} copy(bf16[192,8,2,128]{3,0,2,1:T(8,128)(2,1)} %fusion.12) | data formatting | bytes 1572864 | tf_op jit(solution)/shard_map/convert_element_type | solution.py:65
  174.5 3.1 %convert_element_type.68 = bf16[1,192,2048]{2,1,0:T(8,128)(2,1)} reshape(bf16[192,8,2,128]{3,2,1,0:T(2,128)(2,1)} %copy.59) | data formatting | bytes 1572864 | tf_op jit(solution)/shard_map/convert_element_type | solution.py:65
  177.6 16.3 %reduce-scatter.7.cloned.1.call-done = f32[832,32]{1,0:T(8,128)} async-done(((f32[3328,32]{1,0:T(8,128)}), f32[832,32]{1,0:T(8,128)}) %reduce-scatter.7.cloned.1.call-update) | async-done | bytes 106512
  194.0 0.8 fusion.11
  194.7 0.8 copy.57
  195.5 1.5 convert_element_type.63
  197.0 20.2 %reduce-scatter.9.cloned.1.call-done = f32[208,32]{1,0:T(8,128)} async-done(((f32[832,32]{1,0:T(8,128)}), f32[208,32]{1,0:T(8,128)}) %reduce-scatter.9.cloned.1.call-update) | async-done | bytes 26640
  217.2 0.9 slice.53
  218.1 0.7 copy.85
  218.8 0.8 slice.54
  219.6 0.7 copy.86
  (28 shorter events, 0.2 us)
Async XLA Ops:
  7.2 87.6 %all-gather.4.cloned.1.call-start = ((), (), s32[]{:S(2)}) async-start(), calls=%async_computation.2 | async-start | bytes 10027008 | tf_op jit(solution)/shard_map/all_gather | solution.py:76
  7.9 186.0 %reduce-scatter.7.cloned.1.call-start = ((), (), s32[]{:S(2)}) async-start(), calls=%async_computation.3 | async-start | bytes 2129920
  100.5 5.1 %copy-start.6 = (bf16[1,192,2048]{2,1,0:T(8,128)(2,1)S(1)}, bf16[1,192,2048]{2,1,0:T(8,128)(2,1)}, u32[]{:S(2)}) copy-start(bf16[1,192,2048]{2,1,0:T(8,128)(2,1)} %param.7) | copy-start | bytes 2359300
  102.1 22.1 %collective-permute-start = (bf16[2,192,1040]{2,1,0:T(8,128)(2,1)}, bf16[2,192,1040]{2,1,0:T(8,128)(2,1)}, u32[]{:S(2)}, u32[]{:S(2)}) collective-permute-start(bf16[2,192,1040]{2,1,0:T(8,128)(2,1)} %pad_maximum_fusion), channel_id=1, source_target_pairs={{0,4},{4,8},{8,12},{1,5},{5,9},{9,13},{2,6},{6,10},{10,14},{3,7},{... | collective-permute-start | bytes 2396168 | tf_op jit(solution)/shard_map/ppermute | solution.py:19
  106.1 19.6 %copy-start.7 = (bf16[192,8,2,128]{3,2,1,0:T(2,128)(2,1)}, bf16[192,8,2,128]{3,2,1,0:T(2,128)(2,1)S(1)}, u32[]{:S(2)}) copy-start(bf16[192,8,2,128]{3,2,1,0:T(2,128)(2,1)S(1)} %reshape_squeeze.10) | copy-start | bytes 2359300
  109.3 21.4 %copy-start.2 = (bf16[192,8,128]{2,0,1:T(8,128)(2,1)}, bf16[192,8,128]{2,0,1:T(8,128)(2,1)S(1)}, u32[]{:S(2)}) copy-start(bf16[192,8,128]{2,0,1:T(8,128)(2,1)S(1)} %copy.53) | copy-start | bytes 1179652
  109.5 18.1 %copy-start.8 = (bf16[192,8,128]{2,0,1:T(8,128)(2,1)}, bf16[192,8,128]{2,0,1:T(8,128)(2,1)S(1)}, u32[]{:S(2)}) copy-start(bf16[192,8,128]{2,0,1:T(8,128)(2,1)S(1)} %copy.55) | copy-start | bytes 1179652
  125.5 5.2 %copy-start.4 = (bf16[192,8,128]{2,0,1:T(8,128)(2,1)}, bf16[192,8,128]{2,0,1:T(8,128)(2,1)S(1)}, u32[]{:S(2)}) copy-start(bf16[192,8,128]{2,0,1:T(8,128)(2,1)S(1)} %copy.52) | copy-start | bytes 1179652
  125.7 1.8 copy-start.10
  127.5 3.2 %copy-start.1 = (f32[8,384,192,2]{1,2,3,0:T(8,128)}, f32[8,384,192,2]{1,2,3,0:T(8,128)S(1)}, u32[]{:S(2)}) copy-start(f32[8,384,192,2]{1,2,3,0:T(8,128)S(1)} %get-tuple-element.9) | copy-start | bytes 14155780
  142.3 7.4 %copy-start = (bf16[1,192,2304]{2,1,0:T(8,128)(2,1)S(1)}, bf16[1,192,2304]{2,1,0:T(8,128)(2,1)}, u32[]{:S(2)}) copy-start(bf16[1,192,2304]{2,1,0:T(8,128)(2,1)} %param.6) | copy-start | bytes 2654212
  152.1 6.1 %collective-permute-start.1 = (bf16[2,192,16]{1,2,0:T(8,128)(2,1)S(1)}, bf16[2,192,16]{1,2,0:T(8,128)(2,1)S(1)}, u32[]{:S(2)}, u32[]{:S(2)}) collective-permute-start(bf16[2,192,16]{1,2,0:T(8,128)(2,1)S(1)} %convolution_convert_fusion.1), channel_id=1, source_target_pairs={{4,0},{8,4},{12,8},{5,1},{9,5},{13,9},{6,2},{10,6},{14,10},{7,3},{... | collective-permute-start | bytes 36872 | tf_op jit(solution)/shard_map/ppermute | solution.py:19
  160.2 3.2 %copy-start.9 = (bf16[192,8,128]{2,0,1:T(8,128)(2,1)S(1)}, bf16[192,8,128]{2,0,1:T(8,128)(2,1)}, u32[]{:S(2)}) copy-start(bf16[192,8,128]{2,0,1:T(8,128)(2,1)} %copy-done.8) | copy-start | bytes 1179652
  163.3 30.6 %copy-start.3 = (bf16[192,8,128]{2,0,1:T(8,128)(2,1)S(1)}, bf16[192,8,128]{2,0,1:T(8,128)(2,1)}, u32[]{:S(2)}) copy-start(bf16[192,8,128]{2,0,1:T(8,128)(2,1)} %copy-done.2) | copy-start | bytes 1179652
  163.3 30.6 %copy-start.5 = (bf16[192,8,128]{2,0,1:T(8,128)(2,1)S(1)}, bf16[192,8,128]{2,0,1:T(8,128)(2,1)}, u32[]{:S(2)}) copy-start(bf16[192,8,128]{2,0,1:T(8,128)(2,1)} %copy-done.4) | copy-start | bytes 1179652
  163.3 53.9 %reduce-scatter.9.cloned.1.call-start = ((), (), s32[]{:S(2)}) async-start(), calls=%async_computation.4 | async-start | bytes 532480
Sparse Core Ops, SparseCore 0:
  10.3 84.4 all-gather.3
  163.4 30.4 reduce-scatter.6
  196.3 20.8 reduce-scatter.8

commit v3 on v2

--- a/solution.py
+++ b/solution.py
@@ -22,50 +22,54 @@
 def attend(query_rows, key_rows, value_rows, grad_rows, is_first):
     length = query_rows.shape[0]
     group_size = HEADS // KV_HEADS
-    queries_g = query_rows.reshape(length, KV_HEADS, group_size, HEAD_DIM)
-    grads_g = grad_rows.reshape(length, KV_HEADS, group_size, HEAD_DIM)
-    keys_g = key_rows.reshape(2 * length, KV_HEADS, HEAD_DIM)
-    values_g = value_rows.reshape(2 * length, KV_HEADS, HEAD_DIM)
-    query_pos = lax.broadcasted_iota(jnp.int32, (length, 2 * length), 0)
-    key_pos = lax.broadcasted_iota(jnp.int32, (length, 2 * length), 1)
+
+    def by_head(rows):
+        return (
+            rows.reshape(length, KV_HEADS, group_size, HEAD_DIM)
+            .transpose(1, 2, 0, 3)
+            .reshape(KV_HEADS, group_size * length, HEAD_DIM)
+        )
+
+    def from_head(parts):
+        return (
+            parts.reshape(KV_HEADS, group_size, length, HEAD_DIM)
+            .transpose(2, 0, 1, 3)
+            .reshape(length, HEADS * HEAD_DIM)
+            .astype(jnp.bfloat16)
+        )
+
+    queries_g = by_head(query_rows)
+    grads_g = by_head(grad_rows)
+    keys_g = key_rows.reshape(2 * length, KV_HEADS, HEAD_DIM).transpose(1, 0, 2)
+    values_g = value_rows.reshape(2 * length, KV_HEADS, HEAD_DIM).transpose(1, 0, 2)
+    query_pos = lax.broadcasted_iota(jnp.int32, (group_size * length, 2 * length), 0) % length
+    key_pos = lax.broadcasted_iota(jnp.int32, (group_size * length, 2 * length), 1)
     visible = (
         (key_pos > query_pos)
         & (key_pos <= query_pos + length)
         & (jnp.logical_not(is_first) | (key_pos >= length))
     )
     raw_score = (
-        jnp.einsum("rgjd,kgd->gjrk", queries_g, keys_g, preferred_element_type=jnp.float32)
+        jnp.einsum("gqd,gkd->gqk", queries_g, keys_g, preferred_element_type=jnp.float32)
         * query_scale
     )
     bent_score = jnp.tanh(raw_score / logit_cap)
     expo_terms = jnp.where(visible, jnp.exp(logit_cap * bent_score), 0.0)
     denominator = jnp.sum(expo_terms, axis=-1, keepdims=True)
     attn_prob = (expo_terms / denominator).astype(jnp.bfloat16)
-    head_out = jnp.einsum(
-        "gjrk,kgd->rgjd", attn_prob, values_g, preferred_element_type=jnp.float32
-    )
-    prob_grad = jnp.einsum(
-        "rgjd,kgd->gjrk", grads_g, values_g, preferred_element_type=jnp.float32
-    )
+    head_out = jnp.einsum("gqk,gkd->gqd", attn_prob, values_g, preferred_element_type=jnp.float32)
+    prob_grad = jnp.einsum("gqd,gkd->gqk", grads_g, values_g, preferred_element_type=jnp.float32)
     prob_wide = attn_prob.astype(jnp.float32)
     row_delta = jnp.sum(prob_wide * prob_grad, axis=-1, keepdims=True)
     score_grad = (
         prob_wide * (prob_grad - row_delta) * (1.0 - bent_score * bent_score) * query_scale
     ).astype(jnp.bfloat16)
-    head_qgrad = jnp.einsum(
-        "gjrk,kgd->rgjd", score_grad, keys_g, preferred_element_type=jnp.float32
-    )
-    key_part = jnp.einsum(
-        "gjrk,rgjd->kgd", score_grad, queries_g, preferred_element_type=jnp.float32
-    )
-    value_part = jnp.einsum(
-        "gjrk,rgjd->kgd", attn_prob, grads_g, preferred_element_type=jnp.float32
-    )
-    attended = head_out.reshape(length, HEADS * HEAD_DIM).astype(jnp.bfloat16)
-    query_grad = head_qgrad.reshape(length, HEADS * HEAD_DIM).astype(jnp.bfloat16)
+    head_qgrad = jnp.einsum("gqk,gkd->gqd", score_grad, keys_g, preferred_element_type=jnp.float32)
+    key_part = jnp.einsum("gqk,gqd->kgd", score_grad, queries_g, preferred_element_type=jnp.float32)
+    value_part = jnp.einsum("gqk,gqd->kgd", attn_prob, grads_g, preferred_element_type=jnp.float32)
     key_grad = key_part.reshape(2 * length, KV_HEADS * HEAD_DIM)
     value_grad = value_part.reshape(2 * length, KV_HEADS * HEAD_DIM)
-    return (attended, query_grad, jnp.stack([key_grad, value_grad]))
+    return (from_head(head_out), from_head(head_qgrad), jnp.stack([key_grad, value_grad]))
 
 
 def project_rows(row_block, kv_weight, down_full, up_full):
@@ -128,14 +132,16 @@
     query_rows = queries[0]
     grad_rows = out_grad[0]
     length = rows_own.shape[0]
+    rows_previous = shifted(rows_own, "ctx", 1)
     down_full, up_full = gather_adapters(adapter_down, adapter_up)
     is_first = lax.axis_index("ctx") == 0
-    low_rank, key_value = project_rows(rows_own, kv_weight, down_full, up_full)
-    width = key_value.shape[2]
-    previous = shifted(jnp.concatenate([key_value, low_rank], axis=2), "ctx", 1)
-    low_previous = previous[:, :, width:]
-    key_rows = jnp.concatenate([previous[0, :, :width], key_value[0]], axis=0)
-    value_rows = jnp.concatenate([previous[1, :, :width], key_value[1]], axis=0)
+    low_both, kv_both = project_rows(
+        jnp.concatenate([rows_previous, rows_own], axis=0), kv_weight, down_full, up_full
+    )
+    low_previous = low_both[:, :length]
+    low_rank = low_both[:, length:]
+    key_rows = kv_both[0]
+    value_rows = kv_both[1]
     attended, query_grad, kv_grads = attend(query_rows, key_rows, value_rows, grad_rows, is_first)
     kv_rounded = kv_grads.astype(jnp.bfloat16)
     far_part = kv_rounded[:, :length]

time: 228 us -> 218 us (0.956)
  waiting for transfers between devices: 109 us -> 63.6 us
  blocking collectives: 24.5 us -> 47.6 us
  local copies, waits for them, and re-layouts: 29.4 us -> 35.3 us
  matrix products: 40 us -> 45 us
  starting transfers between devices: 5.05 us -> 7.5 us
    all_gather x1, waiting for transfers between devices: 56.4 us -> 28.2 us  [project_rows(): lax.all_gather(kv_weight, ('ctx', 'dp', 'sub'), axis=0, tiled=False)]
    all_gather x1, blocking collectives: 24.5 us -> 47.6 us  [gather_adapters(): gathered = lax.all_gather(joined, axes, axis=0, tiled=False)]
    ppermute x2, waiting for transfers between devices: 15.4 us -> 0.01 us  [shifted(): return lax.ppermute(value, axis, pairs)]
    dot_general x1, matrix products: 5.67 us -> 8.51 us  [project_rows(): jnp.einsum('rcd,cimdn->mrin', row_block.reshape(row_block.shape[0], row_s...]
    transpose x0 -> x3, local copies, waits for them, and re-layouts: none -> 2.38 us  [the longest x2 2.18 us: by_head(): return rows.reshape(length, KV_HEADS, group_size, HEAD_DIM).transpose(1,...]
    ppermute x0 -> x1, local copies, waits for them, and re-layouts: none -> 2.35 us  [shifted(): return lax.ppermute(value, axis, pairs)]
    another operation x5 -> x4, local copies, waits for them, and re-layouts: 10.7 us -> 8.82 us  [the longest x2 5.12 us: by_head(): rows.reshape(length, KV_HEADS, group_size, HEAD_DIM).transpose(1, 2, 0, 3)]
    unnamed x33 -> x27, local copies, waits for them, and re-layouts: 4.86 us -> 6.23 us
  transfers between devices with their start and end apart: 5 -> 5, of which waited for: 5 -> 3; matrix products, arithmetic and copies ran while one was open for 14% -> 17% of each run, Pallas kernels for 0% -> 0%
where the time goes in v3:
time: 218 us; the launch traced here: 217 us
  waiting for transfers between devices  63.6 us (29%)
  blocking collectives  47.6 us (22%)
  matrix products  45 us (21%)
  local copies, waits for them, and re-layouts  35.3 us (16%)
  between operations  14 us (6%)
  starting transfers between devices  7.5 us (3%)
  other arithmetic  3.67 us (2%)
    all_gather x1, blocking collectives, gather_adapters(): gathered = lax.all_gather(joined, axes, axis=0, tiled=False)  47.6 us
    unnamed x5, waiting for transfers between devices  35.4 us
    all_gather x1, waiting for transfers between devices, project_rows(): lax.all_gather(kv_weight, ('ctx', 'dp', 'sub'), axis=0, tiled=False)  28.2 us
    dot_general x1, matrix products, attend(): jnp.einsum('gqk,gkd->gqd', score_grad, keys_g, preferred_element_type=jnp...  8.65 us
    dot_general x1, matrix products, project_rows(): jnp.einsum('rcd,cimdn->mrin', row_block.reshape(row_block.shape[0], row_s...  8.51 us
    dot_general x1, matrix products, attend(): jnp.einsum('gqk,gqd->kgd', score_grad, queries_g, preferred_element_type=...  8.42 us
    convert_element_type x4, local copies, waits for them, and re-layouts, from_head(): return parts.reshape(KV_HEADS, group_size, length, HEAD_DIM).transpose(2,...  8.27 us
    ppermute x2, starting transfers between devices, shifted(): return lax.ppermute(value, axis, pairs)  7.16 us
  transfers between devices with their start and end apart: 5, of which 3 were waited for; matrix products, arithmetic and copies ran while one was open for 17% of the time, Pallas kernels for 0%

profile of v3, /device:TPU:0, one launch (start us, length us, event | category | flops | bytes accessed | tf_op | source)
XLA Modules:
  0.0 216.7 jit_solution(5349081201159808083)
XLA Ops:
  7.2 0.0 all-gather.4.cloned.1.call-start
  7.2 0.7 all-gather.4.cloned.1.call-update
  7.9 0.0 reduce-scatter.7.cloned.1.call-start
  7.9 5.9 %collective-permute-start = (bf16[192,2304]{1,0:T(8,128)(2,1)}, bf16[192,2304]{1,0:T(8,128)(2,1)}, u32[]{:S(2)}, u32[]{:S(2)}) collective-permute-start(bf16[192,2304]{1,0:T(8,128)(2,1)} %bitcast.153), channel_id=1, source_target_pairs={{0,4},{4,8},{8,12},{1,5},{5,9},{9,13},{2,6},{6,10},{10,14},{3,7},{... | collective-permute-start | bytes 2654216 | tf_op jit(solution)/shard_map/ppermute | solution.py:19
  13.8 1.5 copy.73
  15.3 0.8 pad_maximum_fusion.3
  16.2 47.6 %all-gather.1 = bf16[32,16,208]{2,1,0:T(8,128)(2,1)S(1)} all-gather(bf16[2,16,208]{2,1,0:T(8,128)(2,1)S(1)} %pad_maximum_fusion.3), channel_id=3, replica_groups=mesh['groups'=2,'ctx'=4,'dp'=2,'sub'=2] {'ctx','dp','sub'}, dimensions={0}, use_global_device_ids=true | all-gather | bytes 226304 | tf_op jit(solution)/shard_map/all_gather | solution.py:97
  63.8 0.1 slice.41
  63.9 0.2 copy.134
  64.1 0.3 reshape.78
  64.4 0.1 copy.135
  64.4 0.1 reshape.79
  64.6 2.6 %reshape_squeeze.13 = bf16[192,8,2,128]{3,2,1,0:T(2,128)(2,1)S(1)} reshape(bf16[1,192,2048]{2,1,0:T(8,128)(2,1)} %param.7) | data formatting | bytes 1572864 | tf_op jit(solution)/shard_map/reshape;squeeze | solution.py:28
  67.2 1.1 copy.80
  68.3 2.6 %reshape_squeeze.15 = bf16[192,8,2,128]{3,2,1,0:T(2,128)(2,1)S(1)} reshape(bf16[1,192,2048]{2,1,0:T(8,128)(2,1)} %param.11) | data formatting | bytes 1572864 | tf_op jit(solution)/shard_map/reshape;squeeze | solution.py:28
  70.8 1.1 copy.84
  71.9 0.2 fusion.35
  72.2 2.4 %copy.72 = bf16[192,2304]{0,1:T(8,128)(2,1)} copy(bf16[192,2304]{1,0:T(8,128)(2,1)} %collective-permute-done) | data formatting | bytes 1769472 | tf_op jit(solution)/shard_map/ppermute | solution.py:19
  74.5 1.8 fusion.19
  76.3 28.2 %all-gather.4.cloned.1.call-done = bf16[32,576,256]{2,1,0:T(8,128)(2,1)} async-done(((bf16[2,576,256]{2,1,0:T(8,128)(2,1)}), bf16[32,576,256]{2,1,0:T(8,128)(2,1)}) %all-gather.4.cloned.1.call-update) | async-done | bytes 9437200 | tf_op jit(solution)/shard_map/all_gather | solution.py:80
  104.5 8.5 %convolution_bitcast_fusion = f32[2,384,4,256]{1,3,0,2:T(8,128)S(1)} fusion(bf16[4,4,2,576,256]{4,3,2,1,0:T(8,128)(2,1)} %bitcast.180, bf16[192,4,576]{0,2,1:T(8,128)(2,1)S(1)} %bitcast.166, bf16[192,4,576]{0,2,1:T(8,128)(2,1)} %bitcast.167), kind=kOutput, calls=%fused_computation.16 | convolution fusion | flops 3627417600 | bytes 14352384 | tf_op jit(solution)/shard_map/rcd,cimdn->mrin/dot_general | solution.py:82
  113.1 0.2 copy.75
  113.3 2.3 %copy.78 = f32[2,384,1024]{2,1,0:T(8,128)} copy(f32[2,384,1024]{1,2,0:T(8,128)S(1)} %bitcast.152) | data formatting | bytes 6291456 | tf_op jit(solution)/shard_map/reshape | solution.py:87
  115.6 2.6 %add_convert_fusion = bf16[2,384,1024]{2,1,0:T(8,128)(2,1)S(1)} fusion(f32[2,384,1024]{2,1,0:T(8,128)} %copy.78, bf16[2,16,384]{2,1,0:T(8,128)(2,1)S(1)} %fusion.19, bf16[2,16,1024]{2,1,0:T(8,128)(2,1)S(1)} %reshape.79), kind=kOutput, calls=%fused_computation.15 | convolution fusion | flops 27525120 | bytes 4808704 | tf_op jit(solution)/shard_map/mrk,mkc->mrc/dot_general | solution.py:88
  118.2 0.1 slice_bitcast_fusion
  118.3 0.2 copy.112
  118.5 0.2 copy.113
  118.7 0.0 copy-start.1
  118.7 0.7 copy-done.5
  119.4 1.7 fusion.6
  121.0 1.5 divide_convert_fusion
  122.5 0.2 copy-done.3
  122.7 2.9 %fusion.24 = f32[8,384,384]{2,1,0:T(8,128)} fusion(bf16[8,384,128]{2,1,0:T(8,128)(2,1)S(1)} %bitcast.157, bf16[384,8,128]{2,1,0:T(8,128)(2,1)S(1)} %bitcast.155), kind=kOutput, calls=%fused_computation.47 | convolution fusion | flops 301989888 | bytes 6291456 | tf_op jit(solution)/shard_map/gqd,gkd->gqk/dot_general | solution.py:61
  125.7 1.8 convolution_convert_fusion
  127.5 8.4 %fusion.16 = bf16[8,384,128]{1,2,0:T(8,128)(2,1)} fusion(bf16[8,384,128]{2,1,0:T(8,128)(2,1)S(1)} %bitcast.172, bf16[8,384,384]{1,2,0:T(8,128)(2,1)S(1)} %divide_convert_fusion, f32[8,384,384]{2,1,0:T(8,128)} %fusion.24, f32[8,384,384]{2,1,0:T(8,128)} %copy-done.4), kind=kOutput, calls=%fused_computation.28 | convolution fusion | flops 315362688 | bytes 13369344 | tf_op jit(solution)/shard_map/gqk,gqd->kgd/dot_general | solution.py:68
  135.9 1.4 copy.91
  137.3 2.3 %copy.92 = bf16[1,384,1024]{2,1,0:T(8,128)(2,1)} copy(bf16[1,384,1024]{1,2,0:T(8,128)(2,1)} %bitcast.162) | data formatting | bytes 1572864 | tf_op jit(solution)/shard_map/stack;reshape | solution.py:72
  139.6 1.3 convolution_convert_fusion.2
  140.9 1.9 fusion.20
  142.8 1.3 collective-permute-start.1
  144.1 1.3 fusion.37
  145.4 1.9 fusion.18
  147.2 1.1 concatenate.27
  148.3 0.8 copy.94
  149.1 1.5 fusion.5
  150.5 0.8 concatenate.26
  151.3 0.1 copy.93
  151.4 1.2 maximum_bitcast_fusion.4
  152.6 1.7 copy.107
  154.4 0.0 reduce-scatter.7.cloned.1.call-update
  154.4 0.3 reduce-scatter.9.cloned.1.call-start
  154.7 8.6 %fusion.15 = bf16[8,384,128]{2,1,0:T(8,128)(2,1)} fusion(bf16[8,384,384]{1,2,0:T(8,128)(2,1)S(1)} %divide_convert_fusion, f32[8,384,384]{2,1,0:T(8,128)} %fusion.24, f32[8,384,384]{2,1,0:T(8,128)} %copy-done.4, bf16[384,8,128]{2,1,0:T(8,128)(2,1)} %bitcast.170), kind=kOutput, calls=%fused_computation.27 | convolution fusion | flops 315362688 | bytes 13369344 | tf_op jit(solution)/shard_map/gqk,gkd->gqd/dot_general | solution.py:67
  163.3 2.9 %copy.86 = bf16[192,8,2,128]{3,2,1,0:T(2,128)(2,1)} copy(bf16[192,8,2,128]{3,0,2,1:T(8,128)(2,1)} %bitcast.173) | data formatting | bytes 1572864 | tf_op jit(solution)/shard_map/convert_element_type | solution.py:38
  166.2 3.1 %convert_element_type.75 = bf16[1,192,2048]{2,1,0:T(8,128)(2,1)} reshape(bf16[192,8,2,128]{3,2,1,0:T(2,128)(2,1)} %copy.86) | data formatting | bytes 1572864 | tf_op jit(solution)/shard_map/convert_element_type | solution.py:38
  169.3 14.6 %reduce-scatter.7.cloned.1.call-done = f32[832,32]{1,0:T(8,128)} async-done(((f32[3328,32]{1,0:T(8,128)}), f32[832,32]{1,0:T(8,128)}) %reduce-scatter.7.cloned.1.call-update) | async-done | bytes 106512
  183.9 0.0 reduce-scatter.9.cloned.1.call-update
  183.9 0.9 convolution_convert_fusion.1
  184.8 0.8 copy.83
  185.6 1.5 convert_element_type.69
  187.1 20.0 %reduce-scatter.9.cloned.1.call-done = f32[208,32]{1,0:T(8,128)} async-done(((f32[832,32]{1,0:T(8,128)}), f32[208,32]{1,0:T(8,128)}) %reduce-scatter.9.cloned.1.call-update) | async-done | bytes 26640
  207.2 0.9 slice.48
  208.1 0.7 copy.110
  208.8 0.8 slice.49
  209.5 0.7 copy.111
  (19 shorter events, 0.1 us)
Async XLA Ops:
  7.2 97.4 %all-gather.4.cloned.1.call-start = ((), (), s32[]{:S(2)}) async-start(), calls=%async_computation.2 | async-start | bytes 10027008 | tf_op jit(solution)/shard_map/all_gather | solution.py:80
  7.9 176.0 %reduce-scatter.7.cloned.1.call-start = ((), (), s32[]{:S(2)}) async-start(), calls=%async_computation.3 | async-start | bytes 2129920
  7.9 64.2 %collective-permute-start = (bf16[192,2304]{1,0:T(8,128)(2,1)}, bf16[192,2304]{1,0:T(8,128)(2,1)}, u32[]{:S(2)}, u32[]{:S(2)}) collective-permute-start(bf16[192,2304]{1,0:T(8,128)(2,1)} %bitcast.153), channel_id=1, source_target_pairs={{0,4},{4,8},{8,12},{1,5},{5,9},{9,13},{2,6},{6,10},{10,14},{3,7},{... | collective-permute-start | bytes 2654216 | tf_op jit(solution)/shard_map/ppermute | solution.py:19
  64.1 10.5 %copy-start = (bf16[1,192,2304]{2,1,0:T(8,128)(2,1)S(1)}, bf16[1,192,2304]{2,1,0:T(8,128)(2,1)}, u32[]{:S(2)}) copy-start(bf16[1,192,2304]{2,1,0:T(8,128)(2,1)} %param.6) | copy-start | bytes 2654212
  76.3 39.3 %copy-start.7 = (bf16[2,16,384]{2,1,0:T(8,128)(2,1)}, bf16[2,16,384]{2,1,0:T(8,128)(2,1)S(1)}, u32[]{:S(2)}) copy-start(bf16[2,16,384]{2,1,0:T(8,128)(2,1)S(1)} %fusion.19) | copy-start | bytes 73732
  115.6 3.8 %copy-start.6 = (bf16[8,2,192,128]{3,2,1,0:T(8,128)(2,1)S(1)}, bf16[8,2,192,128]{3,2,1,0:T(8,128)(2,1)}, u32[]{:S(2)}) copy-start(bf16[8,2,192,128]{3,2,1,0:T(8,128)(2,1)} %copy.80) | copy-start | bytes 2359300
  118.5 0.9 copy-start.5
  118.7 3.8 %copy-start.1 = (bf16[48,8,8,128]{3,2,1,0:T(8,128)(2,1)}, bf16[48,8,8,128]{3,2,1,0:T(8,128)(2,1)S(1)}, u32[]{:S(2)}) copy-start(bf16[48,8,8,128]{3,2,1,0:T(8,128)(2,1)S(1)} %copy.113) | copy-start | bytes 2359300
  121.0 4.7 %copy-start.4 = (f32[8,384,384]{2,1,0:T(8,128)}, f32[8,384,384]{2,1,0:T(8,128)S(1)}, u32[]{:S(2)}) copy-start(f32[8,384,384]{2,1,0:T(8,128)S(1)} %get-tuple-element.7) | copy-start | bytes 14155780
  121.0 1.7 copy-start.3
  135.9 8.2 %copy-start.8 = (bf16[2,16,384]{2,1,0:T(8,128)(2,1)S(1)}, bf16[2,16,384]{2,1,0:T(8,128)(2,1)}, u32[]{:S(2)}) copy-start(bf16[2,16,384]{2,1,0:T(8,128)(2,1)} %copy-done.7) | copy-start | bytes 73732
  142.8 6.3 %collective-permute-start.1 = (bf16[2,192,16]{1,2,0:T(8,128)(2,1)S(1)}, bf16[2,192,16]{1,2,0:T(8,128)(2,1)S(1)}, u32[]{:S(2)}, u32[]{:S(2)}) collective-permute-start(bf16[2,192,16]{1,2,0:T(8,128)(2,1)S(1)} %convolution_convert_fusion.2), channel_id=1, source_target_pairs={{4,0},{8,4},{12,8},{5,1},{9,5},{13,9},{6,2},{10,6},{14,10},{7,3},{... | collective-permute-start | bytes 36872 | tf_op jit(solution)/shard_map/ppermute | solution.py:19
  154.4 29.5 %copy-start.2 = (bf16[48,8,8,128]{3,2,1,0:T(8,128)(2,1)S(1)}, bf16[48,8,8,128]{3,2,1,0:T(8,128)(2,1)}, u32[]{:S(2)}) copy-start(bf16[48,8,8,128]{3,2,1,0:T(8,128)(2,1)} %copy-done.1) | copy-start | bytes 2359300
  154.4 52.8 %reduce-scatter.9.cloned.1.call-start = ((), (), s32[]{:S(2)}) async-start(), calls=%async_computation.4 | async-start | bytes 532480
Sparse Core Ops, SparseCore 0:
  10.3 94.2 all-gather.3
  154.5 29.3 reduce-scatter.6
  186.3 20.8 reduce-scatter.8

commit v4 on v3

--- a/solution.py
+++ b/solution.py
@@ -1,6 +1,8 @@
 import jax
 import jax.numpy as jnp
 from jax import lax
+from jax.experimental import pallas as pl
+from jax.experimental.pallas import tpu as pltpu
 from jax.sharding import PartitionSpec as P
 
 HEADS = 16
@@ -17,6 +19,55 @@
     length = lax.axis_size(axis)
     pairs = [(i, i + by) for i in range(length) if 0 <= i + by < length]
     return lax.ppermute(value, axis, pairs)
+
+
+def attention_kernel(mask_ref, q_ref, do_ref, k_ref, v_ref, out_ref, dq_ref, dk_ref, dv_ref):
+    q = q_ref[0]
+    do = do_ref[0]
+    k = k_ref[0]
+    v = v_ref[0]
+    visible = mask_ref[...] != 0
+    contract_last = (((1,), (1,)), ((), ()))
+    raw_score = lax.dot_general(q, k, contract_last, preferred_element_type=jnp.float32) * query_scale
+    bent_score = jnp.tanh(raw_score / logit_cap)
+    expo_terms = jnp.where(visible, jnp.exp(logit_cap * bent_score), 0.0)
+    denominator = jnp.sum(expo_terms, axis=-1, keepdims=True)
+    prob_wide = (expo_terms / denominator).astype(jnp.bfloat16).astype(jnp.float32)
+    attn_prob = prob_wide.astype(jnp.bfloat16)
+    out_ref[0] = jnp.dot(attn_prob, v, preferred_element_type=jnp.float32).astype(out_ref.dtype)
+    prob_grad = lax.dot_general(do, v, contract_last, preferred_element_type=jnp.float32)
+    row_delta = jnp.sum(prob_wide * prob_grad, axis=-1, keepdims=True)
+    score_wide = prob_wide * (prob_grad - row_delta) * (1.0 - bent_score * bent_score) * query_scale
+    score_grad = score_wide.astype(jnp.bfloat16)
+    dq_ref[0] = jnp.dot(score_grad, k, preferred_element_type=jnp.float32).astype(dq_ref.dtype)
+    score_t = score_grad.astype(jnp.float32).T.astype(jnp.bfloat16)
+    prob_t = prob_wide.T.astype(jnp.bfloat16)
+    dk_ref[0] = jnp.dot(score_t, q, preferred_element_type=jnp.float32).astype(dk_ref.dtype)
+    dv_ref[0] = jnp.dot(prob_t, do, preferred_element_type=jnp.float32).astype(dv_ref.dtype)
+
+
+def attention_heads(mask, q, do, k, v):
+    heads, rows, dim = q.shape
+    keys = k.shape[1]
+    head_block = lambda n: pl.BlockSpec((1, n, dim), lambda g: (g, 0, 0))
+    return pl.pallas_call(
+        attention_kernel,
+        grid=(heads,),
+        in_specs=[
+            pl.BlockSpec((rows, keys), lambda g: (0, 0)),
+            head_block(rows),
+            head_block(rows),
+            head_block(keys),
+            head_block(keys),
+        ],
+        out_specs=[head_block(rows), head_block(rows), head_block(keys), head_block(keys)],
+        out_shape=[
+            jax.ShapeDtypeStruct((heads, rows, dim), jnp.bfloat16),
+            jax.ShapeDtypeStruct((heads, rows, dim), jnp.bfloat16),
+            jax.ShapeDtypeStruct((heads, keys, dim), jnp.bfloat16),
+            jax.ShapeDtypeStruct((heads, keys, dim), jnp.bfloat16),
+        ],
+    )(mask, q, do, k, v)
 
 
 def attend(query_rows, key_rows, value_rows, grad_rows, is_first):
@@ -35,13 +86,14 @@
             parts.reshape(KV_HEADS, group_size, length, HEAD_DIM)
             .transpose(2, 0, 1, 3)
             .reshape(length, HEADS * HEAD_DIM)
-            .astype(jnp.bfloat16)
         )
 
-    queries_g = by_head(query_rows)
-    grads_g = by_head(grad_rows)
-    keys_g = key_rows.reshape(2 * length, KV_HEADS, HEAD_DIM).transpose(1, 0, 2)
-    values_g = value_rows.reshape(2 * length, KV_HEADS, HEAD_DIM).transpose(1, 0, 2)
+    def kv_by_head(rows):
+        return rows.reshape(2 * length, KV_HEADS, HEAD_DIM).transpose(1, 0, 2)
+
+    def kv_from_head(parts):
+        return parts.transpose(1, 0, 2).reshape(2 * length, KV_HEADS * HEAD_DIM)
+
     query_pos = lax.broadcasted_iota(jnp.int32, (group_size * length, 2 * length), 0) % length
     key_pos = lax.broadcasted_iota(jnp.int32, (group_size * length, 2 * length), 1)
     visible = (
@@ -49,27 +101,15 @@
         & (key_pos <= query_pos + length)
         & (jnp.logical_not(is_first) | (key_pos >= length))
     )
-    raw_score = (
-        jnp.einsum("gqd,gkd->gqk", queries_g, keys_g, preferred_element_type=jnp.float32)
-        * query_scale
-    )
-    bent_score = jnp.tanh(raw_score / logit_cap)
-    expo_terms = jnp.where(visible, jnp.exp(logit_cap * bent_score), 0.0)
-    denominator = jnp.sum(expo_terms, axis=-1, keepdims=True)
-    attn_prob = (expo_terms / denominator).astype(jnp.bfloat16)
-    head_out = jnp.einsum("gqk,gkd->gqd", attn_prob, values_g, preferred_element_type=jnp.float32)
-    prob_grad = jnp.einsum("gqd,gkd->gqk", grads_g, values_g, preferred_element_type=jnp.float32)
-    prob_wide = attn_prob.astype(jnp.float32)
-    row_delta = jnp.sum(prob_wide * prob_grad, axis=-1, keepdims=True)
-    score_grad = (
-        prob_wide * (prob_grad - row_delta) * (1.0 - bent_score * bent_score) * query_scale
-    ).astype(jnp.bfloat16)
-    head_qgrad = jnp.einsum("gqk,gkd->gqd", score_grad, keys_g, preferred_element_type=jnp.float32)
-    key_part = jnp.einsum("gqk,gqd->kgd", score_grad, queries_g, preferred_element_type=jnp.float32)
-    value_part = jnp.einsum("gqk,gqd->kgd", attn_prob, grads_g, preferred_element_type=jnp.float32)
-    key_grad = key_part.reshape(2 * length, KV_HEADS * HEAD_DIM)
-    value_grad = value_part.reshape(2 * length, KV_HEADS * HEAD_DIM)
-    return (from_head(head_out), from_head(head_qgrad), jnp.stack([key_grad, value_grad]))
+    head_out, head_qgrad, key_part, value_part = attention_heads(
+        visible.astype(jnp.int32),
+        by_head(query_rows),
+        by_head(grad_rows),
+        kv_by_head(key_rows),
+        kv_by_head(value_rows),
+    )
+    kv_grads = jnp.stack([kv_from_head(key_part), kv_from_head(value_part)])
+    return (from_head(head_out), from_head(head_qgrad), kv_grads)
 
 
 def project_rows(row_block, kv_weight, down_full, up_full):
@@ -143,7 +183,7 @@
     key_rows = kv_both[0]
     value_rows = kv_both[1]
     attended, query_grad, kv_grads = attend(query_rows, key_rows, value_rows, grad_rows, is_first)
-    kv_rounded = kv_grads.astype(jnp.bfloat16)
+    kv_rounded = kv_grads
     far_part = kv_rounded[:, :length]
     near_part = kv_rounded[:, length:]
     projected_far = jnp.einsum(

time: 218 us -> 206 us (0.945)
  matrix products: 45 us -> 14.1 us
  waiting for transfers between devices: 63.6 us -> 79.9 us
  Pallas kernels: 0 us -> 11.5 us
  local copies, waits for them, and re-layouts: 35.3 us -> 28.4 us
  other arithmetic: 3.67 us -> 1.38 us
    dot_general x6 -> x0, matrix products: 24.3 us -> none  [the longest x1 8.65 us: attend(): jnp.einsum('gqk,gkd->gqd', score_grad, keys_g, preferred_element_type=jnp...]
    pallas_call x0 -> x1, Pallas kernels: none -> 11.5 us  [attention_heads(): pl.pallas_call(attention_kernel, grid=(heads,), in_specs=[pl.BlockSpec((r...]
    unnamed x5, waiting for transfers between devices: 35.4 us -> 46.8 us
    convert_element_type x4 -> x0, local copies, waits for them, and re-layouts: 8.27 us -> none  [from_head(): return parts.reshape(KV_HEADS, group_size, length, HEAD_DIM).transpose(2,...]
    ppermute x2, waiting for transfers between devices: 0.01 us -> 3.37 us  [shifted(): return lax.ppermute(value, axis, pairs)]
    another operation x2 -> x6, local copies, waits for them, and re-layouts: 3.7 us -> 5.9 us  [the longest x2 2.95 us: on_device(): return (attended[None], query_grad[None], down_part, up_part)]
    unnamed x27 -> x22, local copies, waits for them, and re-layouts: 6.23 us -> 5.47 us
    another operation x2 -> x4, local copies, waits for them, and re-layouts: 5.12 us -> 5.29 us  [by_head(): rows.reshape(length, KV_HEADS, group_size, HEAD_DIM).transpose(1, 2, 0, 3)]
  transfers between devices with their start and end apart: 5 -> 5, of which waited for: 3 -> 4; matrix products, arithmetic and copies ran while one was open for 17% -> 8% of each run, Pallas kernels for 0% -> 0%
where the time goes in v4:
time: 206 us; the launch traced here: 205 us
  waiting for transfers between devices  79.9 us (39%)
  blocking collectives  48.4 us (23%)
  local copies, waits for them, and re-layouts  28.4 us (14%)
  matrix products  14.1 us (7%)
  between operations  14 us (7%)
  Pallas kernels  11.5 us (6%)
  starting transfers between devices  7.6 us (4%)
    all_gather x1, blocking collectives, gather_adapters(): gathered = lax.all_gather(joined, axes, axis=0, tiled=False)  48.4 us
    unnamed x5, waiting for transfers between devices  46.8 us
    all_gather x1, waiting for transfers between devices, project_rows(): lax.all_gather(kv_weight, ('ctx', 'dp', 'sub'), axis=0, tiled=False)  29.8 us
    pallas_call x1, Pallas kernels, attention_heads(): pl.pallas_call(attention_kernel, grid=(heads,), in_specs=[pl.BlockSpec((r...  11.5 us
    dot_general x1, matrix products, project_rows(): jnp.einsum('rcd,cimdn->mrin', row_block.reshape(row_block.shape[0], row_s...  8.16 us
    ppermute x2, starting transfers between devices, shifted(): return lax.ppermute(value, axis, pairs)  7.49 us
    unnamed x22, local copies, waits for them, and re-layouts  5.47 us
    another operation x4, local copies, waits for them, and re-layouts, by_head(): rows.reshape(length, KV_HEADS, group_size, HEAD_DIM).transpose(1, 2, 0, 3)  5.29 us
  transfers between devices with their start and end apart: 5, of which 4 were waited for; matrix products, arithmetic and copies ran while one was open for 8% of the time, Pallas kernels for 0%

profile of v4, /device:TPU:0, one launch (start us, length us, event | category | flops | bytes accessed | tf_op | source)
XLA Modules:
  0.0 205.4 jit_solution(8169986889651680994)
XLA Ops:
  7.2 0.0 all-gather.4.cloned.1.call-start
  7.2 0.7 all-gather.4.cloned.1.call-update
  7.9 0.0 reduce-scatter.7.cloned.1.call-start
  8.0 6.0 %collective-permute-start = (bf16[192,2304]{1,0:T(8,128)(2,1)}, bf16[192,2304]{1,0:T(8,128)(2,1)}, u32[]{:S(2)}, u32[]{:S(2)}) collective-permute-start(bf16[192,2304]{1,0:T(8,128)(2,1)} %bitcast.89), channel_id=1, source_target_pairs={{0,4},{4,8},{8,12},{1,5},{5,9},{9,13},{2,6},{6,10},{10,14},{3,7},{... | collective-permute-start | bytes 2654216 | tf_op jit(solution)/shard_map/ppermute | solution.py:21
  14.0 1.5 copy.42
  15.5 0.1 pad_maximum_fusion.3
  15.6 48.4 %all-gather.1 = bf16[32,16,208]{2,1,0:T(8,128)(2,1)S(1)} all-gather(bf16[2,16,208]{2,1,0:T(8,128)(2,1)S(1)} %pad_maximum_fusion.3), channel_id=3, replica_groups=mesh['groups'=2,'ctx'=4,'dp'=2,'sub'=2] {'ctx','dp','sub'}, dimensions={0}, use_global_device_ids=true | all-gather | bytes 226304 | tf_op jit(solution)/shard_map/all_gather | solution.py:137
  64.0 0.1 slice.41
  64.1 0.2 copy.73
  64.2 0.3 reshape.56
  64.6 0.1 copy.74
  64.6 0.1 reshape.57
  64.8 0.6 reshape_squeeze.12
  65.3 1.1 copy.39
  66.4 2.6 %reshape_squeeze.13 = bf16[192,8,2,128]{3,2,1,0:T(2,128)(2,1)S(1)} reshape(bf16[1,192,2048]{2,1,0:T(8,128)(2,1)} %param.11) | data formatting | bytes 1572864 | tf_op jit(solution)/shard_map/reshape;squeeze | solution.py:79
  69.0 0.0 copy-start
  69.0 1.1 copy.40
  70.1 1.1 fusion.16.mask_ref
  71.2 0.0 collective-permute-done
  71.2 1.5 copy.41
  72.7 1.8 fusion.9
  74.5 29.8 %all-gather.4.cloned.1.call-done = bf16[32,576,256]{2,1,0:T(8,128)(2,1)} async-done(((bf16[2,576,256]{2,1,0:T(8,128)(2,1)}), bf16[32,576,256]{2,1,0:T(8,128)(2,1)}) %all-gather.4.cloned.1.call-update) | async-done | bytes 9437200 | tf_op jit(solution)/shard_map/all_gather | solution.py:120
  104.3 8.2 %convolution_bitcast_fusion = f32[2,384,4,256]{1,3,0,2:T(8,128)S(1)} fusion(bf16[4,4,2,576,256]{4,3,2,1,0:T(8,128)(2,1)} %bitcast.114, bf16[192,4,576]{0,2,1:T(8,128)(2,1)S(1)} %bitcast.102, bf16[192,4,576]{0,2,1:T(8,128)(2,1)S(1)} %bitcast.103), kind=kOutput, calls=%fused_computation.4 | convolution fusion | flops 3627417600 | bytes 14352384 | tf_op jit(solution)/shard_map/rcd,cimdn->mrin/dot_general | solution.py:122
  112.4 0.2 copy.44
  112.7 2.4 %copy.47 = f32[2,384,1024]{2,1,0:T(8,128)} copy(f32[2,384,1024]{1,2,0:T(8,128)S(1)} %bitcast.88) | data formatting | bytes 6291456 | tf_op jit(solution)/shard_map/reshape | solution.py:127
  115.0 2.5 %add_convert_fusion = bf16[2,384,1024]{2,1,0:T(8,128)(2,1)S(1)} fusion(f32[2,384,1024]{2,1,0:T(8,128)} %copy.47, bf16[2,16,384]{2,1,0:T(8,128)(2,1)S(1)} %fusion.9, bf16[2,16,1024]{2,1,0:T(8,128)(2,1)S(1)} %reshape.57), kind=kOutput, calls=%fused_computation.3 | convolution fusion | flops 27525120 | bytes 4808704 | tf_op jit(solution)/shard_map/mrk,mkc->mrc/dot_general | solution.py:128
  117.5 0.1 fusion.32
  117.6 0.4 copy.48
  118.0 1.2 copy.49
  119.2 0.4 copy.50
  119.5 1.2 copy.51
  120.7 11.5 %shard_map.93 = (bf16[8,384,128]{2,1,0:T(8,128)(2,1)}, bf16[8,384,128]{2,1,0:T(8,128)(2,1)}, bf16[8,384,128]{2,1,0:T(8,128)(2,1)}, bf16[8,384,128]{2,1,0:T(8,128)(2,1)}) custom-call(s32[384,384]{1,0:T(8,128)} %fusion.16.mask_ref, bf16[8,384,128]{2,1,0:T(8,128)(2,1)} %bitcast.92, bf16[8,384,128]{2,1,0:T(8,128)(2,1)} %bitcast.93, ...), custom_call_target="tpu_custom_call" | custom-call | tf_op jit(solution)/shard_map/pallas_call | solution.py:53
  132.2 1.6 copy.54
  133.8 0.3 copy.56
  134.1 0.4 copy.55
  134.5 0.0 copy-start.1
  134.5 0.3 copy.57
  134.8 0.3 convolution_convert_fusion
  135.1 0.6 copy-done.1
  135.6 0.6 fusion.10
  136.2 1.5 collective-permute-start.1
  137.7 0.3 fusion.18
  138.0 0.2 fusion.8
  138.2 0.2 concatenate.27
  138.4 0.1 copy.59
  138.5 3.4 %collective-permute-done.1 = bf16[2,192,16]{1,2,0:T(8,128)(2,1)S(1)} collective-permute-done((bf16[2,192,16]{1,2,0:T(8,128)(2,1)S(1)}, bf16[2,192,16]{1,2,0:T(8,128)(2,1)S(1)}, u32[]{:S(2)}, u32[]{:S(2)}) %collective-permute-start.1) | collective-permute-done | bytes 12320 | tf_op jit(solution)/shard_map/ppermute | solution.py:21
  141.8 0.3 fusion.1
  142.1 0.8 concatenate.26
  142.9 0.1 copy.58
  143.0 0.2 maximum_bitcast_fusion.4
  143.3 1.8 copy.66
  145.1 0.0 reduce-scatter.7.cloned.1.call-update
  145.1 0.0 reduce-scatter.9.cloned.1.call-start
  145.1 27.3 %reduce-scatter.7.cloned.1.call-done = f32[832,32]{1,0:T(8,128)} async-done(((f32[3328,32]{1,0:T(8,128)}), f32[832,32]{1,0:T(8,128)}) %reduce-scatter.7.cloned.1.call-update) | async-done | bytes 106512
  172.4 0.0 reduce-scatter.9.cloned.1.call-update
  172.5 0.8 copy.52
  173.3 1.5 broadcast_in_dim_reshape.6
  174.8 0.8 copy.53
  175.6 1.5 broadcast_in_dim_reshape.7
  177.1 18.7 %reduce-scatter.9.cloned.1.call-done = f32[208,32]{1,0:T(8,128)} async-done(((f32[832,32]{1,0:T(8,128)}), f32[208,32]{1,0:T(8,128)}) %reduce-scatter.9.cloned.1.call-update) | async-done | bytes 26640
  195.8 0.9 slice.48
  196.7 0.7 copy.69
  197.4 0.8 slice.49
  198.1 0.7 copy.70
  (15 shorter events, 0.0 us)
Async XLA Ops:
  7.2 8.3 %copy-start.7 = (bf16[2,16,64]{2,1,0:T(8,128)(2,1)S(1)}, bf16[2,16,64]{2,1,0:T(8,128)(2,1)}, u32[]{:S(2)}) copy-start(bf16[2,16,64]{2,1,0:T(8,128)(2,1)} %param.10) | copy-start | bytes 12292
  7.2 8.3 %copy-start.6 = (bf16[2,16,144]{2,1,0:T(8,128)(2,1)S(1)}, bf16[2,16,144]{2,1,0:T(8,128)(2,1)}, u32[]{:S(2)}) copy-start(bf16[2,16,144]{2,1,0:T(8,128)(2,1)} %param.9) | copy-start | bytes 27652
  7.2 97.1 %all-gather.4.cloned.1.call-start = ((), (), s32[]{:S(2)}) async-start(), calls=%async_computation.2 | async-start | bytes 10027008 | tf_op jit(solution)/shard_map/all_gather | solution.py:120
  7.9 164.5 %reduce-scatter.7.cloned.1.call-start = ((), (), s32[]{:S(2)}) async-start(), calls=%async_computation.3 | async-start | bytes 2129920
  8.0 56.8 %copy-start.2 = (bf16[1,192,2048]{2,1,0:T(8,128)(2,1)S(1)}, bf16[1,192,2048]{2,1,0:T(8,128)(2,1)}, u32[]{:S(2)}) copy-start(bf16[1,192,2048]{2,1,0:T(8,128)(2,1)} %param.7) | copy-start | bytes 2359300
  8.0 63.2 %collective-permute-start = (bf16[192,2304]{1,0:T(8,128)(2,1)}, bf16[192,2304]{1,0:T(8,128)(2,1)}, u32[]{:S(2)}, u32[]{:S(2)}) collective-permute-start(bf16[192,2304]{1,0:T(8,128)(2,1)} %bitcast.89), channel_id=1, source_target_pairs={{0,4},{4,8},{8,12},{1,5},{5,9},{9,13},{2,6},{6,10},{10,14},{3,7},{... | collective-permute-start | bytes 2654216 | tf_op jit(solution)/shard_map/ppermute | solution.py:21
  69.0 3.7 %copy-start = (bf16[1,192,2304]{2,1,0:T(8,128)(2,1)S(1)}, bf16[1,192,2304]{2,1,0:T(8,128)(2,1)}, u32[]{:S(2)}) copy-start(bf16[1,192,2304]{2,1,0:T(8,128)(2,1)} %param.6) | copy-start | bytes 2654212
  132.2 1.9 copy-start.5
  134.5 1.2 copy-start.1
  136.2 5.6 %collective-permute-start.1 = (bf16[2,192,16]{1,2,0:T(8,128)(2,1)S(1)}, bf16[2,192,16]{1,2,0:T(8,128)(2,1)S(1)}, u32[]{:S(2)}, u32[]{:S(2)}) collective-permute-start(bf16[2,192,16]{1,2,0:T(8,128)(2,1)S(1)} %convolution_convert_fusion), channel_id=1, source_target_pairs={{4,0},{8,4},{12,8},{5,1},{9,5},{13,9},{6,2},{10,6},{14,10},{7,3},{... | collective-permute-start | bytes 36872 | tf_op jit(solution)/shard_map/ppermute | solution.py:21
  143.3 29.2 %copy-start.4 = (bf16[8,384,128]{2,1,0:T(8,128)(2,1)S(1)}, bf16[8,384,128]{2,1,0:T(8,128)(2,1)}, u32[]{:S(2)}) copy-start(bf16[8,384,128]{2,1,0:T(8,128)(2,1)} %get-tuple-element.8) | copy-start | bytes 2359300
  145.1 50.7 %reduce-scatter.9.cloned.1.call-start = ((), (), s32[]{:S(2)}) async-start(), calls=%async_computation.4 | async-start | bytes 532480
  172.4 2.3 %copy-start.3 = (bf16[8,384,128]{2,1,0:T(8,128)(2,1)S(1)}, bf16[8,384,128]{2,1,0:T(8,128)(2,1)}, u32[]{:S(2)}) copy-start(bf16[8,384,128]{2,1,0:T(8,128)(2,1)} %get-tuple-element.9) | copy-start | bytes 2359300
Sparse Core Ops, SparseCore 0:
  10.3 93.9 all-gather.3
  145.2 27.1 reduce-scatter.6
  174.8 20.9 reduce-scatter.8

commit v5 on v4

v5 whole, which is shorter than its diff:
```python
import jax
import jax.numpy as jnp
from jax import lax
from jax.experimental import pallas as pl
from jax.experimental.pallas import tpu as pltpu
from jax.sharding import PartitionSpec as P

HEADS = 16
KV_HEADS = 8
HEAD_DIM = 128


query_scale = 1.0 / 12.0
logit_cap = 50.0
adapter_scale = 0.5


def shifted(value, axis, by):
    length = lax.axis_size(axis)
    pairs = [(i, i + by) for i in range(length) if 0 <= i + by < length]
    return lax.ppermute(value, axis, pairs)


def attention_kernel(mask_ref, q_ref, do_ref, kv_ref, out_ref, dq_ref, dkv_ref):
    half = HEAD_DIM
    q = jnp.concatenate([q_ref[:, :half], q_ref[:, half:]], axis=0)
    do = jnp.concatenate([do_ref[:, :half], do_ref[:, half:]], axis=0)
    k = kv_ref[0]
    v = kv_ref[1]
    rows = q_ref.shape[0]
    visible = mask_ref[...] != 0
    contract_last = (((1,), (1,)), ((), ()))
    raw_score = lax.dot_general(q, k, contract_last, preferred_element_type=jnp.float32) * query_scale
    bent_score = jnp.tanh(raw_score / logit_cap)
    expo_terms = jnp.where(visible, jnp.exp(logit_cap * bent_score), 0.0)
    denominator = jnp.sum(expo_terms, axis=-1, keepdims=True)
    prob_wide = (expo_terms / denominator).astype(jnp.bfloat16).astype(jnp.float32)
    attn_prob = prob_wide.astype(jnp.bfloat16)
    head_out = jnp.dot(attn_prob, v, preferred_element_type=jnp.float32).astype(out_ref.dtype)
    out_ref[:, :half] = head_out[:rows]
    out_ref[:, half:] = head_out[rows:]
    prob_grad = lax.dot_general(do, v, contract_last, preferred_element_type=jnp.float32)
    row_delta = jnp.sum(prob_wide * prob_grad, axis=-1, keepdims=True)
    score_wide = prob_wide * (prob_grad - row_delta) * (1.0 - bent_score * bent_score) * query_scale
    score_grad = score_wide.astype(jnp.bfloat16)
    head_qgrad = jnp.dot(score_grad, k, preferred_element_type=jnp.float32).astype(dq_ref.dtype)
    dq_ref[:, :half] = head_qgrad[:rows]
    dq_ref[:, half:] = head_qgrad[rows:]
    score_t = score_grad.astype(jnp.float32).T.astype(jnp.bfloat16)
    prob_t = prob_wide.T.astype(jnp.bfloat16)
    dkv_ref[0] = jnp.dot(score_t, q, preferred_element_type=jnp.float32).astype(dkv_ref.dtype)
    dkv_ref[1] = jnp.dot(prob_t, do, preferred_element_type=jnp.float32).astype(dkv_ref.dtype)


def attention_heads(mask, queries, grads, key_value):
    rows, width = queries.shape
    keys, kv_width = key_value.shape[1], key_value.shape[2]
    heads = kv_width // HEAD_DIM
    group_cols = width // heads
    row_block = pl.BlockSpec((rows, group_cols), lambda g: (0, g))
    kv_block = pl.BlockSpec((2, keys, HEAD_DIM), lambda g: (0, 0, g))
    return pl.pallas_call(
        attention_kernel,
        grid=(heads,),
        in_specs=[pl.BlockSpec(mask.shape, lambda g: (0, 0)), row_block, row_block, kv_block],
        out_specs=[row_block, row_block, kv_block],
        out_shape=[
            jax.ShapeDtypeStruct((rows, width), jnp.bfloat16),
            jax.ShapeDtypeStruct((rows, width), jnp.bfloat16),
            jax.ShapeDtypeStruct(key_value.shape, jnp.bfloat16),
        ],
    )(mask, queries, grads, key_value)


def attend(query_rows, key_value, grad_rows, is_first):
    length = query_rows.shape[0]
    group_size = HEADS // KV_HEADS
    query_pos = lax.broadcasted_iota(jnp.int32, (group_size * length, 2 * length), 0) % length
    key_pos = lax.broadcasted_iota(jnp.int32, (group_size * length, 2 * length), 1)
    visible = (
        (key_pos > query_pos)
        & (key_pos <= query_pos + length)
        & (jnp.logical_not(is_first) | (key_pos >= length))
    )
    return attention_heads(visible.astype(jnp.int32), query_rows, grad_rows, key_value)


def project_rows(row_block, kv_weight, down_full, up_full):
    low_rank = jnp.einsum(
        "rd,mkd->mrk", row_block, down_full, preferred_element_type=jnp.float32
    ).astype(jnp.bfloat16)
    row_shards, col_shards = lax.axis_size("ctx"), lax.axis_size(("dp", "sub"))
    gathered = lax.all_gather(kv_weight, ("ctx", "dp", "sub"), axis=0, tiled=False)
    gathered = gathered.reshape((row_shards, col_shards) + kv_weight.shape)
    base_part = jnp.einsum(
        "rcd,cimdn->mrin",
        row_block.reshape(row_block.shape[0], row_shards, kv_weight.shape[1]),
        gathered,
        preferred_element_type=jnp.float32,
    ).reshape(2, row_block.shape[0], col_shards * kv_weight.shape[2])
    extra_part = jnp.einsum("mrk,mkc->mrc", low_rank, up_full, preferred_element_type=jnp.float32)
    key_value = (base_part + adapter_scale * extra_part).astype(jnp.bfloat16)
    return (low_rank, key_value)


def gather_adapters(adapter_down, adapter_up):
    axes = ("ctx", "dp", "sub")
    down_cols = adapter_down.shape[2]
    joined = jnp.concatenate([adapter_down, adapter_up], axis=2)
    gathered = lax.all_gather(joined, axes, axis=0, tiled=False)
    shards = gathered.shape[0]

    def unshard(piece):
        return piece.transpose(1, 2, 0, 3).reshape(2, piece.shape[2], shards * piece.shape[3])

    return unshard(gathered[..., :down_cols]), unshard(gathered[..., down_cols:])


def scatter_adapter_grads(joined_down, joined_up):
    members_rank = joined_down.shape[-1]
    down_cols = joined_down.shape[2]
    joined = jnp.concatenate([joined_down, joined_up], axis=2)
    partial = lax.psum_scatter(
        joined.reshape(-1, members_rank), ("dp", "sub"), scatter_dimension=0, tiled=True
    )
    mine = lax.psum_scatter(partial, "ctx", scatter_dimension=0, tiled=True)

    def unshard(piece):
        return piece.reshape(piece.shape[0], 2, -1).transpose(1, 2, 0)

    return unshard(mine[:down_cols]), unshard(mine[down_cols:])


def on_device(hidden, queries, kv_weight, adapter_down, adapter_up, out_grad):
    rows_own = hidden[0]
    query_rows = queries[0]
    grad_rows = out_grad[0]
    length = rows_own.shape[0]
    row_shards, col_shards = lax.axis_size("ctx"), lax.axis_size(("dp", "sub"))
    rows_previous = shifted(rows_own, "ctx", 1)
    down_full, up_full = gather_adapters(adapter_down, adapter_up)
    is_first = lax.axis_index("ctx") == 0
    low_both, kv_both = project_rows(
        jnp.concatenate([rows_previous, rows_own], axis=0), kv_weight, down_full, up_full
    )
    low_previous = low_both[:, :length]
    low_rank = low_both[:, length:]
    attended, query_grad, kv_grads = attend(query_rows, kv_both, grad_rows, is_first)
    far_part = kv_grads[:, :length]
    near_part = kv_grads[:, length:]
    projected_far = jnp.einsum(
        "mrc,mkc->mrk", far_part, up_full, preferred_element_type=jnp.float32
    ).astype(jnp.bfloat16)
    projected_returned = shifted(projected_far, "ctx", -1)
    projected_near = jnp.einsum(
        "mrc,mkc->mrk", near_part, up_full, preferred_element_type=jnp.float32
    ).astype(jnp.bfloat16)
    shards = row_shards * col_shards
    rows_split = rows_own.reshape(length, row_shards, col_shards, -1)

    def split_cols(part):
        return part.reshape(part.shape[:2] + (row_shards, col_shards, -1))

    up_terms = jnp.einsum(
        "mrk,mrcij->icjmk", low_rank, split_cols(near_part), preferred_element_type=jnp.float32
    ) + jnp.einsum(
        "mrk,mrcij->icjmk", low_previous, split_cols(far_part), preferred_element_type=jnp.float32
    )
    down_terms = jnp.einsum(
        "mrk,rcij->icjmk", projected_near, rows_split, preferred_element_type=jnp.float32
    ) + jnp.einsum(
        "mrk,rcij->icjmk", projected_returned, rows_split, preferred_element_type=jnp.float32
    )
    factor = adapter_scale / (lax.axis_size("dp") * lax.axis_size("sub"))
    flat = lambda terms: (terms * factor).reshape(terms.shape[:3] + (-1,))
    down_part, up_part = scatter_adapter_grads(flat(down_terms), flat(up_terms))
    return (attended[None], query_grad[None], down_part, up_part)


def solution(mesh):
    placed = (
        P(("groups", "dp", "sub"), "ctx", None),
        P(("groups", "dp", "sub"), "ctx", None),
        P(None, "ctx", ("dp", "sub")),
        P(None, None, ("ctx", "dp", "sub")),
        P(None, None, ("ctx", "dp", "sub")),
        P(("groups", "dp", "sub"), "ctx", None),
    )
    return jax.shard_map(
        on_device,
        mesh=mesh,
        in_specs=placed,
        out_specs=(
            P(("groups", "dp", "sub"), "ctx", None),
            P(("groups", "dp", "sub"), "ctx", None),
            P("groups", None, ("ctx", "dp", "sub")),
            P("groups", None, ("ctx", "dp", "sub")),
        ),
        check_vma=False,
    )
```

time: 206 us -> 212 us (1.029)
  waiting for transfers between devices: 79.9 us -> 90.1 us
  local copies, waits for them, and re-layouts: 28.4 us -> 19.5 us
  matrix products: 14.1 us -> 19.6 us
    another operation x10 -> x0, local copies, waits for them, and re-layouts: 11.2 us -> none  [the longest x4 5.29 us: by_head(): rows.reshape(length, KV_HEADS, group_size, HEAD_DIM).transpose(1, 2, 0, 3)]
    all_gather x1, waiting for transfers between devices: 29.8 us -> 35.5 us  [project_rows(): lax.all_gather(kv_weight, ('ctx', 'dp', 'sub'), axis=0, tiled=False)]
    unnamed x5, waiting for transfers between devices: 46.8 us -> 51.3 us
    slice x3, local copies, waits for them, and re-layouts: 0.83 us -> 4.51 us  [the longest x2 3.99 us: on_device(): far_part = kv_grads[:, :length]]
    transpose x4 -> x0, local copies, waits for them, and re-layouts: 3.54 us -> none  [the longest x2 1.92 us: kv_from_head(): return parts.transpose(1, 0, 2).reshape(2 * length, KV_HEADS * HEAD_DIM)]
    transpose x1, local copies, waits for them, and re-layouts: 0.2 us -> 3.25 us  [project_rows(): jnp.einsum('rcd,cimdn->mrin', row_block.reshape(row_block.shape[0], row_s...]
    dot_general x4, matrix products: 1.35 us -> 4.24 us  [the longest x1 2.71 us: on_device(): jnp.einsum('mrk,rcij->icjmk', projected_near, rows_split, preferred_eleme...]
    unnamed x22 -> x20, local copies, waits for them, and re-layouts: 5.47 us -> 4.86 us
  transfers between devices with their start and end apart: 5 -> 5, of which waited for: 4 -> 4; matrix products, arithmetic and copies ran while one was open for 8% -> 4% of each run, Pallas kernels for 0% -> 0%
where the time goes in v5:
time: 212 us
  waiting for transfers between devices  90.1 us (42%)
  blocking collectives  48.3 us (23%)
  matrix products  19.6 us (9%)
  local copies, waits for them, and re-layouts  19.5 us (9%)
  between operations  13.9 us (7%)
  Pallas kernels  11.6 us (5%)
  starting transfers between devices  7.38 us (3%)
    unnamed x5, waiting for transfers between devices  51.3 us
    all_gather x1, blocking collectives, gather_adapters(): gathered = lax.all_gather(joined, axes, axis=0, tiled=False)  48.3 us
    all_gather x1, waiting for transfers between devices, project_rows(): lax.all_gather(kv_weight, ('ctx', 'dp', 'sub'), axis=0, tiled=False)  35.5 us
    pallas_call x1, Pallas kernels, attention_heads(): pl.pallas_call(attention_kernel, grid=(heads,), in_specs=[pl.BlockSpec(ma...  11.6 us
    dot_general x1, matrix products, project_rows(): jnp.einsum('rcd,cimdn->mrin', row_block.reshape(row_block.shape[0], row_s...  9.66 us
    ppermute x2, starting transfers between devices, shifted(): return lax.ppermute(value, axis, pairs)  7.27 us
    unnamed x20, local copies, waits for them, and re-layouts  4.86 us
  transfers between devices with their start and end apart: 5, of which 4 were waited for; matrix products, arithmetic and copies ran while one was open for 4% of the time, Pallas kernels for 0%

profile of v5, /device:TPU:0, one launch (start us, length us, event | category | flops | bytes accessed | tf_op | source)
XLA Modules:
  0.0 211.8 jit_solution(15644115040335254474)
XLA Ops:
  7.2 0.0 copy-start.6
  7.2 0.0 copy-start.5
  7.2 0.0 all-gather.4.cloned.1.call-start
  7.2 0.7 all-gather.4.cloned.1.call-update
  7.9 0.0 reduce-scatter.7.cloned.1.call-start
  8.0 5.9 %collective-permute-start = (bf16[192,2304]{1,0:T(8,128)(2,1)}, bf16[192,2304]{1,0:T(8,128)(2,1)}, u32[]{:S(2)}, u32[]{:S(2)}) collective-permute-start(bf16[192,2304]{1,0:T(8,128)(2,1)} %bitcast.103), channel_id=1, source_target_pairs={{0,4},{4,8},{8,12},{1,5},{5,9},{9,13},{2,6},{6,10},{10,14},{3,7},{... | collective-permute-start | bytes 2654216 | tf_op jit(solution)/shard_map/ppermute | solution.py:21
  13.8 1.5 copy.43
  15.3 0.0 copy-start
  15.4 0.0 copy-done.6
  15.4 0.0 copy-done.5
  15.4 0.1 pad_maximum_fusion.1
  15.5 48.3 %all-gather.1 = bf16[32,16,208]{2,1,0:T(8,128)(2,1)S(1)} all-gather(bf16[2,16,208]{2,1,0:T(8,128)(2,1)S(1)} %pad_maximum_fusion.1), channel_id=3, replica_groups=mesh['groups'=2,'ctx'=4,'dp'=2,'sub'=2] {'ctx','dp','sub'}, dimensions={0}, use_global_device_ids=true | all-gather | bytes 226304 | tf_op jit(solution)/shard_map/all_gather | solution.py:110
  63.8 0.1 slice.33
  63.9 0.2 copy.72
  64.1 0.0 copy-start.4
  64.1 0.3 reshape.47
  64.4 0.1 copy.73
  64.5 0.1 reshape.48
  64.7 1.1 fusion.14.mask_ref
  65.7 0.0 collective-permute-done
  65.7 1.5 copy.42
  67.2 0.0 copy-done.4
  67.2 1.8 fusion.9
  69.0 35.5 %all-gather.4.cloned.1.call-done = bf16[32,576,256]{2,1,0:T(8,128)(2,1)} async-done(((bf16[2,576,256]{2,1,0:T(8,128)(2,1)}), bf16[32,576,256]{2,1,0:T(8,128)(2,1)}) %all-gather.4.cloned.1.call-update) | async-done | bytes 9437200 | tf_op jit(solution)/shard_map/all_gather | solution.py:93
  104.6 0.0 copy-done
  104.6 9.7 %convolution_bitcast_fusion = f32[2,384,4,256]{1,3,0,2:T(8,128)} fusion(bf16[4,4,2,576,256]{4,3,2,1,0:T(8,128)(2,1)} %bitcast.112, bf16[192,4,576]{0,2,1:T(8,128)(2,1)S(1)} %bitcast.91, bf16[192,4,576]{0,2,1:T(8,128)(2,1)S(1)} %bitcast.100), kind=kOutput, calls=%fused_computation.1 | convolution fusion | flops 3627417600 | bytes 14352384 | tf_op jit(solution)/shard_map/rcd,cimdn->mrin/dot_general | solution.py:95
  114.2 3.2 %copy.45 = f32[2,384,4,256]{3,2,1,0:T(4,128)S(1)} copy(f32[2,384,4,256]{1,3,0,2:T(8,128)} %convolution_bitcast_fusion) | data formatting | bytes 6291456 | tf_op jit(solution)/shard_map/rcd,cimdn->mrin/transpose | solution.py:95
  117.5 3.0 %reshape.46 = f32[2,384,1024]{2,1,0:T(8,128)} reshape(f32[2,384,4,256]{3,2,1,0:T(4,128)S(1)} %copy.45) | data formatting | bytes 6291456 | tf_op jit(solution)/shard_map/reshape | solution.py:100
  120.5 3.7 %add_convert_fusion.kv_ref = bf16[2,384,1024]{2,1,0:T(8,128)(2,1)} fusion(f32[2,384,1024]{2,1,0:T(8,128)} %reshape.46, bf16[2,16,384]{2,1,0:T(8,128)(2,1)S(1)} %fusion.9, bf16[2,16,1024]{2,1,0:T(8,128)(2,1)S(1)} %reshape.48), kind=kOutput, calls=%fused_computation | convolution fusion | flops 27525120 | bytes 4808704 | tf_op jit(solution)/shard_map/mrk,mkc->mrc/dot_general | solution.py:101
  124.2 11.6 %shard_map.93 = (bf16[192,2048]{1,0:T(8,128)(2,1)}, bf16[192,2048]{1,0:T(8,128)(2,1)}, bf16[2,384,1024]{2,1,0:T(8,128)(2,1)}) custom-call(s32[384,384]{1,0:T(8,128)} %fusion.14.mask_ref, bf16[192,2048]{1,0:T(8,128)(2,1)} %bitcast.105, bf16[192,2048]{1,0:T(8,128)(2,1)} %bitcast.106, bf16[2,384,1024]{2,1,0:T(8,128)(2,1)} %add_convert_fusion.kv_ref), custom_call_target="tpu_custom_call" | custom-call | tf_op jit(solution)/shard_map/pallas_call | solution.py:62
  135.8 0.0 copy-start.2
  135.8 2.6 %fusion.27 = (bf16[2,192,1024]{2,1,0:T(8,128)(2,1)}, bf16[2,192,1024]{2,1,0:T(8,128)(2,1)S(1)}) fusion(bf16[2,384,1024]{2,1,0:T(8,128)(2,1)} %get-tuple-element.9), kind=kLoop, calls=%fused_computation.44 | loop fusion | bytes 3145728 | tf_op jit(solution)/shard_map/slice | solution.py:149
  138.4 0.0 copy-done.2
  138.4 0.3 convolution_convert_fusion
  138.7 0.0 copy-start.1
  138.7 0.5 copy.50
  139.2 1.4 copy.51
  140.6 0.0 copy-done.1
  140.6 2.7 %fusion.11 = f32[2,16,4,4,144]{4,1,3,2,0:T(8,128)} fusion(bf16[192,4,4,144,1]{0,3,2,1,4:T(8,128)(2,1)S(1)} %bitcast.92, bf16[2,16,1024]{2,1,0:T(8,128)(2,1)S(1)} %reshape.48, bf16[2,384,1024]{2,1,0:T(8,128)(2,1)} %get-tuple-element.9), kind=kOutput, calls=%fused_computation.21 | convolution fusion | flops 40900608 | bytes 2031616 | tf_op jit(solution)/shard_map/mrk,rcij->icjmk/dot_general | solution.py:169
  143.4 0.0 copy-start.3
  143.4 1.4 collective-permute-start.1
  144.8 0.5 fusion.15
  145.3 0.5 fusion.8
  145.9 3.2 %collective-permute-done.1 = bf16[2,192,16]{1,2,0:T(8,128)(2,1)S(1)} collective-permute-done((bf16[2,192,16]{1,2,0:T(8,128)(2,1)S(1)}, bf16[2,192,16]{1,2,0:T(8,128)(2,1)S(1)}, u32[]{:S(2)}, u32[]{:S(2)}) %collective-permute-start.1) | collective-permute-done | bytes 12320 | tf_op jit(solution)/shard_map/ppermute | solution.py:21
  149.1 0.0 copy-done.3
  149.1 0.5 fusion.6
  149.6 0.1 pad_maximum_fusion
  149.8 1.7 copy.64
  151.5 0.0 reduce-scatter.7.cloned.1.call-update
  151.5 0.0 reduce-scatter.9.cloned.1.call-start
  151.6 27.4 %reduce-scatter.7.cloned.1.call-done = f32[832,32]{1,0:T(8,128)} async-done(((f32[3328,32]{1,0:T(8,128)}), f32[832,32]{1,0:T(8,128)}) %reduce-scatter.7.cloned.1.call-update) | async-done | bytes 106512
  179.0 0.0 reduce-scatter.9.cloned.1.call-update
  179.0 23.2 %reduce-scatter.9.cloned.1.call-done = f32[208,32]{1,0:T(8,128)} async-done(((f32[832,32]{1,0:T(8,128)}), f32[208,32]{1,0:T(8,128)}) %reduce-scatter.9.cloned.1.call-update) | async-done | bytes 26640
  202.2 0.9 slice.36
  203.1 0.7 copy.68
  203.8 0.8 slice.37
  204.6 0.7 copy.69
  (4 shorter events, 0.1 us)
Async XLA Ops:
  7.2 8.2 %copy-start.6 = (bf16[2,16,64]{2,1,0:T(8,128)(2,1)S(1)}, bf16[2,16,64]{2,1,0:T(8,128)(2,1)}, u32[]{:S(2)}) copy-start(bf16[2,16,64]{2,1,0:T(8,128)(2,1)} %param.10) | copy-start | bytes 12292
  7.2 8.2 %copy-start.5 = (bf16[2,16,144]{2,1,0:T(8,128)(2,1)S(1)}, bf16[2,16,144]{2,1,0:T(8,128)(2,1)}, u32[]{:S(2)}) copy-start(bf16[2,16,144]{2,1,0:T(8,128)(2,1)} %param.9) | copy-start | bytes 27652
  7.2 97.4 %all-gather.4.cloned.1.call-start = ((), (), s32[]{:S(2)}) async-start(), calls=%async_computation.2 | async-start | bytes 10027008 | tf_op jit(solution)/shard_map/all_gather | solution.py:93
  7.9 171.0 %reduce-scatter.7.cloned.1.call-start = ((), (), s32[]{:S(2)}) async-start(), calls=%async_computation.3 | async-start | bytes 2129920
  8.0 57.7 %collective-permute-start = (bf16[192,2304]{1,0:T(8,128)(2,1)}, bf16[192,2304]{1,0:T(8,128)(2,1)}, u32[]{:S(2)}, u32[]{:S(2)}) collective-permute-start(bf16[192,2304]{1,0:T(8,128)(2,1)} %bitcast.103), channel_id=1, source_target_pairs={{0,4},{4,8},{8,12},{1,5},{5,9},{9,13},{2,6},{6,10},{10,14},{3,7},{... | collective-permute-start | bytes 2654216 | tf_op jit(solution)/shard_map/ppermute | solution.py:21
  15.3 89.2 %copy-start = (bf16[1,192,2304]{1,2,0:T(8,128)(2,1)}, bf16[1,192,2304]{1,2,0:T(8,128)(2,1)S(1)}, u32[]{:S(2)}) copy-start(bf16[1,192,2304]{1,2,0:T(8,128)(2,1)S(1)} %copy.43) | copy-start | bytes 2654212
  64.1 3.2 %copy-start.4 = (bf16[1,192,2304]{2,1,0:T(8,128)(2,1)S(1)}, bf16[1,192,2304]{2,1,0:T(8,128)(2,1)}, u32[]{:S(2)}) copy-start(bf16[1,192,2304]{2,1,0:T(8,128)(2,1)} %param.6) | copy-start | bytes 2654212
  135.8 2.6 %copy-start.2 = (bf16[2,384,1024]{2,1,0:T(8,128)(2,1)S(1)}, bf16[2,384,1024]{2,1,0:T(8,128)(2,1)}, u32[]{:S(2)}) copy-start(bf16[2,384,1024]{2,1,0:T(8,128)(2,1)} %get-tuple-element.9) | copy-start | bytes 4718596
  138.7 2.0 copy-start.1
  143.4 5.8 %copy-start.3 = (f32[2,16,4,4,144]{4,1,3,2,0:T(8,128)S(1)}, f32[2,16,4,4,144]{4,1,3,2,0:T(8,128)}, u32[]{:S(2)}) copy-start(f32[2,16,4,4,144]{4,1,3,2,0:T(8,128)} %fusion.11) | copy-start | bytes 884740
  143.4 5.8 %collective-permute-start.1 = (bf16[2,192,16]{1,2,0:T(8,128)(2,1)S(1)}, bf16[2,192,16]{1,2,0:T(8,128)(2,1)S(1)}, u32[]{:S(2)}, u32[]{:S(2)}) collective-permute-start(bf16[2,192,16]{1,2,0:T(8,128)(2,1)S(1)} %convolution_convert_fusion), channel_id=1, source_target_pairs={{4,0},{8,4},{12,8},{5,1},{9,5},{13,9},{6,2},{10,6},{14,10},{7,3},{... | collective-permute-start | bytes 36872 | tf_op jit(solution)/shard_map/ppermute | solution.py:21
  151.5 50.7 %reduce-scatter.9.cloned.1.call-start = ((), (), s32[]{:S(2)}) async-start(), calls=%async_computation.4 | async-start | bytes 532480
Sparse Core Ops, SparseCore 0:
  10.3 94.2 all-gather.3
  151.7 27.2 reduce-scatter.6
  181.3 20.8 reduce-scatter.8

commit v6 on v5

--- a/solution.py
+++ b/solution.py
@@ -85,22 +85,57 @@
     return attention_heads(visible.astype(jnp.int32), query_rows, grad_rows, key_value)
 
 
-def project_rows(row_block, kv_weight, down_full, up_full):
-    low_rank = jnp.einsum(
-        "rd,mkd->mrk", row_block, down_full, preferred_element_type=jnp.float32
-    ).astype(jnp.bfloat16)
+def projection_kernel(prev_ref, own_ref, weight_ref, low_prev_ref, low_own_ref, up_ref, out_ref):
+    row_shards = weight_ref.shape[0]
+    depth = weight_ref.shape[3]
+    rows = own_ref.shape[0]
+    up = up_ref[0]
+    for half, (rows_ref, low_ref) in enumerate(((prev_ref, low_prev_ref), (own_ref, low_own_ref))):
+        total = jnp.dot(low_ref[0], up, preferred_element_type=jnp.float32) * adapter_scale
+        base = jnp.dot(
+            rows_ref[:, :depth], weight_ref[0, 0, 0], preferred_element_type=jnp.float32
+        )
+        for c in range(1, row_shards):
+            base = base + jnp.dot(
+                rows_ref[:, c * depth:(c + 1) * depth],
+                weight_ref[c, 0, 0],
+                preferred_element_type=jnp.float32,
+            )
+        out_ref[0, half * rows:(half + 1) * rows, :] = (base + total).astype(out_ref.dtype)
+
+
+def project_pair(rows_prev, rows_own, gathered, low_prev, low_own, up_full):
+    row_shards, col_shards, members, depth, cols = gathered.shape
+    rows, width = rows_own.shape
+    rank = up_full.shape[1]
+    return pl.pallas_call(
+        projection_kernel,
+        grid=(members, col_shards),
+        in_specs=[
+            pl.BlockSpec((rows, width), lambda m, i: (0, 0)),
+            pl.BlockSpec((rows, width), lambda m, i: (0, 0)),
+            pl.BlockSpec((row_shards, 1, 1, depth, cols), lambda m, i: (0, i, m, 0, 0)),
+            pl.BlockSpec((1, rows, rank), lambda m, i: (m, 0, 0)),
+            pl.BlockSpec((1, rows, rank), lambda m, i: (m, 0, 0)),
+            pl.BlockSpec((1, rank, cols), lambda m, i: (m, 0, i)),
+        ],
+        out_specs=pl.BlockSpec((1, 2 * rows, cols), lambda m, i: (m, 0, i)),
+        out_shape=jax.ShapeDtypeStruct((members, 2 * rows, col_shards * cols), jnp.bfloat16),
+    )(rows_prev, rows_own, gathered, low_prev, low_own, up_full)
+
+
+def project_rows(rows_previous, rows_own, kv_weight, down_full, up_full):
+    def low_of(rows):
+        return jnp.einsum(
+            "rd,mkd->mrk", rows, down_full, preferred_element_type=jnp.float32
+        ).astype(jnp.bfloat16)
+
+    low_previous, low_rank = low_of(rows_previous), low_of(rows_own)
     row_shards, col_shards = lax.axis_size("ctx"), lax.axis_size(("dp", "sub"))
     gathered = lax.all_gather(kv_weight, ("ctx", "dp", "sub"), axis=0, tiled=False)
     gathered = gathered.reshape((row_shards, col_shards) + kv_weight.shape)
-    base_part = jnp.einsum(
-        "rcd,cimdn->mrin",
-        row_block.reshape(row_block.shape[0], row_shards, kv_weight.shape[1]),
-        gathered,
-        preferred_element_type=jnp.float32,
-    ).reshape(2, row_block.shape[0], col_shards * kv_weight.shape[2])
-    extra_part = jnp.einsum("mrk,mkc->mrc", low_rank, up_full, preferred_element_type=jnp.float32)
-    key_value = (base_part + adapter_scale * extra_part).astype(jnp.bfloat16)
-    return (low_rank, key_value)
+    key_value = project_pair(rows_previous, rows_own, gathered, low_previous, low_rank, up_full)
+    return low_previous, low_rank, key_value
 
 
 def gather_adapters(adapter_down, adapter_up):
@@ -140,11 +175,9 @@
     rows_previous = shifted(rows_own, "ctx", 1)
     down_full, up_full = gather_adapters(adapter_down, adapter_up)
     is_first = lax.axis_index("ctx") == 0
-    low_both, kv_both = project_rows(
-        jnp.concatenate([rows_previous, rows_own], axis=0), kv_weight, down_full, up_full
-    )
-    low_previous = low_both[:, :length]
-    low_rank = low_both[:, length:]
+    low_previous, low_rank, kv_both = project_rows(
+        rows_previous, rows_own, kv_weight, down_full, up_full
+    )
     attended, query_grad, kv_grads = attend(query_rows, kv_both, grad_rows, is_first)
     far_part = kv_grads[:, :length]
     near_part = kv_grads[:, length:]

time: 212 us -> 204 us (0.962)
  matrix products: 19.6 us -> 4.34 us
  Pallas kernels: 11.6 us -> 22.8 us
  local copies, waits for them, and re-layouts: 19.5 us -> 13.9 us
    dot_general x3 -> x2, matrix products: 15.1 us -> 0.69 us  [low_of(): jnp.einsum('rd,mkd->mrk', rows, down_full, preferred_element_type=jnp.flo...]
    pallas_call x0 -> x1, Pallas kernels: none -> 11.2 us  [project_pair(): pl.pallas_call(projection_kernel, grid=(members, col_shards), in_specs=[p...]
    transpose x1 -> x0, local copies, waits for them, and re-layouts: 3.25 us -> none  [project_rows(): jnp.einsum('rcd,cimdn->mrin', row_block.reshape(row_block.shape[0], row_s...]
    reshape x1 -> x0, local copies, waits for them, and re-layouts: 3.04 us -> none  [project_rows(): base_part = jnp.einsum('rcd,cimdn->mrin', row_block.reshape(row_block.sha...]
    unnamed x20 -> x18, local copies, waits for them, and re-layouts: 4.86 us -> 4.94 us
  transfers between devices with their start and end apart: 5 -> 5, of which waited for: 4 -> 4; matrix products, arithmetic and copies ran while one was open for 4% -> 3% of each run, Pallas kernels for 0% -> 0%
where the time goes in v6:
time: 204 us; the launch traced here: 203 us
  waiting for transfers between devices  91.1 us (45%)
  blocking collectives  49.1 us (24%)
  Pallas kernels  22.8 us (11%)
  local copies, waits for them, and re-layouts  13.9 us (7%)
  between operations  13.9 us (7%)
  starting transfers between devices  6.4 us (3%)
  matrix products  4.34 us (2%)
    unnamed x5, waiting for transfers between devices  51.4 us
    all_gather x1, blocking collectives, gather_adapters(): gathered = lax.all_gather(joined, axes, axis=0, tiled=False)  49.1 us
    all_gather x1, waiting for transfers between devices, project_rows(): lax.all_gather(kv_weight, ('ctx', 'dp', 'sub'), axis=0, tiled=False)  35.9 us
    pallas_call x1, Pallas kernels, attention_heads(): pl.pallas_call(attention_kernel, grid=(heads,), in_specs=[pl.BlockSpec(ma...  11.6 us
    pallas_call x1, Pallas kernels, project_pair(): pl.pallas_call(projection_kernel, grid=(members, col_shards), in_specs=[p...  11.2 us
    ppermute x2, starting transfers between devices, shifted(): return lax.ppermute(value, axis, pairs)  6.28 us
    unnamed x18, local copies, waits for them, and re-layouts  4.94 us
  transfers between devices with their start and end apart: 5, of which 4 were waited for; matrix products, arithmetic and copies ran while one was open for 3% of the time, Pallas kernels for 0%

profile of v6, /device:TPU:0, one launch (start us, length us, event | category | flops | bytes accessed | tf_op | source)
XLA Modules:
  0.0 202.9 jit_solution(17042823217621760341)
XLA Ops:
  7.2 0.0 copy-start.5
  7.2 0.0 copy-start.4
  7.2 0.0 all-gather.4.cloned.1.call-start
  7.2 0.7 all-gather.4.cloned.1.call-update
  7.9 0.0 reduce-scatter.7.cloned.1.call-start
  8.0 5.0 %collective-permute-start = (bf16[192,2304]{1,0:T(8,128)(2,1)}, bf16[192,2304]{1,0:T(8,128)(2,1)S(1)}, u32[]{:S(2)}, u32[]{:S(2)}) collective-permute-start(bf16[192,2304]{1,0:T(8,128)(2,1)} %bitcast.78), channel_id=1, source_target_pairs={{0,4},{4,8},{8,12},{1,5},{5,9},{9,13},{2,6},{6,10},{10,14},{3,7},{... | collective-permute-start | bytes 2654216 | tf_op jit(solution)/shard_map/ppermute | solution.py:21
  13.0 0.0 copy-start
  13.0 1.6 copy.59
  14.6 0.0 copy-done.5
  14.6 0.0 copy-done.4
  14.6 0.1 pad_maximum_fusion.1
  14.7 49.1 %all-gather.1 = bf16[32,16,208]{2,1,0:T(8,128)(2,1)S(1)} all-gather(bf16[2,16,208]{2,1,0:T(8,128)(2,1)S(1)} %pad_maximum_fusion.1), channel_id=3, replica_groups=mesh['groups'=2,'ctx'=4,'dp'=2,'sub'=2] {'ctx','dp','sub'}, dimensions={0}, use_global_device_ids=true | all-gather | bytes 226304 | tf_op jit(solution)/shard_map/all_gather | solution.py:145
  63.8 0.1 slice.25
  63.9 0.2 copy.81
  64.1 0.3 reshape.39
  64.4 0.0 copy-done
  64.4 0.3 convolution_convert_fusion.2
  64.8 0.8 copy.57
  65.6 0.1 copy.82
  65.6 0.8 reshape.40.up_ref
  66.4 1.1 fusion.10.mask_ref
  67.5 0.0 collective-permute-done.prev_ref
  67.5 0.0 copy-start.1
  67.5 0.3 convolution_convert_fusion.3
  67.8 0.8 copy.56
  68.6 35.9 %all-gather.4.cloned.1.call-done = bf16[32,576,256]{2,1,0:T(8,128)(2,1)} async-done(((bf16[2,576,256]{2,1,0:T(8,128)(2,1)}), bf16[32,576,256]{2,1,0:T(8,128)(2,1)}) %all-gather.4.cloned.1.call-update) | async-done | bytes 9437200 | tf_op jit(solution)/shard_map/all_gather | solution.py:135
  104.6 0.0 copy-done.1
  104.6 11.2 %shard_map.93.kv_ref = bf16[2,384,1024]{2,1,0:T(8,128)(2,1)} custom-call(bf16[192,2304]{1,0:T(8,128)(2,1)} %copy-done.1, bf16[192,2304]{1,0:T(8,128)(2,1)} %bitcast.79, bf16[4,4,2,576,256]{4,3,2,1,0:T(8,128)(2,1)} %bitcast.77, bf16[2,192,16]{2,1,0:T(8,128)(2,1)} %bitcast.92, bf16[2,192,16]{2,1,0:T(8,128)(2,1)} %bitcast.91, bf16[2,16,1024]{2,1,0:T(8,128)(2,1)} %reshape.40.up_ref), custom_call_target="tpu_custom_call" | custom-call | tf_op jit(solution)/shard_map/pallas_call | solution.py:111
  115.8 11.6 %shard_map.94 = (bf16[192,2048]{1,0:T(8,128)(2,1)}, bf16[192,2048]{1,0:T(8,128)(2,1)}, bf16[2,384,1024]{2,1,0:T(8,128)(2,1)}) custom-call(s32[384,384]{1,0:T(8,128)} %fusion.10.mask_ref, bf16[192,2048]{1,0:T(8,128)(2,1)} %bitcast.88, bf16[192,2048]{1,0:T(8,128)(2,1)} %bitcast.89, bf16[2,384,1024]{2,1,0:T(8,128)(2,1)} %shard_map.93.kv_ref), custom_call_target="tpu_custom_call" | custom-call | tf_op jit(solution)/shard_map/pallas_call | solution.py:62
  127.4 0.0 copy-start.2
  127.4 0.0 copy-start.3
  127.4 2.5 %fusion.23 = (bf16[2,192,1024]{2,1,0:T(8,128)(2,1)S(1)}, bf16[2,192,1024]{2,1,0:T(8,128)(2,1)}) fusion(bf16[2,384,1024]{2,1,0:T(8,128)(2,1)} %get-tuple-element.9), kind=kLoop, calls=%fused_computation.37 | loop fusion | bytes 3145728 | tf_op jit(solution)/shard_map/slice | solution.py:182
  129.9 0.0 copy-done.2
  129.9 0.0 copy-done.3
  129.9 0.3 convolution_convert_fusion
  130.2 1.4 copy.61
  131.7 0.5 fusion.12
  132.2 0.5 copy.62
  132.7 1.9 fusion.7
  134.6 1.3 collective-permute-start.1
  135.9 0.5 fusion.3
  136.4 3.8 %collective-permute-done.1 = bf16[2,192,16]{1,2,0:T(8,128)(2,1)S(1)} collective-permute-done((bf16[2,192,16]{1,2,0:T(8,128)(2,1)S(1)}, bf16[2,192,16]{1,2,0:T(8,128)(2,1)S(1)}, u32[]{:S(2)}, u32[]{:S(2)}) %collective-permute-start.1) | collective-permute-done | bytes 12320 | tf_op jit(solution)/shard_map/ppermute | solution.py:21
  140.2 0.5 fusion.1
  140.7 0.1 pad_maximum_fusion
  140.9 1.7 copy.73
  142.6 0.0 reduce-scatter.7.cloned.1.call-update
  142.7 0.0 reduce-scatter.9.cloned.1.call-start
  142.7 27.4 %reduce-scatter.7.cloned.1.call-done = f32[832,32]{1,0:T(8,128)} async-done(((f32[3328,32]{1,0:T(8,128)}), f32[832,32]{1,0:T(8,128)}) %reduce-scatter.7.cloned.1.call-update) | async-done | bytes 106512
  170.1 0.0 reduce-scatter.9.cloned.1.call-update
  170.1 23.3 %reduce-scatter.9.cloned.1.call-done = f32[208,32]{1,0:T(8,128)} async-done(((f32[832,32]{1,0:T(8,128)}), f32[208,32]{1,0:T(8,128)}) %reduce-scatter.9.cloned.1.call-update) | async-done | bytes 26640
  193.4 0.9 slice.26
  194.3 0.7 copy.77
  195.0 0.8 slice.27
  195.7 0.7 copy.78
  (4 shorter events, 0.1 us)
Async XLA Ops:
  7.2 7.4 %copy-start.5 = (bf16[2,16,64]{2,1,0:T(8,128)(2,1)S(1)}, bf16[2,16,64]{2,1,0:T(8,128)(2,1)}, u32[]{:S(2)}) copy-start(bf16[2,16,64]{2,1,0:T(8,128)(2,1)} %param.10) | copy-start | bytes 12292
  7.2 7.4 %copy-start.4 = (bf16[2,16,144]{2,1,0:T(8,128)(2,1)S(1)}, bf16[2,16,144]{2,1,0:T(8,128)(2,1)}, u32[]{:S(2)}) copy-start(bf16[2,16,144]{2,1,0:T(8,128)(2,1)} %param.9) | copy-start | bytes 27652
  7.2 97.4 %all-gather.4.cloned.1.call-start = ((), (), s32[]{:S(2)}) async-start(), calls=%async_computation.2 | async-start | bytes 10027008 | tf_op jit(solution)/shard_map/all_gather | solution.py:135
  7.9 162.1 %reduce-scatter.7.cloned.1.call-start = ((), (), s32[]{:S(2)}) async-start(), calls=%async_computation.3 | async-start | bytes 2129920
  8.0 59.5 %collective-permute-start = (bf16[192,2304]{1,0:T(8,128)(2,1)}, bf16[192,2304]{1,0:T(8,128)(2,1)S(1)}, u32[]{:S(2)}, u32[]{:S(2)}) collective-permute-start(bf16[192,2304]{1,0:T(8,128)(2,1)} %bitcast.78), channel_id=1, source_target_pairs={{0,4},{4,8},{8,12},{1,5},{5,9},{9,13},{2,6},{6,10},{10,14},{3,7},{... | collective-permute-start | bytes 2654216 | tf_op jit(solution)/shard_map/ppermute | solution.py:21
  13.0 51.4 %copy-start = (bf16[1,192,2304]{2,1,0:T(8,128)(2,1)S(1)}, bf16[1,192,2304]{2,1,0:T(8,128)(2,1)}, u32[]{:S(2)}) copy-start(bf16[1,192,2304]{2,1,0:T(8,128)(2,1)} %param.6) | copy-start | bytes 2654212
  67.5 37.1 %copy-start.1 = (bf16[192,2304]{1,0:T(8,128)(2,1)}, bf16[192,2304]{1,0:T(8,128)(2,1)S(1)}, u32[]{:S(2)}) copy-start(bf16[192,2304]{1,0:T(8,128)(2,1)S(1)} %collective-permute-done.prev_ref) | copy-start | bytes 2654212
  127.4 2.5 %copy-start.2 = (bf16[2,384,1024]{2,1,0:T(8,128)(2,1)S(1)}, bf16[2,384,1024]{2,1,0:T(8,128)(2,1)}, u32[]{:S(2)}) copy-start(bf16[2,384,1024]{2,1,0:T(8,128)(2,1)} %get-tuple-element.9) | copy-start | bytes 4718596
  127.4 2.5 %copy-start.3 = (bf16[2,16,1024]{2,1,0:T(8,128)(2,1)S(1)}, bf16[2,16,1024]{2,1,0:T(8,128)(2,1)}, u32[]{:S(2)}) copy-start(bf16[2,16,1024]{2,1,0:T(8,128)(2,1)} %reshape.40.up_ref) | copy-start | bytes 196612
  134.6 5.6 %collective-permute-start.1 = (bf16[2,192,16]{1,2,0:T(8,128)(2,1)S(1)}, bf16[2,192,16]{1,2,0:T(8,128)(2,1)S(1)}, u32[]{:S(2)}, u32[]{:S(2)}) collective-permute-start(bf16[2,192,16]{1,2,0:T(8,128)(2,1)S(1)} %convolution_convert_fusion), channel_id=1, source_target_pairs={{4,0},{8,4},{12,8},{5,1},{9,5},{13,9},{6,2},{10,6},{14,10},{7,3},{... | collective-permute-start | bytes 36872 | tf_op jit(solution)/shard_map/ppermute | solution.py:21
  142.7 50.7 %reduce-scatter.9.cloned.1.call-start = ((), (), s32[]{:S(2)}) async-start(), calls=%async_computation.4 | async-start | bytes 532480
Sparse Core Ops, SparseCore 0:
  10.3 94.2 all-gather.3
  142.8 27.2 reduce-scatter.6
  172.5 20.8 reduce-scatter.8

commit v7 on v6

--- a/solution.py
+++ b/solution.py
@@ -92,15 +92,19 @@
     up = up_ref[0]
     for half, (rows_ref, low_ref) in enumerate(((prev_ref, low_prev_ref), (own_ref, low_own_ref))):
         total = jnp.dot(low_ref[0], up, preferred_element_type=jnp.float32) * adapter_scale
-        base = jnp.dot(
-            rows_ref[:, :depth], weight_ref[0, 0, 0], preferred_element_type=jnp.float32
-        )
-        for c in range(1, row_shards):
-            base = base + jnp.dot(
-                rows_ref[:, c * depth:(c + 1) * depth],
-                weight_ref[c, 0, 0],
-                preferred_element_type=jnp.float32,
+        if depth % 16 == 0:
+            weight = jnp.concatenate([weight_ref[c, 0, 0] for c in range(row_shards)], axis=0)
+            base = jnp.dot(rows_ref[...], weight, preferred_element_type=jnp.float32)
+        else:
+            base = jnp.dot(
+                rows_ref[:, :depth], weight_ref[0, 0, 0], preferred_element_type=jnp.float32
             )
+            for c in range(1, row_shards):
+                base = base + jnp.dot(
+                    rows_ref[:, c * depth:(c + 1) * depth],
+                    weight_ref[c, 0, 0],
+                    preferred_element_type=jnp.float32,
+                )
         out_ref[0, half * rows:(half + 1) * rows, :] = (base + total).astype(out_ref.dtype)
 
 
@@ -151,14 +155,32 @@
     return unshard(gathered[..., :down_cols]), unshard(gathered[..., down_cols:])
 
 
+def halving_scatter(blocks, axis):
+    size = lax.axis_size(axis)
+    if size & (size - 1):
+        return lax.psum_scatter(blocks, axis, scatter_dimension=0, tiled=True)[0]
+    me = lax.axis_index(axis)
+    stride = size // 2
+    while stride >= 1:
+        halves = blocks.reshape((2, blocks.shape[0] // 2) + blocks.shape[1:])
+        bit = (me // stride) % 2
+        keep = lax.dynamic_index_in_dim(halves, bit, axis=0, keepdims=False)
+        send = lax.dynamic_index_in_dim(halves, 1 - bit, axis=0, keepdims=False)
+        pairs = [(i, i ^ stride) for i in range(size)]
+        blocks = keep + lax.ppermute(send, axis, pairs)
+        stride //= 2
+    return blocks[0]
+
+
 def scatter_adapter_grads(joined_down, joined_up):
     members_rank = joined_down.shape[-1]
     down_cols = joined_down.shape[2]
     joined = jnp.concatenate([joined_down, joined_up], axis=2)
-    partial = lax.psum_scatter(
-        joined.reshape(-1, members_rank), ("dp", "sub"), scatter_dimension=0, tiled=True
-    )
-    mine = lax.psum_scatter(partial, "ctx", scatter_dimension=0, tiled=True)
+    dp_size, sub_size = lax.axis_size("dp"), lax.axis_size("sub")
+    joined = joined.reshape((dp_size, sub_size) + joined.shape[1:])
+    mine = halving_scatter(joined.swapaxes(0, 1), "sub")
+    mine = halving_scatter(mine, "dp")
+    mine = halving_scatter(mine, "ctx")
 
     def unshard(piece):
         return piece.reshape(piece.shape[0], 2, -1).transpose(1, 2, 0)

time: 204 us -> 166 us (0.81)
  waiting for transfers between devices: 91.1 us -> 47.8 us
  starting transfers between devices: 6.4 us -> 12 us
  matrix products: 4.34 us -> 9.01 us
  local copies, waits for them, and re-layouts: 13.9 us -> 9.91 us
    unnamed x5 -> x1, waiting for transfers between devices: 51.4 us -> 0.68 us
    ppermute x0 -> x4, waiting for transfers between devices: none -> 11.6 us  [halving_scatter(): blocks = keep + lax.ppermute(send, axis, pairs)]
    ppermute x0 -> x4, starting transfers between devices: none -> 5.59 us  [halving_scatter(): blocks = keep + lax.ppermute(send, axis, pairs)]
    ppermute x2, waiting for transfers between devices: 3.78 us -> 0.01 us  [shifted(): return lax.ppermute(value, axis, pairs)]
    unnamed x18 -> x23, local copies, waits for them, and re-layouts: 4.94 us -> 1.84 us
  transfers between devices with their start and end apart: 5 -> 7, of which waited for: 4 -> 5; matrix products, arithmetic and copies ran while one was open for 3% -> 7% of each run, Pallas kernels for 0% -> 0%
where the time goes in v7:
time: 166 us; the launch traced here: 165 us
  blocking collectives  49.1 us (30%)
  waiting for transfers between devices  47.8 us (29%)
  Pallas kernels  21.9 us (13%)
  between operations  14.3 us (9%)
  starting transfers between devices  12 us (7%)
  local copies, waits for them, and re-layouts  9.91 us (6%)
  matrix products  9.01 us (5%)
    all_gather x1, blocking collectives, gather_adapters(): gathered = lax.all_gather(joined, axes, axis=0, tiled=False)  49.1 us
    all_gather x1, waiting for transfers between devices, project_rows(): lax.all_gather(kv_weight, ('ctx', 'dp', 'sub'), axis=0, tiled=False)  35.5 us
    pallas_call x1, Pallas kernels, attention_heads(): pl.pallas_call(attention_kernel, grid=(heads,), in_specs=[pl.BlockSpec(ma...  11.7 us
    ppermute x4, waiting for transfers between devices, halving_scatter(): blocks = keep + lax.ppermute(send, axis, pairs)  11.6 us
    pallas_call x1, Pallas kernels, project_pair(): pl.pallas_call(projection_kernel, grid=(members, col_shards), in_specs=[p...  10.2 us
    ppermute x2, starting transfers between devices, shifted(): return lax.ppermute(value, axis, pairs)  6.4 us
    ppermute x4, starting transfers between devices, halving_scatter(): blocks = keep + lax.ppermute(send, axis, pairs)  5.59 us
  transfers between devices with their start and end apart: 7, of which 5 were waited for; matrix products, arithmetic and copies ran while one was open for 7% of the time, Pallas kernels for 0%

profile of v7, /device:TPU:0, one launch (start us, length us, event | category | flops | bytes accessed | tf_op | source)
XLA Modules:
  0.0 165.5 jit_solution(10191078903021851237)
XLA Ops:
  7.2 0.0 copy-start.9
  7.2 0.0 copy-start.8
  7.2 0.0 all-gather.4.cloned.1.call-start
  7.2 0.7 all-gather.4.cloned.1.call-update
  7.9 5.0 %collective-permute-start = (bf16[192,2304]{1,0:T(8,128)(2,1)}, bf16[192,2304]{1,0:T(8,128)(2,1)S(1)}, u32[]{:S(2)}, u32[]{:S(2)}) collective-permute-start(bf16[192,2304]{1,0:T(8,128)(2,1)} %bitcast.91), channel_id=1, source_target_pairs={{0,4},{4,8},{8,12},{1,5},{5,9},{9,13},{2,6},{6,10},{10,14},{3,7},{... | collective-permute-start | bytes 2654216 | tf_op jit(solution)/shard_map/ppermute | solution.py:21
  12.9 0.0 copy-start
  12.9 1.6 copy.46
  14.5 0.0 copy-done.9
  14.6 0.0 copy-done.8
  14.6 0.1 pad_maximum_fusion
  14.6 49.1 %all-gather.1 = bf16[32,16,208]{2,1,0:T(8,128)(2,1)S(1)} all-gather(bf16[2,16,208]{2,1,0:T(8,128)(2,1)S(1)} %pad_maximum_fusion), channel_id=3, replica_groups=mesh['groups'=2,'ctx'=4,'dp'=2,'sub'=2] {'ctx','dp','sub'}, dimensions={0}, use_global_device_ids=true | all-gather | bytes 226304 | tf_op jit(solution)/shard_map/all_gather | solution.py:149
  63.8 0.1 slice.27
  63.9 0.2 copy.59
  64.0 0.3 reshape.57
  64.4 0.0 copy-done
  64.4 0.3 convolution_convert_fusion.2
  64.7 0.0 copy-start.5
  64.7 0.8 copy.44
  65.5 0.1 copy.60
  65.6 0.8 reshape.58.up_ref
  66.4 1.0 fusion.10.mask_ref
  67.4 0.0 collective-permute-done.prev_ref
  67.4 0.0 copy-start.1
  67.4 0.3 convolution_convert_fusion.3
  67.8 0.8 copy.43
  68.6 35.5 %all-gather.4.cloned.1.call-done = bf16[32,576,256]{2,1,0:T(8,128)(2,1)} async-done(((bf16[2,576,256]{2,1,0:T(8,128)(2,1)}), bf16[32,576,256]{2,1,0:T(8,128)(2,1)}) %all-gather.4.cloned.1.call-update) | async-done | bytes 9437200 | tf_op jit(solution)/shard_map/all_gather | solution.py:139
  104.1 0.0 copy-done.1
  104.1 10.2 %shard_map.93.kv_ref = bf16[2,384,1024]{2,1,0:T(8,128)(2,1)} custom-call(bf16[192,2304]{1,0:T(8,128)(2,1)} %copy-done.1, bf16[192,2304]{1,0:T(8,128)(2,1)} %bitcast.92, bf16[4,4,2,576,256]{4,3,2,1,0:T(8,128)(2,1)} %bitcast.90, bf16[2,192,16]{2,1,0:T(8,128)(2,1)} %bitcast.108, bf16[2,192,16]{2,1,0:T(8,128)(2,1)} %bitcast.107, bf16[2,16,1024]{2,1,0:T(8,128)(2,1)} %reshape.58.up_ref), custom_call_target="tpu_custom_call" | custom-call | tf_op jit(solution)/shard_map/pallas_call | solution.py:115
  114.3 0.0 copy-done.5
  114.3 0.0 copy-start.4
  114.3 11.7 %shard_map.94 = (bf16[192,2048]{1,0:T(8,128)(2,1)}, bf16[192,2048]{1,0:T(8,128)(2,1)}, bf16[2,384,1024]{2,1,0:T(8,128)(2,1)}) custom-call(s32[384,384]{1,0:T(8,128)} %fusion.10.mask_ref, bf16[192,2048]{1,0:T(8,128)(2,1)} %bitcast.102, bf16[192,2048]{1,0:T(8,128)(2,1)} %bitcast.103, bf16[2,384,1024]{2,1,0:T(8,128)(2,1)} %shard_map.93.kv_ref), custom_call_target="tpu_custom_call" | custom-call | tf_op jit(solution)/shard_map/pallas_call | solution.py:62
  126.0 0.0 copy-done.4
  126.0 2.1 %convolution_convert_fusion = bf16[2,192,16]{1,2,0:T(8,128)(2,1)} fusion(bf16[2,16,1024]{2,1,0:T(8,128)(2,1)S(1)} %copy-done.4, bf16[2,384,1024]{2,1,0:T(8,128)(2,1)} %get-tuple-element.9), kind=kOutput, calls=%fused_computation.6 | convolution fusion | flops 12589056 | bytes 864256 | tf_op jit(solution)/shard_map/mrc,mkc->mrk/dot_general | solution.py:206
  128.0 0.0 copy-start.2
  128.0 2.6 %fusion.28 = (bf16[2,192,1024]{2,1,0:T(8,128)(2,1)S(1)}, bf16[2,192,1024]{2,1,0:T(8,128)(2,1)}) fusion(bf16[2,384,1024]{2,1,0:T(8,128)(2,1)} %get-tuple-element.9), kind=kLoop, calls=%fused_computation.51 | loop fusion | bytes 3145728 | tf_op jit(solution)/shard_map/slice | solution.py:204
  130.6 0.0 copy-done.2
  130.6 2.4 %fusion.7 = f32[2,16,4,4,144]{4,1,3,2,0:T(8,128)} fusion(bf16[192,4,4,144,1]{0,3,2,1,4:T(8,128)(2,1)S(1)} %bitcast.88, bf16[2,16,1024]{2,1,0:T(8,128)(2,1)} %reshape.58.up_ref, bf16[2,384,1024]{2,1,0:T(8,128)(2,1)S(1)} %copy-done.2), kind=kOutput, calls=%fused_computation.18 | convolution fusion | flops 40900608 | bytes 2326528 | tf_op jit(solution)/shard_map/mrk,rcij->icjmk/dot_general | solution.py:224
  133.0 0.0 copy-start.6
  133.0 1.4 collective-permute-start.1
  134.4 1.4 copy.48
  135.9 0.0 copy-done.6
  135.9 1.2 fusion.17
  137.1 0.0 copy-start.3
  137.1 0.5 copy.49
  137.6 1.4 fusion.3
  139.1 0.0 collective-permute-done.1
  139.1 0.0 copy-done.3
  139.1 1.2 fusion.1
  140.4 0.1 fusion.12
  140.5 0.3 collective-permute-start.2
  140.8 1.3 collective-permute-done.2
  142.1 0.1 fusion.15
  142.2 0.8 collective-permute-start.3
  143.0 4.9 %collective-permute-done.3 = f32[1,4,208,32]{2,3,1,0:T(8,128)S(1)} collective-permute-done((f32[1,4,208,32]{2,3,1,0:T(8,128)S(1)}, f32[1,4,208,32]{2,3,1,0:T(8,128)S(1)}, u32[]{:S(2)}, u32[]{:S(2)}) %collective-permute-start.3) | collective-permute-done | bytes 106528 | tf_op jit(solution)/shard_map/ppermute | solution.py:170
  148.0 2.6 %collective-permute-start.4 = (f32[2,208,32]{1,2,0:T(8,128)S(1)}, f32[2,208,32]{1,2,0:T(8,128)S(1)}, u32[]{:S(2)}, u32[]{:S(2)}) collective-permute-start(f32[2,208,32]{1,2,0:T(8,128)S(1)} %dynamic-slice_bitcast_fusion.1), channel_id=1, source_target_pairs={{0,8},{4,12},{8,0},{12,4},{1,9},{5,13},{9,1},{13,5},{2,10},{6,14},... | collective-permute-start | bytes 159752 | tf_op jit(solution)/shard_map/ppermute | solution.py:170
  150.6 3.3 %collective-permute-done.4 = f32[2,208,32]{1,2,0:T(8,128)S(1)} collective-permute-done((f32[2,208,32]{1,2,0:T(8,128)S(1)}, f32[2,208,32]{1,2,0:T(8,128)S(1)}, u32[]{:S(2)}, u32[]{:S(2)}) %collective-permute-start.4) | collective-permute-done | bytes 53280 | tf_op jit(solution)/shard_map/ppermute | solution.py:170
  153.9 1.9 %collective-permute-start.5 = (f32[1,208,32]{1,2,0:T(8,128)S(1)}, f32[1,208,32]{1,2,0:T(8,128)S(1)}, u32[]{:S(2)}, u32[]{:S(2)}) collective-permute-start(f32[1,208,32]{1,2,0:T(8,128)S(1)} %constant_dynamic-slice_fusion), channel_id=1, source_target_pairs={{0,4},{4,0},{8,12},{12,8},{1,5},{5,1},{9,13},{13,9},{2,6},{6,2},{1... | collective-permute-start | bytes 79880 | tf_op jit(solution)/shard_map/ppermute | solution.py:170
  155.8 2.1 %collective-permute-done.5 = f32[1,208,32]{1,2,0:T(8,128)S(1)} collective-permute-done((f32[1,208,32]{1,2,0:T(8,128)S(1)}, f32[1,208,32]{1,2,0:T(8,128)S(1)}, u32[]{:S(2)}, u32[]{:S(2)}) %collective-permute-start.5) | collective-permute-done | bytes 26656 | tf_op jit(solution)/shard_map/ppermute | solution.py:170
  157.9 0.0 copy-start.7
  157.9 0.7 slice.29
  158.6 0.0 copy-done.7
  (10 shorter events, 0.2 us)
Async XLA Ops:
  7.2 7.4 %copy-start.9 = (bf16[2,16,64]{2,1,0:T(8,128)(2,1)S(1)}, bf16[2,16,64]{2,1,0:T(8,128)(2,1)}, u32[]{:S(2)}) copy-start(bf16[2,16,64]{2,1,0:T(8,128)(2,1)} %param.10) | copy-start | bytes 12292
  7.2 7.4 %copy-start.8 = (bf16[2,16,144]{2,1,0:T(8,128)(2,1)S(1)}, bf16[2,16,144]{2,1,0:T(8,128)(2,1)}, u32[]{:S(2)}) copy-start(bf16[2,16,144]{2,1,0:T(8,128)(2,1)} %param.9) | copy-start | bytes 27652
  7.2 96.9 %all-gather.4.cloned.1.call-start = ((), (), s32[]{:S(2)}) async-start(), calls=%async_computation | async-start | bytes 10027008 | tf_op jit(solution)/shard_map/all_gather | solution.py:139
  7.9 59.5 %collective-permute-start = (bf16[192,2304]{1,0:T(8,128)(2,1)}, bf16[192,2304]{1,0:T(8,128)(2,1)S(1)}, u32[]{:S(2)}, u32[]{:S(2)}) collective-permute-start(bf16[192,2304]{1,0:T(8,128)(2,1)} %bitcast.91), channel_id=1, source_target_pairs={{0,4},{4,8},{8,12},{1,5},{5,9},{9,13},{2,6},{6,10},{10,14},{3,7},{... | collective-permute-start | bytes 2654216 | tf_op jit(solution)/shard_map/ppermute | solution.py:21
  12.9 51.5 %copy-start = (bf16[1,192,2304]{2,1,0:T(8,128)(2,1)S(1)}, bf16[1,192,2304]{2,1,0:T(8,128)(2,1)}, u32[]{:S(2)}) copy-start(bf16[1,192,2304]{2,1,0:T(8,128)(2,1)} %param.6) | copy-start | bytes 2654212
  64.7 49.6 %copy-start.5 = (bf16[2,16,192]{2,1,0:T(8,128)(2,1)}, bf16[2,16,192]{2,1,0:T(8,128)(2,1)S(1)}, u32[]{:S(2)}) copy-start(bf16[2,16,192]{2,1,0:T(8,128)(2,1)S(1)} %convolution_convert_fusion.2) | copy-start | bytes 36868
  67.4 36.7 %copy-start.1 = (bf16[192,2304]{1,0:T(8,128)(2,1)}, bf16[192,2304]{1,0:T(8,128)(2,1)S(1)}, u32[]{:S(2)}) copy-start(bf16[192,2304]{1,0:T(8,128)(2,1)S(1)} %collective-permute-done.prev_ref) | copy-start | bytes 2654212
  114.3 11.7 %copy-start.4 = (bf16[2,16,1024]{2,1,0:T(8,128)(2,1)S(1)}, bf16[2,16,1024]{2,1,0:T(8,128)(2,1)}, u32[]{:S(2)}) copy-start(bf16[2,16,1024]{2,1,0:T(8,128)(2,1)} %reshape.58.up_ref) | copy-start | bytes 196612
  128.0 2.6 %copy-start.2 = (bf16[2,384,1024]{2,1,0:T(8,128)(2,1)S(1)}, bf16[2,384,1024]{2,1,0:T(8,128)(2,1)}, u32[]{:S(2)}) copy-start(bf16[2,384,1024]{2,1,0:T(8,128)(2,1)} %get-tuple-element.9) | copy-start | bytes 4718596
  133.0 2.9 %copy-start.6 = (bf16[2,16,192]{2,1,0:T(8,128)(2,1)S(1)}, bf16[2,16,192]{2,1,0:T(8,128)(2,1)}, u32[]{:S(2)}) copy-start(bf16[2,16,192]{2,1,0:T(8,128)(2,1)} %copy-done.5) | copy-start | bytes 36868
  133.0 6.1 %collective-permute-start.1 = (bf16[2,192,16]{1,2,0:T(8,128)(2,1)}, bf16[2,192,16]{1,2,0:T(8,128)(2,1)}, u32[]{:S(2)}, u32[]{:S(2)}) collective-permute-start(bf16[2,192,16]{1,2,0:T(8,128)(2,1)} %convolution_convert_fusion), channel_id=1, source_target_pairs={{4,0},{8,4},{12,8},{5,1},{9,5},{13,9},{6,2},{10,6},{14,10},{7,3},{... | collective-permute-start | bytes 36872 | tf_op jit(solution)/shard_map/ppermute | solution.py:21
  137.1 2.0 %copy-start.3 = (f32[2,16,4,4,144]{4,1,3,2,0:T(8,128)S(1)}, f32[2,16,4,4,144]{4,1,3,2,0:T(8,128)}, u32[]{:S(2)}) copy-start(f32[2,16,4,4,144]{4,1,3,2,0:T(8,128)} %fusion.7) | copy-start | bytes 884740
  140.5 1.6 collective-permute-start.2
  142.2 5.7 %collective-permute-start.3 = (f32[1,4,208,32]{2,3,1,0:T(8,128)S(1)}, f32[1,4,208,32]{2,3,1,0:T(8,128)S(1)}, u32[]{:S(2)}, u32[]{:S(2)}) collective-permute-start(f32[1,4,208,32]{2,3,1,0:T(8,128)S(1)} %dynamic-slice_bitcast_fusion), channel_id=1, source_target_pairs={{0,2},{2,0},{1,3},{3,1},{4,6},{6,4},{5,7},{7,5},{8,10},{10,8},{9,1... | collective-permute-start | bytes 319496 | tf_op jit(solution)/shard_map/ppermute | solution.py:170
  148.0 5.9 %collective-permute-start.4 = (f32[2,208,32]{1,2,0:T(8,128)S(1)}, f32[2,208,32]{1,2,0:T(8,128)S(1)}, u32[]{:S(2)}, u32[]{:S(2)}) collective-permute-start(f32[2,208,32]{1,2,0:T(8,128)S(1)} %dynamic-slice_bitcast_fusion.1), channel_id=1, source_target_pairs={{0,8},{4,12},{8,0},{12,4},{1,9},{5,13},{9,1},{13,5},{2,10},{6,14},... | collective-permute-start | bytes 159752 | tf_op jit(solution)/shard_map/ppermute | solution.py:170
  153.9 4.0 %collective-permute-start.5 = (f32[1,208,32]{1,2,0:T(8,128)S(1)}, f32[1,208,32]{1,2,0:T(8,128)S(1)}, u32[]{:S(2)}, u32[]{:S(2)}) collective-permute-start(f32[1,208,32]{1,2,0:T(8,128)S(1)} %constant_dynamic-slice_fusion), channel_id=1, source_target_pairs={{0,4},{4,0},{8,12},{12,8},{1,5},{5,1},{9,13},{13,9},{2,6},{6,2},{1... | collective-permute-start | bytes 79880 | tf_op jit(solution)/shard_map/ppermute | solution.py:170
  157.9 0.7 copy-start.7
Sparse Core Ops, SparseCore 0:
  10.3 93.7 all-gather.3

commit v8 on v7

--- a/solution.py
+++ b/solution.py
@@ -85,47 +85,30 @@
     return attention_heads(visible.astype(jnp.int32), query_rows, grad_rows, key_value)
 
 
-def projection_kernel(prev_ref, own_ref, weight_ref, low_prev_ref, low_own_ref, up_ref, out_ref):
+def projection_kernel(rows_ref, weight_ref, low_ref, up_ref, out_ref):
     row_shards = weight_ref.shape[0]
-    depth = weight_ref.shape[3]
-    rows = own_ref.shape[0]
-    up = up_ref[0]
-    for half, (rows_ref, low_ref) in enumerate(((prev_ref, low_prev_ref), (own_ref, low_own_ref))):
-        total = jnp.dot(low_ref[0], up, preferred_element_type=jnp.float32) * adapter_scale
-        if depth % 16 == 0:
-            weight = jnp.concatenate([weight_ref[c, 0, 0] for c in range(row_shards)], axis=0)
-            base = jnp.dot(rows_ref[...], weight, preferred_element_type=jnp.float32)
-        else:
-            base = jnp.dot(
-                rows_ref[:, :depth], weight_ref[0, 0, 0], preferred_element_type=jnp.float32
-            )
-            for c in range(1, row_shards):
-                base = base + jnp.dot(
-                    rows_ref[:, c * depth:(c + 1) * depth],
-                    weight_ref[c, 0, 0],
-                    preferred_element_type=jnp.float32,
-                )
-        out_ref[0, half * rows:(half + 1) * rows, :] = (base + total).astype(out_ref.dtype)
-
-
-def project_pair(rows_prev, rows_own, gathered, low_prev, low_own, up_full):
+    base = jnp.dot(low_ref[0], up_ref[0], preferred_element_type=jnp.float32) * adapter_scale
+    for c in range(row_shards):
+        base = base + jnp.dot(rows_ref[c], weight_ref[c, 0, 0], preferred_element_type=jnp.float32)
+    out_ref[0] = base.astype(out_ref.dtype)
+
+
+def project_pair(rows_split, gathered, low_rows, up_full):
     row_shards, col_shards, members, depth, cols = gathered.shape
-    rows, width = rows_own.shape
+    rows = rows_split.shape[1]
     rank = up_full.shape[1]
     return pl.pallas_call(
         projection_kernel,
         grid=(members, col_shards),
         in_specs=[
-            pl.BlockSpec((rows, width), lambda m, i: (0, 0)),
-            pl.BlockSpec((rows, width), lambda m, i: (0, 0)),
+            pl.BlockSpec((row_shards, rows, depth), lambda m, i: (0, 0, 0)),
             pl.BlockSpec((row_shards, 1, 1, depth, cols), lambda m, i: (0, i, m, 0, 0)),
-            pl.BlockSpec((1, rows, rank), lambda m, i: (m, 0, 0)),
             pl.BlockSpec((1, rows, rank), lambda m, i: (m, 0, 0)),
             pl.BlockSpec((1, rank, cols), lambda m, i: (m, 0, i)),
         ],
-        out_specs=pl.BlockSpec((1, 2 * rows, cols), lambda m, i: (m, 0, i)),
-        out_shape=jax.ShapeDtypeStruct((members, 2 * rows, col_shards * cols), jnp.bfloat16),
-    )(rows_prev, rows_own, gathered, low_prev, low_own, up_full)
+        out_specs=pl.BlockSpec((1, rows, cols), lambda m, i: (m, 0, i)),
+        out_shape=jax.ShapeDtypeStruct((members, rows, col_shards * cols), jnp.bfloat16),
+    )(rows_split, gathered, low_rows, up_full)
 
 
 def project_rows(rows_previous, rows_own, kv_weight, down_full, up_full):
@@ -136,9 +119,12 @@
 
     low_previous, low_rank = low_of(rows_previous), low_of(rows_own)
     row_shards, col_shards = lax.axis_size("ctx"), lax.axis_size(("dp", "sub"))
+    rows_both = jnp.concatenate([rows_previous, rows_own], axis=0)
+    rows_split = rows_both.reshape(rows_both.shape[0], row_shards, -1).swapaxes(0, 1)
     gathered = lax.all_gather(kv_weight, ("ctx", "dp", "sub"), axis=0, tiled=False)
     gathered = gathered.reshape((row_shards, col_shards) + kv_weight.shape)
-    key_value = project_pair(rows_previous, rows_own, gathered, low_previous, low_rank, up_full)
+    low_rows = jnp.concatenate([low_previous, low_rank], axis=1)
+    key_value = project_pair(rows_split, gathered, low_rows, up_full)
     return low_previous, low_rank, key_value
 
 

time: 166 us -> 167 us (level)
  waiting for transfers between devices: 47.8 us -> 42 us
  local copies, waits for them, and re-layouts: 9.91 us -> 15.6 us
  blocking collectives: 49.1 us -> 45.5 us
    concatenate x0 -> x5, local copies, waits for them, and re-layouts: none -> 8.23 us  [the longest x4 7.41 us: project_rows(): rows_both = jnp.concatenate([rows_previous, rows_own], axis=0)]
    all_gather x1, waiting for transfers between devices: 35.5 us -> 29.7 us  [project_rows(): lax.all_gather(kv_weight, ('ctx', 'dp', 'sub'), axis=0, tiled=False)]
    all_gather x1, blocking collectives: 49.1 us -> 45.5 us  [gather_adapters(): gathered = lax.all_gather(joined, axes, axis=0, tiled=False)]
  transfers between devices with their start and end apart: 7 -> 7, of which waited for: 5 -> 5; matrix products, arithmetic and copies ran while one was open for 7% -> 12% of each run, Pallas kernels for 0% -> 0%
where the time goes in v8:
time: 167 us; the launch traced here: 166 us
  blocking collectives  45.5 us (27%)
  waiting for transfers between devices  42 us (25%)
  Pallas kernels  22.8 us (14%)
  local copies, waits for them, and re-layouts  15.6 us (9%)
  between operations  14.3 us (9%)
  starting transfers between devices  12.9 us (8%)
  matrix products  10.3 us (6%)
  other arithmetic  2.97 us (2%)
    all_gather x1, blocking collectives, gather_adapters(): gathered = lax.all_gather(joined, axes, axis=0, tiled=False)  45.5 us
    all_gather x1, waiting for transfers between devices, project_rows(): lax.all_gather(kv_weight, ('ctx', 'dp', 'sub'), axis=0, tiled=False)  29.7 us
    ppermute x4, waiting for transfers between devices, halving_scatter(): blocks = keep + lax.ppermute(send, axis, pairs)  11.7 us
    pallas_call x1, Pallas kernels, attention_heads(): pl.pallas_call(attention_kernel, grid=(heads,), in_specs=[pl.BlockSpec(ma...  11.7 us
    pallas_call x1, Pallas kernels, project_pair(): pl.pallas_call(projection_kernel, grid=(members, col_shards), in_specs=[p...  11.1 us
    concatenate x4, local copies, waits for them, and re-layouts, project_rows(): rows_both = jnp.concatenate([rows_previous, rows_own], axis=0)  7.41 us
    ppermute x2, starting transfers between devices, shifted(): return lax.ppermute(value, axis, pairs)  7.29 us
    ppermute x4, starting transfers between devices, halving_scatter(): blocks = keep + lax.ppermute(send, axis, pairs)  5.58 us
  transfers between devices with their start and end apart: 7, of which 5 were waited for; matrix products, arithmetic and copies ran while one was open for 12% of the time, Pallas kernels for 0%

profile of v8, /device:TPU:0, one launch (start us, length us, event | category | flops | bytes accessed | tf_op | source)
XLA Modules:
  0.0 166.3 jit_solution(16500654073547277264)
XLA Ops:
  7.2 0.0 copy-start
  7.2 0.0 all-gather.4.cloned.1.call-start
  7.2 0.7 all-gather.4.cloned.1.call-update
  7.9 5.9 %collective-permute-start = (bf16[192,2304]{1,0:T(8,128)(2,1)}, bf16[192,2304]{1,0:T(8,128)(2,1)}, u32[]{:S(2)}, u32[]{:S(2)}) collective-permute-start(bf16[192,2304]{1,0:T(8,128)(2,1)} %bitcast.93), channel_id=1, source_target_pairs={{0,4},{4,8},{8,12},{1,5},{5,9},{9,13},{2,6},{6,10},{10,14},{3,7},{... | collective-permute-start | bytes 2654216 | tf_op jit(solution)/shard_map/ppermute | solution.py:21
  13.8 2.6 %concatenate.23 = bf16[192,4,576]{2,1,0:T(4,128)(2,1)S(1)} reshape(bf16[1,192,2304]{2,1,0:T(8,128)(2,1)} %param.6) | data formatting | bytes 1769472 | tf_op jit(solution)/shard_map/concatenate | solution.py:122
  16.4 0.0 copy-done
  16.4 0.0 copy-start.9
  16.4 0.0 copy-start.10
  16.5 0.6 copy.38
  17.1 1.1 copy.34
  18.1 0.0 copy-done.9
  18.2 0.0 copy-done.10
  18.2 0.1 pad_maximum_fusion.1
  18.2 45.5 %all-gather.1 = bf16[32,16,208]{2,1,0:T(8,128)(2,1)S(1)} all-gather(bf16[2,16,208]{2,1,0:T(8,128)(2,1)S(1)} %pad_maximum_fusion.1), channel_id=3, replica_groups=mesh['groups'=2,'ctx'=4,'dp'=2,'sub'=2] {'ctx','dp','sub'}, dimensions={0}, use_global_device_ids=true | all-gather | bytes 226304 | tf_op jit(solution)/shard_map/all_gather | solution.py:135
  63.8 0.1 slice.27
  63.9 0.2 copy.51
  64.0 0.3 reshape.61
  64.4 0.1 copy.52
  64.4 0.8 reshape.62.up_ref
  65.2 1.1 fusion.10.mask_ref
  66.2 0.3 convolution_convert_fusion.2
  66.6 0.0 copy-start.6
  66.6 0.0 collective-permute-done
  66.7 2.6 %concatenate.22 = bf16[192,4,576]{2,1,0:T(4,128)(2,1)S(1)} reshape(bf16[192,2304]{1,0:T(8,128)(2,1)} %collective-permute-done) | data formatting | bytes 1769472 | tf_op jit(solution)/shard_map/concatenate | solution.py:122
  69.3 0.0 copy-start.1
  69.3 1.1 copy.33
  70.4 0.0 copy-start.2
  70.4 1.6 convolution_convert_fusion.3
  72.0 0.0 copy-done.6
  72.0 0.1 pad_maximum_fusion
  72.1 0.8 copy.37.low_ref
  72.9 0.0 copy-done.1
  73.0 0.0 copy-done.2
  73.0 1.5 maximum_bitcast_fusion.rows_ref
  74.4 29.7 %all-gather.4.cloned.1.call-done = bf16[32,576,256]{2,1,0:T(8,128)(2,1)} async-done(((bf16[2,576,256]{2,1,0:T(8,128)(2,1)}), bf16[32,576,256]{2,1,0:T(8,128)(2,1)}) %all-gather.4.cloned.1.call-update) | async-done | bytes 9437200 | tf_op jit(solution)/shard_map/all_gather | solution.py:124
  104.1 11.1 %shard_map.93.kv_ref = bf16[2,384,1024]{2,1,0:T(8,128)(2,1)} custom-call(bf16[4,384,576]{2,1,0:T(8,128)(2,1)} %maximum_bitcast_fusion.rows_ref, bf16[4,4,2,576,256]{4,3,2,1,0:T(8,128)(2,1)} %bitcast.92, bf16[2,384,16]{2,1,0:T(8,128)(2,1)} %copy.37.low_ref, bf16[2,16,1024]{2,1,0:T(8,128)(2,1)} %reshape.62.up_ref), custom_call_target="tpu_custom_call" | custom-call | tf_op jit(solution)/shard_map/pallas_call | solution.py:100
  115.2 0.0 copy-start.5
  115.2 11.7 %shard_map.94 = (bf16[192,2048]{1,0:T(8,128)(2,1)}, bf16[192,2048]{1,0:T(8,128)(2,1)}, bf16[2,384,1024]{2,1,0:T(8,128)(2,1)}) custom-call(s32[384,384]{1,0:T(8,128)} %fusion.10.mask_ref, bf16[192,2048]{1,0:T(8,128)(2,1)} %bitcast.103, bf16[192,2048]{1,0:T(8,128)(2,1)} %bitcast.104, bf16[2,384,1024]{2,1,0:T(8,128)(2,1)} %shard_map.93.kv_ref), custom_call_target="tpu_custom_call" | custom-call | tf_op jit(solution)/shard_map/pallas_call | solution.py:62
  126.8 0.0 copy-done.5
  126.8 2.1 %convolution_convert_fusion = bf16[2,192,16]{1,2,0:T(8,128)(2,1)} fusion(bf16[2,16,1024]{2,1,0:T(8,128)(2,1)S(1)} %copy-done.5, bf16[2,384,1024]{2,1,0:T(8,128)(2,1)} %get-tuple-element.9), kind=kOutput, calls=%fused_computation.7 | convolution fusion | flops 12589056 | bytes 864256 | tf_op jit(solution)/shard_map/mrc,mkc->mrk/dot_general | solution.py:192
  128.9 2.5 %fusion.28 = (bf16[2,192,1024]{2,1,0:T(8,128)(2,1)S(1)}, bf16[2,192,1024]{2,1,0:T(8,128)(2,1)}) fusion(bf16[2,384,1024]{2,1,0:T(8,128)(2,1)} %get-tuple-element.9), kind=kLoop, calls=%fused_computation.53 | loop fusion | bytes 3145728 | tf_op jit(solution)/shard_map/slice | solution.py:190
  131.4 0.0 copy-done.3
  131.4 2.4 %fusion.7 = f32[2,16,4,4,144]{4,1,3,2,0:T(8,128)} fusion(bf16[192,4,4,144,1]{0,3,2,1,4:T(8,128)(2,1)S(1)} %bitcast.90, bf16[2,16,1024]{2,1,0:T(8,128)(2,1)} %reshape.62.up_ref, bf16[2,384,1024]{2,1,0:T(8,128)(2,1)S(1)} %copy-done.3), kind=kOutput, calls=%fused_computation.19 | convolution fusion | flops 40900608 | bytes 2326528 | tf_op jit(solution)/shard_map/mrk,rcij->icjmk/dot_general | solution.py:210
  133.8 1.4 collective-permute-start.1
  135.3 1.4 copy.40
  136.7 0.0 copy-done.7
  136.7 1.2 fusion.17
  137.9 0.5 copy.41
  138.4 1.4 fusion.3
  140.0 0.0 collective-permute-done.1
  140.0 0.0 copy-done.4
  140.0 1.2 fusion.1
  141.2 0.1 fusion.12
  141.3 0.3 collective-permute-start.2
  141.7 1.3 collective-permute-done.2
  142.9 0.1 fusion.15
  143.1 0.8 collective-permute-start.3
  143.8 5.0 %collective-permute-done.3 = f32[1,4,208,32]{2,3,1,0:T(8,128)S(1)} collective-permute-done((f32[1,4,208,32]{2,3,1,0:T(8,128)S(1)}, f32[1,4,208,32]{2,3,1,0:T(8,128)S(1)}, u32[]{:S(2)}, u32[]{:S(2)}) %collective-permute-start.3) | collective-permute-done | bytes 106528 | tf_op jit(solution)/shard_map/ppermute | solution.py:156
  148.9 2.6 %collective-permute-start.4 = (f32[2,208,32]{1,2,0:T(8,128)S(1)}, f32[2,208,32]{1,2,0:T(8,128)S(1)}, u32[]{:S(2)}, u32[]{:S(2)}) collective-permute-start(f32[2,208,32]{1,2,0:T(8,128)S(1)} %dynamic-slice_bitcast_fusion.1), channel_id=1, source_target_pairs={{0,8},{4,12},{8,0},{12,4},{1,9},{5,13},{9,1},{13,5},{2,10},{6,14},... | collective-permute-start | bytes 159752 | tf_op jit(solution)/shard_map/ppermute | solution.py:156
  151.5 3.3 %collective-permute-done.4 = f32[2,208,32]{1,2,0:T(8,128)S(1)} collective-permute-done((f32[2,208,32]{1,2,0:T(8,128)S(1)}, f32[2,208,32]{1,2,0:T(8,128)S(1)}, u32[]{:S(2)}, u32[]{:S(2)}) %collective-permute-start.4) | collective-permute-done | bytes 53280 | tf_op jit(solution)/shard_map/ppermute | solution.py:156
  154.8 1.9 %collective-permute-start.5 = (f32[1,208,32]{1,2,0:T(8,128)S(1)}, f32[1,208,32]{1,2,0:T(8,128)S(1)}, u32[]{:S(2)}, u32[]{:S(2)}) collective-permute-start(f32[1,208,32]{1,2,0:T(8,128)S(1)} %constant_dynamic-slice_fusion), channel_id=1, source_target_pairs={{0,4},{4,0},{8,12},{12,8},{1,5},{5,1},{9,13},{13,9},{2,6},{6,2},{1... | collective-permute-start | bytes 79880 | tf_op jit(solution)/shard_map/ppermute | solution.py:156
  156.7 2.1 %collective-permute-done.5 = f32[1,208,32]{1,2,0:T(8,128)S(1)} collective-permute-done((f32[1,208,32]{1,2,0:T(8,128)S(1)}, f32[1,208,32]{1,2,0:T(8,128)S(1)}, u32[]{:S(2)}, u32[]{:S(2)}) %collective-permute-start.5) | collective-permute-done | bytes 26656 | tf_op jit(solution)/shard_map/ppermute | solution.py:156
  158.8 0.7 slice.29
  159.5 0.0 copy-done.8
  (14 shorter events, 0.2 us)
Async XLA Ops:
  7.2 9.3 %copy-start = (bf16[1,192,2304]{2,1,0:T(8,128)(2,1)S(1)}, bf16[1,192,2304]{2,1,0:T(8,128)(2,1)}, u32[]{:S(2)}) copy-start(bf16[1,192,2304]{2,1,0:T(8,128)(2,1)} %param.6) | copy-start | bytes 2654212
  7.2 96.9 %all-gather.4.cloned.1.call-start = ((), (), s32[]{:S(2)}) async-start(), calls=%async_computation | async-start | bytes 10027008 | tf_op jit(solution)/shard_map/all_gather | solution.py:124
  7.9 58.7 %collective-permute-start = (bf16[192,2304]{1,0:T(8,128)(2,1)}, bf16[192,2304]{1,0:T(8,128)(2,1)}, u32[]{:S(2)}, u32[]{:S(2)}) collective-permute-start(bf16[192,2304]{1,0:T(8,128)(2,1)} %bitcast.93), channel_id=1, source_target_pairs={{0,4},{4,8},{8,12},{1,5},{5,9},{9,13},{2,6},{6,10},{10,14},{3,7},{... | collective-permute-start | bytes 2654216 | tf_op jit(solution)/shard_map/ppermute | solution.py:21
  16.4 1.7 %copy-start.9 = (bf16[2,16,144]{2,1,0:T(8,128)(2,1)S(1)}, bf16[2,16,144]{2,1,0:T(8,128)(2,1)}, u32[]{:S(2)}) copy-start(bf16[2,16,144]{2,1,0:T(8,128)(2,1)} %param.9) | copy-start | bytes 27652
  16.4 1.7 %copy-start.10 = (bf16[2,16,64]{2,1,0:T(8,128)(2,1)S(1)}, bf16[2,16,64]{2,1,0:T(8,128)(2,1)}, u32[]{:S(2)}) copy-start(bf16[2,16,64]{2,1,0:T(8,128)(2,1)} %param.10) | copy-start | bytes 12292
  66.6 5.4 %copy-start.6 = (bf16[2,16,192]{2,1,0:T(8,128)(2,1)}, bf16[2,16,192]{2,1,0:T(8,128)(2,1)S(1)}, u32[]{:S(2)}) copy-start(bf16[2,16,192]{2,1,0:T(8,128)(2,1)S(1)} %convolution_convert_fusion.2) | copy-start | bytes 36868
  69.3 3.7 %copy-start.1 = (bf16[192,4,576]{2,0,1:T(8,128)(2,1)S(1)}, bf16[192,4,576]{2,0,1:T(8,128)(2,1)}, u32[]{:S(2)}) copy-start(bf16[192,4,576]{2,0,1:T(8,128)(2,1)} %copy.34) | copy-start | bytes 2654212
  70.4 2.6 %copy-start.2 = (bf16[192,4,576]{2,0,1:T(8,128)(2,1)S(1)}, bf16[192,4,576]{2,0,1:T(8,128)(2,1)}, u32[]{:S(2)}) copy-start(bf16[192,4,576]{2,0,1:T(8,128)(2,1)} %copy.33) | copy-start | bytes 2654212
  115.2 11.7 %copy-start.5 = (bf16[2,16,1024]{2,1,0:T(8,128)(2,1)S(1)}, bf16[2,16,1024]{2,1,0:T(8,128)(2,1)}, u32[]{:S(2)}) copy-start(bf16[2,16,1024]{2,1,0:T(8,128)(2,1)} %reshape.62.up_ref) | copy-start | bytes 196612
  128.9 2.6 %copy-start.3 = (bf16[2,384,1024]{2,1,0:T(8,128)(2,1)S(1)}, bf16[2,384,1024]{2,1,0:T(8,128)(2,1)}, u32[]{:S(2)}) copy-start(bf16[2,384,1024]{2,1,0:T(8,128)(2,1)} %get-tuple-element.9) | copy-start | bytes 4718596
  133.8 2.9 %copy-start.7 = (bf16[2,16,192]{2,1,0:T(8,128)(2,1)S(1)}, bf16[2,16,192]{2,1,0:T(8,128)(2,1)}, u32[]{:S(2)}) copy-start(bf16[2,16,192]{2,1,0:T(8,128)(2,1)} %copy-done.6) | copy-start | bytes 36868
  133.8 6.1 %collective-permute-start.1 = (bf16[2,192,16]{1,2,0:T(8,128)(2,1)}, bf16[2,192,16]{1,2,0:T(8,128)(2,1)}, u32[]{:S(2)}, u32[]{:S(2)}) collective-permute-start(bf16[2,192,16]{1,2,0:T(8,128)(2,1)} %convolution_convert_fusion), channel_id=1, source_target_pairs={{4,0},{8,4},{12,8},{5,1},{9,5},{13,9},{6,2},{10,6},{14,10},{7,3},{... | collective-permute-start | bytes 36872 | tf_op jit(solution)/shard_map/ppermute | solution.py:21
  137.9 2.0 %copy-start.4 = (f32[2,16,4,4,144]{4,1,3,2,0:T(8,128)S(1)}, f32[2,16,4,4,144]{4,1,3,2,0:T(8,128)}, u32[]{:S(2)}) copy-start(f32[2,16,4,4,144]{4,1,3,2,0:T(8,128)} %fusion.7) | copy-start | bytes 884740
  141.3 1.6 collective-permute-start.2
  143.1 5.7 %collective-permute-start.3 = (f32[1,4,208,32]{2,3,1,0:T(8,128)S(1)}, f32[1,4,208,32]{2,3,1,0:T(8,128)S(1)}, u32[]{:S(2)}, u32[]{:S(2)}) collective-permute-start(f32[1,4,208,32]{2,3,1,0:T(8,128)S(1)} %dynamic-slice_bitcast_fusion), channel_id=1, source_target_pairs={{0,2},{2,0},{1,3},{3,1},{4,6},{6,4},{5,7},{7,5},{8,10},{10,8},{9,1... | collective-permute-start | bytes 319496 | tf_op jit(solution)/shard_map/ppermute | solution.py:156
  148.9 5.9 %collective-permute-start.4 = (f32[2,208,32]{1,2,0:T(8,128)S(1)}, f32[2,208,32]{1,2,0:T(8,128)S(1)}, u32[]{:S(2)}, u32[]{:S(2)}) collective-permute-start(f32[2,208,32]{1,2,0:T(8,128)S(1)} %dynamic-slice_bitcast_fusion.1), channel_id=1, source_target_pairs={{0,8},{4,12},{8,0},{12,4},{1,9},{5,13},{9,1},{13,5},{2,10},{6,14},... | collective-permute-start | bytes 159752 | tf_op jit(solution)/shard_map/ppermute | solution.py:156
  154.8 4.0 %collective-permute-start.5 = (f32[1,208,32]{1,2,0:T(8,128)S(1)}, f32[1,208,32]{1,2,0:T(8,128)S(1)}, u32[]{:S(2)}, u32[]{:S(2)}) collective-permute-start(f32[1,208,32]{1,2,0:T(8,128)S(1)} %constant_dynamic-slice_fusion), channel_id=1, source_target_pairs={{0,4},{4,0},{8,12},{12,8},{1,5},{5,1},{9,13},{13,9},{2,6},{6,2},{1... | collective-permute-start | bytes 79880 | tf_op jit(solution)/shard_map/ppermute | solution.py:156
  158.8 0.7 copy-start.8
Sparse Core Ops, SparseCore 0:
  10.3 93.7 all-gather.3

commit v9 on v8

--- a/solution.py
+++ b/solution.py
@@ -21,7 +21,11 @@
     return lax.ppermute(value, axis, pairs)
 
 
-def attention_kernel(mask_ref, q_ref, do_ref, kv_ref, out_ref, dq_ref, dkv_ref):
+def attention_kernel(
+    mask_ref, q_ref, do_ref, kv_ref, low_ref, up_ref,
+    out_ref, dq_ref, projected_ref, up_terms_ref, projected_acc,
+):
+    head = pl.program_id(0)
     half = HEAD_DIM
     q = jnp.concatenate([q_ref[:, :half], q_ref[:, half:]], axis=0)
     do = jnp.concatenate([do_ref[:, :half], do_ref[:, half:]], axis=0)
@@ -30,6 +34,7 @@
     rows = q_ref.shape[0]
     visible = mask_ref[...] != 0
     contract_last = (((1,), (1,)), ((), ()))
+    contract_first = (((0,), (0,)), ((), ()))
     raw_score = lax.dot_general(q, k, contract_last, preferred_element_type=jnp.float32) * query_scale
     bent_score = jnp.tanh(raw_score / logit_cap)
     expo_terms = jnp.where(visible, jnp.exp(logit_cap * bent_score), 0.0)
@@ -48,31 +53,63 @@
     dq_ref[:, half:] = head_qgrad[rows:]
     score_t = score_grad.astype(jnp.float32).T.astype(jnp.bfloat16)
     prob_t = prob_wide.T.astype(jnp.bfloat16)
-    dkv_ref[0] = jnp.dot(score_t, q, preferred_element_type=jnp.float32).astype(dkv_ref.dtype)
-    dkv_ref[1] = jnp.dot(prob_t, do, preferred_element_type=jnp.float32).astype(dkv_ref.dtype)
-
-
-def attention_heads(mask, queries, grads, key_value):
+    key_grad = jnp.dot(score_t, q, preferred_element_type=jnp.float32).astype(jnp.bfloat16)
+    value_grad = jnp.dot(prob_t, do, preferred_element_type=jnp.float32).astype(jnp.bfloat16)
+
+    @pl.when(head == 0)
+    def _():
+        projected_acc[...] = jnp.zeros_like(projected_acc)
+
+    for member, grad in enumerate((key_grad, value_grad)):
+        projected_acc[member] += lax.dot_general(
+            grad, up_ref[member], contract_last, preferred_element_type=jnp.float32
+        )
+        up_terms_ref[member] = lax.dot_general(
+            low_ref[member], grad, contract_first, preferred_element_type=jnp.float32
+        )
+
+    @pl.when(head == pl.num_programs(0) - 1)
+    def _():
+        projected_ref[...] = projected_acc[...].astype(projected_ref.dtype)
+
+
+def attention_heads(mask, queries, grads, key_value, low_rows, up_full):
     rows, width = queries.shape
-    keys, kv_width = key_value.shape[1], key_value.shape[2]
+    members, keys, kv_width = key_value.shape
+    rank = up_full.shape[1]
     heads = kv_width // HEAD_DIM
     group_cols = width // heads
     row_block = pl.BlockSpec((rows, group_cols), lambda g: (0, g))
-    kv_block = pl.BlockSpec((2, keys, HEAD_DIM), lambda g: (0, 0, g))
+    kv_block = pl.BlockSpec((members, keys, HEAD_DIM), lambda g: (0, 0, g))
+    whole = lambda shape: pl.BlockSpec(shape, lambda g: (0,) * len(shape))
     return pl.pallas_call(
         attention_kernel,
         grid=(heads,),
-        in_specs=[pl.BlockSpec(mask.shape, lambda g: (0, 0)), row_block, row_block, kv_block],
-        out_specs=[row_block, row_block, kv_block],
+        in_specs=[
+            whole(mask.shape),
+            row_block,
+            row_block,
+            kv_block,
+            whole(low_rows.shape),
+            pl.BlockSpec((members, rank, HEAD_DIM), lambda g: (0, 0, g)),
+        ],
+        out_specs=[
+            row_block,
+            row_block,
+            whole((members, keys, rank)),
+            pl.BlockSpec((members, rank, HEAD_DIM), lambda g: (0, 0, g)),
+        ],
         out_shape=[
             jax.ShapeDtypeStruct((rows, width), jnp.bfloat16),
             jax.ShapeDtypeStruct((rows, width), jnp.bfloat16),
-            jax.ShapeDtypeStruct(key_value.shape, jnp.bfloat16),
-        ],
-    )(mask, queries, grads, key_value)
-
-
-def attend(query_rows, key_value, grad_rows, is_first):
+            jax.ShapeDtypeStruct((members, keys, rank), jnp.bfloat16),
+            jax.ShapeDtypeStruct((members, rank, kv_width), jnp.float32),
+        ],
+        scratch_shapes=[pltpu.VMEM((members, keys, rank), jnp.float32)],
+    )(mask, queries, grads, key_value, low_rows, up_full)
+
+
+def attend(query_rows, key_value, grad_rows, is_first, low_rows, up_full):
     length = query_rows.shape[0]
     group_size = HEADS // KV_HEADS
     query_pos = lax.broadcasted_iota(jnp.int32, (group_size * length, 2 * length), 0) % length
@@ -82,7 +119,7 @@
         & (key_pos <= query_pos + length)
         & (jnp.logical_not(is_first) | (key_pos >= length))
     )
-    return attention_heads(visible.astype(jnp.int32), query_rows, grad_rows, key_value)
+    return attention_heads(visible.astype(jnp.int32), query_rows, grad_rows, key_value, low_rows, up_full)
 
 
 def projection_kernel(rows_ref, weight_ref, low_ref, up_ref, out_ref):
@@ -125,7 +162,7 @@
     gathered = gathered.reshape((row_shards, col_shards) + kv_weight.shape)
     low_rows = jnp.concatenate([low_previous, low_rank], axis=1)
     key_value = project_pair(rows_split, gathered, low_rows, up_full)
-    return low_previous, low_rank, key_value
+    return low_rows, key_value
 
 
 def gather_adapters(adapter_down, adapter_up):
@@ -183,30 +220,14 @@
     rows_previous = shifted(rows_own, "ctx", 1)
     down_full, up_full = gather_adapters(adapter_down, adapter_up)
     is_first = lax.axis_index("ctx") == 0
-    low_previous, low_rank, kv_both = project_rows(
-        rows_previous, rows_own, kv_weight, down_full, up_full
-    )
-    attended, query_grad, kv_grads = attend(query_rows, kv_both, grad_rows, is_first)
-    far_part = kv_grads[:, :length]
-    near_part = kv_grads[:, length:]
-    projected_far = jnp.einsum(
-        "mrc,mkc->mrk", far_part, up_full, preferred_element_type=jnp.float32
-    ).astype(jnp.bfloat16)
-    projected_returned = shifted(projected_far, "ctx", -1)
-    projected_near = jnp.einsum(
-        "mrc,mkc->mrk", near_part, up_full, preferred_element_type=jnp.float32
-    ).astype(jnp.bfloat16)
-    shards = row_shards * col_shards
+    low_rows, kv_both = project_rows(rows_previous, rows_own, kv_weight, down_full, up_full)
+    attended, query_grad, projected, up_terms = attend(
+        query_rows, kv_both, grad_rows, is_first, low_rows, up_full
+    )
+    projected_returned = shifted(projected[:, :length], "ctx", -1)
+    projected_near = projected[:, length:]
     rows_split = rows_own.reshape(length, row_shards, col_shards, -1)
-
-    def split_cols(part):
-        return part.reshape(part.shape[:2] + (row_shards, col_shards, -1))
-
-    up_terms = jnp.einsum(
-        "mrk,mrcij->icjmk", low_rank, split_cols(near_part), preferred_element_type=jnp.float32
-    ) + jnp.einsum(
-        "mrk,mrcij->icjmk", low_previous, split_cols(far_part), preferred_element_type=jnp.float32
-    )
+    up_terms = up_terms.reshape(up_terms.shape[:2] + (row_shards, col_shards, -1)).transpose(3, 2, 4, 0, 1)
     down_terms = jnp.einsum(
         "mrk,rcij->icjmk", projected_near, rows_split, preferred_element_type=jnp.float32
     ) + jnp.einsum(

time: 167 us -> 164 us (0.982)
  waiting for transfers between devices: 42 us -> 50.3 us
  matrix products: 10.3 us -> 3.94 us
  starting transfers between devices: 12.9 us -> 9.6 us
  local copies, waits for them, and re-layouts: 15.6 us -> 12.3 us
  Pallas kernels: 22.8 us -> 24.9 us
    ppermute x2, waiting for transfers between devices: 0.04 us -> 5.28 us  [shifted(): return lax.ppermute(value, axis, pairs)]
    dot_general x3 -> x0, matrix products: 4.73 us -> none  [the longest x1 2.06 us: on_device(): jnp.einsum('mrc,mkc->mrk', far_part, up_full, preferred_element_type=jnp....]
    slice x3 -> x1, local copies, waits for them, and re-layouts: 4.48 us -> 0.94 us  [on_device(): projected_returned = shifted(projected[:, :length], 'ctx', -1)]
    ppermute x4, starting transfers between devices: 5.58 us -> 2.4 us  [halving_scatter(): blocks = keep + lax.ppermute(send, axis, pairs)]
    ppermute x4, waiting for transfers between devices: 11.7 us -> 14.7 us  [halving_scatter(): blocks = keep + lax.ppermute(send, axis, pairs)]
    pallas_call x1, Pallas kernels: 11.7 us -> 13.8 us  [attention_heads(): pl.pallas_call(attention_kernel, grid=(heads,), in_specs=[whole(mask.shap...]
  transfers between devices with their start and end apart: 7 -> 7, of which waited for: 5 -> 6; matrix products, arithmetic and copies ran while one was open for 12% -> 9% of each run, Pallas kernels for 0% -> 0%
where the time goes in v9:
time: 164 us
  waiting for transfers between devices  50.3 us (31%)
  blocking collectives  45.6 us (28%)
  Pallas kernels  24.9 us (15%)
  between operations  14.3 us (9%)
  local copies, waits for them, and re-layouts  12.3 us (8%)
  starting transfers between devices  9.6 us (6%)
  matrix products  3.94 us (2%)
  other arithmetic  3 us (2%)
    all_gather x1, blocking collectives, gather_adapters(): gathered = lax.all_gather(joined, axes, axis=0, tiled=False)  45.6 us
    all_gather x1, waiting for transfers between devices, project_rows(): lax.all_gather(kv_weight, ('ctx', 'dp', 'sub'), axis=0, tiled=False)  29.6 us
    ppermute x4, waiting for transfers between devices, halving_scatter(): blocks = keep + lax.ppermute(send, axis, pairs)  14.7 us
    pallas_call x1, Pallas kernels, attention_heads(): pl.pallas_call(attention_kernel, grid=(heads,), in_specs=[whole(mask.shap...  13.8 us
    pallas_call x1, Pallas kernels, project_pair(): pl.pallas_call(projection_kernel, grid=(members, col_shards), in_specs=[p...  11.1 us
    concatenate x4, local copies, waits for them, and re-layouts, project_rows(): rows_both = jnp.concatenate([rows_previous, rows_own], axis=0)  7.44 us
    ppermute x2, starting transfers between devices, shifted(): return lax.ppermute(value, axis, pairs)  7.16 us
    ppermute x2, waiting for transfers between devices, shifted(): return lax.ppermute(value, axis, pairs)  5.28 us
  transfers between devices with their start and end apart: 7, of which 6 were waited for; matrix products, arithmetic and copies ran while one was open for 9% of the time, Pallas kernels for 0%

profile of v9, /device:TPU:0, one launch (start us, length us, event | category | flops | bytes accessed | tf_op | source)
XLA Modules:
  0.0 163.9 jit_solution(10308136256466469932)
XLA Ops:
  7.2 0.0 copy-start
  7.2 0.0 all-gather.4.cloned.1.call-start
  7.2 0.7 all-gather.4.cloned.1.call-update
  7.9 5.9 %collective-permute-start = (bf16[192,2304]{1,0:T(8,128)(2,1)}, bf16[192,2304]{1,0:T(8,128)(2,1)}, u32[]{:S(2)}, u32[]{:S(2)}) collective-permute-start(bf16[192,2304]{1,0:T(8,128)(2,1)} %bitcast.77), channel_id=1, source_target_pairs={{0,4},{4,8},{8,12},{1,5},{5,9},{9,13},{2,6},{6,10},{10,14},{3,7},{... | collective-permute-start | bytes 2654216 | tf_op jit(solution)/shard_map/ppermute | solution.py:21
  13.8 2.6 %concatenate.23 = bf16[192,4,576]{2,1,0:T(4,128)(2,1)S(1)} reshape(bf16[1,192,2304]{2,1,0:T(8,128)(2,1)} %param.6) | data formatting | bytes 1769472 | tf_op jit(solution)/shard_map/concatenate | solution.py:159
  16.4 0.0 copy-done
  16.4 0.0 copy-start.5
  16.4 0.0 copy-start.6
  16.4 0.6 copy.36
  17.1 1.1 copy.31
  18.1 0.0 copy-done.5
  18.1 0.0 copy-done.6
  18.1 0.1 pad_maximum_fusion.1
  18.2 45.6 %all-gather.1 = bf16[32,16,208]{2,1,0:T(8,128)(2,1)S(1)} all-gather(bf16[2,16,208]{2,1,0:T(8,128)(2,1)S(1)} %pad_maximum_fusion.1), channel_id=3, replica_groups=mesh['groups'=2,'ctx'=4,'dp'=2,'sub'=2] {'ctx','dp','sub'}, dimensions={0}, use_global_device_ids=true | all-gather | bytes 226304 | tf_op jit(solution)/shard_map/all_gather | solution.py:172
  63.8 0.1 slice.27
  63.9 0.2 copy.51
  64.0 0.3 reshape.58
  64.4 0.1 copy.52
  64.4 0.8 reshape.59.up_ref
  65.2 1.1 fusion.8.mask_ref
  66.3 0.3 fusion.3
  66.6 0.0 collective-permute-done
  66.7 2.7 %concatenate.22 = bf16[192,4,576]{2,1,0:T(4,128)(2,1)S(1)} reshape(bf16[192,2304]{1,0:T(8,128)(2,1)} %collective-permute-done) | data formatting | bytes 1769472 | tf_op jit(solution)/shard_map/concatenate | solution.py:159
  69.3 0.0 copy-start.1
  69.3 1.1 copy.30
  70.4 0.0 copy-start.2
  70.4 1.6 fusion.2
  72.0 0.1 pad_maximum_fusion
  72.2 0.8 copy.34.low_ref
  73.0 0.0 copy-done.1
  73.0 0.0 copy-done.2
  73.0 1.4 maximum_bitcast_fusion.rows_ref
  74.4 29.6 %all-gather.4.cloned.1.call-done = bf16[32,576,256]{2,1,0:T(8,128)(2,1)} async-done(((bf16[2,576,256]{2,1,0:T(8,128)(2,1)}), bf16[32,576,256]{2,1,0:T(8,128)(2,1)}) %all-gather.4.cloned.1.call-update) | async-done | bytes 9437200 | tf_op jit(solution)/shard_map/all_gather | solution.py:161
  104.1 11.1 %shard_map.93.kv_ref = bf16[2,384,1024]{2,1,0:T(8,128)(2,1)} custom-call(bf16[4,384,576]{2,1,0:T(8,128)(2,1)} %maximum_bitcast_fusion.rows_ref, bf16[4,4,2,576,256]{4,3,2,1,0:T(8,128)(2,1)} %bitcast.76, bf16[2,384,16]{2,1,0:T(8,128)(2,1)} %copy.34.low_ref, bf16[2,16,1024]{2,1,0:T(8,128)(2,1)} %reshape.59.up_ref), custom_call_target="tpu_custom_call" | custom-call | tf_op jit(solution)/shard_map/pallas_call | solution.py:137
  115.2 13.8 %shard_map.94 = (bf16[192,2048]{1,0:T(8,128)(2,1)}, bf16[192,2048]{1,0:T(8,128)(2,1)}, bf16[2,384,16]{2,1,0:T(8,128)(2,1)}, f32[2,16,1024]{2,1,0:T(8,128)}) custom-call(s32[384,384]{1,0:T(8,128)} %fusion.8.mask_ref, bf16[192,2048]{1,0:T(8,128)(2,1)} %bitcast.86, bf16[192,2048]{1,0:T(8,128)(2,1)} %bitcast.87, bf16[2,384,1024]{2,1,0:T(8,128)(2,1)} %shard_map.93.kv_ref, ...), custom_call_target="tpu_custom_call" | custom-call | tf_op jit(solution)/shard_map/pallas_call | solution.py:85
  129.0 0.0 copy-start.3
  129.0 0.9 slice.23
  130.0 1.4 fusion.15
  131.4 1.3 collective-permute-start.1
  132.7 0.0 copy-done.3
  132.7 0.2 mul.26
  132.9 0.1 copy.40
  133.0 5.3 %collective-permute-done.1 = bf16[2,192,16]{2,1,0:T(8,128)(2,1)S(1)} collective-permute-done((bf16[2,192,16]{2,1,0:T(8,128)(2,1)S(1)}, bf16[2,192,16]{2,1,0:T(8,128)(2,1)S(1)}, u32[]{:S(2)}, u32[]{:S(2)}) %collective-permute-start.1) | collective-permute-done | bytes 12320 | tf_op jit(solution)/shard_map/ppermute | solution.py:21
  138.3 0.6 fusion.1
  138.9 0.1 fusion.10
  139.0 0.1 collective-permute-start.2
  139.1 1.5 collective-permute-done.2
  140.6 0.1 fusion.13
  140.7 0.7 collective-permute-start.3
  141.5 4.9 %collective-permute-done.3 = f32[1,4,208,32]{2,3,1,0:T(8,128)S(1)} collective-permute-done((f32[1,4,208,32]{2,3,1,0:T(8,128)S(1)}, f32[1,4,208,32]{2,3,1,0:T(8,128)S(1)}, u32[]{:S(2)}, u32[]{:S(2)}) %collective-permute-start.3) | collective-permute-done | bytes 106528 | tf_op jit(solution)/shard_map/ppermute | solution.py:193
  146.4 1.5 collective-permute-start.4
  147.9 4.4 %collective-permute-done.4 = f32[2,208,32]{1,2,0:T(8,128)S(1)} collective-permute-done((f32[2,208,32]{1,2,0:T(8,128)S(1)}, f32[2,208,32]{1,2,0:T(8,128)S(1)}, u32[]{:S(2)}, u32[]{:S(2)}) %collective-permute-start.4) | collective-permute-done | bytes 53280 | tf_op jit(solution)/shard_map/ppermute | solution.py:193
  152.3 0.1 collective-permute-start.5
  152.4 3.9 %collective-permute-done.5 = f32[1,208,32]{1,2,0:T(8,128)S(1)} collective-permute-done((f32[1,208,32]{1,2,0:T(8,128)S(1)}, f32[1,208,32]{1,2,0:T(8,128)S(1)}, u32[]{:S(2)}, u32[]{:S(2)}) %collective-permute-start.5) | collective-permute-done | bytes 26656 | tf_op jit(solution)/shard_map/ppermute | solution.py:193
  156.3 0.0 copy-start.4
  156.3 0.7 slice.29
  157.0 0.0 copy-done.4
  (10 shorter events, 0.1 us)
Async XLA Ops:
  7.2 9.2 %copy-start = (bf16[1,192,2304]{2,1,0:T(8,128)(2,1)S(1)}, bf16[1,192,2304]{2,1,0:T(8,128)(2,1)}, u32[]{:S(2)}) copy-start(bf16[1,192,2304]{2,1,0:T(8,128)(2,1)} %param.6) | copy-start | bytes 2654212
  7.2 96.9 %all-gather.4.cloned.1.call-start = ((), (), s32[]{:S(2)}) async-start(), calls=%async_computation | async-start | bytes 10027008 | tf_op jit(solution)/shard_map/all_gather | solution.py:161
  7.9 58.7 %collective-permute-start = (bf16[192,2304]{1,0:T(8,128)(2,1)}, bf16[192,2304]{1,0:T(8,128)(2,1)}, u32[]{:S(2)}, u32[]{:S(2)}) collective-permute-start(bf16[192,2304]{1,0:T(8,128)(2,1)} %bitcast.77), channel_id=1, source_target_pairs={{0,4},{4,8},{8,12},{1,5},{5,9},{9,13},{2,6},{6,10},{10,14},{3,7},{... | collective-permute-start | bytes 2654216 | tf_op jit(solution)/shard_map/ppermute | solution.py:21
  16.4 1.7 %copy-start.5 = (bf16[2,16,144]{2,1,0:T(8,128)(2,1)S(1)}, bf16[2,16,144]{2,1,0:T(8,128)(2,1)}, u32[]{:S(2)}) copy-start(bf16[2,16,144]{2,1,0:T(8,128)(2,1)} %param.9) | copy-start | bytes 27652
  16.4 1.7 %copy-start.6 = (bf16[2,16,64]{2,1,0:T(8,128)(2,1)S(1)}, bf16[2,16,64]{2,1,0:T(8,128)(2,1)}, u32[]{:S(2)}) copy-start(bf16[2,16,64]{2,1,0:T(8,128)(2,1)} %param.10) | copy-start | bytes 12292
  69.3 3.7 %copy-start.1 = (bf16[192,4,576]{2,0,1:T(8,128)(2,1)S(1)}, bf16[192,4,576]{2,0,1:T(8,128)(2,1)}, u32[]{:S(2)}) copy-start(bf16[192,4,576]{2,0,1:T(8,128)(2,1)} %copy.31) | copy-start | bytes 2654212
  70.4 2.6 %copy-start.2 = (bf16[192,4,576]{2,0,1:T(8,128)(2,1)S(1)}, bf16[192,4,576]{2,0,1:T(8,128)(2,1)}, u32[]{:S(2)}) copy-start(bf16[192,4,576]{2,0,1:T(8,128)(2,1)} %copy.30) | copy-start | bytes 2654212
  129.0 3.7 %copy-start.3 = (f32[2,16,1024]{2,1,0:T(8,128)S(1)}, f32[2,16,1024]{2,1,0:T(8,128)}, u32[]{:S(2)}) copy-start(f32[2,16,1024]{2,1,0:T(8,128)} %get-tuple-element.11) | copy-start | bytes 393220
  131.4 6.9 %collective-permute-start.1 = (bf16[2,192,16]{2,1,0:T(8,128)(2,1)S(1)}, bf16[2,192,16]{2,1,0:T(8,128)(2,1)S(1)}, u32[]{:S(2)}, u32[]{:S(2)}) collective-permute-start(bf16[2,192,16]{2,1,0:T(8,128)(2,1)S(1)} %slice.23), channel_id=1, source_target_pairs={{4,0},{8,4},{12,8},{5,1},{9,5},{13,9},{6,2},{10,6},{14,10},{7,3},{... | collective-permute-start | bytes 36872 | tf_op jit(solution)/shard_map/ppermute | solution.py:21
  139.0 1.6 collective-permute-start.2
  140.7 5.6 %collective-permute-start.3 = (f32[1,4,208,32]{2,3,1,0:T(8,128)S(1)}, f32[1,4,208,32]{2,3,1,0:T(8,128)S(1)}, u32[]{:S(2)}, u32[]{:S(2)}) collective-permute-start(f32[1,4,208,32]{2,3,1,0:T(8,128)S(1)} %dynamic-slice_bitcast_fusion), channel_id=1, source_target_pairs={{0,2},{2,0},{1,3},{3,1},{4,6},{6,4},{5,7},{7,5},{8,10},{10,8},{9,1... | collective-permute-start | bytes 319496 | tf_op jit(solution)/shard_map/ppermute | solution.py:193
  146.4 5.9 %collective-permute-start.4 = (f32[2,208,32]{1,2,0:T(8,128)S(1)}, f32[2,208,32]{1,2,0:T(8,128)S(1)}, u32[]{:S(2)}, u32[]{:S(2)}) collective-permute-start(f32[2,208,32]{1,2,0:T(8,128)S(1)} %dynamic-slice_bitcast_fusion.1), channel_id=1, source_target_pairs={{0,8},{4,12},{8,0},{12,4},{1,9},{5,13},{9,1},{13,5},{2,10},{6,14},... | collective-permute-start | bytes 159752 | tf_op jit(solution)/shard_map/ppermute | solution.py:193
  152.3 4.0 %collective-permute-start.5 = (f32[1,208,32]{1,2,0:T(8,128)S(1)}, f32[1,208,32]{1,2,0:T(8,128)S(1)}, u32[]{:S(2)}, u32[]{:S(2)}) collective-permute-start(f32[1,208,32]{1,2,0:T(8,128)S(1)} %constant_dynamic-slice_fusion), channel_id=1, source_target_pairs={{0,4},{4,0},{8,12},{12,8},{1,5},{5,1},{9,13},{13,9},{2,6},{6,2},{1... | collective-permute-start | bytes 79880 | tf_op jit(solution)/shard_map/ppermute | solution.py:193
  156.3 0.7 copy-start.4
Sparse Core Ops, SparseCore 0:
  10.3 93.7 all-gather.3

commit v10 on v9

--- a/solution.py
+++ b/solution.py
@@ -162,7 +162,7 @@
     gathered = gathered.reshape((row_shards, col_shards) + kv_weight.shape)
     low_rows = jnp.concatenate([low_previous, low_rank], axis=1)
     key_value = project_pair(rows_split, gathered, low_rows, up_full)
-    return low_rows, key_value
+    return rows_both, low_rows, key_value
 
 
 def gather_adapters(adapter_down, adapter_up):
@@ -178,8 +178,20 @@
     return unshard(gathered[..., :down_cols]), unshard(gathered[..., down_cols:])
 
 
+def exchange_scatter(blocks, axis):
+    size = lax.axis_size(axis)
+    me = lax.axis_index(axis)
+    total = lax.dynamic_index_in_dim(blocks, me, axis=0, keepdims=False)
+    for shift in range(1, size):
+        send = lax.dynamic_index_in_dim(blocks, (me + shift) % size, axis=0, keepdims=False)
+        total = total + lax.ppermute(send, axis, [(i, (i + shift) % size) for i in range(size)])
+    return total
+
+
 def halving_scatter(blocks, axis):
     size = lax.axis_size(axis)
+    if size <= 4:
+        return exchange_scatter(blocks, axis)
     if size & (size - 1):
         return lax.psum_scatter(blocks, axis, scatter_dimension=0, tiled=True)[0]
     me = lax.axis_index(axis)
@@ -199,10 +211,7 @@
     members_rank = joined_down.shape[-1]
     down_cols = joined_down.shape[2]
     joined = jnp.concatenate([joined_down, joined_up], axis=2)
-    dp_size, sub_size = lax.axis_size("dp"), lax.axis_size("sub")
-    joined = joined.reshape((dp_size, sub_size) + joined.shape[1:])
-    mine = halving_scatter(joined.swapaxes(0, 1), "sub")
-    mine = halving_scatter(mine, "dp")
+    mine = halving_scatter(joined, ("dp", "sub"))
     mine = halving_scatter(mine, "ctx")
 
     def unshard(piece):
@@ -220,18 +229,18 @@
     rows_previous = shifted(rows_own, "ctx", 1)
     down_full, up_full = gather_adapters(adapter_down, adapter_up)
     is_first = lax.axis_index("ctx") == 0
-    low_rows, kv_both = project_rows(rows_previous, rows_own, kv_weight, down_full, up_full)
+    rows_both, low_rows, kv_both = project_rows(
+        rows_previous, rows_own, kv_weight, down_full, up_full
+    )
     attended, query_grad, projected, up_terms = attend(
         query_rows, kv_both, grad_rows, is_first, low_rows, up_full
     )
-    projected_returned = shifted(projected[:, :length], "ctx", -1)
-    projected_near = projected[:, length:]
-    rows_split = rows_own.reshape(length, row_shards, col_shards, -1)
     up_terms = up_terms.reshape(up_terms.shape[:2] + (row_shards, col_shards, -1)).transpose(3, 2, 4, 0, 1)
     down_terms = jnp.einsum(
-        "mrk,rcij->icjmk", projected_near, rows_split, preferred_element_type=jnp.float32
-    ) + jnp.einsum(
-        "mrk,rcij->icjmk", projected_returned, rows_split, preferred_element_type=jnp.float32
+        "mrk,rcij->icjmk",
+        projected,
+        rows_both.reshape(rows_both.shape[0], row_shards, col_shards, -1),
+        preferred_element_type=jnp.float32,
     )
     factor = adapter_scale / (lax.axis_size("dp") * lax.axis_size("sub"))
     flat = lambda terms: (terms * factor).reshape(terms.shape[:3] + (-1,))

time: 164 us -> 157 us (0.957)
  waiting for transfers between devices: 50.3 us -> 39.2 us
  local copies, waits for them, and re-layouts: 12.3 us -> 15.3 us
  other arithmetic: 3 us -> 5.35 us
    ppermute x2 -> x1, waiting for transfers between devices: 5.28 us -> 0.01 us  [shifted(): return lax.ppermute(value, axis, pairs)]
    ppermute x4 -> x6, waiting for transfers between devices: 14.7 us -> 11.1 us  [exchange_scatter(): lax.ppermute(send, axis, [(i, (i + shift) % size) for i in range(size)])]
    ppermute x4 -> x6, starting transfers between devices: 2.4 us -> 5.48 us  [exchange_scatter(): lax.ppermute(send, axis, [(i, (i + shift) % size) for i in range(size)])]
    concatenate x4, local copies, waits for them, and re-layouts: 7.44 us -> 10.2 us  [project_rows(): rows_both = jnp.concatenate([rows_previous, rows_own], axis=0)]
    all_gather x1, waiting for transfers between devices: 29.6 us -> 27.4 us  [project_rows(): lax.all_gather(kv_weight, ('ctx', 'dp', 'sub'), axis=0, tiled=False)]
    ppermute x2 -> x1, starting transfers between devices: 7.16 us -> 4.98 us  [shifted(): return lax.ppermute(value, axis, pairs)]
  transfers between devices with their start and end apart: 7 -> 8, of which waited for: 6 -> 6; matrix products, arithmetic and copies ran while one was open for 9% -> 12% of each run, Pallas kernels for 0% -> 0%
where the time goes in v10:
time: 157 us
  blocking collectives  44.4 us (28%)
  waiting for transfers between devices  39.2 us (25%)
  Pallas kernels  25 us (16%)
  local copies, waits for them, and re-layouts  15.3 us (10%)
  between operations  14.2 us (9%)
  starting transfers between devices  10.5 us (7%)
  other arithmetic  5.35 us (3%)
  matrix products  2.5 us (2%)
    all_gather x1, blocking collectives, gather_adapters(): gathered = lax.all_gather(joined, axes, axis=0, tiled=False)  44.4 us
    all_gather x1, waiting for transfers between devices, project_rows(): lax.all_gather(kv_weight, ('ctx', 'dp', 'sub'), axis=0, tiled=False)  27.4 us
    pallas_call x1, Pallas kernels, attention_heads(): pl.pallas_call(attention_kernel, grid=(heads,), in_specs=[whole(mask.shap...  13.9 us
    ppermute x6, waiting for transfers between devices, exchange_scatter(): lax.ppermute(send, axis, [(i, (i + shift) % size) for i in range(size)])  11.1 us
    pallas_call x1, Pallas kernels, project_pair(): pl.pallas_call(projection_kernel, grid=(members, col_shards), in_specs=[p...  11.1 us
    concatenate x4, local copies, waits for them, and re-layouts, project_rows(): rows_both = jnp.concatenate([rows_previous, rows_own], axis=0)  10.2 us
    ppermute x6, starting transfers between devices, exchange_scatter(): lax.ppermute(send, axis, [(i, (i + shift) % size) for i in range(size)])  5.48 us
    ppermute x1, starting transfers between devices, shifted(): return lax.ppermute(value, axis, pairs)  4.98 us
  transfers between devices with their start and end apart: 8, of which 6 were waited for; matrix products, arithmetic and copies ran while one was open for 12% of the time, Pallas kernels for 0%

profile of v10, /device:TPU:0, one launch (start us, length us, event | category | flops | bytes accessed | tf_op | source)
XLA Modules:
  0.0 156.5 jit_solution(18179101012463061990)
XLA Ops:
  7.2 0.0 copy-start
  7.2 0.0 all-gather.4.cloned.1.call-start
  7.2 0.7 all-gather.4.cloned.1.call-update
  7.9 5.0 %collective-permute-start = (bf16[192,2304]{1,0:T(8,128)(2,1)}, bf16[192,2304]{1,0:T(8,128)(2,1)S(1)}, u32[]{:S(2)}, u32[]{:S(2)}) collective-permute-start(bf16[192,2304]{1,0:T(8,128)(2,1)} %bitcast.84), channel_id=1, source_target_pairs={{0,4},{4,8},{8,12},{1,5},{5,9},{9,13},{2,6},{6,10},{10,14},{3,7},{... | collective-permute-start | bytes 2654216 | tf_op jit(solution)/shard_map/ppermute | solution.py:21
  12.9 3.4 %concatenate.25 = bf16[192,4,576]{2,1,0:T(4,128)(2,1)} reshape(bf16[1,192,2304]{2,1,0:T(8,128)(2,1)} %param.6) | data formatting | bytes 1769472 | tf_op jit(solution)/shard_map/concatenate | solution.py:159
  16.3 0.0 copy-done
  16.3 0.0 copy-start.3
  16.3 0.0 copy-start.4
  16.3 0.6 copy.35
  17.0 2.3 %copy.29 = bf16[192,4,576]{2,0,1:T(8,128)(2,1)} copy(bf16[192,4,576]{2,1,0:T(4,128)(2,1)} %concatenate.25) | data formatting | bytes 1769472 | tf_op jit(solution)/shard_map/concatenate | solution.py:159
  19.2 0.0 copy-done.3
  19.3 0.0 copy-done.4
  19.3 0.1 pad_maximum_fusion.1
  19.3 44.4 %all-gather.1 = bf16[32,16,208]{2,1,0:T(8,128)(2,1)S(1)} all-gather(bf16[2,16,208]{2,1,0:T(8,128)(2,1)S(1)} %pad_maximum_fusion.1), channel_id=3, replica_groups=mesh['groups'=2,'ctx'=4,'dp'=2,'sub'=2] {'ctx','dp','sub'}, dimensions={0}, use_global_device_ids=true | all-gather | bytes 226304 | tf_op jit(solution)/shard_map/all_gather | solution.py:172
  63.8 0.1 slice.17
  63.9 0.2 copy.45
  64.0 0.3 reshape.41
  64.4 0.1 copy.46
  64.4 0.8 reshape.42.up_ref
  65.2 1.0 fusion.10.mask_ref
  66.2 0.3 fusion.5
  66.6 0.0 collective-permute-done
  66.6 2.1 %concatenate.24 = bf16[192,4,576]{2,1,0:T(4,128)(2,1)} reshape(bf16[192,2304]{1,0:T(8,128)(2,1)S(1)} %collective-permute-done) | data formatting | bytes 1769472 | tf_op jit(solution)/shard_map/concatenate | solution.py:159
  68.7 2.3 %copy.28 = bf16[192,4,576]{2,0,1:T(8,128)(2,1)} copy(bf16[192,4,576]{2,1,0:T(4,128)(2,1)} %concatenate.24) | data formatting | bytes 1769472 | tf_op jit(solution)/shard_map/concatenate | solution.py:159
  71.1 0.3 fusion.4
  71.4 0.1 pad_maximum_fusion
  71.5 0.8 copy.32.low_ref
  72.4 1.4 copy.34
  73.8 2.9 %maximum_bitcast_fusion.rows_ref = bf16[4,384,576]{2,1,0:T(8,128)(2,1)} fusion(bf16[192,4,576]{2,0,1:T(8,128)(2,1)} %copy.29, bf16[192,4,576]{2,0,1:T(8,128)(2,1)} %copy.28), kind=kLoop, calls=%fused_computation | loop fusion | flops 3538944 | bytes 3538944 | tf_op jit(solution)/shard_map/transpose | solution.py:160
  76.7 27.4 %all-gather.4.cloned.1.call-done = bf16[32,576,256]{2,1,0:T(8,128)(2,1)} async-done(((bf16[2,576,256]{2,1,0:T(8,128)(2,1)}), bf16[32,576,256]{2,1,0:T(8,128)(2,1)}) %all-gather.4.cloned.1.call-update) | async-done | bytes 9437200 | tf_op jit(solution)/shard_map/all_gather | solution.py:161
  104.1 11.1 %shard_map.93.kv_ref = bf16[2,384,1024]{2,1,0:T(8,128)(2,1)} custom-call(bf16[4,384,576]{2,1,0:T(8,128)(2,1)} %maximum_bitcast_fusion.rows_ref, bf16[4,4,2,576,256]{4,3,2,1,0:T(8,128)(2,1)} %bitcast.83, bf16[2,384,16]{2,1,0:T(8,128)(2,1)} %copy.32.low_ref, bf16[2,16,1024]{2,1,0:T(8,128)(2,1)} %reshape.42.up_ref), custom_call_target="tpu_custom_call" | custom-call | tf_op jit(solution)/shard_map/pallas_call | solution.py:137
  115.2 0.0 copy-start.1
  115.2 13.9 %shard_map.94 = (bf16[192,2048]{1,0:T(8,128)(2,1)}, bf16[192,2048]{1,0:T(8,128)(2,1)}, bf16[2,384,16]{2,1,0:T(8,128)(2,1)}, f32[2,16,1024]{2,1,0:T(8,128)}) custom-call(s32[384,384]{1,0:T(8,128)} %fusion.10.mask_ref, bf16[192,2048]{1,0:T(8,128)(2,1)} %bitcast.93, bf16[192,2048]{1,0:T(8,128)(2,1)} %bitcast.94, bf16[2,384,1024]{2,1,0:T(8,128)(2,1)} %shard_map.93.kv_ref, ...), custom_call_target="tpu_custom_call" | custom-call | tf_op jit(solution)/shard_map/pallas_call | solution.py:85
  129.1 0.9 broadcast_multiply_fusion
  130.0 0.2 mul.29
  130.2 0.1 copy.37
  130.3 0.0 copy-done.1
  130.3 1.8 %fusion.3 = f32[4,4,144,2,16]{2,4,3,1,0:T(8,128)S(1)} fusion(bf16[192,4,4,144]{0,3,2,1:T(8,128)(2,1)S(1)} %bitcast.85, bf16[192,4,4,144]{0,3,2,1:T(8,128)(2,1)S(1)} %bitcast.86, bf16[2,384,16]{2,1,0:T(8,128)(2,1)} %get-tuple-element.10), kind=kOutput, calls=%fused_computation.5 | convolution fusion | flops 60235776 | bytes 2088960 | tf_op jit(solution)/shard_map/mrk,rcij->icjmk/dot_general | solution.py:239
  132.1 0.1 fusion.20
  132.2 0.6 collective-permute-start.3
  132.9 1.3 collective-permute-start.2
  134.2 0.0 collective-permute-start.1
  134.2 2.6 %collective-permute-done.3 = f32[4,208,32]{1,2,0:T(8,128)S(1)} collective-permute-done((f32[4,208,32]{1,2,0:T(8,128)S(1)}, f32[4,208,32]{1,2,0:T(8,128)S(1)}, u32[]{:S(2)}, u32[]{:S(2)}) %collective-permute-start.3) | collective-permute-done | bytes 106528 | tf_op jit(solution)/shard_map/ppermute | solution.py:187
  136.7 4.3 %collective-permute-done.2 = f32[4,208,32]{1,2,0:T(8,128)S(1)} collective-permute-done((f32[4,208,32]{1,2,0:T(8,128)S(1)}, f32[4,208,32]{1,2,0:T(8,128)S(1)}, u32[]{:S(2)}, u32[]{:S(2)}) %collective-permute-start.2) | collective-permute-done | bytes 106528 | tf_op jit(solution)/shard_map/ppermute | solution.py:187
  141.0 0.0 collective-permute-done.1
  141.0 0.1 fusion.18
  141.1 1.5 collective-permute-start.6
  142.6 0.7 collective-permute-start.5
  143.3 1.4 collective-permute-start.4
  144.7 0.4 collective-permute-done.6
  145.1 2.6 %collective-permute-done.5 = f32[208,32]{0,1:T(8,128)S(1)} collective-permute-done((f32[208,32]{0,1:T(8,128)S(1)}, f32[208,32]{0,1:T(8,128)S(1)}, u32[]{:S(2)}, u32[]{:S(2)}) %collective-permute-start.5) | collective-permute-done | bytes 26656 | tf_op jit(solution)/shard_map/ppermute | solution.py:187
  147.8 1.2 collective-permute-done.4
  149.0 0.0 copy-start.2
  149.0 0.7 slice.19
  149.7 0.0 copy-done.2
  (4 shorter events, 0.0 us)
Async XLA Ops:
  7.2 9.1 %copy-start = (bf16[1,192,2304]{2,1,0:T(8,128)(2,1)S(1)}, bf16[1,192,2304]{2,1,0:T(8,128)(2,1)}, u32[]{:S(2)}) copy-start(bf16[1,192,2304]{2,1,0:T(8,128)(2,1)} %param.6) | copy-start | bytes 2654212
  7.2 96.9 %all-gather.4.cloned.1.call-start = ((), (), s32[]{:S(2)}) async-start(), calls=%async_computation | async-start | bytes 10027008 | tf_op jit(solution)/shard_map/all_gather | solution.py:161
  7.9 58.7 %collective-permute-start = (bf16[192,2304]{1,0:T(8,128)(2,1)}, bf16[192,2304]{1,0:T(8,128)(2,1)S(1)}, u32[]{:S(2)}, u32[]{:S(2)}) collective-permute-start(bf16[192,2304]{1,0:T(8,128)(2,1)} %bitcast.84), channel_id=1, source_target_pairs={{0,4},{4,8},{8,12},{1,5},{5,9},{9,13},{2,6},{6,10},{10,14},{3,7},{... | collective-permute-start | bytes 2654216 | tf_op jit(solution)/shard_map/ppermute | solution.py:21
  16.3 2.9 %copy-start.3 = (bf16[2,16,144]{2,1,0:T(8,128)(2,1)S(1)}, bf16[2,16,144]{2,1,0:T(8,128)(2,1)}, u32[]{:S(2)}) copy-start(bf16[2,16,144]{2,1,0:T(8,128)(2,1)} %param.9) | copy-start | bytes 27652
  16.3 2.9 %copy-start.4 = (bf16[2,16,64]{2,1,0:T(8,128)(2,1)S(1)}, bf16[2,16,64]{2,1,0:T(8,128)(2,1)}, u32[]{:S(2)}) copy-start(bf16[2,16,64]{2,1,0:T(8,128)(2,1)} %param.10) | copy-start | bytes 12292
  115.2 15.1 %copy-start.1 = (bf16[192,2304]{0,1:T(8,128)(2,1)S(1)}, bf16[192,2304]{0,1:T(8,128)(2,1)}, u32[]{:S(2)}) copy-start(bf16[192,2304]{0,1:T(8,128)(2,1)} %copy.34) | copy-start | bytes 2654212
  132.2 4.5 %collective-permute-start.3 = (f32[4,208,32]{1,2,0:T(8,128)S(1)}, f32[4,208,32]{1,2,0:T(8,128)S(1)}, u32[]{:S(2)}, u32[]{:S(2)}) collective-permute-start(f32[4,208,32]{1,2,0:T(8,128)S(1)} %get-tuple-element.14), channel_id=1, source_target_pairs={{0,3},{1,0},{2,1},{3,2},{4,7},{5,4},{6,5},{7,6},{8,11},{9,8},{10,9... | collective-permute-start | bytes 319496 | tf_op jit(solution)/shard_map/ppermute | solution.py:187
  132.9 8.2 %collective-permute-start.2 = (f32[4,208,32]{1,2,0:T(8,128)S(1)}, f32[4,208,32]{1,2,0:T(8,128)S(1)}, u32[]{:S(2)}, u32[]{:S(2)}) collective-permute-start(f32[4,208,32]{1,2,0:T(8,128)S(1)} %get-tuple-element.13), channel_id=1, source_target_pairs={{0,2},{1,3},{2,0},{3,1},{4,6},{5,7},{6,4},{7,5},{8,10},{9,11},{10,... | collective-permute-start | bytes 319496 | tf_op jit(solution)/shard_map/ppermute | solution.py:187
  134.2 6.8 %collective-permute-start.1 = (f32[4,208,32]{1,2,0:T(8,128)S(1)}, f32[4,208,32]{1,2,0:T(8,128)S(1)}, u32[]{:S(2)}, u32[]{:S(2)}) collective-permute-start(f32[4,208,32]{1,2,0:T(8,128)S(1)} %get-tuple-element.12), channel_id=1, source_target_pairs={{0,1},{1,2},{2,3},{3,0},{4,5},{5,6},{6,7},{7,4},{8,9},{9,10},{10,1... | collective-permute-start | bytes 319496 | tf_op jit(solution)/shard_map/ppermute | solution.py:187
  141.1 4.0 %collective-permute-start.6 = (f32[208,32]{0,1:T(8,128)S(1)}, f32[208,32]{0,1:T(8,128)S(1)}, u32[]{:S(2)}, u32[]{:S(2)}) collective-permute-start(f32[208,32]{0,1:T(8,128)S(1)} %get-tuple-element.16), channel_id=1, source_target_pairs={{0,12},{4,0},{8,4},{12,8},{1,13},{5,1},{9,5},{13,9},{2,14},{6,2},{... | collective-permute-start | bytes 79880 | tf_op jit(solution)/shard_map/ppermute | solution.py:187
  142.6 5.2 %collective-permute-start.5 = (f32[208,32]{0,1:T(8,128)S(1)}, f32[208,32]{0,1:T(8,128)S(1)}, u32[]{:S(2)}, u32[]{:S(2)}) collective-permute-start(f32[208,32]{0,1:T(8,128)S(1)} %get-tuple-element.17), channel_id=1, source_target_pairs={{0,8},{4,12},{8,0},{12,4},{1,9},{5,13},{9,1},{13,5},{2,10},{6,14},... | collective-permute-start | bytes 79880 | tf_op jit(solution)/shard_map/ppermute | solution.py:187
  143.3 5.7 %collective-permute-start.4 = (f32[208,32]{0,1:T(8,128)S(1)}, f32[208,32]{0,1:T(8,128)S(1)}, u32[]{:S(2)}, u32[]{:S(2)}) collective-permute-start(f32[208,32]{0,1:T(8,128)S(1)} %get-tuple-element.15), channel_id=1, source_target_pairs={{0,4},{4,8},{8,12},{12,0},{1,5},{5,9},{9,13},{13,1},{2,6},{6,10},{... | collective-permute-start | bytes 79880 | tf_op jit(solution)/shard_map/ppermute | solution.py:187
  149.0 0.7 copy-start.2
Sparse Core Ops, SparseCore 0:
  10.3 93.7 all-gather.3

commit v11 on v10

--- a/solution.py
+++ b/solution.py
@@ -39,7 +39,7 @@
     bent_score = jnp.tanh(raw_score / logit_cap)
     expo_terms = jnp.where(visible, jnp.exp(logit_cap * bent_score), 0.0)
     denominator = jnp.sum(expo_terms, axis=-1, keepdims=True)
-    prob_wide = (expo_terms / denominator).astype(jnp.bfloat16).astype(jnp.float32)
+    prob_wide = (expo_terms * (1.0 / denominator)).astype(jnp.bfloat16).astype(jnp.float32)
     attn_prob = prob_wide.astype(jnp.bfloat16)
     head_out = jnp.dot(attn_prob, v, preferred_element_type=jnp.float32).astype(out_ref.dtype)
     out_ref[:, :half] = head_out[:rows]
@@ -51,10 +51,12 @@
     head_qgrad = jnp.dot(score_grad, k, preferred_element_type=jnp.float32).astype(dq_ref.dtype)
     dq_ref[:, :half] = head_qgrad[:rows]
     dq_ref[:, half:] = head_qgrad[rows:]
-    score_t = score_grad.astype(jnp.float32).T.astype(jnp.bfloat16)
-    prob_t = prob_wide.T.astype(jnp.bfloat16)
-    key_grad = jnp.dot(score_t, q, preferred_element_type=jnp.float32).astype(jnp.bfloat16)
-    value_grad = jnp.dot(prob_t, do, preferred_element_type=jnp.float32).astype(jnp.bfloat16)
+    key_grad = lax.dot_general(
+        score_grad, q, contract_first, preferred_element_type=jnp.float32
+    ).astype(jnp.bfloat16)
+    value_grad = lax.dot_general(
+        attn_prob, do, contract_first, preferred_element_type=jnp.float32
+    ).astype(jnp.bfloat16)
 
     @pl.when(head == 0)
     def _():

time: 157 us -> 157 us (level)
  no operation moved by 1% of the time
where the time goes in v11:
time: 157 us; the launch traced here: 156 us
  blocking collectives  44.4 us (28%)
  waiting for transfers between devices  39.2 us (25%)
  Pallas kernels  24.5 us (16%)
  local copies, waits for them, and re-layouts  15.3 us (10%)
  between operations  14.2 us (9%)
  starting transfers between devices  10.5 us (7%)
  other arithmetic  5.35 us (3%)
  matrix products  2.5 us (2%)
    all_gather x1, blocking collectives, gather_adapters(): gathered = lax.all_gather(joined, axes, axis=0, tiled=False)  44.4 us
    all_gather x1, waiting for transfers between devices, project_rows(): lax.all_gather(kv_weight, ('ctx', 'dp', 'sub'), axis=0, tiled=False)  27.4 us
    pallas_call x1, Pallas kernels, attention_heads(): pl.pallas_call(attention_kernel, grid=(heads,), in_specs=[whole(mask.shap...  13.4 us
    ppermute x6, waiting for transfers between devices, exchange_scatter(): lax.ppermute(send, axis, [(i, (i + shift) % size) for i in range(size)])  11.1 us
    pallas_call x1, Pallas kernels, project_pair(): pl.pallas_call(projection_kernel, grid=(members, col_shards), in_specs=[p...  11.1 us
    concatenate x4, local copies, waits for them, and re-layouts, project_rows(): rows_both = jnp.concatenate([rows_previous, rows_own], axis=0)  10.2 us
    ppermute x6, starting transfers between devices, exchange_scatter(): lax.ppermute(send, axis, [(i, (i + shift) % size) for i in range(size)])  5.47 us
    ppermute x1, starting transfers between devices, shifted(): return lax.ppermute(value, axis, pairs)  4.98 us
  transfers between devices with their start and end apart: 8, of which 6 were waited for; matrix products, arithmetic and copies ran while one was open for 12% of the time, Pallas kernels for 0%

profile of v11, /device:TPU:0, one launch (start us, length us, event | category | flops | bytes accessed | tf_op | source)
XLA Modules:
  0.0 156.0 jit_solution(9777045131146346346)
XLA Ops:
  7.2 0.0 copy-start
  7.2 0.0 all-gather.4.cloned.1.call-start
  7.2 0.7 all-gather.4.cloned.1.call-update
  7.9 5.0 %collective-permute-start = (bf16[192,2304]{1,0:T(8,128)(2,1)}, bf16[192,2304]{1,0:T(8,128)(2,1)S(1)}, u32[]{:S(2)}, u32[]{:S(2)}) collective-permute-start(bf16[192,2304]{1,0:T(8,128)(2,1)} %bitcast.84), channel_id=1, source_target_pairs={{0,4},{4,8},{8,12},{1,5},{5,9},{9,13},{2,6},{6,10},{10,14},{3,7},{... | collective-permute-start | bytes 2654216 | tf_op jit(solution)/shard_map/ppermute | solution.py:21
  12.9 3.4 %concatenate.25 = bf16[192,4,576]{2,1,0:T(4,128)(2,1)} reshape(bf16[1,192,2304]{2,1,0:T(8,128)(2,1)} %param.6) | data formatting | bytes 1769472 | tf_op jit(solution)/shard_map/concatenate | solution.py:161
  16.3 0.0 copy-done
  16.3 0.0 copy-start.3
  16.3 0.0 copy-start.4
  16.3 0.6 copy.35
  17.0 2.3 %copy.29 = bf16[192,4,576]{2,0,1:T(8,128)(2,1)} copy(bf16[192,4,576]{2,1,0:T(4,128)(2,1)} %concatenate.25) | data formatting | bytes 1769472 | tf_op jit(solution)/shard_map/concatenate | solution.py:161
  19.2 0.0 copy-done.3
  19.3 0.0 copy-done.4
  19.3 0.1 pad_maximum_fusion.1
  19.3 44.4 %all-gather.1 = bf16[32,16,208]{2,1,0:T(8,128)(2,1)S(1)} all-gather(bf16[2,16,208]{2,1,0:T(8,128)(2,1)S(1)} %pad_maximum_fusion.1), channel_id=3, replica_groups=mesh['groups'=2,'ctx'=4,'dp'=2,'sub'=2] {'ctx','dp','sub'}, dimensions={0}, use_global_device_ids=true | all-gather | bytes 226304 | tf_op jit(solution)/shard_map/all_gather | solution.py:174
  63.8 0.1 slice.17
  63.9 0.2 copy.45
  64.0 0.3 reshape.41
  64.4 0.1 copy.46
  64.4 0.8 reshape.42.up_ref
  65.2 1.0 fusion.10.mask_ref
  66.2 0.3 fusion.5
  66.6 0.0 collective-permute-done
  66.6 2.1 %concatenate.24 = bf16[192,4,576]{2,1,0:T(4,128)(2,1)} reshape(bf16[192,2304]{1,0:T(8,128)(2,1)S(1)} %collective-permute-done) | data formatting | bytes 1769472 | tf_op jit(solution)/shard_map/concatenate | solution.py:161
  68.7 2.3 %copy.28 = bf16[192,4,576]{2,0,1:T(8,128)(2,1)} copy(bf16[192,4,576]{2,1,0:T(4,128)(2,1)} %concatenate.24) | data formatting | bytes 1769472 | tf_op jit(solution)/shard_map/concatenate | solution.py:161
  71.1 0.3 fusion.4
  71.4 0.1 pad_maximum_fusion
  71.5 0.8 copy.32.low_ref
  72.4 1.4 copy.34
  73.8 2.9 %maximum_bitcast_fusion.rows_ref = bf16[4,384,576]{2,1,0:T(8,128)(2,1)} fusion(bf16[192,4,576]{2,0,1:T(8,128)(2,1)} %copy.29, bf16[192,4,576]{2,0,1:T(8,128)(2,1)} %copy.28), kind=kLoop, calls=%fused_computation | loop fusion | flops 3538944 | bytes 3538944 | tf_op jit(solution)/shard_map/transpose | solution.py:162
  76.7 27.4 %all-gather.4.cloned.1.call-done = bf16[32,576,256]{2,1,0:T(8,128)(2,1)} async-done(((bf16[2,576,256]{2,1,0:T(8,128)(2,1)}), bf16[32,576,256]{2,1,0:T(8,128)(2,1)}) %all-gather.4.cloned.1.call-update) | async-done | bytes 9437200 | tf_op jit(solution)/shard_map/all_gather | solution.py:163
  104.1 11.1 %shard_map.93.kv_ref = bf16[2,384,1024]{2,1,0:T(8,128)(2,1)} custom-call(bf16[4,384,576]{2,1,0:T(8,128)(2,1)} %maximum_bitcast_fusion.rows_ref, bf16[4,4,2,576,256]{4,3,2,1,0:T(8,128)(2,1)} %bitcast.83, bf16[2,384,16]{2,1,0:T(8,128)(2,1)} %copy.32.low_ref, bf16[2,16,1024]{2,1,0:T(8,128)(2,1)} %reshape.42.up_ref), custom_call_target="tpu_custom_call" | custom-call | tf_op jit(solution)/shard_map/pallas_call | solution.py:139
  115.2 0.0 copy-start.1
  115.2 13.4 %shard_map.94 = (bf16[192,2048]{1,0:T(8,128)(2,1)}, bf16[192,2048]{1,0:T(8,128)(2,1)}, bf16[2,384,16]{2,1,0:T(8,128)(2,1)}, f32[2,16,1024]{2,1,0:T(8,128)}) custom-call(s32[384,384]{1,0:T(8,128)} %fusion.10.mask_ref, bf16[192,2048]{1,0:T(8,128)(2,1)} %bitcast.93, bf16[192,2048]{1,0:T(8,128)(2,1)} %bitcast.94, bf16[2,384,1024]{2,1,0:T(8,128)(2,1)} %shard_map.93.kv_ref, ...), custom_call_target="tpu_custom_call" | custom-call | tf_op jit(solution)/shard_map/pallas_call | solution.py:87
  128.6 0.9 broadcast_multiply_fusion
  129.5 0.2 mul.29
  129.7 0.1 copy.37
  129.8 0.0 copy-done.1
  129.8 1.8 %fusion.3 = f32[4,4,144,2,16]{2,4,3,1,0:T(8,128)S(1)} fusion(bf16[192,4,4,144]{0,3,2,1:T(8,128)(2,1)S(1)} %bitcast.85, bf16[192,4,4,144]{0,3,2,1:T(8,128)(2,1)S(1)} %bitcast.86, bf16[2,384,16]{2,1,0:T(8,128)(2,1)} %get-tuple-element.10), kind=kOutput, calls=%fused_computation.5 | convolution fusion | flops 60235776 | bytes 2088960 | tf_op jit(solution)/shard_map/mrk,rcij->icjmk/dot_general | solution.py:241
  131.6 0.1 fusion.20
  131.7 0.6 collective-permute-start.3
  132.4 1.3 collective-permute-start.2
  133.7 0.0 collective-permute-start.1
  133.7 2.6 %collective-permute-done.3 = f32[4,208,32]{1,2,0:T(8,128)S(1)} collective-permute-done((f32[4,208,32]{1,2,0:T(8,128)S(1)}, f32[4,208,32]{1,2,0:T(8,128)S(1)}, u32[]{:S(2)}, u32[]{:S(2)}) %collective-permute-start.3) | collective-permute-done | bytes 106528 | tf_op jit(solution)/shard_map/ppermute | solution.py:189
  136.2 4.3 %collective-permute-done.2 = f32[4,208,32]{1,2,0:T(8,128)S(1)} collective-permute-done((f32[4,208,32]{1,2,0:T(8,128)S(1)}, f32[4,208,32]{1,2,0:T(8,128)S(1)}, u32[]{:S(2)}, u32[]{:S(2)}) %collective-permute-start.2) | collective-permute-done | bytes 106528 | tf_op jit(solution)/shard_map/ppermute | solution.py:189
  140.5 0.0 collective-permute-done.1
  140.5 0.1 fusion.18
  140.6 1.5 collective-permute-start.6
  142.1 0.7 collective-permute-start.5
  142.8 1.4 collective-permute-start.4
  144.2 0.4 collective-permute-done.6
  144.6 2.6 %collective-permute-done.5 = f32[208,32]{0,1:T(8,128)S(1)} collective-permute-done((f32[208,32]{0,1:T(8,128)S(1)}, f32[208,32]{0,1:T(8,128)S(1)}, u32[]{:S(2)}, u32[]{:S(2)}) %collective-permute-start.5) | collective-permute-done | bytes 26656 | tf_op jit(solution)/shard_map/ppermute | solution.py:189
  147.3 1.2 collective-permute-done.4
  148.5 0.0 copy-start.2
  148.5 0.7 slice.19
  149.2 0.0 copy-done.2
  (4 shorter events, 0.0 us)
Async XLA Ops:
  7.2 9.1 %copy-start = (bf16[1,192,2304]{2,1,0:T(8,128)(2,1)S(1)}, bf16[1,192,2304]{2,1,0:T(8,128)(2,1)}, u32[]{:S(2)}) copy-start(bf16[1,192,2304]{2,1,0:T(8,128)(2,1)} %param.6) | copy-start | bytes 2654212
  7.2 96.9 %all-gather.4.cloned.1.call-start = ((), (), s32[]{:S(2)}) async-start(), calls=%async_computation | async-start | bytes 10027008 | tf_op jit(solution)/shard_map/all_gather | solution.py:163
  7.9 58.7 %collective-permute-start = (bf16[192,2304]{1,0:T(8,128)(2,1)}, bf16[192,2304]{1,0:T(8,128)(2,1)S(1)}, u32[]{:S(2)}, u32[]{:S(2)}) collective-permute-start(bf16[192,2304]{1,0:T(8,128)(2,1)} %bitcast.84), channel_id=1, source_target_pairs={{0,4},{4,8},{8,12},{1,5},{5,9},{9,13},{2,6},{6,10},{10,14},{3,7},{... | collective-permute-start | bytes 2654216 | tf_op jit(solution)/shard_map/ppermute | solution.py:21
  16.3 2.9 %copy-start.3 = (bf16[2,16,144]{2,1,0:T(8,128)(2,1)S(1)}, bf16[2,16,144]{2,1,0:T(8,128)(2,1)}, u32[]{:S(2)}) copy-start(bf16[2,16,144]{2,1,0:T(8,128)(2,1)} %param.9) | copy-start | bytes 27652
  16.3 2.9 %copy-start.4 = (bf16[2,16,64]{2,1,0:T(8,128)(2,1)S(1)}, bf16[2,16,64]{2,1,0:T(8,128)(2,1)}, u32[]{:S(2)}) copy-start(bf16[2,16,64]{2,1,0:T(8,128)(2,1)} %param.10) | copy-start | bytes 12292
  115.2 14.6 %copy-start.1 = (bf16[192,2304]{0,1:T(8,128)(2,1)S(1)}, bf16[192,2304]{0,1:T(8,128)(2,1)}, u32[]{:S(2)}) copy-start(bf16[192,2304]{0,1:T(8,128)(2,1)} %copy.34) | copy-start | bytes 2654212
  131.7 4.5 %collective-permute-start.3 = (f32[4,208,32]{1,2,0:T(8,128)S(1)}, f32[4,208,32]{1,2,0:T(8,128)S(1)}, u32[]{:S(2)}, u32[]{:S(2)}) collective-permute-start(f32[4,208,32]{1,2,0:T(8,128)S(1)} %get-tuple-element.14), channel_id=1, source_target_pairs={{0,3},{1,0},{2,1},{3,2},{4,7},{5,4},{6,5},{7,6},{8,11},{9,8},{10,9... | collective-permute-start | bytes 319496 | tf_op jit(solution)/shard_map/ppermute | solution.py:189
  132.4 8.2 %collective-permute-start.2 = (f32[4,208,32]{1,2,0:T(8,128)S(1)}, f32[4,208,32]{1,2,0:T(8,128)S(1)}, u32[]{:S(2)}, u32[]{:S(2)}) collective-permute-start(f32[4,208,32]{1,2,0:T(8,128)S(1)} %get-tuple-element.13), channel_id=1, source_target_pairs={{0,2},{1,3},{2,0},{3,1},{4,6},{5,7},{6,4},{7,5},{8,10},{9,11},{10,... | collective-permute-start | bytes 319496 | tf_op jit(solution)/shard_map/ppermute | solution.py:189
  133.7 6.8 %collective-permute-start.1 = (f32[4,208,32]{1,2,0:T(8,128)S(1)}, f32[4,208,32]{1,2,0:T(8,128)S(1)}, u32[]{:S(2)}, u32[]{:S(2)}) collective-permute-start(f32[4,208,32]{1,2,0:T(8,128)S(1)} %get-tuple-element.12), channel_id=1, source_target_pairs={{0,1},{1,2},{2,3},{3,0},{4,5},{5,6},{6,7},{7,4},{8,9},{9,10},{10,1... | collective-permute-start | bytes 319496 | tf_op jit(solution)/shard_map/ppermute | solution.py:189
  140.6 4.0 %collective-permute-start.6 = (f32[208,32]{0,1:T(8,128)S(1)}, f32[208,32]{0,1:T(8,128)S(1)}, u32[]{:S(2)}, u32[]{:S(2)}) collective-permute-start(f32[208,32]{0,1:T(8,128)S(1)} %get-tuple-element.16), channel_id=1, source_target_pairs={{0,12},{4,0},{8,4},{12,8},{1,13},{5,1},{9,5},{13,9},{2,14},{6,2},{... | collective-permute-start | bytes 79880 | tf_op jit(solution)/shard_map/ppermute | solution.py:189
  142.1 5.2 %collective-permute-start.5 = (f32[208,32]{0,1:T(8,128)S(1)}, f32[208,32]{0,1:T(8,128)S(1)}, u32[]{:S(2)}, u32[]{:S(2)}) collective-permute-start(f32[208,32]{0,1:T(8,128)S(1)} %get-tuple-element.17), channel_id=1, source_target_pairs={{0,8},{4,12},{8,0},{12,4},{1,9},{5,13},{9,1},{13,5},{2,10},{6,14},... | collective-permute-start | bytes 79880 | tf_op jit(solution)/shard_map/ppermute | solution.py:189
  142.8 5.7 %collective-permute-start.4 = (f32[208,32]{0,1:T(8,128)S(1)}, f32[208,32]{0,1:T(8,128)S(1)}, u32[]{:S(2)}, u32[]{:S(2)}) collective-permute-start(f32[208,32]{0,1:T(8,128)S(1)} %get-tuple-element.15), channel_id=1, source_target_pairs={{0,4},{4,8},{8,12},{12,0},{1,5},{5,9},{9,13},{13,1},{2,6},{6,10},{... | collective-permute-start | bytes 79880 | tf_op jit(solution)/shard_map/ppermute | solution.py:189
  148.5 0.7 copy-start.2
Sparse Core Ops, SparseCore 0:
  10.3 93.7 all-gather.3

commit v12 on v11

--- a/solution.py
+++ b/solution.py
@@ -167,11 +167,25 @@
     return rows_both, low_rows, key_value
 
 
+def exchange_gather(block, axis):
+    size = lax.axis_size(axis)
+    me = lax.axis_index(axis)
+    received = [block] + [
+        lax.ppermute(block, axis, [(i, (i + shift) % size) for i in range(size)])
+        for shift in range(1, size)
+    ]
+    order = (me - jnp.arange(size)) % size
+    return jnp.take(jnp.stack(received), order, axis=0)
+
+
 def gather_adapters(adapter_down, adapter_up):
-    axes = ("ctx", "dp", "sub")
     down_cols = adapter_down.shape[2]
     joined = jnp.concatenate([adapter_down, adapter_up], axis=2)
-    gathered = lax.all_gather(joined, axes, axis=0, tiled=False)
+    if lax.axis_size(("dp", "sub")) <= 4 and lax.axis_size("ctx") <= 4:
+        gathered = exchange_gather(exchange_gather(joined, ("dp", "sub")), "ctx")
+        gathered = gathered.reshape((-1,) + joined.shape)
+    else:
+        gathered = lax.all_gather(joined, ("ctx", "dp", "sub"), axis=0, tiled=False)
     shards = gathered.shape[0]
 
     def unshard(piece):

time: 157 us -> 159 us (1.013)
  blocking collectives: 44.4 us -> 0 us
  waiting for transfers between devices: 39.2 us -> 71.4 us
  starting transfers between devices: 10.5 us -> 20 us
  local copies, waits for them, and re-layouts: 15.3 us -> 18 us
  other arithmetic: 5.35 us -> 7.4 us
    all_gather x1 -> x0, blocking collectives: 44.4 us -> none  [gather_adapters(): gathered = lax.all_gather(joined, axes, axis=0, tiled=False)]
    ppermute x0 -> x6, waiting for transfers between devices: none -> 26.8 us  [exchange_gather(): lax.ppermute(block, axis, [(i, (i + shift) % size) for i in range(size)])]
    ppermute x0 -> x6, starting transfers between devices: none -> 9.87 us  [exchange_gather(): lax.ppermute(block, axis, [(i, (i + shift) % size) for i in range(size)])]
    all_gather x1, waiting for transfers between devices: 27.4 us -> 37.2 us  [project_rows(): lax.all_gather(kv_weight, ('ctx', 'dp', 'sub'), axis=0, tiled=False)]
    ppermute x6, waiting for transfers between devices: 11.1 us -> 6.69 us  [exchange_scatter(): lax.ppermute(send, axis, [(i, (i + shift) % size) for i in range(size)])]
  transfers between devices with their start and end apart: 8 -> 14, of which waited for: 6 -> 9; matrix products, arithmetic and copies ran while one was open for 12% -> 15% of each run, Pallas kernels for 0% -> 0%
where the time goes in v12:
time: 159 us; the launch traced here: 158 us
  waiting for transfers between devices  71.4 us (45%)
  Pallas kernels  24.5 us (15%)
  starting transfers between devices  20 us (13%)
  local copies, waits for them, and re-layouts  18 us (11%)
  between operations  14.3 us (9%)
  other arithmetic  7.4 us (5%)
  matrix products  2.57 us (2%)
    all_gather x1, waiting for transfers between devices, project_rows(): lax.all_gather(kv_weight, ('ctx', 'dp', 'sub'), axis=0, tiled=False)  37.2 us
    ppermute x6, waiting for transfers between devices, exchange_gather(): lax.ppermute(block, axis, [(i, (i + shift) % size) for i in range(size)])  26.8 us
    pallas_call x1, Pallas kernels, attention_heads(): pl.pallas_call(attention_kernel, grid=(heads,), in_specs=[whole(mask.shap...  13.4 us
    pallas_call x1, Pallas kernels, project_pair(): pl.pallas_call(projection_kernel, grid=(members, col_shards), in_specs=[p...  11.1 us
    concatenate x4, local copies, waits for them, and re-layouts, project_rows(): rows_both = jnp.concatenate([rows_previous, rows_own], axis=0)  10.1 us
    ppermute x6, starting transfers between devices, exchange_gather(): lax.ppermute(block, axis, [(i, (i + shift) % size) for i in range(size)])  9.87 us
    ppermute x6, waiting for transfers between devices, exchange_scatter(): lax.ppermute(send, axis, [(i, (i + shift) % size) for i in range(size)])  6.69 us
    ppermute x6, starting transfers between devices, exchange_scatter(): lax.ppermute(send, axis, [(i, (i + shift) % size) for i in range(size)])  6.54 us
  transfers between devices with their start and end apart: 14, of which 9 were waited for; matrix products, arithmetic and copies ran while one was open for 15% of the time, Pallas kernels for 0%

profile of v12, /device:TPU:0, one launch (start us, length us, event | category | flops | bytes accessed | tf_op | source)
XLA Modules:
  0.0 158.1 jit_solution(4161357820951811410)
XLA Ops:
  7.2 0.0 copy-start
  7.2 0.0 all-gather.3.cloned.1.call-start
  7.2 0.7 all-gather.3.cloned.1.call-update
  7.9 0.8 pad_maximum_fusion.3
  8.7 0.5 collective-permute-start.1
  9.2 2.6 %collective-permute-start.2 = (bf16[2,16,208]{2,1,0:T(8,128)(2,1)S(1)}, bf16[2,16,208]{2,1,0:T(8,128)(2,1)S(1)}, u32[]{:S(2)}, u32[]{:S(2)}) collective-permute-start(bf16[2,16,208]{2,1,0:T(8,128)(2,1)S(1)} %pad_maximum_fusion.3), channel_id=1, source_target_pairs={{0,2},{1,3},{2,0},{3,1},{4,6},{5,7},{6,4},{7,5},{8,10},{9,11},{10,... | collective-permute-start | bytes 39944 | tf_op jit(solution)/shard_map/ppermute | solution.py:174
  11.7 1.4 collective-permute-start.3
  13.1 3.5 %collective-permute-start = (bf16[192,2304]{1,0:T(8,128)(2,1)}, bf16[192,2304]{1,0:T(8,128)(2,1)S(1)}, u32[]{:S(2)}, u32[]{:S(2)}) collective-permute-start(bf16[192,2304]{1,0:T(8,128)(2,1)} %bitcast.95), channel_id=1, source_target_pairs={{0,4},{4,8},{8,12},{1,5},{5,9},{9,13},{2,6},{6,10},{10,14},{3,7},{... | collective-permute-start | bytes 2654216 | tf_op jit(solution)/shard_map/ppermute | solution.py:21
  16.8 0.8 fusion.39
  17.6 1.1 fusion.10.mask_ref
  18.7 3.4 %concatenate.25 = bf16[192,4,576]{2,1,0:T(4,128)(2,1)} reshape(bf16[1,192,2304]{2,1,0:T(8,128)(2,1)} %param.6) | data formatting | bytes 1769472 | tf_op jit(solution)/shard_map/concatenate | solution.py:161
  22.1 0.6 copy.32
  22.7 0.1 broadcast_in_dim.34
  22.8 0.1 broadcast_in_dim.35
  22.9 2.3 %copy.27 = bf16[192,4,576]{2,0,1:T(8,128)(2,1)} copy(bf16[192,4,576]{2,1,0:T(4,128)(2,1)} %concatenate.25) | data formatting | bytes 1769472 | tf_op jit(solution)/shard_map/concatenate | solution.py:161
  25.2 0.0 collective-permute-done.1
  25.2 0.0 collective-permute-done.2
  25.2 0.0 collective-permute-done.3
  25.2 0.6 gather_fusion
  25.8 0.1 broadcast_select_fusion
  25.8 1.5 collective-permute-start.4
  27.4 1.1 collective-permute-start.5
  28.5 2.9 %collective-permute-start.6 = (bf16[4,2,16,208]{3,2,1,0:T(8,128)(2,1)S(1)}, bf16[4,2,16,208]{3,2,1,0:T(8,128)(2,1)S(1)}, u32[]{:S(2)}, u32[]{:S(2)}) collective-permute-start(bf16[4,2,16,208]{3,2,1,0:T(8,128)(2,1)S(1)} %broadcast_select_fusion), channel_id=1, source_target_pairs={{0,12},{4,0},{8,4},{12,8},{1,13},{5,1},{9,5},{13,9},{2,14},{6,2},{... | collective-permute-start | bytes 159752 | tf_op jit(solution)/shard_map/ppermute | solution.py:174
  31.3 0.1 bitcast_select_fusion
  31.4 22.6 %collective-permute-done.4 = bf16[4,2,16,208]{3,2,1,0:T(8,128)(2,1)S(1)} collective-permute-done((bf16[4,2,16,208]{3,2,1,0:T(8,128)(2,1)S(1)}, bf16[4,2,16,208]{3,2,1,0:T(8,128)(2,1)S(1)}, u32[]{:S(2)}, u32[]{:S(2)}) %collective-permute-start.4) | collective-permute-done | bytes 53280 | tf_op jit(solution)/shard_map/ppermute | solution.py:174
  54.0 2.1 %collective-permute-done.5 = bf16[4,2,16,208]{3,2,1,0:T(8,128)(2,1)S(1)} collective-permute-done((bf16[4,2,16,208]{3,2,1,0:T(8,128)(2,1)S(1)}, bf16[4,2,16,208]{3,2,1,0:T(8,128)(2,1)S(1)}, u32[]{:S(2)}, u32[]{:S(2)}) %collective-permute-start.5) | collective-permute-done | bytes 53280 | tf_op jit(solution)/shard_map/ppermute | solution.py:174
  56.1 2.1 %collective-permute-done.6 = bf16[4,2,16,208]{3,2,1,0:T(8,128)(2,1)S(1)} collective-permute-done((bf16[4,2,16,208]{3,2,1,0:T(8,128)(2,1)S(1)}, bf16[4,2,16,208]{3,2,1,0:T(8,128)(2,1)S(1)}, u32[]{:S(2)}, u32[]{:S(2)}) %collective-permute-start.6) | collective-permute-done | bytes 53280 | tf_op jit(solution)/shard_map/ppermute | solution.py:174
  58.2 0.1 pad_maximum_fusion
  58.2 0.6 gather_fusion.1
  58.8 0.2 copy_select_fusion
  59.0 0.7 slice_bitcast_fusion
  59.7 1.3 reshape.159
  61.0 0.1 slice_bitcast_fusion.1
  61.1 0.8 reshape.160.up_ref
  61.9 0.3 fusion.5
  62.3 0.4 fusion.4
  62.7 0.1 pad_maximum_fusion.2
  62.8 0.8 copy.29.low_ref
  63.6 2.1 %concatenate.24 = bf16[192,4,576]{2,1,0:T(4,128)(2,1)} reshape(bf16[192,2304]{1,0:T(8,128)(2,1)S(1)} %collective-permute-done) | data formatting | bytes 1769472 | tf_op jit(solution)/shard_map/concatenate | solution.py:161
  65.7 2.3 %copy.26 = bf16[192,4,576]{2,0,1:T(8,128)(2,1)} copy(bf16[192,4,576]{2,1,0:T(4,128)(2,1)} %concatenate.24) | data formatting | bytes 1769472 | tf_op jit(solution)/shard_map/concatenate | solution.py:161
  68.0 1.4 copy.31
  69.4 3.0 %maximum_bitcast_fusion.rows_ref = bf16[4,384,576]{2,1,0:T(8,128)(2,1)} fusion(bf16[192,4,576]{2,0,1:T(8,128)(2,1)} %copy.27, bf16[192,4,576]{2,0,1:T(8,128)(2,1)} %copy.26), kind=kLoop, calls=%fused_computation.2 | loop fusion | flops 3538944 | bytes 3538944 | tf_op jit(solution)/shard_map/transpose | solution.py:162
  72.4 37.2 %all-gather.3.cloned.1.call-done = bf16[32,576,256]{2,1,0:T(8,128)(2,1)} async-done(((bf16[2,576,256]{2,1,0:T(8,128)(2,1)}), bf16[32,576,256]{2,1,0:T(8,128)(2,1)}) %all-gather.3.cloned.1.call-update) | async-done | bytes 9437200 | tf_op jit(solution)/shard_map/all_gather | solution.py:163
  109.6 11.1 %shard_map.93.kv_ref = bf16[2,384,1024]{2,1,0:T(8,128)(2,1)} custom-call(bf16[4,384,576]{2,1,0:T(8,128)(2,1)} %maximum_bitcast_fusion.rows_ref, bf16[4,4,2,576,256]{4,3,2,1,0:T(8,128)(2,1)} %bitcast.94, bf16[2,384,16]{2,1,0:T(8,128)(2,1)} %copy.29.low_ref, bf16[2,16,1024]{2,1,0:T(8,128)(2,1)} %reshape.160.up_ref), custom_call_target="tpu_custom_call" | custom-call | tf_op jit(solution)/shard_map/pallas_call | solution.py:139
  120.7 13.4 %shard_map.94 = (bf16[192,2048]{1,0:T(8,128)(2,1)}, bf16[192,2048]{1,0:T(8,128)(2,1)}, bf16[2,384,16]{2,1,0:T(8,128)(2,1)}, f32[2,16,1024]{2,1,0:T(8,128)}) custom-call(s32[384,384]{1,0:T(8,128)} %fusion.10.mask_ref, bf16[192,2048]{1,0:T(8,128)(2,1)} %bitcast.102, bf16[192,2048]{1,0:T(8,128)(2,1)} %bitcast.103, bf16[2,384,1024]{2,1,0:T(8,128)(2,1)} %shard_map.93.kv_ref, ...), custom_call_target="tpu_custom_call" | custom-call | tf_op jit(solution)/shard_map/pallas_call | solution.py:87
  134.1 0.9 broadcast_multiply_fusion
  135.0 0.2 mul.31
  135.2 0.1 copy.34
  135.3 1.8 %fusion.3 = f32[4,4,144,2,16]{2,4,3,1,0:T(8,128)S(1)} fusion(bf16[192,4,4,144]{0,3,2,1:T(8,128)(2,1)S(1)} %bitcast.96, bf16[192,4,4,144]{0,3,2,1:T(8,128)(2,1)S(1)} %bitcast.97, bf16[2,384,16]{2,1,0:T(8,128)(2,1)} %get-tuple-element.10), kind=kOutput, calls=%fused_computation.7 | convolution fusion | flops 60235776 | bytes 2088960 | tf_op jit(solution)/shard_map/mrk,rcij->icjmk/dot_general | solution.py:255
  137.1 0.1 fusion.20
  137.2 0.3 collective-permute-start.7
  137.5 0.6 collective-permute-start.8
  138.1 1.2 collective-permute-start.9
  139.3 3.0 %collective-permute-done.7 = f32[4,208,32]{1,2,0:T(8,128)S(1)} collective-permute-done((f32[4,208,32]{1,2,0:T(8,128)S(1)}, f32[4,208,32]{1,2,0:T(8,128)S(1)}, u32[]{:S(2)}, u32[]{:S(2)}) %collective-permute-start.7) | collective-permute-done | bytes 106528 | tf_op jit(solution)/shard_map/ppermute | solution.py:203
  142.3 1.6 %collective-permute-done.8 = f32[4,208,32]{1,2,0:T(8,128)S(1)} collective-permute-done((f32[4,208,32]{1,2,0:T(8,128)S(1)}, f32[4,208,32]{1,2,0:T(8,128)S(1)}, u32[]{:S(2)}, u32[]{:S(2)}) %collective-permute-start.8) | collective-permute-done | bytes 106528 | tf_op jit(solution)/shard_map/ppermute | solution.py:203
  143.9 0.1 collective-permute-done.9
  144.0 0.1 fusion.18
  144.1 0.7 collective-permute-start.10
  144.7 1.5 collective-permute-start.11
  146.3 2.3 %collective-permute-start.12 = (f32[208,32]{0,1:T(8,128)S(1)}, f32[208,32]{0,1:T(8,128)S(1)}, u32[]{:S(2)}, u32[]{:S(2)}) collective-permute-start(f32[208,32]{0,1:T(8,128)S(1)} %get-tuple-element.16), channel_id=1, source_target_pairs={{0,12},{4,0},{8,4},{12,8},{1,13},{5,1},{9,5},{13,9},{2,14},{6,2},{... | collective-permute-start | bytes 79880 | tf_op jit(solution)/shard_map/ppermute | solution.py:203
  148.5 1.4 collective-permute-done.10
  149.9 0.7 collective-permute-done.12
  150.6 0.0 copy-start.2
  150.6 0.7 slice.23
  (16 shorter events, 0.1 us)
Async XLA Ops:
  7.2 14.9 %copy-start = (bf16[1,192,2304]{2,1,0:T(8,128)(2,1)S(1)}, bf16[1,192,2304]{2,1,0:T(8,128)(2,1)}, u32[]{:S(2)}) copy-start(bf16[1,192,2304]{2,1,0:T(8,128)(2,1)} %param.6) | copy-start | bytes 2654212
  7.2 102.4 %all-gather.3.cloned.1.call-start = ((), (), s32[]{:S(2)}) async-start(), calls=%async_computation | async-start | bytes 10027008 | tf_op jit(solution)/shard_map/all_gather | solution.py:163
  8.7 16.4 %collective-permute-start.1 = (bf16[2,16,208]{2,1,0:T(8,128)(2,1)S(1)}, bf16[2,16,208]{2,1,0:T(8,128)(2,1)S(1)}, u32[]{:S(2)}, u32[]{:S(2)}) collective-permute-start(bf16[2,16,208]{2,1,0:T(8,128)(2,1)S(1)} %pad_maximum_fusion.3), channel_id=1, source_target_pairs={{0,1},{1,2},{2,3},{3,0},{4,5},{5,6},{6,7},{7,4},{8,9},{9,10},{10,1... | collective-permute-start | bytes 39944 | tf_op jit(solution)/shard_map/ppermute | solution.py:174
  9.2 16.0 %collective-permute-start.2 = (bf16[2,16,208]{2,1,0:T(8,128)(2,1)S(1)}, bf16[2,16,208]{2,1,0:T(8,128)(2,1)S(1)}, u32[]{:S(2)}, u32[]{:S(2)}) collective-permute-start(bf16[2,16,208]{2,1,0:T(8,128)(2,1)S(1)} %pad_maximum_fusion.3), channel_id=1, source_target_pairs={{0,2},{1,3},{2,0},{3,1},{4,6},{5,7},{6,4},{7,5},{8,10},{9,11},{10,... | collective-permute-start | bytes 39944 | tf_op jit(solution)/shard_map/ppermute | solution.py:174
  11.7 13.4 %collective-permute-start.3 = (bf16[2,16,208]{2,1,0:T(8,128)(2,1)S(1)}, bf16[2,16,208]{2,1,0:T(8,128)(2,1)S(1)}, u32[]{:S(2)}, u32[]{:S(2)}) collective-permute-start(bf16[2,16,208]{2,1,0:T(8,128)(2,1)S(1)} %pad_maximum_fusion.3), channel_id=1, source_target_pairs={{0,3},{1,0},{2,1},{3,2},{4,7},{5,4},{6,5},{7,6},{8,11},{9,8},{10,9... | collective-permute-start | bytes 39944 | tf_op jit(solution)/shard_map/ppermute | solution.py:174
  13.1 49.1 %collective-permute-start = (bf16[192,2304]{1,0:T(8,128)(2,1)}, bf16[192,2304]{1,0:T(8,128)(2,1)S(1)}, u32[]{:S(2)}, u32[]{:S(2)}) collective-permute-start(bf16[192,2304]{1,0:T(8,128)(2,1)} %bitcast.95), channel_id=1, source_target_pairs={{0,4},{4,8},{8,12},{1,5},{5,9},{9,13},{2,6},{6,10},{10,14},{3,7},{... | collective-permute-start | bytes 2654216 | tf_op jit(solution)/shard_map/ppermute | solution.py:21
  25.8 28.1 %collective-permute-start.4 = (bf16[4,2,16,208]{3,2,1,0:T(8,128)(2,1)S(1)}, bf16[4,2,16,208]{3,2,1,0:T(8,128)(2,1)S(1)}, u32[]{:S(2)}, u32[]{:S(2)}) collective-permute-start(bf16[4,2,16,208]{3,2,1,0:T(8,128)(2,1)S(1)} %broadcast_select_fusion), channel_id=1, source_target_pairs={{0,4},{4,8},{8,12},{12,0},{1,5},{5,9},{9,13},{13,1},{2,6},{6,10},{... | collective-permute-start | bytes 159752 | tf_op jit(solution)/shard_map/ppermute | solution.py:174
  27.4 28.7 %collective-permute-start.5 = (bf16[4,2,16,208]{3,2,1,0:T(8,128)(2,1)S(1)}, bf16[4,2,16,208]{3,2,1,0:T(8,128)(2,1)S(1)}, u32[]{:S(2)}, u32[]{:S(2)}) collective-permute-start(bf16[4,2,16,208]{3,2,1,0:T(8,128)(2,1)S(1)} %broadcast_select_fusion), channel_id=1, source_target_pairs={{0,8},{4,12},{8,0},{12,4},{1,9},{5,13},{9,1},{13,5},{2,10},{6,14},... | collective-permute-start | bytes 159752 | tf_op jit(solution)/shard_map/ppermute | solution.py:174
  28.5 29.7 %collective-permute-start.6 = (bf16[4,2,16,208]{3,2,1,0:T(8,128)(2,1)S(1)}, bf16[4,2,16,208]{3,2,1,0:T(8,128)(2,1)S(1)}, u32[]{:S(2)}, u32[]{:S(2)}) collective-permute-start(bf16[4,2,16,208]{3,2,1,0:T(8,128)(2,1)S(1)} %broadcast_select_fusion), channel_id=1, source_target_pairs={{0,12},{4,0},{8,4},{12,8},{1,13},{5,1},{9,5},{13,9},{2,14},{6,2},{... | collective-permute-start | bytes 159752 | tf_op jit(solution)/shard_map/ppermute | solution.py:174
  120.7 14.6 %copy-start.1 = (bf16[192,2304]{0,1:T(8,128)(2,1)S(1)}, bf16[192,2304]{0,1:T(8,128)(2,1)}, u32[]{:S(2)}) copy-start(bf16[192,2304]{0,1:T(8,128)(2,1)} %copy.31) | copy-start | bytes 2654212
  137.2 5.0 %collective-permute-start.7 = (f32[4,208,32]{1,2,0:T(8,128)S(1)}, f32[4,208,32]{1,2,0:T(8,128)S(1)}, u32[]{:S(2)}, u32[]{:S(2)}) collective-permute-start(f32[4,208,32]{1,2,0:T(8,128)S(1)} %get-tuple-element.12), channel_id=1, source_target_pairs={{0,1},{1,2},{2,3},{3,0},{4,5},{5,6},{6,7},{7,4},{8,9},{9,10},{10,1... | collective-permute-start | bytes 319496 | tf_op jit(solution)/shard_map/ppermute | solution.py:203
  137.5 6.3 %collective-permute-start.8 = (f32[4,208,32]{1,2,0:T(8,128)S(1)}, f32[4,208,32]{1,2,0:T(8,128)S(1)}, u32[]{:S(2)}, u32[]{:S(2)}) collective-permute-start(f32[4,208,32]{1,2,0:T(8,128)S(1)} %get-tuple-element.13), channel_id=1, source_target_pairs={{0,2},{1,3},{2,0},{3,1},{4,6},{5,7},{6,4},{7,5},{8,10},{9,11},{10,... | collective-permute-start | bytes 319496 | tf_op jit(solution)/shard_map/ppermute | solution.py:203
  138.1 5.9 %collective-permute-start.9 = (f32[4,208,32]{1,2,0:T(8,128)S(1)}, f32[4,208,32]{1,2,0:T(8,128)S(1)}, u32[]{:S(2)}, u32[]{:S(2)}) collective-permute-start(f32[4,208,32]{1,2,0:T(8,128)S(1)} %get-tuple-element.14), channel_id=1, source_target_pairs={{0,3},{1,0},{2,1},{3,2},{4,7},{5,4},{6,5},{7,6},{8,11},{9,8},{10,9... | collective-permute-start | bytes 319496 | tf_op jit(solution)/shard_map/ppermute | solution.py:203
  144.1 5.8 %collective-permute-start.10 = (f32[208,32]{0,1:T(8,128)S(1)}, f32[208,32]{0,1:T(8,128)S(1)}, u32[]{:S(2)}, u32[]{:S(2)}) collective-permute-start(f32[208,32]{0,1:T(8,128)S(1)} %get-tuple-element.15), channel_id=1, source_target_pairs={{0,4},{4,8},{8,12},{12,0},{1,5},{5,9},{9,13},{13,1},{2,6},{6,10},{... | collective-permute-start | bytes 79880 | tf_op jit(solution)/shard_map/ppermute | solution.py:203
  144.7 5.2 %collective-permute-start.11 = (f32[208,32]{0,1:T(8,128)S(1)}, f32[208,32]{0,1:T(8,128)S(1)}, u32[]{:S(2)}, u32[]{:S(2)}) collective-permute-start(f32[208,32]{0,1:T(8,128)S(1)} %get-tuple-element.17), channel_id=1, source_target_pairs={{0,8},{4,12},{8,0},{12,4},{1,9},{5,13},{9,1},{13,5},{2,10},{6,14},... | collective-permute-start | bytes 79880 | tf_op jit(solution)/shard_map/ppermute | solution.py:203
  146.3 4.3 %collective-permute-start.12 = (f32[208,32]{0,1:T(8,128)S(1)}, f32[208,32]{0,1:T(8,128)S(1)}, u32[]{:S(2)}, u32[]{:S(2)}) collective-permute-start(f32[208,32]{0,1:T(8,128)S(1)} %get-tuple-element.16), channel_id=1, source_target_pairs={{0,12},{4,0},{8,4},{12,8},{1,13},{5,1},{9,5},{13,9},{2,14},{6,2},{... | collective-permute-start | bytes 79880 | tf_op jit(solution)/shard_map/ppermute | solution.py:203
  150.6 0.7 copy-start.2
Sparse Core Ops, SparseCore 0:
  10.3 99.2 all-gather.2

commit v13 on v11

--- a/solution.py
+++ b/solution.py
@@ -22,15 +22,26 @@
 
 
 def attention_kernel(
-    mask_ref, q_ref, do_ref, kv_ref, low_ref, up_ref,
+    mask_ref, q_ref, do_ref, rows_ref, weight_ref, low_ref, up_ref,
     out_ref, dq_ref, projected_ref, up_terms_ref, projected_acc,
 ):
     head = pl.program_id(0)
     half = HEAD_DIM
     q = jnp.concatenate([q_ref[:, :half], q_ref[:, half:]], axis=0)
     do = jnp.concatenate([do_ref[:, :half], do_ref[:, half:]], axis=0)
-    k = kv_ref[0]
-    v = kv_ref[1]
+    row_shards = weight_ref.shape[0]
+
+    def project(member):
+        base = jnp.dot(low_ref[member], up_ref[member], preferred_element_type=jnp.float32)
+        base = base * adapter_scale
+        for c in range(row_shards):
+            base = base + jnp.dot(
+                rows_ref[c], weight_ref[c, 0, member], preferred_element_type=jnp.float32
+            )
+        return base.astype(jnp.bfloat16)
+
+    k = project(0)
+    v = project(1)
     rows = q_ref.shape[0]
     visible = mask_ref[...] != 0
     contract_last = (((1,), (1,)), ((), ()))
@@ -75,14 +86,16 @@
         projected_ref[...] = projected_acc[...].astype(projected_ref.dtype)
 
 
-def attention_heads(mask, queries, grads, key_value, low_rows, up_full):
+def attention_heads(mask, queries, grads, rows_split, gathered, low_rows, up_full):
     rows, width = queries.shape
-    members, keys, kv_width = key_value.shape
+    row_shards, col_shards, members, depth, cols = gathered.shape
+    keys = rows_split.shape[1]
     rank = up_full.shape[1]
+    kv_width = col_shards * cols
     heads = kv_width // HEAD_DIM
+    per_shard = cols // HEAD_DIM
     group_cols = width // heads
     row_block = pl.BlockSpec((rows, group_cols), lambda g: (0, g))
-    kv_block = pl.BlockSpec((members, keys, HEAD_DIM), lambda g: (0, 0, g))
     whole = lambda shape: pl.BlockSpec(shape, lambda g: (0,) * len(shape))
     return pl.pallas_call(
         attention_kernel,
@@ -91,7 +104,11 @@
             whole(mask.shape),
             row_block,
             row_block,
-            kv_block,
+            whole(rows_split.shape),
+            pl.BlockSpec(
+                (row_shards, 1, members, depth, HEAD_DIM),
+                lambda g: (0, g // per_shard, 0, 0, g % per_shard),
+            ),
             whole(low_rows.shape),
             pl.BlockSpec((members, rank, HEAD_DIM), lambda g: (0, 0, g)),
         ],
@@ -108,10 +125,10 @@
             jax.ShapeDtypeStruct((members, rank, kv_width), jnp.float32),
         ],
         scratch_shapes=[pltpu.VMEM((members, keys, rank), jnp.float32)],
-    )(mask, queries, grads, key_value, low_rows, up_full)
-
-
-def attend(query_rows, key_value, grad_rows, is_first, low_rows, up_full):
+    )(mask, queries, grads, rows_split, gathered, low_rows, up_full)
+
+
+def attend(query_rows, rows_split, gathered, grad_rows, is_first, low_rows, up_full):
     length = query_rows.shape[0]
     group_size = HEADS // KV_HEADS
     query_pos = lax.broadcasted_iota(jnp.int32, (group_size * length, 2 * length), 0) % length
@@ -121,33 +138,9 @@
         & (key_pos <= query_pos + length)
         & (jnp.logical_not(is_first) | (key_pos >= length))
     )
-    return attention_heads(visible.astype(jnp.int32), query_rows, grad_rows, key_value, low_rows, up_full)
-
-
-def projection_kernel(rows_ref, weight_ref, low_ref, up_ref, out_ref):
-    row_shards = weight_ref.shape[0]
-    base = jnp.dot(low_ref[0], up_ref[0], preferred_element_type=jnp.float32) * adapter_scale
-    for c in range(row_shards):
-        base = base + jnp.dot(rows_ref[c], weight_ref[c, 0, 0], preferred_element_type=jnp.float32)
-    out_ref[0] = base.astype(out_ref.dtype)
-
-
-def project_pair(rows_split, gathered, low_rows, up_full):
-    row_shards, col_shards, members, depth, cols = gathered.shape
-    rows = rows_split.shape[1]
-    rank = up_full.shape[1]
-    return pl.pallas_call(
-        projection_kernel,
-        grid=(members, col_shards),
-        in_specs=[
-            pl.BlockSpec((row_shards, rows, depth), lambda m, i: (0, 0, 0)),
-            pl.BlockSpec((row_shards, 1, 1, depth, cols), lambda m, i: (0, i, m, 0, 0)),
-            pl.BlockSpec((1, rows, rank), lambda m, i: (m, 0, 0)),
-            pl.BlockSpec((1, rank, cols), lambda m, i: (m, 0, i)),
-        ],
-        out_specs=pl.BlockSpec((1, rows, cols), lambda m, i: (m, 0, i)),
-        out_shape=jax.ShapeDtypeStruct((members, rows, col_shards * cols), jnp.bfloat16),
-    )(rows_split, gathered, low_rows, up_full)
+    return attention_heads(
+        visible.astype(jnp.int32), query_rows, grad_rows, rows_split, gathered, low_rows, up_full
+    )
 
 
 def project_rows(rows_previous, rows_own, kv_weight, down_full, up_full):
@@ -163,8 +156,7 @@
     gathered = lax.all_gather(kv_weight, ("ctx", "dp", "sub"), axis=0, tiled=False)
     gathered = gathered.reshape((row_shards, col_shards) + kv_weight.shape)
     low_rows = jnp.concatenate([low_previous, low_rank], axis=1)
-    key_value = project_pair(rows_split, gathered, low_rows, up_full)
-    return rows_both, low_rows, key_value
+    return rows_both, rows_split, gathered, low_rows
 
 
 def gather_adapters(adapter_down, adapter_up):
@@ -231,11 +223,11 @@
     rows_previous = shifted(rows_own, "ctx", 1)
     down_full, up_full = gather_adapters(adapter_down, adapter_up)
     is_first = lax.axis_index("ctx") == 0
-    rows_both, low_rows, kv_both = project_rows(
+    rows_both, rows_split, gathered, low_rows = project_rows(
         rows_previous, rows_own, kv_weight, down_full, up_full
     )
     attended, query_grad, projected, up_terms = attend(
-        query_rows, kv_both, grad_rows, is_first, low_rows, up_full
+        query_rows, rows_split, gathered, grad_rows, is_first, low_rows, up_full
     )
     up_terms = up_terms.reshape(up_terms.shape[:2] + (row_shards, col_shards, -1)).transpose(3, 2, 4, 0, 1)
     down_terms = jnp.einsum(

time: 157 us -> 155 us (0.987)
  Pallas kernels: 24.5 us -> 22.8 us
    pallas_call x1 -> x0, Pallas kernels: 11.1 us -> none  [project_pair(): pl.pallas_call(projection_kernel, grid=(members, col_shards), in_specs=[p...]
    pallas_call x1, Pallas kernels: 13.4 us -> 22.8 us  [attention_heads(): pl.pallas_call(attention_kernel, grid=(heads,), in_specs=[whole(mask.shap...]
where the time goes in v13:
time: 155 us; the launch traced here: 154 us
  blocking collectives  44.4 us (29%)
  waiting for transfers between devices  39.2 us (25%)
  Pallas kernels  22.8 us (15%)
  local copies, waits for them, and re-layouts  15.3 us (10%)
  between operations  14.2 us (9%)
  starting transfers between devices  10.5 us (7%)
  other arithmetic  5.35 us (3%)
  matrix products  2.5 us (2%)
    all_gather x1, blocking collectives, gather_adapters(): gathered = lax.all_gather(joined, axes, axis=0, tiled=False)  44.4 us
    all_gather x1, waiting for transfers between devices, project_rows(): lax.all_gather(kv_weight, ('ctx', 'dp', 'sub'), axis=0, tiled=False)  27.4 us
    pallas_call x1, Pallas kernels, attention_heads(): pl.pallas_call(attention_kernel, grid=(heads,), in_specs=[whole(mask.shap...  22.8 us
    ppermute x6, waiting for transfers between devices, exchange_scatter(): lax.ppermute(send, axis, [(i, (i + shift) % size) for i in range(size)])  11.1 us
    concatenate x4, local copies, waits for them, and re-layouts, project_rows(): rows_both = jnp.concatenate([rows_previous, rows_own], axis=0)  10.2 us
    ppermute x6, starting transfers between devices, exchange_scatter(): lax.ppermute(send, axis, [(i, (i + shift) % size) for i in range(size)])  5.47 us
    ppermute x1, starting transfers between devices, shifted(): return lax.ppermute(value, axis, pairs)  4.98 us
  transfers between devices with their start and end apart: 8, of which 6 were waited for; matrix products, arithmetic and copies ran while one was open for 12% of the time, Pallas kernels for 0%

profile of v13, /device:TPU:0, one launch (start us, length us, event | category | flops | bytes accessed | tf_op | source)
XLA Modules:
  0.0 154.3 jit_solution(2706885050665482199)
XLA Ops:
  7.2 0.0 copy-start
  7.2 0.0 all-gather.4.cloned.1.call-start
  7.2 0.7 all-gather.4.cloned.1.call-update
  7.9 5.0 %collective-permute-start = (bf16[192,2304]{1,0:T(8,128)(2,1)}, bf16[192,2304]{1,0:T(8,128)(2,1)S(1)}, u32[]{:S(2)}, u32[]{:S(2)}) collective-permute-start(bf16[192,2304]{1,0:T(8,128)(2,1)} %bitcast.84), channel_id=1, source_target_pairs={{0,4},{4,8},{8,12},{1,5},{5,9},{9,13},{2,6},{6,10},{10,14},{3,7},{... | collective-permute-start | bytes 2654216 | tf_op jit(solution)/shard_map/ppermute | solution.py:21
  12.9 3.4 %concatenate.25 = bf16[192,4,576]{2,1,0:T(4,128)(2,1)} reshape(bf16[1,192,2304]{2,1,0:T(8,128)(2,1)} %param.6) | data formatting | bytes 1769472 | tf_op jit(solution)/shard_map/concatenate | solution.py:154
  16.3 0.0 copy-done
  16.3 0.0 copy-start.3
  16.3 0.0 copy-start.4
  16.3 0.6 copy.34
  17.0 2.3 %copy.29 = bf16[192,4,576]{2,0,1:T(8,128)(2,1)} copy(bf16[192,4,576]{2,1,0:T(4,128)(2,1)} %concatenate.25) | data formatting | bytes 1769472 | tf_op jit(solution)/shard_map/concatenate | solution.py:154
  19.3 0.0 copy-done.3
  19.3 0.0 copy-done.4
  19.3 0.1 pad_maximum_fusion.1
  19.4 44.4 %all-gather.1 = bf16[32,16,208]{2,1,0:T(8,128)(2,1)S(1)} all-gather(bf16[2,16,208]{2,1,0:T(8,128)(2,1)S(1)} %pad_maximum_fusion.1), channel_id=3, replica_groups=mesh['groups'=2,'ctx'=4,'dp'=2,'sub'=2] {'ctx','dp','sub'}, dimensions={0}, use_global_device_ids=true | all-gather | bytes 226304 | tf_op jit(solution)/shard_map/all_gather | solution.py:166
  63.8 0.1 slice.17
  63.9 0.2 copy.44
  64.0 0.3 reshape.41
  64.4 0.1 copy.45
  64.4 0.8 reshape.42.up_ref
  65.2 1.0 fusion.10.mask_ref
  66.2 0.3 fusion.5
  66.6 0.0 collective-permute-done
  66.6 2.1 %concatenate.24 = bf16[192,4,576]{2,1,0:T(4,128)(2,1)} reshape(bf16[192,2304]{1,0:T(8,128)(2,1)S(1)} %collective-permute-done) | data formatting | bytes 1769472 | tf_op jit(solution)/shard_map/concatenate | solution.py:154
  68.7 2.3 %copy.28 = bf16[192,4,576]{2,0,1:T(8,128)(2,1)} copy(bf16[192,4,576]{2,1,0:T(4,128)(2,1)} %concatenate.24) | data formatting | bytes 1769472 | tf_op jit(solution)/shard_map/concatenate | solution.py:154
  71.0 0.3 fusion.4
  71.4 0.1 pad_maximum_fusion
  71.5 0.8 copy.32.low_ref
  72.3 1.4 copy.33
  73.7 2.9 %maximum_bitcast_fusion.rows_ref = bf16[4,384,576]{2,1,0:T(8,128)(2,1)} fusion(bf16[192,4,576]{2,0,1:T(8,128)(2,1)} %copy.29, bf16[192,4,576]{2,0,1:T(8,128)(2,1)} %copy.28), kind=kLoop, calls=%fused_computation | loop fusion | flops 3538944 | bytes 3538944 | tf_op jit(solution)/shard_map/transpose | solution.py:155
  76.7 27.4 %all-gather.4.cloned.1.call-done = bf16[32,576,256]{2,1,0:T(8,128)(2,1)} async-done(((bf16[2,576,256]{2,1,0:T(8,128)(2,1)}), bf16[32,576,256]{2,1,0:T(8,128)(2,1)}) %all-gather.4.cloned.1.call-update) | async-done | bytes 9437200 | tf_op jit(solution)/shard_map/all_gather | solution.py:156
  104.1 0.0 copy-start.1
  104.1 22.8 %shard_map.93 = (bf16[192,2048]{1,0:T(8,128)(2,1)}, bf16[192,2048]{1,0:T(8,128)(2,1)}, bf16[2,384,16]{2,1,0:T(8,128)(2,1)}, f32[2,16,1024]{2,1,0:T(8,128)}) custom-call(s32[384,384]{1,0:T(8,128)} %fusion.10.mask_ref, bf16[192,2048]{1,0:T(8,128)(2,1)} %bitcast.93, bf16[192,2048]{1,0:T(8,128)(2,1)} %bitcast.94, ...), custom_call_target="tpu_custom_call" | custom-call | tf_op jit(solution)/shard_map/pallas_call | solution.py:100
  126.9 0.9 broadcast_multiply_fusion
  127.8 0.2 mul.29
  127.9 0.1 copy.36
  128.0 0.0 copy-done.1
  128.1 1.8 %fusion.3 = f32[4,4,144,2,16]{2,4,3,1,0:T(8,128)S(1)} fusion(bf16[192,4,4,144]{0,3,2,1:T(8,128)(2,1)S(1)} %bitcast.85, bf16[192,4,4,144]{0,3,2,1:T(8,128)(2,1)S(1)} %bitcast.86, bf16[2,384,16]{2,1,0:T(8,128)(2,1)} %get-tuple-element.10), kind=kOutput, calls=%fused_computation.5 | convolution fusion | flops 60235776 | bytes 2088960 | tf_op jit(solution)/shard_map/mrk,rcij->icjmk/dot_general | solution.py:233
  129.9 0.1 fusion.20
  130.0 0.6 collective-permute-start.3
  130.6 1.3 collective-permute-start.2
  131.9 0.0 collective-permute-start.1
  132.0 2.6 %collective-permute-done.3 = f32[4,208,32]{1,2,0:T(8,128)S(1)} collective-permute-done((f32[4,208,32]{1,2,0:T(8,128)S(1)}, f32[4,208,32]{1,2,0:T(8,128)S(1)}, u32[]{:S(2)}, u32[]{:S(2)}) %collective-permute-start.3) | collective-permute-done | bytes 106528 | tf_op jit(solution)/shard_map/ppermute | solution.py:181
  134.5 4.3 %collective-permute-done.2 = f32[4,208,32]{1,2,0:T(8,128)S(1)} collective-permute-done((f32[4,208,32]{1,2,0:T(8,128)S(1)}, f32[4,208,32]{1,2,0:T(8,128)S(1)}, u32[]{:S(2)}, u32[]{:S(2)}) %collective-permute-start.2) | collective-permute-done | bytes 106528 | tf_op jit(solution)/shard_map/ppermute | solution.py:181
  138.8 0.0 collective-permute-done.1
  138.8 0.1 fusion.18
  138.9 1.5 collective-permute-start.6
  140.4 0.7 collective-permute-start.5
  141.0 1.4 collective-permute-start.4
  142.4 0.4 collective-permute-done.6
  142.9 2.6 %collective-permute-done.5 = f32[208,32]{0,1:T(8,128)S(1)} collective-permute-done((f32[208,32]{0,1:T(8,128)S(1)}, f32[208,32]{0,1:T(8,128)S(1)}, u32[]{:S(2)}, u32[]{:S(2)}) %collective-permute-start.5) | collective-permute-done | bytes 26656 | tf_op jit(solution)/shard_map/ppermute | solution.py:181
  145.5 1.2 collective-permute-done.4
  146.8 0.0 copy-start.2
  146.8 0.7 slice.19
  147.4 0.0 copy-done.2
  (4 shorter events, 0.0 us)
Async XLA Ops:
  7.2 9.1 %copy-start = (bf16[1,192,2304]{2,1,0:T(8,128)(2,1)S(1)}, bf16[1,192,2304]{2,1,0:T(8,128)(2,1)}, u32[]{:S(2)}) copy-start(bf16[1,192,2304]{2,1,0:T(8,128)(2,1)} %param.6) | copy-start | bytes 2654212
  7.2 96.9 %all-gather.4.cloned.1.call-start = ((), (), s32[]{:S(2)}) async-start(), calls=%async_computation | async-start | bytes 10027008 | tf_op jit(solution)/shard_map/all_gather | solution.py:156
  7.9 58.7 %collective-permute-start = (bf16[192,2304]{1,0:T(8,128)(2,1)}, bf16[192,2304]{1,0:T(8,128)(2,1)S(1)}, u32[]{:S(2)}, u32[]{:S(2)}) collective-permute-start(bf16[192,2304]{1,0:T(8,128)(2,1)} %bitcast.84), channel_id=1, source_target_pairs={{0,4},{4,8},{8,12},{1,5},{5,9},{9,13},{2,6},{6,10},{10,14},{3,7},{... | collective-permute-start | bytes 2654216 | tf_op jit(solution)/shard_map/ppermute | solution.py:21
  16.3 3.0 %copy-start.3 = (bf16[2,16,144]{2,1,0:T(8,128)(2,1)S(1)}, bf16[2,16,144]{2,1,0:T(8,128)(2,1)}, u32[]{:S(2)}) copy-start(bf16[2,16,144]{2,1,0:T(8,128)(2,1)} %param.9) | copy-start | bytes 27652
  16.3 3.0 %copy-start.4 = (bf16[2,16,64]{2,1,0:T(8,128)(2,1)S(1)}, bf16[2,16,64]{2,1,0:T(8,128)(2,1)}, u32[]{:S(2)}) copy-start(bf16[2,16,64]{2,1,0:T(8,128)(2,1)} %param.10) | copy-start | bytes 12292
  104.1 24.0 %copy-start.1 = (bf16[192,2304]{0,1:T(8,128)(2,1)S(1)}, bf16[192,2304]{0,1:T(8,128)(2,1)}, u32[]{:S(2)}) copy-start(bf16[192,2304]{0,1:T(8,128)(2,1)} %copy.33) | copy-start | bytes 2654212
  130.0 4.5 %collective-permute-start.3 = (f32[4,208,32]{1,2,0:T(8,128)S(1)}, f32[4,208,32]{1,2,0:T(8,128)S(1)}, u32[]{:S(2)}, u32[]{:S(2)}) collective-permute-start(f32[4,208,32]{1,2,0:T(8,128)S(1)} %get-tuple-element.14), channel_id=1, source_target_pairs={{0,3},{1,0},{2,1},{3,2},{4,7},{5,4},{6,5},{7,6},{8,11},{9,8},{10,9... | collective-permute-start | bytes 319496 | tf_op jit(solution)/shard_map/ppermute | solution.py:181
  130.6 8.2 %collective-permute-start.2 = (f32[4,208,32]{1,2,0:T(8,128)S(1)}, f32[4,208,32]{1,2,0:T(8,128)S(1)}, u32[]{:S(2)}, u32[]{:S(2)}) collective-permute-start(f32[4,208,32]{1,2,0:T(8,128)S(1)} %get-tuple-element.13), channel_id=1, source_target_pairs={{0,2},{1,3},{2,0},{3,1},{4,6},{5,7},{6,4},{7,5},{8,10},{9,11},{10,... | collective-permute-start | bytes 319496 | tf_op jit(solution)/shard_map/ppermute | solution.py:181
  131.9 6.8 %collective-permute-start.1 = (f32[4,208,32]{1,2,0:T(8,128)S(1)}, f32[4,208,32]{1,2,0:T(8,128)S(1)}, u32[]{:S(2)}, u32[]{:S(2)}) collective-permute-start(f32[4,208,32]{1,2,0:T(8,128)S(1)} %get-tuple-element.12), channel_id=1, source_target_pairs={{0,1},{1,2},{2,3},{3,0},{4,5},{5,6},{6,7},{7,4},{8,9},{9,10},{10,1... | collective-permute-start | bytes 319496 | tf_op jit(solution)/shard_map/ppermute | solution.py:181
  138.9 4.0 %collective-permute-start.6 = (f32[208,32]{0,1:T(8,128)S(1)}, f32[208,32]{0,1:T(8,128)S(1)}, u32[]{:S(2)}, u32[]{:S(2)}) collective-permute-start(f32[208,32]{0,1:T(8,128)S(1)} %get-tuple-element.16), channel_id=1, source_target_pairs={{0,12},{4,0},{8,4},{12,8},{1,13},{5,1},{9,5},{13,9},{2,14},{6,2},{... | collective-permute-start | bytes 79880 | tf_op jit(solution)/shard_map/ppermute | solution.py:181
  140.4 5.2 %collective-permute-start.5 = (f32[208,32]{0,1:T(8,128)S(1)}, f32[208,32]{0,1:T(8,128)S(1)}, u32[]{:S(2)}, u32[]{:S(2)}) collective-permute-start(f32[208,32]{0,1:T(8,128)S(1)} %get-tuple-element.17), channel_id=1, source_target_pairs={{0,8},{4,12},{8,0},{12,4},{1,9},{5,13},{9,1},{13,5},{2,10},{6,14},... | collective-permute-start | bytes 79880 | tf_op jit(solution)/shard_map/ppermute | solution.py:181
  141.0 5.7 %collective-permute-start.4 = (f32[208,32]{0,1:T(8,128)S(1)}, f32[208,32]{0,1:T(8,128)S(1)}, u32[]{:S(2)}, u32[]{:S(2)}) collective-permute-start(f32[208,32]{0,1:T(8,128)S(1)} %get-tuple-element.15), channel_id=1, source_target_pairs={{0,4},{4,8},{8,12},{12,0},{1,5},{5,9},{9,13},{13,1},{2,6},{6,10},{... | collective-permute-start | bytes 79880 | tf_op jit(solution)/shard_map/ppermute | solution.py:181
  146.8 0.7 copy-start.2
Sparse Core Ops, SparseCore 0:
  10.3 93.7 all-gather.3

commit v14 on v13

--- a/solution.py
+++ b/solution.py
@@ -25,11 +25,14 @@
     mask_ref, q_ref, do_ref, rows_ref, weight_ref, low_ref, up_ref,
     out_ref, dq_ref, projected_ref, up_terms_ref, projected_acc,
 ):
-    head = pl.program_id(0)
+    step = pl.program_id(0)
     half = HEAD_DIM
-    q = jnp.concatenate([q_ref[:, :half], q_ref[:, half:]], axis=0)
-    do = jnp.concatenate([do_ref[:, :half], do_ref[:, half:]], axis=0)
     row_shards = weight_ref.shape[0]
+    heads_here = weight_ref.shape[4] // HEAD_DIM
+    rows = q_ref.shape[0]
+    visible = mask_ref[...] != 0
+    contract_last = (((1,), (1,)), ((), ()))
+    contract_first = (((0,), (0,)), ((), ()))
 
     def project(member):
         base = jnp.dot(low_ref[member], up_ref[member], preferred_element_type=jnp.float32)
@@ -40,48 +43,52 @@
             )
         return base.astype(jnp.bfloat16)
 
-    k = project(0)
-    v = project(1)
-    rows = q_ref.shape[0]
-    visible = mask_ref[...] != 0
-    contract_last = (((1,), (1,)), ((), ()))
-    contract_first = (((0,), (0,)), ((), ()))
-    raw_score = lax.dot_general(q, k, contract_last, preferred_element_type=jnp.float32) * query_scale
-    bent_score = jnp.tanh(raw_score / logit_cap)
-    expo_terms = jnp.where(visible, jnp.exp(logit_cap * bent_score), 0.0)
-    denominator = jnp.sum(expo_terms, axis=-1, keepdims=True)
-    prob_wide = (expo_terms * (1.0 / denominator)).astype(jnp.bfloat16).astype(jnp.float32)
-    attn_prob = prob_wide.astype(jnp.bfloat16)
-    head_out = jnp.dot(attn_prob, v, preferred_element_type=jnp.float32).astype(out_ref.dtype)
-    out_ref[:, :half] = head_out[:rows]
-    out_ref[:, half:] = head_out[rows:]
-    prob_grad = lax.dot_general(do, v, contract_last, preferred_element_type=jnp.float32)
-    row_delta = jnp.sum(prob_wide * prob_grad, axis=-1, keepdims=True)
-    score_wide = prob_wide * (prob_grad - row_delta) * (1.0 - bent_score * bent_score) * query_scale
-    score_grad = score_wide.astype(jnp.bfloat16)
-    head_qgrad = jnp.dot(score_grad, k, preferred_element_type=jnp.float32).astype(dq_ref.dtype)
-    dq_ref[:, :half] = head_qgrad[:rows]
-    dq_ref[:, half:] = head_qgrad[rows:]
-    key_grad = lax.dot_general(
-        score_grad, q, contract_first, preferred_element_type=jnp.float32
-    ).astype(jnp.bfloat16)
-    value_grad = lax.dot_general(
-        attn_prob, do, contract_first, preferred_element_type=jnp.float32
-    ).astype(jnp.bfloat16)
-
-    @pl.when(head == 0)
+    keys_here = project(0)
+    values_here = project(1)
+
+    @pl.when(step == 0)
     def _():
         projected_acc[...] = jnp.zeros_like(projected_acc)
 
-    for member, grad in enumerate((key_grad, value_grad)):
-        projected_acc[member] += lax.dot_general(
-            grad, up_ref[member], contract_last, preferred_element_type=jnp.float32
-        )
-        up_terms_ref[member] = lax.dot_general(
-            low_ref[member], grad, contract_first, preferred_element_type=jnp.float32
-        )
-
-    @pl.when(head == pl.num_programs(0) - 1)
+    for h in range(heads_here):
+        cols = slice(h * HEAD_DIM, (h + 1) * HEAD_DIM)
+        qa = slice(2 * h * half, (2 * h + 1) * half)
+        qb = slice((2 * h + 1) * half, (2 * h + 2) * half)
+        q = jnp.concatenate([q_ref[:, qa], q_ref[:, qb]], axis=0)
+        do = jnp.concatenate([do_ref[:, qa], do_ref[:, qb]], axis=0)
+        k = keys_here[:, cols]
+        v = values_here[:, cols]
+        raw_score = lax.dot_general(q, k, contract_last, preferred_element_type=jnp.float32) * query_scale
+        bent_score = jnp.tanh(raw_score / logit_cap)
+        expo_terms = jnp.where(visible, jnp.exp(logit_cap * bent_score), 0.0)
+        denominator = jnp.sum(expo_terms, axis=-1, keepdims=True)
+        prob_wide = (expo_terms * (1.0 / denominator)).astype(jnp.bfloat16).astype(jnp.float32)
+        attn_prob = prob_wide.astype(jnp.bfloat16)
+        head_out = jnp.dot(attn_prob, v, preferred_element_type=jnp.float32).astype(out_ref.dtype)
+        out_ref[:, qa] = head_out[:rows]
+        out_ref[:, qb] = head_out[rows:]
+        prob_grad = lax.dot_general(do, v, contract_last, preferred_element_type=jnp.float32)
+        row_delta = jnp.sum(prob_wide * prob_grad, axis=-1, keepdims=True)
+        score_wide = prob_wide * (prob_grad - row_delta) * (1.0 - bent_score * bent_score) * query_scale
+        score_grad = score_wide.astype(jnp.bfloat16)
+        head_qgrad = jnp.dot(score_grad, k, preferred_element_type=jnp.float32).astype(dq_ref.dtype)
+        dq_ref[:, qa] = head_qgrad[:rows]
+        dq_ref[:, qb] = head_qgrad[rows:]
+        key_grad = lax.dot_general(
+            score_grad, q, contract_first, preferred_element_type=jnp.float32
+        ).astype(jnp.bfloat16)
+        value_grad = lax.dot_general(
+            attn_prob, do, contract_first, preferred_element_type=jnp.float32
+        ).astype(jnp.bfloat16)
+        for member, grad in enumerate((key_grad, value_grad)):
+            projected_acc[member] += lax.dot_general(
+                grad, up_ref[member, :, cols], contract_last, preferred_element_type=jnp.float32
+            )
+            up_terms_ref[member, :, cols] = lax.dot_general(
+                low_ref[member], grad, contract_first, preferred_element_type=jnp.float32
+            )
+
+    @pl.when(step == pl.num_programs(0) - 1)
     def _():
         projected_ref[...] = projected_acc[...].astype(projected_ref.dtype)
 
@@ -93,30 +100,26 @@
     rank = up_full.shape[1]
     kv_width = col_shards * cols
     heads = kv_width // HEAD_DIM
-    per_shard = cols // HEAD_DIM
-    group_cols = width // heads
-    row_block = pl.BlockSpec((rows, group_cols), lambda g: (0, g))
-    whole = lambda shape: pl.BlockSpec(shape, lambda g: (0,) * len(shape))
+    step_cols = width // col_shards
+    row_block = pl.BlockSpec((rows, step_cols), lambda i: (0, i))
+    whole = lambda shape: pl.BlockSpec(shape, lambda i: (0,) * len(shape))
     return pl.pallas_call(
         attention_kernel,
-        grid=(heads,),
+        grid=(col_shards,),
         in_specs=[
             whole(mask.shape),
             row_block,
             row_block,
             whole(rows_split.shape),
-            pl.BlockSpec(
-                (row_shards, 1, members, depth, HEAD_DIM),
-                lambda g: (0, g // per_shard, 0, 0, g % per_shard),
-            ),
+            pl.BlockSpec((row_shards, 1, members, depth, cols), lambda i: (0, i, 0, 0, 0)),
             whole(low_rows.shape),
-            pl.BlockSpec((members, rank, HEAD_DIM), lambda g: (0, 0, g)),
+            pl.BlockSpec((members, rank, cols), lambda i: (0, 0, i)),
         ],
         out_specs=[
             row_block,
             row_block,
             whole((members, keys, rank)),
-            pl.BlockSpec((members, rank, HEAD_DIM), lambda g: (0, 0, g)),
+            pl.BlockSpec((members, rank, cols), lambda i: (0, 0, i)),
         ],
         out_shape=[
             jax.ShapeDtypeStruct((rows, width), jnp.bfloat16),

time: 155 us -> 151 us (0.974)
  Pallas kernels: 22.8 us -> 19.5 us
    pallas_call x1, Pallas kernels: 22.8 us -> 19.5 us  [attention_heads(): pl.pallas_call(attention_kernel, grid=(col_shards,), in_specs=[whole(mask...]
  transfers between devices with their start and end apart: 8 -> 8, of which waited for: 6 -> 6; matrix products, arithmetic and copies ran while one was open for 12% -> 13% of each run, Pallas kernels for 0% -> 0%
where the time goes in v14:
time: 151 us
  blocking collectives  44.4 us (29%)
  waiting for transfers between devices  39.2 us (26%)
  Pallas kernels  19.5 us (13%)
  local copies, waits for them, and re-layouts  15.3 us (10%)
  between operations  14.2 us (9%)
  starting transfers between devices  10.5 us (7%)
  other arithmetic  5.35 us (4%)
  matrix products  2.5 us (2%)
    all_gather x1, blocking collectives, gather_adapters(): gathered = lax.all_gather(joined, axes, axis=0, tiled=False)  44.4 us
    all_gather x1, waiting for transfers between devices, project_rows(): lax.all_gather(kv_weight, ('ctx', 'dp', 'sub'), axis=0, tiled=False)  27.4 us
    pallas_call x1, Pallas kernels, attention_heads(): pl.pallas_call(attention_kernel, grid=(col_shards,), in_specs=[whole(mask...  19.5 us
    ppermute x6, waiting for transfers between devices, exchange_scatter(): lax.ppermute(send, axis, [(i, (i + shift) % size) for i in range(size)])  11.1 us
    concatenate x4, local copies, waits for them, and re-layouts, project_rows(): rows_both = jnp.concatenate([rows_previous, rows_own], axis=0)  10.2 us
    ppermute x6, starting transfers between devices, exchange_scatter(): lax.ppermute(send, axis, [(i, (i + shift) % size) for i in range(size)])  5.49 us
    ppermute x1, starting transfers between devices, shifted(): return lax.ppermute(value, axis, pairs)  4.98 us
  transfers between devices with their start and end apart: 8, of which 6 were waited for; matrix products, arithmetic and copies ran while one was open for 13% of the time, Pallas kernels for 0%

profile of v14, /device:TPU:0, one launch (start us, length us, event | category | flops | bytes accessed | tf_op | source)
XLA Modules:
  0.0 151.1 jit_solution(11654695855894864170)
XLA Ops:
  7.2 0.0 copy-start
  7.2 0.0 all-gather.4.cloned.1.call-start
  7.2 0.7 all-gather.4.cloned.1.call-update
  7.9 5.0 %collective-permute-start = (bf16[192,2304]{1,0:T(8,128)(2,1)}, bf16[192,2304]{1,0:T(8,128)(2,1)S(1)}, u32[]{:S(2)}, u32[]{:S(2)}) collective-permute-start(bf16[192,2304]{1,0:T(8,128)(2,1)} %bitcast.84), channel_id=1, source_target_pairs={{0,4},{4,8},{8,12},{1,5},{5,9},{9,13},{2,6},{6,10},{10,14},{3,7},{... | collective-permute-start | bytes 2654216 | tf_op jit(solution)/shard_map/ppermute | solution.py:21
  12.9 3.4 %concatenate.25 = bf16[192,4,576]{2,1,0:T(4,128)(2,1)} reshape(bf16[1,192,2304]{2,1,0:T(8,128)(2,1)} %param.6) | data formatting | bytes 1769472 | tf_op jit(solution)/shard_map/concatenate | solution.py:157
  16.3 0.0 copy-done
  16.3 0.0 copy-start.3
  16.3 0.0 copy-start.4
  16.3 0.6 copy.34
  17.0 2.3 %copy.29 = bf16[192,4,576]{2,0,1:T(8,128)(2,1)} copy(bf16[192,4,576]{2,1,0:T(4,128)(2,1)} %concatenate.25) | data formatting | bytes 1769472 | tf_op jit(solution)/shard_map/concatenate | solution.py:157
  19.3 0.0 copy-done.3
  19.3 0.0 copy-done.4
  19.3 0.1 pad_maximum_fusion.1
  19.4 44.4 %all-gather.1 = bf16[32,16,208]{2,1,0:T(8,128)(2,1)S(1)} all-gather(bf16[2,16,208]{2,1,0:T(8,128)(2,1)S(1)} %pad_maximum_fusion.1), channel_id=3, replica_groups=mesh['groups'=2,'ctx'=4,'dp'=2,'sub'=2] {'ctx','dp','sub'}, dimensions={0}, use_global_device_ids=true | all-gather | bytes 226304 | tf_op jit(solution)/shard_map/all_gather | solution.py:169
  63.8 0.1 slice.17
  63.9 0.2 copy.44
  64.0 0.3 reshape.41
  64.4 0.1 copy.45
  64.4 0.8 reshape.42.up_ref
  65.2 1.0 fusion.10.mask_ref
  66.2 0.3 fusion.5
  66.6 0.0 collective-permute-done
  66.6 2.1 %concatenate.24 = bf16[192,4,576]{2,1,0:T(4,128)(2,1)} reshape(bf16[192,2304]{1,0:T(8,128)(2,1)S(1)} %collective-permute-done) | data formatting | bytes 1769472 | tf_op jit(solution)/shard_map/concatenate | solution.py:157
  68.7 2.3 %copy.28 = bf16[192,4,576]{2,0,1:T(8,128)(2,1)} copy(bf16[192,4,576]{2,1,0:T(4,128)(2,1)} %concatenate.24) | data formatting | bytes 1769472 | tf_op jit(solution)/shard_map/concatenate | solution.py:157
  71.0 0.3 fusion.4
  71.4 0.1 pad_maximum_fusion
  71.5 0.8 copy.32.low_ref
  72.3 1.4 copy.33
  73.7 2.9 %maximum_bitcast_fusion.rows_ref = bf16[4,384,576]{2,1,0:T(8,128)(2,1)} fusion(bf16[192,4,576]{2,0,1:T(8,128)(2,1)} %copy.29, bf16[192,4,576]{2,0,1:T(8,128)(2,1)} %copy.28), kind=kLoop, calls=%fused_computation | loop fusion | flops 3538944 | bytes 3538944 | tf_op jit(solution)/shard_map/transpose | solution.py:158
  76.7 27.4 %all-gather.4.cloned.1.call-done = bf16[32,576,256]{2,1,0:T(8,128)(2,1)} async-done(((bf16[2,576,256]{2,1,0:T(8,128)(2,1)}), bf16[32,576,256]{2,1,0:T(8,128)(2,1)}) %all-gather.4.cloned.1.call-update) | async-done | bytes 9437200 | tf_op jit(solution)/shard_map/all_gather | solution.py:159
  104.1 0.0 copy-start.1
  104.1 19.5 %shard_map.93 = (bf16[192,2048]{1,0:T(8,128)(2,1)}, bf16[192,2048]{1,0:T(8,128)(2,1)}, bf16[2,384,16]{2,1,0:T(8,128)(2,1)}, f32[2,16,1024]{2,1,0:T(8,128)}) custom-call(s32[384,384]{1,0:T(8,128)} %fusion.10.mask_ref, bf16[192,2048]{1,0:T(8,128)(2,1)} %bitcast.93, bf16[192,2048]{1,0:T(8,128)(2,1)} %bitcast.94, ...), custom_call_target="tpu_custom_call" | custom-call | tf_op jit(solution)/shard_map/pallas_call | solution.py:106
  123.6 0.9 broadcast_multiply_fusion
  124.5 0.2 mul.29
  124.7 0.1 copy.36
  124.8 0.0 copy-done.1
  124.8 1.8 %fusion.3 = f32[4,4,144,2,16]{2,4,3,1,0:T(8,128)S(1)} fusion(bf16[192,4,4,144]{0,3,2,1:T(8,128)(2,1)S(1)} %bitcast.85, bf16[192,4,4,144]{0,3,2,1:T(8,128)(2,1)S(1)} %bitcast.86, bf16[2,384,16]{2,1,0:T(8,128)(2,1)} %get-tuple-element.10), kind=kOutput, calls=%fused_computation.5 | convolution fusion | flops 60235776 | bytes 2088960 | tf_op jit(solution)/shard_map/mrk,rcij->icjmk/dot_general | solution.py:236
  126.6 0.1 fusion.20
  126.8 0.6 collective-permute-start.3
  127.4 1.3 collective-permute-start.2
  128.7 0.0 collective-permute-start.1
  128.7 2.5 %collective-permute-done.3 = f32[4,208,32]{1,2,0:T(8,128)S(1)} collective-permute-done((f32[4,208,32]{1,2,0:T(8,128)S(1)}, f32[4,208,32]{1,2,0:T(8,128)S(1)}, u32[]{:S(2)}, u32[]{:S(2)}) %collective-permute-start.3) | collective-permute-done | bytes 106528 | tf_op jit(solution)/shard_map/ppermute | solution.py:184
  131.3 4.3 %collective-permute-done.2 = f32[4,208,32]{1,2,0:T(8,128)S(1)} collective-permute-done((f32[4,208,32]{1,2,0:T(8,128)S(1)}, f32[4,208,32]{1,2,0:T(8,128)S(1)}, u32[]{:S(2)}, u32[]{:S(2)}) %collective-permute-start.2) | collective-permute-done | bytes 106528 | tf_op jit(solution)/shard_map/ppermute | solution.py:184
  135.5 0.0 collective-permute-done.1
  135.5 0.1 fusion.18
  135.7 1.5 collective-permute-start.6
  137.1 0.7 collective-permute-start.5
  137.8 1.4 collective-permute-start.4
  139.2 0.4 collective-permute-done.6
  139.6 2.7 %collective-permute-done.5 = f32[208,32]{0,1:T(8,128)S(1)} collective-permute-done((f32[208,32]{0,1:T(8,128)S(1)}, f32[208,32]{0,1:T(8,128)S(1)}, u32[]{:S(2)}, u32[]{:S(2)}) %collective-permute-start.5) | collective-permute-done | bytes 26656 | tf_op jit(solution)/shard_map/ppermute | solution.py:184
  142.3 1.2 collective-permute-done.4
  143.5 0.0 copy-start.2
  143.5 0.7 slice.19
  144.2 0.0 copy-done.2
  (4 shorter events, 0.0 us)
Async XLA Ops:
  7.2 9.1 %copy-start = (bf16[1,192,2304]{2,1,0:T(8,128)(2,1)S(1)}, bf16[1,192,2304]{2,1,0:T(8,128)(2,1)}, u32[]{:S(2)}) copy-start(bf16[1,192,2304]{2,1,0:T(8,128)(2,1)} %param.6) | copy-start | bytes 2654212
  7.2 96.9 %all-gather.4.cloned.1.call-start = ((), (), s32[]{:S(2)}) async-start(), calls=%async_computation | async-start | bytes 10027008 | tf_op jit(solution)/shard_map/all_gather | solution.py:159
  7.9 58.7 %collective-permute-start = (bf16[192,2304]{1,0:T(8,128)(2,1)}, bf16[192,2304]{1,0:T(8,128)(2,1)S(1)}, u32[]{:S(2)}, u32[]{:S(2)}) collective-permute-start(bf16[192,2304]{1,0:T(8,128)(2,1)} %bitcast.84), channel_id=1, source_target_pairs={{0,4},{4,8},{8,12},{1,5},{5,9},{9,13},{2,6},{6,10},{10,14},{3,7},{... | collective-permute-start | bytes 2654216 | tf_op jit(solution)/shard_map/ppermute | solution.py:21
  16.3 3.0 %copy-start.3 = (bf16[2,16,144]{2,1,0:T(8,128)(2,1)S(1)}, bf16[2,16,144]{2,1,0:T(8,128)(2,1)}, u32[]{:S(2)}) copy-start(bf16[2,16,144]{2,1,0:T(8,128)(2,1)} %param.9) | copy-start | bytes 27652
  16.3 3.0 %copy-start.4 = (bf16[2,16,64]{2,1,0:T(8,128)(2,1)S(1)}, bf16[2,16,64]{2,1,0:T(8,128)(2,1)}, u32[]{:S(2)}) copy-start(bf16[2,16,64]{2,1,0:T(8,128)(2,1)} %param.10) | copy-start | bytes 12292
  104.1 20.7 %copy-start.1 = (bf16[192,2304]{0,1:T(8,128)(2,1)S(1)}, bf16[192,2304]{0,1:T(8,128)(2,1)}, u32[]{:S(2)}) copy-start(bf16[192,2304]{0,1:T(8,128)(2,1)} %copy.33) | copy-start | bytes 2654212
  126.8 4.5 %collective-permute-start.3 = (f32[4,208,32]{1,2,0:T(8,128)S(1)}, f32[4,208,32]{1,2,0:T(8,128)S(1)}, u32[]{:S(2)}, u32[]{:S(2)}) collective-permute-start(f32[4,208,32]{1,2,0:T(8,128)S(1)} %get-tuple-element.14), channel_id=1, source_target_pairs={{0,3},{1,0},{2,1},{3,2},{4,7},{5,4},{6,5},{7,6},{8,11},{9,8},{10,9... | collective-permute-start | bytes 319496 | tf_op jit(solution)/shard_map/ppermute | solution.py:184
  127.4 8.2 %collective-permute-start.2 = (f32[4,208,32]{1,2,0:T(8,128)S(1)}, f32[4,208,32]{1,2,0:T(8,128)S(1)}, u32[]{:S(2)}, u32[]{:S(2)}) collective-permute-start(f32[4,208,32]{1,2,0:T(8,128)S(1)} %get-tuple-element.13), channel_id=1, source_target_pairs={{0,2},{1,3},{2,0},{3,1},{4,6},{5,7},{6,4},{7,5},{8,10},{9,11},{10,... | collective-permute-start | bytes 319496 | tf_op jit(solution)/shard_map/ppermute | solution.py:184
  128.7 6.8 %collective-permute-start.1 = (f32[4,208,32]{1,2,0:T(8,128)S(1)}, f32[4,208,32]{1,2,0:T(8,128)S(1)}, u32[]{:S(2)}, u32[]{:S(2)}) collective-permute-start(f32[4,208,32]{1,2,0:T(8,128)S(1)} %get-tuple-element.12), channel_id=1, source_target_pairs={{0,1},{1,2},{2,3},{3,0},{4,5},{5,6},{6,7},{7,4},{8,9},{9,10},{10,1... | collective-permute-start | bytes 319496 | tf_op jit(solution)/shard_map/ppermute | solution.py:184
  135.7 4.0 %collective-permute-start.6 = (f32[208,32]{0,1:T(8,128)S(1)}, f32[208,32]{0,1:T(8,128)S(1)}, u32[]{:S(2)}, u32[]{:S(2)}) collective-permute-start(f32[208,32]{0,1:T(8,128)S(1)} %get-tuple-element.16), channel_id=1, source_target_pairs={{0,12},{4,0},{8,4},{12,8},{1,13},{5,1},{9,5},{13,9},{2,14},{6,2},{... | collective-permute-start | bytes 79880 | tf_op jit(solution)/shard_map/ppermute | solution.py:184
  137.1 5.2 %collective-permute-start.5 = (f32[208,32]{0,1:T(8,128)S(1)}, f32[208,32]{0,1:T(8,128)S(1)}, u32[]{:S(2)}, u32[]{:S(2)}) collective-permute-start(f32[208,32]{0,1:T(8,128)S(1)} %get-tuple-element.17), channel_id=1, source_target_pairs={{0,8},{4,12},{8,0},{12,4},{1,9},{5,13},{9,1},{13,5},{2,10},{6,14},... | collective-permute-start | bytes 79880 | tf_op jit(solution)/shard_map/ppermute | solution.py:184
  137.8 5.7 %collective-permute-start.4 = (f32[208,32]{0,1:T(8,128)S(1)}, f32[208,32]{0,1:T(8,128)S(1)}, u32[]{:S(2)}, u32[]{:S(2)}) collective-permute-start(f32[208,32]{0,1:T(8,128)S(1)} %get-tuple-element.15), channel_id=1, source_target_pairs={{0,4},{4,8},{8,12},{12,0},{1,5},{5,9},{9,13},{13,1},{2,6},{6,10},{... | collective-permute-start | bytes 79880 | tf_op jit(solution)/shard_map/ppermute | solution.py:184
  143.5 0.7 copy-start.2
Sparse Core Ops, SparseCore 0:
  10.3 93.7 all-gather.3

commit v15 on v14

--- a/solution.py
+++ b/solution.py
@@ -208,8 +208,12 @@
     members_rank = joined_down.shape[-1]
     down_cols = joined_down.shape[2]
     joined = jnp.concatenate([joined_down, joined_up], axis=2)
-    mine = halving_scatter(joined, ("dp", "sub"))
-    mine = halving_scatter(mine, "ctx")
+    if lax.axis_size(("ctx", "dp", "sub")) <= 16:
+        owners = joined.swapaxes(0, 1).reshape((-1,) + joined.shape[2:])
+        mine = exchange_scatter(owners, ("ctx", "dp", "sub"))
+    else:
+        mine = halving_scatter(joined, ("dp", "sub"))
+        mine = halving_scatter(mine, "ctx")
 
     def unshard(piece):
         return piece.reshape(piece.shape[0], 2, -1).transpose(1, 2, 0)

time: 151 us -> 160 us (1.060)
  starting transfers between devices: 10.5 us -> 23.9 us
  waiting for transfers between devices: 39.2 us -> 34.1 us
    ppermute x6 -> x15, starting transfers between devices: 5.49 us -> 18.9 us  [exchange_scatter(): lax.ppermute(send, axis, [(i, (i + shift) % size) for i in range(size)])]
    ppermute x6 -> x15, waiting for transfers between devices: 11.1 us -> 6.06 us  [exchange_scatter(): lax.ppermute(send, axis, [(i, (i + shift) % size) for i in range(size)])]
  transfers between devices with their start and end apart: 8 -> 17, of which waited for: 6 -> 6; matrix products, arithmetic and copies ran while one was open for 13% -> 12% of each run, Pallas kernels for 0% -> 0%
where the time goes in v15:
time: 160 us; the launch traced here: 159 us
  blocking collectives  44.2 us (28%)
  waiting for transfers between devices  34.1 us (21%)
  starting transfers between devices  23.9 us (15%)
  Pallas kernels  19.5 us (12%)
  local copies, waits for them, and re-layouts  15.4 us (10%)
  between operations  14.4 us (9%)
  other arithmetic  5.3 us (3%)
  matrix products  2.5 us (2%)
    all_gather x1, blocking collectives, gather_adapters(): gathered = lax.all_gather(joined, axes, axis=0, tiled=False)  44.2 us
    all_gather x1, waiting for transfers between devices, project_rows(): lax.all_gather(kv_weight, ('ctx', 'dp', 'sub'), axis=0, tiled=False)  27.4 us
    pallas_call x1, Pallas kernels, attention_heads(): pl.pallas_call(attention_kernel, grid=(col_shards,), in_specs=[whole(mask...  19.5 us
    ppermute x15, starting transfers between devices, exchange_scatter(): lax.ppermute(send, axis, [(i, (i + shift) % size) for i in range(size)])  18.9 us
    concatenate x4, local copies, waits for them, and re-layouts, project_rows(): rows_both = jnp.concatenate([rows_previous, rows_own], axis=0)  10.2 us
    ppermute x15, waiting for transfers between devices, exchange_scatter(): lax.ppermute(send, axis, [(i, (i + shift) % size) for i in range(size)])  6.06 us
    ppermute x1, starting transfers between devices, shifted(): return lax.ppermute(value, axis, pairs)  4.98 us
  transfers between devices with their start and end apart: 17, of which 6 were waited for; matrix products, arithmetic and copies ran while one was open for 12% of the time, Pallas kernels for 0%

profile of v15, /device:TPU:0, one launch (start us, length us, event | category | flops | bytes accessed | tf_op | source)
XLA Modules:
  0.0 159.4 jit_solution(9178112520829035095)
XLA Ops:
  7.2 0.0 all-gather.4.cloned.1.call-start
  7.2 0.7 all-gather.4.cloned.1.call-update
  7.9 5.0 %collective-permute-start = (bf16[192,2304]{1,0:T(8,128)(2,1)}, bf16[192,2304]{1,0:T(8,128)(2,1)S(1)}, u32[]{:S(2)}, u32[]{:S(2)}) collective-permute-start(bf16[192,2304]{1,0:T(8,128)(2,1)} %bitcast.121), channel_id=1, source_target_pairs={{0,4},{4,8},{8,12},{1,5},{5,9},{9,13},{2,6},{6,10},{10,14},{3,7},{... | collective-permute-start | bytes 2654216 | tf_op jit(solution)/shard_map/ppermute | solution.py:21
  12.9 3.4 %concatenate.25 = bf16[192,4,576]{2,1,0:T(4,128)(2,1)} reshape(bf16[1,192,2304]{2,1,0:T(8,128)(2,1)} %param.6) | data formatting | bytes 1769472 | tf_op jit(solution)/shard_map/concatenate | solution.py:157
  16.3 0.6 copy.34
  17.1 2.3 %copy.29 = bf16[192,4,576]{2,0,1:T(8,128)(2,1)} copy(bf16[192,4,576]{2,1,0:T(4,128)(2,1)} %concatenate.25) | data formatting | bytes 1769472 | tf_op jit(solution)/shard_map/concatenate | solution.py:157
  19.4 0.1 pad_maximum_fusion.2
  19.5 44.2 %all-gather.1 = bf16[32,16,208]{2,1,0:T(8,128)(2,1)S(1)} all-gather(bf16[2,16,208]{2,1,0:T(8,128)(2,1)S(1)} %pad_maximum_fusion.2), channel_id=3, replica_groups=mesh['groups'=2,'ctx'=4,'dp'=2,'sub'=2] {'ctx','dp','sub'}, dimensions={0}, use_global_device_ids=true | all-gather | bytes 226304 | tf_op jit(solution)/shard_map/all_gather | solution.py:169
  63.8 0.1 slice.17
  63.9 0.2 copy.44
  64.0 0.3 reshape.44
  64.4 0.1 copy.45
  64.4 0.8 reshape.45.up_ref
  65.2 1.0 fusion.10.mask_ref
  66.2 0.3 fusion.5
  66.6 0.0 collective-permute-done
  66.6 2.2 %concatenate.24 = bf16[192,4,576]{2,1,0:T(4,128)(2,1)} reshape(bf16[192,2304]{1,0:T(8,128)(2,1)S(1)} %collective-permute-done) | data formatting | bytes 1769472 | tf_op jit(solution)/shard_map/concatenate | solution.py:157
  68.8 2.3 %copy.28 = bf16[192,4,576]{2,0,1:T(8,128)(2,1)} copy(bf16[192,4,576]{2,1,0:T(4,128)(2,1)} %concatenate.24) | data formatting | bytes 1769472 | tf_op jit(solution)/shard_map/concatenate | solution.py:157
  71.0 0.3 fusion.4
  71.4 0.1 pad_maximum_fusion.1
  71.5 0.8 copy.32.low_ref
  72.3 1.4 copy.33
  73.8 2.9 %maximum_bitcast_fusion.rows_ref = bf16[4,384,576]{2,1,0:T(8,128)(2,1)} fusion(bf16[192,4,576]{2,0,1:T(8,128)(2,1)} %copy.29, bf16[192,4,576]{2,0,1:T(8,128)(2,1)} %copy.28), kind=kLoop, calls=%fused_computation | loop fusion | flops 3538944 | bytes 3538944 | tf_op jit(solution)/shard_map/transpose | solution.py:158
  76.7 27.4 %all-gather.4.cloned.1.call-done = bf16[32,576,256]{2,1,0:T(8,128)(2,1)} async-done(((bf16[2,576,256]{2,1,0:T(8,128)(2,1)}), bf16[32,576,256]{2,1,0:T(8,128)(2,1)}) %all-gather.4.cloned.1.call-update) | async-done | bytes 9437200 | tf_op jit(solution)/shard_map/all_gather | solution.py:159
  104.1 19.5 %shard_map.93 = (bf16[192,2048]{1,0:T(8,128)(2,1)}, bf16[192,2048]{1,0:T(8,128)(2,1)}, bf16[2,384,16]{2,1,0:T(8,128)(2,1)}, f32[2,16,1024]{2,1,0:T(8,128)}) custom-call(s32[384,384]{1,0:T(8,128)} %fusion.10.mask_ref, bf16[192,2048]{1,0:T(8,128)(2,1)} %bitcast.131, bf16[192,2048]{1,0:T(8,128)(2,1)} %bitcast.132, ...), custom_call_target="tpu_custom_call" | custom-call | tf_op jit(solution)/shard_map/pallas_call | solution.py:106
  123.6 0.9 broadcast_multiply_fusion
  124.5 0.2 mul.32
  124.7 0.1 copy.36
  124.8 1.8 %fusion.3 = f32[4,4,144,2,16]{2,4,3,1,0:T(8,128)S(1)} fusion(bf16[192,4,4,144]{0,3,2,1:T(8,128)(2,1)S(1)} %bitcast.122, bf16[192,4,4,144]{0,3,2,1:T(8,128)(2,1)S(1)} %bitcast.123, bf16[2,384,16]{2,1,0:T(8,128)(2,1)} %get-tuple-element.10), kind=kOutput, calls=%fused_computation.5 | convolution fusion | flops 60235776 | bytes 2088960 | tf_op jit(solution)/shard_map/mrk,rcij->icjmk/dot_general | solution.py:240
  126.6 0.1 pad_maximum_fusion
  126.8 0.1 dynamic-slice_bitcast_fusion.14
  126.9 1.5 collective-permute-start.15
  128.4 1.3 collective-permute-start.14
  129.7 0.2 collective-permute-start.13
  129.8 1.3 collective-permute-start.12
  131.2 1.5 collective-permute-start.11
  132.6 0.0 collective-permute-done.15
  132.7 2.5 %collective-permute-start.10 = (f32[208,32]{0,1:T(8,128)S(1)}, f32[208,32]{0,1:T(8,128)S(1)}, u32[]{:S(2)}, u32[]{:S(2)}) collective-permute-start(f32[208,32]{0,1:T(8,128)S(1)} %get-tuple-element.18), channel_id=1, source_target_pairs={{0,10},{1,11},{2,12},{3,13},{4,14},{5,15},{6,0},{7,1},{8,2},{9,3},... | collective-permute-start | bytes 79880 | tf_op jit(solution)/shard_map/ppermute | solution.py:184
  135.1 0.0 collective-permute-done.14
  135.1 0.0 collective-permute-start.9
  135.1 0.0 collective-permute-done.13
  135.2 1.5 collective-permute-start.8
  136.7 0.0 collective-permute-done.12
  136.7 2.3 %collective-permute-start.7 = (f32[208,32]{0,1:T(8,128)S(1)}, f32[208,32]{0,1:T(8,128)S(1)}, u32[]{:S(2)}, u32[]{:S(2)}) collective-permute-start(f32[208,32]{0,1:T(8,128)S(1)} %get-tuple-element.21), channel_id=1, source_target_pairs={{0,7},{1,8},{2,9},{3,10},{4,11},{5,12},{6,13},{7,14},{8,15},{9,0},... | collective-permute-start | bytes 79880 | tf_op jit(solution)/shard_map/ppermute | solution.py:184
  139.0 0.0 collective-permute-done.11
  139.0 2.3 %collective-permute-start.6 = (f32[208,32]{0,1:T(8,128)S(1)}, f32[208,32]{0,1:T(8,128)S(1)}, u32[]{:S(2)}, u32[]{:S(2)}) collective-permute-start(f32[208,32]{0,1:T(8,128)S(1)} %get-tuple-element.22), channel_id=1, source_target_pairs={{0,6},{1,7},{2,8},{3,9},{4,10},{5,11},{6,12},{7,13},{8,14},{9,15},... | collective-permute-start | bytes 79880 | tf_op jit(solution)/shard_map/ppermute | solution.py:184
  141.2 0.0 collective-permute-done.10
  141.2 0.0 collective-permute-start.5
  141.2 0.0 collective-permute-done.9
  141.2 1.4 collective-permute-start.4
  142.7 0.0 collective-permute-done.8
  142.7 2.1 %collective-permute-start.3 = (f32[208,32]{0,1:T(8,128)S(1)}, f32[208,32]{0,1:T(8,128)S(1)}, u32[]{:S(2)}, u32[]{:S(2)}) collective-permute-start(f32[208,32]{0,1:T(8,128)S(1)} %get-tuple-element.25), channel_id=1, source_target_pairs={{0,3},{1,4},{2,5},{3,6},{4,7},{5,8},{6,9},{7,10},{8,11},{9,12},{10... | collective-permute-start | bytes 79880 | tf_op jit(solution)/shard_map/ppermute | solution.py:184
  144.8 0.0 collective-permute-done.7
  144.8 1.0 collective-permute-start.2
  145.8 0.0 collective-permute-done.6
  145.8 0.0 collective-permute-start.1
  145.8 0.6 collective-permute-done.5
  146.4 0.6 collective-permute-done.4
  147.0 1.0 collective-permute-done.3
  148.0 3.4 %collective-permute-done.2 = f32[208,32]{0,1:T(8,128)S(1)} collective-permute-done((f32[208,32]{0,1:T(8,128)S(1)}, f32[208,32]{0,1:T(8,128)S(1)}, u32[]{:S(2)}, u32[]{:S(2)}) %collective-permute-start.2) | collective-permute-done | bytes 26656 | tf_op jit(solution)/shard_map/ppermute | solution.py:184
  151.4 0.5 collective-permute-done.1
  151.9 0.0 copy-start.2
  151.9 0.7 slice.19
  152.6 0.0 copy-done.2
  (11 shorter events, 0.1 us)
Async XLA Ops:
  7.2 9.2 %copy-start = (bf16[1,192,2304]{2,1,0:T(8,128)(2,1)S(1)}, bf16[1,192,2304]{2,1,0:T(8,128)(2,1)}, u32[]{:S(2)}) copy-start(bf16[1,192,2304]{2,1,0:T(8,128)(2,1)} %param.6) | copy-start | bytes 2654212
  7.2 96.9 %all-gather.4.cloned.1.call-start = ((), (), s32[]{:S(2)}) async-start(), calls=%async_computation | async-start | bytes 10027008 | tf_op jit(solution)/shard_map/all_gather | solution.py:159
  7.9 58.7 %collective-permute-start = (bf16[192,2304]{1,0:T(8,128)(2,1)}, bf16[192,2304]{1,0:T(8,128)(2,1)S(1)}, u32[]{:S(2)}, u32[]{:S(2)}) collective-permute-start(bf16[192,2304]{1,0:T(8,128)(2,1)} %bitcast.121), channel_id=1, source_target_pairs={{0,4},{4,8},{8,12},{1,5},{5,9},{9,13},{2,6},{6,10},{10,14},{3,7},{... | collective-permute-start | bytes 2654216 | tf_op jit(solution)/shard_map/ppermute | solution.py:21
  16.3 3.1 %copy-start.3 = (bf16[2,16,144]{2,1,0:T(8,128)(2,1)S(1)}, bf16[2,16,144]{2,1,0:T(8,128)(2,1)}, u32[]{:S(2)}) copy-start(bf16[2,16,144]{2,1,0:T(8,128)(2,1)} %param.9) | copy-start | bytes 27652
  16.3 3.1 %copy-start.4 = (bf16[2,16,64]{2,1,0:T(8,128)(2,1)S(1)}, bf16[2,16,64]{2,1,0:T(8,128)(2,1)}, u32[]{:S(2)}) copy-start(bf16[2,16,64]{2,1,0:T(8,128)(2,1)} %param.10) | copy-start | bytes 12292
  104.1 20.7 %copy-start.1 = (bf16[192,2304]{0,1:T(8,128)(2,1)S(1)}, bf16[192,2304]{0,1:T(8,128)(2,1)}, u32[]{:S(2)}) copy-start(bf16[192,2304]{0,1:T(8,128)(2,1)} %copy.33) | copy-start | bytes 2654212
  126.9 5.8 %collective-permute-start.15 = (f32[208,32]{0,1:T(8,128)S(1)}, f32[208,32]{0,1:T(8,128)S(1)}, u32[]{:S(2)}, u32[]{:S(2)}) collective-permute-start(f32[208,32]{0,1:T(8,128)S(1)} %get-tuple-element.13), channel_id=1, source_target_pairs={{0,15},{1,0},{2,1},{3,2},{4,3},{5,4},{6,5},{7,6},{8,7},{9,8},{10,9... | collective-permute-start | bytes 79880 | tf_op jit(solution)/shard_map/ppermute | solution.py:184
  128.4 6.8 %collective-permute-start.14 = (f32[208,32]{0,1:T(8,128)S(1)}, f32[208,32]{0,1:T(8,128)S(1)}, u32[]{:S(2)}, u32[]{:S(2)}) collective-permute-start(f32[208,32]{0,1:T(8,128)S(1)} %get-tuple-element.14), channel_id=1, source_target_pairs={{0,14},{1,15},{2,0},{3,1},{4,2},{5,3},{6,4},{7,5},{8,6},{9,7},{10,... | collective-permute-start | bytes 79880 | tf_op jit(solution)/shard_map/ppermute | solution.py:184
  129.7 5.5 %collective-permute-start.13 = (f32[208,32]{0,1:T(8,128)S(1)}, f32[208,32]{0,1:T(8,128)S(1)}, u32[]{:S(2)}, u32[]{:S(2)}) collective-permute-start(f32[208,32]{0,1:T(8,128)S(1)} %get-tuple-element.15), channel_id=1, source_target_pairs={{0,13},{1,14},{2,15},{3,0},{4,1},{5,2},{6,3},{7,4},{8,5},{9,6},{10... | collective-permute-start | bytes 79880 | tf_op jit(solution)/shard_map/ppermute | solution.py:184
  129.8 6.9 %collective-permute-start.12 = (f32[208,32]{0,1:T(8,128)S(1)}, f32[208,32]{0,1:T(8,128)S(1)}, u32[]{:S(2)}, u32[]{:S(2)}) collective-permute-start(f32[208,32]{0,1:T(8,128)S(1)} %get-tuple-element.16), channel_id=1, source_target_pairs={{0,12},{1,13},{2,14},{3,15},{4,0},{5,1},{6,2},{7,3},{8,4},{9,5},{1... | collective-permute-start | bytes 79880 | tf_op jit(solution)/shard_map/ppermute | solution.py:184
  131.2 7.8 %collective-permute-start.11 = (f32[208,32]{0,1:T(8,128)S(1)}, f32[208,32]{0,1:T(8,128)S(1)}, u32[]{:S(2)}, u32[]{:S(2)}) collective-permute-start(f32[208,32]{0,1:T(8,128)S(1)} %get-tuple-element.17), channel_id=1, source_target_pairs={{0,11},{1,12},{2,13},{3,14},{4,15},{5,0},{6,1},{7,2},{8,3},{9,4},{... | collective-permute-start | bytes 79880 | tf_op jit(solution)/shard_map/ppermute | solution.py:184
  132.7 8.6 %collective-permute-start.10 = (f32[208,32]{0,1:T(8,128)S(1)}, f32[208,32]{0,1:T(8,128)S(1)}, u32[]{:S(2)}, u32[]{:S(2)}) collective-permute-start(f32[208,32]{0,1:T(8,128)S(1)} %get-tuple-element.18), channel_id=1, source_target_pairs={{0,10},{1,11},{2,12},{3,13},{4,14},{5,15},{6,0},{7,1},{8,2},{9,3},... | collective-permute-start | bytes 79880 | tf_op jit(solution)/shard_map/ppermute | solution.py:184
  135.1 6.1 %collective-permute-start.9 = (f32[208,32]{0,1:T(8,128)S(1)}, f32[208,32]{0,1:T(8,128)S(1)}, u32[]{:S(2)}, u32[]{:S(2)}) collective-permute-start(f32[208,32]{0,1:T(8,128)S(1)} %get-tuple-element.19), channel_id=1, source_target_pairs={{0,9},{1,10},{2,11},{3,12},{4,13},{5,14},{6,15},{7,0},{8,1},{9,2},... | collective-permute-start | bytes 79880 | tf_op jit(solution)/shard_map/ppermute | solution.py:184
  135.2 7.5 %collective-permute-start.8 = (f32[208,32]{0,1:T(8,128)S(1)}, f32[208,32]{0,1:T(8,128)S(1)}, u32[]{:S(2)}, u32[]{:S(2)}) collective-permute-start(f32[208,32]{0,1:T(8,128)S(1)} %get-tuple-element.20), channel_id=1, source_target_pairs={{0,8},{1,9},{2,10},{3,11},{4,12},{5,13},{6,14},{7,15},{8,0},{9,1},... | collective-permute-start | bytes 79880 | tf_op jit(solution)/shard_map/ppermute | solution.py:184
  136.7 8.1 %collective-permute-start.7 = (f32[208,32]{0,1:T(8,128)S(1)}, f32[208,32]{0,1:T(8,128)S(1)}, u32[]{:S(2)}, u32[]{:S(2)}) collective-permute-start(f32[208,32]{0,1:T(8,128)S(1)} %get-tuple-element.21), channel_id=1, source_target_pairs={{0,7},{1,8},{2,9},{3,10},{4,11},{5,12},{6,13},{7,14},{8,15},{9,0},... | collective-permute-start | bytes 79880 | tf_op jit(solution)/shard_map/ppermute | solution.py:184
  139.0 6.8 %collective-permute-start.6 = (f32[208,32]{0,1:T(8,128)S(1)}, f32[208,32]{0,1:T(8,128)S(1)}, u32[]{:S(2)}, u32[]{:S(2)}) collective-permute-start(f32[208,32]{0,1:T(8,128)S(1)} %get-tuple-element.22), channel_id=1, source_target_pairs={{0,6},{1,7},{2,8},{3,9},{4,10},{5,11},{6,12},{7,13},{8,14},{9,15},... | collective-permute-start | bytes 79880 | tf_op jit(solution)/shard_map/ppermute | solution.py:184
  141.2 5.1 %collective-permute-start.5 = (f32[208,32]{0,1:T(8,128)S(1)}, f32[208,32]{0,1:T(8,128)S(1)}, u32[]{:S(2)}, u32[]{:S(2)}) collective-permute-start(f32[208,32]{0,1:T(8,128)S(1)} %get-tuple-element.23), channel_id=1, source_target_pairs={{0,5},{1,6},{2,7},{3,8},{4,9},{5,10},{6,11},{7,12},{8,13},{9,14},{... | collective-permute-start | bytes 79880 | tf_op jit(solution)/shard_map/ppermute | solution.py:184
  141.2 5.8 %collective-permute-start.4 = (f32[208,32]{0,1:T(8,128)S(1)}, f32[208,32]{0,1:T(8,128)S(1)}, u32[]{:S(2)}, u32[]{:S(2)}) collective-permute-start(f32[208,32]{0,1:T(8,128)S(1)} %get-tuple-element.24), channel_id=1, source_target_pairs={{0,4},{1,5},{2,6},{3,7},{4,8},{5,9},{6,10},{7,11},{8,12},{9,13},{1... | collective-permute-start | bytes 79880 | tf_op jit(solution)/shard_map/ppermute | solution.py:184
  142.7 5.3 %collective-permute-start.3 = (f32[208,32]{0,1:T(8,128)S(1)}, f32[208,32]{0,1:T(8,128)S(1)}, u32[]{:S(2)}, u32[]{:S(2)}) collective-permute-start(f32[208,32]{0,1:T(8,128)S(1)} %get-tuple-element.25), channel_id=1, source_target_pairs={{0,3},{1,4},{2,5},{3,6},{4,7},{5,8},{6,9},{7,10},{8,11},{9,12},{10... | collective-permute-start | bytes 79880 | tf_op jit(solution)/shard_map/ppermute | solution.py:184
  144.8 6.6 %collective-permute-start.2 = (f32[208,32]{0,1:T(8,128)S(1)}, f32[208,32]{0,1:T(8,128)S(1)}, u32[]{:S(2)}, u32[]{:S(2)}) collective-permute-start(f32[208,32]{0,1:T(8,128)S(1)} %get-tuple-element.26), channel_id=1, source_target_pairs={{0,2},{1,3},{2,4},{3,5},{4,6},{5,7},{6,8},{7,9},{8,10},{9,11},{10,... | collective-permute-start | bytes 79880 | tf_op jit(solution)/shard_map/ppermute | solution.py:184
  145.8 6.0 %collective-permute-start.1 = (f32[208,32]{0,1:T(8,128)S(1)}, f32[208,32]{0,1:T(8,128)S(1)}, u32[]{:S(2)}, u32[]{:S(2)}) collective-permute-start(f32[208,32]{0,1:T(8,128)S(1)} %get-tuple-element.12), channel_id=1, source_target_pairs={{0,1},{1,2},{2,3},{3,4},{4,5},{5,6},{6,7},{7,8},{8,9},{9,10},{10,1... | collective-permute-start | bytes 79880 | tf_op jit(solution)/shard_map/ppermute | solution.py:184
  151.9 0.7 copy-start.2
Sparse Core Ops, SparseCore 0:
  10.3 93.7 all-gather.3

commit v16 on v14

--- a/solution.py
+++ b/solution.py
@@ -223,8 +223,9 @@
     grad_rows = out_grad[0]
     length = rows_own.shape[0]
     row_shards, col_shards = lax.axis_size("ctx"), lax.axis_size(("dp", "sub"))
+    down_full, up_full = gather_adapters(adapter_down, adapter_up)
+    rows_own, down_full = lax.optimization_barrier((rows_own, down_full))
     rows_previous = shifted(rows_own, "ctx", 1)
-    down_full, up_full = gather_adapters(adapter_down, adapter_up)
     is_first = lax.axis_index("ctx") == 0
     rows_both, rows_split, gathered, low_rows = project_rows(
         rows_previous, rows_own, kv_weight, down_full, up_full

time: 151 us -> 150 us (level)
  waiting for transfers between devices: 39.2 us -> 71.1 us
  blocking collectives: 44.4 us -> 24.5 us
  local copies, waits for them, and re-layouts: 15.3 us -> 7.69 us
  starting transfers between devices: 10.5 us -> 6.85 us
  other arithmetic: 5.35 us -> 3.29 us
    ppermute x1, waiting for transfers between devices: 0.01 us -> 25.6 us  [shifted(): return lax.ppermute(value, axis, pairs)]
    all_gather x1, blocking collectives: 44.4 us -> 24.5 us  [gather_adapters(): gathered = lax.all_gather(joined, axes, axis=0, tiled=False)]
    concatenate x4 -> x1, local copies, waits for them, and re-layouts: 10.2 us -> 1.09 us  [project_rows(): rows_both = jnp.concatenate([rows_previous, rows_own], axis=0)]
    all_gather x1, waiting for transfers between devices: 27.4 us -> 33.7 us  [project_rows(): lax.all_gather(kv_weight, ('ctx', 'dp', 'sub'), axis=0, tiled=False)]
    ppermute x1, starting transfers between devices: 4.98 us -> 1.35 us  [shifted(): return lax.ppermute(value, axis, pairs)]
    transpose x1 -> x0, other arithmetic: 2.93 us -> none  [project_rows(): rows_both.reshape(rows_both.shape[0], row_shards, -1).swapaxes(0, 1)]
    reshape x0 -> x1, local copies, waits for them, and re-layouts: none -> 2.45 us  [project_rows(): rows_both.reshape(rows_both.shape[0], row_shards, -1).swapaxes(0, 1)]
  transfers between devices with their start and end apart: 8 -> 8, of which waited for: 6 -> 7; matrix products, arithmetic and copies ran while one was open for 13% -> 6% of each run, Pallas kernels for 0% -> 0%
where the time goes in v16:
time: 150 us
  waiting for transfers between devices  71.1 us (47%)
  blocking collectives  24.5 us (16%)
  Pallas kernels  19.4 us (13%)
  between operations  14.3 us (10%)
  local copies, waits for them, and re-layouts  7.69 us (5%)
  starting transfers between devices  6.85 us (5%)
  other arithmetic  3.29 us (2%)
  matrix products  2.48 us (2%)
    all_gather x1, waiting for transfers between devices, project_rows(): lax.all_gather(kv_weight, ('ctx', 'dp', 'sub'), axis=0, tiled=False)  33.7 us
    ppermute x1, waiting for transfers between devices, shifted(): return lax.ppermute(value, axis, pairs)  25.6 us
    all_gather x1, blocking collectives, gather_adapters(): gathered = lax.all_gather(joined, axes, axis=0, tiled=False)  24.5 us
    pallas_call x1, Pallas kernels, attention_heads(): pl.pallas_call(attention_kernel, grid=(col_shards,), in_specs=[whole(mask...  19.4 us
    ppermute x6, waiting for transfers between devices, exchange_scatter(): lax.ppermute(send, axis, [(i, (i + shift) % size) for i in range(size)])  11.1 us
    ppermute x6, starting transfers between devices, exchange_scatter(): lax.ppermute(send, axis, [(i, (i + shift) % size) for i in range(size)])  5.47 us
  transfers between devices with their start and end apart: 8, of which 7 were waited for; matrix products, arithmetic and copies ran while one was open for 6% of the time, Pallas kernels for 0%

profile of v16, /device:TPU:0, one launch (start us, length us, event | category | flops | bytes accessed | tf_op | source)
XLA Modules:
  0.0 149.6 jit_solution(14501736235442194264)
XLA Ops:
  7.2 0.0 copy-start
  7.2 0.0 all-gather.4.cloned.1.call-start
  7.2 0.7 all-gather.4.cloned.1.call-update
  7.9 0.8 pad_maximum_fusion.2
  8.7 24.5 %all-gather = bf16[32,16,208]{2,1,0:T(8,128)(2,1)S(1)} all-gather(bf16[2,16,208]{2,1,0:T(8,128)(2,1)S(1)} %pad_maximum_fusion.2), channel_id=2, replica_groups=mesh['groups'=2,'ctx'=4,'dp'=2,'sub'=2] {'ctx','dp','sub'}, dimensions={0}, use_global_device_ids=true | all-gather | bytes 226304 | tf_op jit(solution)/shard_map/all_gather | solution.py:169
  33.3 0.2 copy.26
  33.4 0.3 reshape.38
  33.7 0.0 copy-start.3
  33.7 0.0 copy-done
  33.8 1.3 collective-permute-start
  35.1 0.1 slice.17
  35.3 0.1 copy.39
  35.3 0.8 reshape.41.up_ref
  36.1 1.1 fusion.6.mask_ref
  37.2 0.3 fusion.1
  37.5 0.0 copy-done.3
  37.6 25.6 %collective-permute-done = bf16[192,2304]{1,0:T(8,128)(2,1)S(1)} collective-permute-done((bf16[192,2304]{1,0:T(8,128)(2,1)S(1)}, bf16[192,2304]{1,0:T(8,128)(2,1)S(1)}, u32[]{:S(2)}, u32[]{:S(2)}) %collective-permute-start) | collective-permute-done | bytes 884768 | tf_op jit(solution)/shard_map/ppermute | solution.py:21
  63.1 0.0 copy-start.1
  63.1 0.9 copy-done.1
  64.0 0.1 pad_maximum_fusion
  64.1 1.1 copy.27
  65.2 0.0 copy-start.2
  65.2 0.0 copy-start.4
  65.3 2.4 %copy.28 = bf16[384,4,576]{2,0,1:T(8,128)(2,1)} copy(bf16[384,4,576]{0,2,1:T(8,128)(2,1)S(1)} %bitcast.78) | data formatting | bytes 3538944 | tf_op jit(solution)/shard_map/reshape | solution.py:158
  67.7 0.0 copy-done.2
  67.7 0.0 copy-done.4
  67.7 0.3 fusion
  68.1 0.1 pad_maximum_fusion.1
  68.2 0.8 copy.30.low_ref
  69.0 33.7 %all-gather.4.cloned.1.call-done = bf16[32,576,256]{2,1,0:T(8,128)(2,1)} async-done(((bf16[2,576,256]{2,1,0:T(8,128)(2,1)}), bf16[32,576,256]{2,1,0:T(8,128)(2,1)}) %all-gather.4.cloned.1.call-update) | async-done | bytes 9437200 | tf_op jit(solution)/shard_map/all_gather | solution.py:159
  102.7 19.4 %shard_map.93 = (bf16[192,2048]{1,0:T(8,128)(2,1)}, bf16[192,2048]{1,0:T(8,128)(2,1)}, bf16[2,384,16]{2,1,0:T(8,128)(2,1)}, f32[2,16,1024]{2,1,0:T(8,128)}) custom-call(s32[384,384]{1,0:T(8,128)} %fusion.6.mask_ref, bf16[192,2048]{1,0:T(8,128)(2,1)} %bitcast.90, bf16[192,2048]{1,0:T(8,128)(2,1)} %bitcast.91, bf16[4,384,576]{2,1,0:T(8,128)(2,1)} %bitcast.81, ...), custom_call_target="tpu_custom_call" | custom-call | tf_op jit(solution)/shard_map/pallas_call | solution.py:106
  122.2 0.9 broadcast_multiply_fusion
  123.1 0.2 mul.29
  123.3 0.1 copy.33
  123.4 1.8 %convolution_multiply_fusion = f32[4,4,144,2,16]{2,4,3,1,0:T(8,128)S(1)} fusion(bf16[384,4,4,144,1]{0,3,4,2,1:T(8,128)(2,1)S(1)} %bitcast.79, bf16[2,384,16]{2,1,0:T(8,128)(2,1)} %get-tuple-element.14), kind=kOutput, calls=%fused_computation.1 | convolution fusion | flops 56696832 | bytes 2088960 | tf_op jit(solution)/shard_map/mrk,rcij->icjmk/dot_general | solution.py:237
  125.2 0.1 fusion.16
  125.3 0.5 collective-permute-start.3
  125.8 1.5 collective-permute-start.2
  127.2 0.0 collective-permute-start.1
  127.2 2.4 %collective-permute-done.3 = f32[4,208,32]{1,2,0:T(8,128)S(1)} collective-permute-done((f32[4,208,32]{1,2,0:T(8,128)S(1)}, f32[4,208,32]{1,2,0:T(8,128)S(1)}, u32[]{:S(2)}, u32[]{:S(2)}) %collective-permute-start.3) | collective-permute-done | bytes 106528 | tf_op jit(solution)/shard_map/ppermute | solution.py:184
  129.7 4.4 %collective-permute-done.2 = f32[4,208,32]{1,2,0:T(8,128)S(1)} collective-permute-done((f32[4,208,32]{1,2,0:T(8,128)S(1)}, f32[4,208,32]{1,2,0:T(8,128)S(1)}, u32[]{:S(2)}, u32[]{:S(2)}) %collective-permute-start.2) | collective-permute-done | bytes 106528 | tf_op jit(solution)/shard_map/ppermute | solution.py:184
  134.1 0.0 collective-permute-done.1
  134.1 0.1 fusion.14
  134.2 2.0 %collective-permute-start.6 = (f32[208,32]{0,1:T(8,128)S(1)}, f32[208,32]{0,1:T(8,128)S(1)}, u32[]{:S(2)}, u32[]{:S(2)}) collective-permute-start(f32[208,32]{0,1:T(8,128)S(1)} %get-tuple-element.20), channel_id=1, source_target_pairs={{0,12},{4,0},{8,4},{12,8},{1,13},{5,1},{9,5},{13,9},{2,14},{6,2},{... | collective-permute-start | bytes 79880 | tf_op jit(solution)/shard_map/ppermute | solution.py:184
  136.2 0.1 collective-permute-start.5
  136.3 1.4 collective-permute-start.4
  137.7 0.4 collective-permute-done.6
  138.2 2.8 %collective-permute-done.5 = f32[208,32]{0,1:T(8,128)S(1)} collective-permute-done((f32[208,32]{0,1:T(8,128)S(1)}, f32[208,32]{0,1:T(8,128)S(1)}, u32[]{:S(2)}, u32[]{:S(2)}) %collective-permute-start.5) | collective-permute-done | bytes 26656 | tf_op jit(solution)/shard_map/ppermute | solution.py:184
  141.0 1.0 collective-permute-done.4
  142.1 0.0 copy-start.5
  142.1 0.7 slice.19
  142.7 0.0 copy-done.5
  (5 shorter events, 0.1 us)
Async XLA Ops:
  7.2 26.6 %copy-start = (bf16[1,192,2304]{2,1,0:T(8,128)(2,1)S(1)}, bf16[1,192,2304]{2,1,0:T(8,128)(2,1)}, u32[]{:S(2)}) copy-start(bf16[1,192,2304]{2,1,0:T(8,128)(2,1)} %param.6) | copy-start | bytes 2654212
  7.2 95.6 %all-gather.4.cloned.1.call-start = ((), (), s32[]{:S(2)}) async-start(), calls=%async_computation | async-start | bytes 10027008 | tf_op jit(solution)/shard_map/all_gather | solution.py:159
  33.7 3.8 %copy-start.3 = (bf16[2,16,2304]{2,1,0:T(8,128)(2,1)}, bf16[2,16,2304]{2,1,0:T(8,128)(2,1)S(1)}, u32[]{:S(2)}) copy-start(bf16[2,16,2304]{2,1,0:T(8,128)(2,1)S(1)} %reshape.38) | copy-start | bytes 442372
  33.8 29.3 %collective-permute-start = (bf16[192,2304]{1,0:T(8,128)(2,1)S(1)}, bf16[192,2304]{1,0:T(8,128)(2,1)S(1)}, u32[]{:S(2)}, u32[]{:S(2)}) collective-permute-start(bf16[192,2304]{1,0:T(8,128)(2,1)S(1)} %bitcast.84), channel_id=1, source_target_pairs={{0,4},{4,8},{8,12},{1,5},{5,9},{9,13},{2,6},{6,10},{10,14},{3,7},{... | collective-permute-start | bytes 2654216 | tf_op jit(solution)/shard_map/ppermute | solution.py:21
  63.1 0.9 copy-start.1
  65.2 2.5 %copy-start.2 = (bf16[192,2304]{1,0:T(8,128)(2,1)S(1)}, bf16[192,2304]{1,0:T(8,128)(2,1)}, u32[]{:S(2)}) copy-start(bf16[192,2304]{1,0:T(8,128)(2,1)} %copy-done.1) | copy-start | bytes 2654212
  65.2 2.5 %copy-start.4 = (bf16[2,16,2304]{2,1,0:T(8,128)(2,1)S(1)}, bf16[2,16,2304]{2,1,0:T(8,128)(2,1)}, u32[]{:S(2)}) copy-start(bf16[2,16,2304]{2,1,0:T(8,128)(2,1)} %copy-done.3) | copy-start | bytes 442372
  125.3 4.4 %collective-permute-start.3 = (f32[4,208,32]{1,2,0:T(8,128)S(1)}, f32[4,208,32]{1,2,0:T(8,128)S(1)}, u32[]{:S(2)}, u32[]{:S(2)}) collective-permute-start(f32[4,208,32]{1,2,0:T(8,128)S(1)} %get-tuple-element.18), channel_id=1, source_target_pairs={{0,3},{1,0},{2,1},{3,2},{4,7},{5,4},{6,5},{7,6},{8,11},{9,8},{10,9... | collective-permute-start | bytes 319496 | tf_op jit(solution)/shard_map/ppermute | solution.py:184
  125.8 8.3 %collective-permute-start.2 = (f32[4,208,32]{1,2,0:T(8,128)S(1)}, f32[4,208,32]{1,2,0:T(8,128)S(1)}, u32[]{:S(2)}, u32[]{:S(2)}) collective-permute-start(f32[4,208,32]{1,2,0:T(8,128)S(1)} %get-tuple-element.17), channel_id=1, source_target_pairs={{0,2},{1,3},{2,0},{3,1},{4,6},{5,7},{6,4},{7,5},{8,10},{9,11},{10,... | collective-permute-start | bytes 319496 | tf_op jit(solution)/shard_map/ppermute | solution.py:184
  127.2 6.8 %collective-permute-start.1 = (f32[4,208,32]{1,2,0:T(8,128)S(1)}, f32[4,208,32]{1,2,0:T(8,128)S(1)}, u32[]{:S(2)}, u32[]{:S(2)}) collective-permute-start(f32[4,208,32]{1,2,0:T(8,128)S(1)} %get-tuple-element.16), channel_id=1, source_target_pairs={{0,1},{1,2},{2,3},{3,0},{4,5},{5,6},{6,7},{7,4},{8,9},{9,10},{10,1... | collective-permute-start | bytes 319496 | tf_op jit(solution)/shard_map/ppermute | solution.py:184
  134.2 4.0 %collective-permute-start.6 = (f32[208,32]{0,1:T(8,128)S(1)}, f32[208,32]{0,1:T(8,128)S(1)}, u32[]{:S(2)}, u32[]{:S(2)}) collective-permute-start(f32[208,32]{0,1:T(8,128)S(1)} %get-tuple-element.20), channel_id=1, source_target_pairs={{0,12},{4,0},{8,4},{12,8},{1,13},{5,1},{9,5},{13,9},{2,14},{6,2},{... | collective-permute-start | bytes 79880 | tf_op jit(solution)/shard_map/ppermute | solution.py:184
  136.2 4.8 %collective-permute-start.5 = (f32[208,32]{0,1:T(8,128)S(1)}, f32[208,32]{0,1:T(8,128)S(1)}, u32[]{:S(2)}, u32[]{:S(2)}) collective-permute-start(f32[208,32]{0,1:T(8,128)S(1)} %get-tuple-element.21), channel_id=1, source_target_pairs={{0,8},{4,12},{8,0},{12,4},{1,9},{5,13},{9,1},{13,5},{2,10},{6,14},... | collective-permute-start | bytes 79880 | tf_op jit(solution)/shard_map/ppermute | solution.py:184
  136.3 5.7 %collective-permute-start.4 = (f32[208,32]{0,1:T(8,128)S(1)}, f32[208,32]{0,1:T(8,128)S(1)}, u32[]{:S(2)}, u32[]{:S(2)}) collective-permute-start(f32[208,32]{0,1:T(8,128)S(1)} %get-tuple-element.19), channel_id=1, source_target_pairs={{0,4},{4,8},{8,12},{12,0},{1,5},{5,9},{9,13},{13,1},{2,6},{6,10},{... | collective-permute-start | bytes 79880 | tf_op jit(solution)/shard_map/ppermute | solution.py:184
  142.1 0.7 copy-start.5
Sparse Core Ops, SparseCore 0:
  10.3 92.3 all-gather.3

commit v17 on v16

--- a/solution.py
+++ b/solution.py
@@ -1,3 +1,5 @@
+import functools
+
 import jax
 import jax.numpy as jnp
 from jax import lax
@@ -22,8 +24,8 @@
 
 
 def attention_kernel(
-    mask_ref, q_ref, do_ref, rows_ref, weight_ref, low_ref, up_ref,
-    out_ref, dq_ref, projected_ref, up_terms_ref, projected_acc,
+    factor, mask_ref, q_ref, do_ref, rows_ref, weight_ref, low_ref, up_ref,
+    out_ref, dq_ref, down_terms_ref, up_terms_ref, projected_acc,
 ):
     step = pl.program_id(0)
     half = HEAD_DIM
@@ -86,14 +88,19 @@
             )
             up_terms_ref[member, :, cols] = lax.dot_general(
                 low_ref[member], grad, contract_first, preferred_element_type=jnp.float32
-            )
+            ) * factor
 
     @pl.when(step == pl.num_programs(0) - 1)
     def _():
-        projected_ref[...] = projected_acc[...].astype(projected_ref.dtype)
-
-
-def attention_heads(mask, queries, grads, rows_split, gathered, low_rows, up_full):
+        for member in range(projected_acc.shape[0]):
+            projected = projected_acc[member].astype(jnp.bfloat16)
+            for c in range(row_shards):
+                down_terms_ref[member, c] = lax.dot_general(
+                    projected, rows_ref[c], contract_first, preferred_element_type=jnp.float32
+                ) * factor
+
+
+def attention_heads(mask, queries, grads, rows_split, gathered, low_rows, up_full, factor):
     rows, width = queries.shape
     row_shards, col_shards, members, depth, cols = gathered.shape
     keys = rows_split.shape[1]
@@ -104,7 +111,7 @@
     row_block = pl.BlockSpec((rows, step_cols), lambda i: (0, i))
     whole = lambda shape: pl.BlockSpec(shape, lambda i: (0,) * len(shape))
     return pl.pallas_call(
-        attention_kernel,
+        functools.partial(attention_kernel, factor),
         grid=(col_shards,),
         in_specs=[
             whole(mask.shape),
@@ -118,20 +125,20 @@
         out_specs=[
             row_block,
             row_block,
-            whole((members, keys, rank)),
+            whole((members, row_shards, rank, depth)),
             pl.BlockSpec((members, rank, cols), lambda i: (0, 0, i)),
         ],
         out_shape=[
             jax.ShapeDtypeStruct((rows, width), jnp.bfloat16),
             jax.ShapeDtypeStruct((rows, width), jnp.bfloat16),
-            jax.ShapeDtypeStruct((members, keys, rank), jnp.bfloat16),
+            jax.ShapeDtypeStruct((members, row_shards, rank, depth), jnp.float32),
             jax.ShapeDtypeStruct((members, rank, kv_width), jnp.float32),
         ],
         scratch_shapes=[pltpu.VMEM((members, keys, rank), jnp.float32)],
     )(mask, queries, grads, rows_split, gathered, low_rows, up_full)
 
 
-def attend(query_rows, rows_split, gathered, grad_rows, is_first, low_rows, up_full):
+def attend(query_rows, rows_split, gathered, grad_rows, is_first, low_rows, up_full, factor):
     length = query_rows.shape[0]
     group_size = HEADS // KV_HEADS
     query_pos = lax.broadcasted_iota(jnp.int32, (group_size * length, 2 * length), 0) % length
@@ -142,7 +149,8 @@
         & (jnp.logical_not(is_first) | (key_pos >= length))
     )
     return attention_heads(
-        visible.astype(jnp.int32), query_rows, grad_rows, rows_split, gathered, low_rows, up_full
+        visible.astype(jnp.int32), query_rows, grad_rows, rows_split, gathered, low_rows, up_full,
+        factor,
     )
 
 
@@ -230,18 +238,14 @@
     rows_both, rows_split, gathered, low_rows = project_rows(
         rows_previous, rows_own, kv_weight, down_full, up_full
     )
-    attended, query_grad, projected, up_terms = attend(
-        query_rows, rows_split, gathered, grad_rows, is_first, low_rows, up_full
-    )
-    up_terms = up_terms.reshape(up_terms.shape[:2] + (row_shards, col_shards, -1)).transpose(3, 2, 4, 0, 1)
-    down_terms = jnp.einsum(
-        "mrk,rcij->icjmk",
-        projected,
-        rows_both.reshape(rows_both.shape[0], row_shards, col_shards, -1),
-        preferred_element_type=jnp.float32,
-    )
     factor = adapter_scale / (lax.axis_size("dp") * lax.axis_size("sub"))
-    flat = lambda terms: (terms * factor).reshape(terms.shape[:3] + (-1,))
+    attended, query_grad, down_terms, up_terms = attend(
+        query_rows, rows_split, gathered, grad_rows, is_first, low_rows, up_full, factor
+    )
+    members, rank = up_terms.shape[0], up_terms.shape[1]
+    up_terms = up_terms.reshape((members, rank, row_shards, col_shards, -1)).transpose(3, 2, 4, 0, 1)
+    down_terms = down_terms.reshape((members, row_shards, rank, col_shards, -1)).transpose(3, 1, 4, 0, 2)
+    flat = lambda terms: terms.reshape(terms.shape[:3] + (-1,))
     down_part, up_part = scatter_adapter_grads(flat(down_terms), flat(up_terms))
     return (attended[None], query_grad[None], down_part, up_part)
 

time: 150 us -> 149 us (level)
  matrix products: 2.48 us -> 0.69 us
    dot_general x1 -> x0, matrix products: 1.79 us -> none  [on_device(): jnp.einsum('mrk,rcij->icjmk', projected, rows_both.reshape(rows_both.shap...]
    reshape x1 -> x3, local copies, waits for them, and re-layouts: 0.09 us -> 1.67 us  [the longest x2 1.5 us: on_device(): down_terms.reshape((members, row_shards, rank, col_shards, -1))]
where the time goes in v17:
time: 149 us
  waiting for transfers between devices  71.1 us (48%)
  blocking collectives  24.5 us (16%)
  Pallas kernels  20.1 us (13%)
  between operations  14.3 us (10%)
  local copies, waits for them, and re-layouts  9.18 us (6%)
  starting transfers between devices  6.85 us (5%)
  other arithmetic  2.39 us (2%)
    all_gather x1, waiting for transfers between devices, project_rows(): lax.all_gather(kv_weight, ('ctx', 'dp', 'sub'), axis=0, tiled=False)  33.7 us
    ppermute x1, waiting for transfers between devices, shifted(): return lax.ppermute(value, axis, pairs)  25.5 us
    all_gather x1, blocking collectives, gather_adapters(): gathered = lax.all_gather(joined, axes, axis=0, tiled=False)  24.5 us
    pallas_call x1, Pallas kernels, attention_heads(): pl.pallas_call(functools.partial(attention_kernel, factor), grid=(col_sha...  20.1 us
    ppermute x6, waiting for transfers between devices, exchange_scatter(): lax.ppermute(send, axis, [(i, (i + shift) % size) for i in range(size)])  11.1 us
    ppermute x6, starting transfers between devices, exchange_scatter(): lax.ppermute(send, axis, [(i, (i + shift) % size) for i in range(size)])  5.47 us
  transfers between devices with their start and end apart: 8, of which 7 were waited for; matrix products, arithmetic and copies ran while one was open for 6% of the time, Pallas kernels for 0%

profile of v17, /device:TPU:0, one launch (start us, length us, event | category | flops | bytes accessed | tf_op | source)
XLA Modules:
  0.0 149.1 jit_solution(10193985443003283959)
XLA Ops:
  7.2 0.0 copy-start
  7.2 0.0 all-gather.4.cloned.1.call-start
  7.2 0.7 all-gather.4.cloned.1.call-update
  7.9 0.8 pad_maximum_fusion.2
  8.7 24.5 %all-gather = bf16[32,16,208]{2,1,0:T(8,128)(2,1)S(1)} all-gather(bf16[2,16,208]{2,1,0:T(8,128)(2,1)S(1)} %pad_maximum_fusion.2), channel_id=2, replica_groups=mesh['groups'=2,'ctx'=4,'dp'=2,'sub'=2] {'ctx','dp','sub'}, dimensions={0}, use_global_device_ids=true | all-gather | bytes 226304 | tf_op jit(solution)/shard_map/all_gather | solution.py:177
  33.3 0.2 copy.23
  33.4 0.3 reshape.38
  33.7 0.0 copy-start.3
  33.7 0.0 copy-done
  33.8 1.3 collective-permute-start
  35.1 0.1 slice.17
  35.3 0.1 copy.32
  35.3 0.8 reshape.41.up_ref
  36.1 1.1 fusion.6.mask_ref
  37.2 0.3 fusion.1
  37.5 0.0 copy-done.3
  37.6 25.5 %collective-permute-done = bf16[192,2304]{1,0:T(8,128)(2,1)S(1)} collective-permute-done((bf16[192,2304]{1,0:T(8,128)(2,1)S(1)}, bf16[192,2304]{1,0:T(8,128)(2,1)S(1)}, u32[]{:S(2)}, u32[]{:S(2)}) %collective-permute-start) | collective-permute-done | bytes 884768 | tf_op jit(solution)/shard_map/ppermute | solution.py:23
  63.1 0.0 copy-start.1
  63.1 0.9 copy-done.1
  64.0 0.1 pad_maximum_fusion
  64.2 1.1 copy.24
  65.3 0.0 copy-start.2
  65.3 0.0 copy-start.4
  65.3 2.4 %copy.25 = bf16[384,4,576]{2,0,1:T(8,128)(2,1)} copy(bf16[384,4,576]{0,2,1:T(8,128)(2,1)S(1)} %bitcast.72) | data formatting | bytes 3538944 | tf_op jit(solution)/shard_map/reshape | solution.py:166
  67.7 0.0 copy-done.2
  67.7 0.0 copy-done.4
  67.7 0.3 fusion
  68.1 0.1 pad_maximum_fusion.1
  68.2 0.8 copy.27.low_ref
  69.0 33.7 %all-gather.4.cloned.1.call-done = bf16[32,576,256]{2,1,0:T(8,128)(2,1)} async-done(((bf16[2,576,256]{2,1,0:T(8,128)(2,1)}), bf16[32,576,256]{2,1,0:T(8,128)(2,1)}) %all-gather.4.cloned.1.call-update) | async-done | bytes 9437200 | tf_op jit(solution)/shard_map/all_gather | solution.py:167
  102.7 20.1 %shard_map.93 = (bf16[192,2048]{1,0:T(8,128)(2,1)}, bf16[192,2048]{1,0:T(8,128)(2,1)}, f32[2,4,16,576]{3,2,1,0:T(8,128)}, f32[2,16,1024]{2,1,0:T(8,128)}) custom-call(s32[384,384]{1,0:T(8,128)} %fusion.6.mask_ref, bf16[192,2048]{1,0:T(8,128)(2,1)} %bitcast.83, bf16[192,2048]{1,0:T(8,128)(2,1)} %bitcast.84, bf16[4,384,576]{2,1,0:T(8,128)(2,1)} %bitcast.71, ...), custom_call_target="tpu_custom_call" | custom-call | tf_op jit(solution)/shard_map/pallas_call | solution.py:113
  122.9 0.0 copy-start.5
  122.9 1.4 reshape.42
  124.3 0.1 copy.28
  124.4 0.0 copy-done.5
  124.4 0.2 reshape.44
  124.6 0.1 copy.29
  124.7 0.1 fusion.15
  124.8 0.5 collective-permute-start.3
  125.3 1.5 collective-permute-start.2
  126.8 0.0 collective-permute-start.1
  126.8 2.4 %collective-permute-done.3 = f32[4,208,32]{1,2,0:T(8,128)S(1)} collective-permute-done((f32[4,208,32]{1,2,0:T(8,128)S(1)}, f32[4,208,32]{1,2,0:T(8,128)S(1)}, u32[]{:S(2)}, u32[]{:S(2)}) %collective-permute-start.3) | collective-permute-done | bytes 106528 | tf_op jit(solution)/shard_map/ppermute | solution.py:192
  129.2 4.4 %collective-permute-done.2 = f32[4,208,32]{1,2,0:T(8,128)S(1)} collective-permute-done((f32[4,208,32]{1,2,0:T(8,128)S(1)}, f32[4,208,32]{1,2,0:T(8,128)S(1)}, u32[]{:S(2)}, u32[]{:S(2)}) %collective-permute-start.2) | collective-permute-done | bytes 106528 | tf_op jit(solution)/shard_map/ppermute | solution.py:192
  133.6 0.0 collective-permute-done.1
  133.6 0.1 fusion.13
  133.7 2.0 %collective-permute-start.6 = (f32[208,32]{0,1:T(8,128)S(1)}, f32[208,32]{0,1:T(8,128)S(1)}, u32[]{:S(2)}, u32[]{:S(2)}) collective-permute-start(f32[208,32]{0,1:T(8,128)S(1)} %get-tuple-element.20), channel_id=1, source_target_pairs={{0,12},{4,0},{8,4},{12,8},{1,13},{5,1},{9,5},{13,9},{2,14},{6,2},{... | collective-permute-start | bytes 79880 | tf_op jit(solution)/shard_map/ppermute | solution.py:192
  135.7 0.1 collective-permute-start.5
  135.9 1.4 collective-permute-start.4
  137.3 0.4 collective-permute-done.6
  137.7 2.8 %collective-permute-done.5 = f32[208,32]{0,1:T(8,128)S(1)} collective-permute-done((f32[208,32]{0,1:T(8,128)S(1)}, f32[208,32]{0,1:T(8,128)S(1)}, u32[]{:S(2)}, u32[]{:S(2)}) %collective-permute-start.5) | collective-permute-done | bytes 26656 | tf_op jit(solution)/shard_map/ppermute | solution.py:192
  140.5 1.0 collective-permute-done.4
  141.6 0.0 copy-start.6
  141.6 0.7 slice.19
  142.3 0.0 copy-done.6
  (5 shorter events, 0.1 us)
Async XLA Ops:
  7.2 26.6 %copy-start = (bf16[1,192,2304]{2,1,0:T(8,128)(2,1)S(1)}, bf16[1,192,2304]{2,1,0:T(8,128)(2,1)}, u32[]{:S(2)}) copy-start(bf16[1,192,2304]{2,1,0:T(8,128)(2,1)} %param.6) | copy-start | bytes 2654212
  7.2 95.6 %all-gather.4.cloned.1.call-start = ((), (), s32[]{:S(2)}) async-start(), calls=%async_computation | async-start | bytes 10027008 | tf_op jit(solution)/shard_map/all_gather | solution.py:167
  33.7 3.8 %copy-start.3 = (bf16[2,16,2304]{2,1,0:T(8,128)(2,1)}, bf16[2,16,2304]{2,1,0:T(8,128)(2,1)S(1)}, u32[]{:S(2)}) copy-start(bf16[2,16,2304]{2,1,0:T(8,128)(2,1)S(1)} %reshape.38) | copy-start | bytes 442372
  33.8 29.3 %collective-permute-start = (bf16[192,2304]{1,0:T(8,128)(2,1)S(1)}, bf16[192,2304]{1,0:T(8,128)(2,1)S(1)}, u32[]{:S(2)}, u32[]{:S(2)}) collective-permute-start(bf16[192,2304]{1,0:T(8,128)(2,1)S(1)} %bitcast.75), channel_id=1, source_target_pairs={{0,4},{4,8},{8,12},{1,5},{5,9},{9,13},{2,6},{6,10},{10,14},{3,7},{... | collective-permute-start | bytes 2654216 | tf_op jit(solution)/shard_map/ppermute | solution.py:23
  63.1 0.9 copy-start.1
  65.3 2.5 %copy-start.2 = (bf16[192,2304]{1,0:T(8,128)(2,1)S(1)}, bf16[192,2304]{1,0:T(8,128)(2,1)}, u32[]{:S(2)}) copy-start(bf16[192,2304]{1,0:T(8,128)(2,1)} %copy-done.1) | copy-start | bytes 2654212
  65.3 2.5 %copy-start.4 = (bf16[2,16,2304]{2,1,0:T(8,128)(2,1)S(1)}, bf16[2,16,2304]{2,1,0:T(8,128)(2,1)}, u32[]{:S(2)}) copy-start(bf16[2,16,2304]{2,1,0:T(8,128)(2,1)} %copy-done.3) | copy-start | bytes 442372
  122.9 1.5 %copy-start.5 = (f32[2,16,1024]{2,1,0:T(8,128)S(1)}, f32[2,16,1024]{2,1,0:T(8,128)}, u32[]{:S(2)}) copy-start(f32[2,16,1024]{2,1,0:T(8,128)} %get-tuple-element.15) | copy-start | bytes 393220
  124.8 4.4 %collective-permute-start.3 = (f32[4,208,32]{1,2,0:T(8,128)S(1)}, f32[4,208,32]{1,2,0:T(8,128)S(1)}, u32[]{:S(2)}, u32[]{:S(2)}) collective-permute-start(f32[4,208,32]{1,2,0:T(8,128)S(1)} %get-tuple-element.18), channel_id=1, source_target_pairs={{0,3},{1,0},{2,1},{3,2},{4,7},{5,4},{6,5},{7,6},{8,11},{9,8},{10,9... | collective-permute-start | bytes 319496 | tf_op jit(solution)/shard_map/ppermute | solution.py:192
  125.3 8.3 %collective-permute-start.2 = (f32[4,208,32]{1,2,0:T(8,128)S(1)}, f32[4,208,32]{1,2,0:T(8,128)S(1)}, u32[]{:S(2)}, u32[]{:S(2)}) collective-permute-start(f32[4,208,32]{1,2,0:T(8,128)S(1)} %get-tuple-element.17), channel_id=1, source_target_pairs={{0,2},{1,3},{2,0},{3,1},{4,6},{5,7},{6,4},{7,5},{8,10},{9,11},{10,... | collective-permute-start | bytes 319496 | tf_op jit(solution)/shard_map/ppermute | solution.py:192
  126.8 6.8 %collective-permute-start.1 = (f32[4,208,32]{1,2,0:T(8,128)S(1)}, f32[4,208,32]{1,2,0:T(8,128)S(1)}, u32[]{:S(2)}, u32[]{:S(2)}) collective-permute-start(f32[4,208,32]{1,2,0:T(8,128)S(1)} %get-tuple-element.16), channel_id=1, source_target_pairs={{0,1},{1,2},{2,3},{3,0},{4,5},{5,6},{6,7},{7,4},{8,9},{9,10},{10,1... | collective-permute-start | bytes 319496 | tf_op jit(solution)/shard_map/ppermute | solution.py:192
  133.7 4.0 %collective-permute-start.6 = (f32[208,32]{0,1:T(8,128)S(1)}, f32[208,32]{0,1:T(8,128)S(1)}, u32[]{:S(2)}, u32[]{:S(2)}) collective-permute-start(f32[208,32]{0,1:T(8,128)S(1)} %get-tuple-element.20), channel_id=1, source_target_pairs={{0,12},{4,0},{8,4},{12,8},{1,13},{5,1},{9,5},{13,9},{2,14},{6,2},{... | collective-permute-start | bytes 79880 | tf_op jit(solution)/shard_map/ppermute | solution.py:192
  135.7 4.8 %collective-permute-start.5 = (f32[208,32]{0,1:T(8,128)S(1)}, f32[208,32]{0,1:T(8,128)S(1)}, u32[]{:S(2)}, u32[]{:S(2)}) collective-permute-start(f32[208,32]{0,1:T(8,128)S(1)} %get-tuple-element.21), channel_id=1, source_target_pairs={{0,8},{4,12},{8,0},{12,4},{1,9},{5,13},{9,1},{13,5},{2,10},{6,14},... | collective-permute-start | bytes 79880 | tf_op jit(solution)/shard_map/ppermute | solution.py:192
  135.9 5.7 %collective-permute-start.4 = (f32[208,32]{0,1:T(8,128)S(1)}, f32[208,32]{0,1:T(8,128)S(1)}, u32[]{:S(2)}, u32[]{:S(2)}) collective-permute-start(f32[208,32]{0,1:T(8,128)S(1)} %get-tuple-element.19), channel_id=1, source_target_pairs={{0,4},{4,8},{8,12},{12,0},{1,5},{5,9},{9,13},{13,1},{2,6},{6,10},{... | collective-permute-start | bytes 79880 | tf_op jit(solution)/shard_map/ppermute | solution.py:192
  141.6 0.7 copy-start.6
Sparse Core Ops, SparseCore 0:
  10.3 92.3 all-gather.3

commit v18 on v17

--- a/solution.py
+++ b/solution.py
@@ -60,8 +60,10 @@
         do = jnp.concatenate([do_ref[:, qa], do_ref[:, qb]], axis=0)
         k = keys_here[:, cols]
         v = values_here[:, cols]
-        raw_score = lax.dot_general(q, k, contract_last, preferred_element_type=jnp.float32) * query_scale
-        bent_score = jnp.tanh(raw_score / logit_cap)
+        bent_score = jnp.tanh(
+            lax.dot_general(q, k, contract_last, preferred_element_type=jnp.float32)
+            * (query_scale / logit_cap)
+        )
         expo_terms = jnp.where(visible, jnp.exp(logit_cap * bent_score), 0.0)
         denominator = jnp.sum(expo_terms, axis=-1, keepdims=True)
         prob_wide = (expo_terms * (1.0 / denominator)).astype(jnp.bfloat16).astype(jnp.float32)

time: 149 us -> 149 us (level)
  no operation moved by 1% of the time
where the time goes in v18:
time: 149 us
  waiting for transfers between devices  71.1 us (48%)
  blocking collectives  24.5 us (16%)
  Pallas kernels  20.1 us (13%)
  between operations  14.3 us (10%)
  local copies, waits for them, and re-layouts  9.18 us (6%)
  starting transfers between devices  6.86 us (5%)
  other arithmetic  2.39 us (2%)
    all_gather x1, waiting for transfers between devices, project_rows(): lax.all_gather(kv_weight, ('ctx', 'dp', 'sub'), axis=0, tiled=False)  33.7 us
    ppermute x1, waiting for transfers between devices, shifted(): return lax.ppermute(value, axis, pairs)  25.5 us
    all_gather x1, blocking collectives, gather_adapters(): gathered = lax.all_gather(joined, axes, axis=0, tiled=False)  24.5 us
    pallas_call x1, Pallas kernels, attention_heads(): pl.pallas_call(functools.partial(attention_kernel, factor), grid=(col_sha...  20.1 us
    ppermute x6, waiting for transfers between devices, exchange_scatter(): lax.ppermute(send, axis, [(i, (i + shift) % size) for i in range(size)])  11.1 us
    ppermute x6, starting transfers between devices, exchange_scatter(): lax.ppermute(send, axis, [(i, (i + shift) % size) for i in range(size)])  5.48 us
  transfers between devices with their start and end apart: 8, of which 7 were waited for; matrix products, arithmetic and copies ran while one was open for 6% of the time, Pallas kernels for 0%

profile of v18, /device:TPU:0, one launch (start us, length us, event | category | flops | bytes accessed | tf_op | source)
XLA Modules:
  0.0 149.0 jit_solution(16464878835853133968)
XLA Ops:
  7.2 0.0 copy-start
  7.2 0.0 all-gather.4.cloned.1.call-start
  7.2 0.7 all-gather.4.cloned.1.call-update
  7.9 0.8 pad_maximum_fusion.2
  8.7 24.5 %all-gather = bf16[32,16,208]{2,1,0:T(8,128)(2,1)S(1)} all-gather(bf16[2,16,208]{2,1,0:T(8,128)(2,1)S(1)} %pad_maximum_fusion.2), channel_id=2, replica_groups=mesh['groups'=2,'ctx'=4,'dp'=2,'sub'=2] {'ctx','dp','sub'}, dimensions={0}, use_global_device_ids=true | all-gather | bytes 226304 | tf_op jit(solution)/shard_map/all_gather | solution.py:179
  33.3 0.2 copy.23
  33.4 0.3 reshape.38
  33.7 0.0 copy-start.3
  33.7 0.0 copy-done
  33.8 1.3 collective-permute-start
  35.1 0.1 slice.17
  35.3 0.1 copy.32
  35.3 0.8 reshape.41.up_ref
  36.1 1.1 fusion.6.mask_ref
  37.2 0.3 fusion.1
  37.5 0.0 copy-done.3
  37.6 25.5 %collective-permute-done = bf16[192,2304]{1,0:T(8,128)(2,1)S(1)} collective-permute-done((bf16[192,2304]{1,0:T(8,128)(2,1)S(1)}, bf16[192,2304]{1,0:T(8,128)(2,1)S(1)}, u32[]{:S(2)}, u32[]{:S(2)}) %collective-permute-start) | collective-permute-done | bytes 884768 | tf_op jit(solution)/shard_map/ppermute | solution.py:23
  63.1 0.0 copy-start.1
  63.1 0.9 copy-done.1
  64.0 0.1 pad_maximum_fusion
  64.2 1.1 copy.24
  65.3 0.0 copy-start.2
  65.3 0.0 copy-start.4
  65.3 2.4 %copy.25 = bf16[384,4,576]{2,0,1:T(8,128)(2,1)} copy(bf16[384,4,576]{0,2,1:T(8,128)(2,1)S(1)} %bitcast.72) | data formatting | bytes 3538944 | tf_op jit(solution)/shard_map/reshape | solution.py:168
  67.7 0.0 copy-done.2
  67.7 0.0 copy-done.4
  67.7 0.3 fusion
  68.1 0.1 pad_maximum_fusion.1
  68.2 0.8 copy.27.low_ref
  69.0 33.7 %all-gather.4.cloned.1.call-done = bf16[32,576,256]{2,1,0:T(8,128)(2,1)} async-done(((bf16[2,576,256]{2,1,0:T(8,128)(2,1)}), bf16[32,576,256]{2,1,0:T(8,128)(2,1)}) %all-gather.4.cloned.1.call-update) | async-done | bytes 9437200 | tf_op jit(solution)/shard_map/all_gather | solution.py:169
  102.7 20.1 %shard_map.93 = (bf16[192,2048]{1,0:T(8,128)(2,1)}, bf16[192,2048]{1,0:T(8,128)(2,1)}, f32[2,4,16,576]{3,2,1,0:T(8,128)}, f32[2,16,1024]{2,1,0:T(8,128)}) custom-call(s32[384,384]{1,0:T(8,128)} %fusion.6.mask_ref, bf16[192,2048]{1,0:T(8,128)(2,1)} %bitcast.83, bf16[192,2048]{1,0:T(8,128)(2,1)} %bitcast.84, bf16[4,384,576]{2,1,0:T(8,128)(2,1)} %bitcast.71, ...), custom_call_target="tpu_custom_call" | custom-call | tf_op jit(solution)/shard_map/pallas_call | solution.py:115
  122.8 0.0 copy-start.5
  122.8 1.4 reshape.42
  124.2 0.1 copy.28
  124.3 0.0 copy-done.5
  124.3 0.2 reshape.44
  124.5 0.1 copy.29
  124.6 0.1 fusion.15
  124.8 0.5 collective-permute-start.3
  125.2 1.5 collective-permute-start.2
  126.7 0.0 collective-permute-start.1
  126.7 2.4 %collective-permute-done.3 = f32[4,208,32]{1,2,0:T(8,128)S(1)} collective-permute-done((f32[4,208,32]{1,2,0:T(8,128)S(1)}, f32[4,208,32]{1,2,0:T(8,128)S(1)}, u32[]{:S(2)}, u32[]{:S(2)}) %collective-permute-start.3) | collective-permute-done | bytes 106528 | tf_op jit(solution)/shard_map/ppermute | solution.py:194
  129.1 4.4 %collective-permute-done.2 = f32[4,208,32]{1,2,0:T(8,128)S(1)} collective-permute-done((f32[4,208,32]{1,2,0:T(8,128)S(1)}, f32[4,208,32]{1,2,0:T(8,128)S(1)}, u32[]{:S(2)}, u32[]{:S(2)}) %collective-permute-start.2) | collective-permute-done | bytes 106528 | tf_op jit(solution)/shard_map/ppermute | solution.py:194
  133.5 0.0 collective-permute-done.1
  133.5 0.1 fusion.13
  133.7 2.0 %collective-permute-start.6 = (f32[208,32]{0,1:T(8,128)S(1)}, f32[208,32]{0,1:T(8,128)S(1)}, u32[]{:S(2)}, u32[]{:S(2)}) collective-permute-start(f32[208,32]{0,1:T(8,128)S(1)} %get-tuple-element.20), channel_id=1, source_target_pairs={{0,12},{4,0},{8,4},{12,8},{1,13},{5,1},{9,5},{13,9},{2,14},{6,2},{... | collective-permute-start | bytes 79880 | tf_op jit(solution)/shard_map/ppermute | solution.py:194
  135.6 0.1 collective-permute-start.5
  135.8 1.4 collective-permute-start.4
  137.2 0.4 collective-permute-done.6
  137.6 2.8 %collective-permute-done.5 = f32[208,32]{0,1:T(8,128)S(1)} collective-permute-done((f32[208,32]{0,1:T(8,128)S(1)}, f32[208,32]{0,1:T(8,128)S(1)}, u32[]{:S(2)}, u32[]{:S(2)}) %collective-permute-start.5) | collective-permute-done | bytes 26656 | tf_op jit(solution)/shard_map/ppermute | solution.py:194
  140.4 1.0 collective-permute-done.4
  141.5 0.0 copy-start.6
  141.5 0.7 slice.19
  142.2 0.0 copy-done.6
  (5 shorter events, 0.1 us)
Async XLA Ops:
  7.2 26.6 %copy-start = (bf16[1,192,2304]{2,1,0:T(8,128)(2,1)S(1)}, bf16[1,192,2304]{2,1,0:T(8,128)(2,1)}, u32[]{:S(2)}) copy-start(bf16[1,192,2304]{2,1,0:T(8,128)(2,1)} %param.6) | copy-start | bytes 2654212
  7.2 95.6 %all-gather.4.cloned.1.call-start = ((), (), s32[]{:S(2)}) async-start(), calls=%async_computation | async-start | bytes 10027008 | tf_op jit(solution)/shard_map/all_gather | solution.py:169
  33.7 3.8 %copy-start.3 = (bf16[2,16,2304]{2,1,0:T(8,128)(2,1)}, bf16[2,16,2304]{2,1,0:T(8,128)(2,1)S(1)}, u32[]{:S(2)}) copy-start(bf16[2,16,2304]{2,1,0:T(8,128)(2,1)S(1)} %reshape.38) | copy-start | bytes 442372
  33.8 29.3 %collective-permute-start = (bf16[192,2304]{1,0:T(8,128)(2,1)S(1)}, bf16[192,2304]{1,0:T(8,128)(2,1)S(1)}, u32[]{:S(2)}, u32[]{:S(2)}) collective-permute-start(bf16[192,2304]{1,0:T(8,128)(2,1)S(1)} %bitcast.75), channel_id=1, source_target_pairs={{0,4},{4,8},{8,12},{1,5},{5,9},{9,13},{2,6},{6,10},{10,14},{3,7},{... | collective-permute-start | bytes 2654216 | tf_op jit(solution)/shard_map/ppermute | solution.py:23
  63.1 0.9 copy-start.1
  65.3 2.5 %copy-start.2 = (bf16[192,2304]{1,0:T(8,128)(2,1)S(1)}, bf16[192,2304]{1,0:T(8,128)(2,1)}, u32[]{:S(2)}) copy-start(bf16[192,2304]{1,0:T(8,128)(2,1)} %copy-done.1) | copy-start | bytes 2654212
  65.3 2.5 %copy-start.4 = (bf16[2,16,2304]{2,1,0:T(8,128)(2,1)S(1)}, bf16[2,16,2304]{2,1,0:T(8,128)(2,1)}, u32[]{:S(2)}) copy-start(bf16[2,16,2304]{2,1,0:T(8,128)(2,1)} %copy-done.3) | copy-start | bytes 442372
  122.8 1.5 %copy-start.5 = (f32[2,16,1024]{2,1,0:T(8,128)S(1)}, f32[2,16,1024]{2,1,0:T(8,128)}, u32[]{:S(2)}) copy-start(f32[2,16,1024]{2,1,0:T(8,128)} %get-tuple-element.15) | copy-start | bytes 393220
  124.8 4.4 %collective-permute-start.3 = (f32[4,208,32]{1,2,0:T(8,128)S(1)}, f32[4,208,32]{1,2,0:T(8,128)S(1)}, u32[]{:S(2)}, u32[]{:S(2)}) collective-permute-start(f32[4,208,32]{1,2,0:T(8,128)S(1)} %get-tuple-element.18), channel_id=1, source_target_pairs={{0,3},{1,0},{2,1},{3,2},{4,7},{5,4},{6,5},{7,6},{8,11},{9,8},{10,9... | collective-permute-start | bytes 319496 | tf_op jit(solution)/shard_map/ppermute | solution.py:194
  125.2 8.3 %collective-permute-start.2 = (f32[4,208,32]{1,2,0:T(8,128)S(1)}, f32[4,208,32]{1,2,0:T(8,128)S(1)}, u32[]{:S(2)}, u32[]{:S(2)}) collective-permute-start(f32[4,208,32]{1,2,0:T(8,128)S(1)} %get-tuple-element.17), channel_id=1, source_target_pairs={{0,2},{1,3},{2,0},{3,1},{4,6},{5,7},{6,4},{7,5},{8,10},{9,11},{10,... | collective-permute-start | bytes 319496 | tf_op jit(solution)/shard_map/ppermute | solution.py:194
  126.7 6.8 %collective-permute-start.1 = (f32[4,208,32]{1,2,0:T(8,128)S(1)}, f32[4,208,32]{1,2,0:T(8,128)S(1)}, u32[]{:S(2)}, u32[]{:S(2)}) collective-permute-start(f32[4,208,32]{1,2,0:T(8,128)S(1)} %get-tuple-element.16), channel_id=1, source_target_pairs={{0,1},{1,2},{2,3},{3,0},{4,5},{5,6},{6,7},{7,4},{8,9},{9,10},{10,1... | collective-permute-start | bytes 319496 | tf_op jit(solution)/shard_map/ppermute | solution.py:194
  133.7 4.0 %collective-permute-start.6 = (f32[208,32]{0,1:T(8,128)S(1)}, f32[208,32]{0,1:T(8,128)S(1)}, u32[]{:S(2)}, u32[]{:S(2)}) collective-permute-start(f32[208,32]{0,1:T(8,128)S(1)} %get-tuple-element.20), channel_id=1, source_target_pairs={{0,12},{4,0},{8,4},{12,8},{1,13},{5,1},{9,5},{13,9},{2,14},{6,2},{... | collective-permute-start | bytes 79880 | tf_op jit(solution)/shard_map/ppermute | solution.py:194
  135.6 4.8 %collective-permute-start.5 = (f32[208,32]{0,1:T(8,128)S(1)}, f32[208,32]{0,1:T(8,128)S(1)}, u32[]{:S(2)}, u32[]{:S(2)}) collective-permute-start(f32[208,32]{0,1:T(8,128)S(1)} %get-tuple-element.21), channel_id=1, source_target_pairs={{0,8},{4,12},{8,0},{12,4},{1,9},{5,13},{9,1},{13,5},{2,10},{6,14},... | collective-permute-start | bytes 79880 | tf_op jit(solution)/shard_map/ppermute | solution.py:194
  135.8 5.7 %collective-permute-start.4 = (f32[208,32]{0,1:T(8,128)S(1)}, f32[208,32]{0,1:T(8,128)S(1)}, u32[]{:S(2)}, u32[]{:S(2)}) collective-permute-start(f32[208,32]{0,1:T(8,128)S(1)} %get-tuple-element.19), channel_id=1, source_target_pairs={{0,4},{4,8},{8,12},{12,0},{1,5},{5,9},{9,13},{13,1},{2,6},{6,10},{... | collective-permute-start | bytes 79880 | tf_op jit(solution)/shard_map/ppermute | solution.py:194
  141.5 0.7 copy-start.6
Sparse Core Ops, SparseCore 0:
  10.3 92.3 all-gather.3

commit v19 on v17

--- a/solution.py
+++ b/solution.py
@@ -32,7 +32,15 @@
     row_shards = weight_ref.shape[0]
     heads_here = weight_ref.shape[4] // HEAD_DIM
     rows = q_ref.shape[0]
-    visible = mask_ref[...] != 0
+    keys = rows_ref.shape[1]
+    query_pos = lax.broadcasted_iota(jnp.int32, (2 * rows, keys), 0)
+    query_pos = jnp.where(query_pos >= rows, query_pos - rows, query_pos)
+    key_pos = lax.broadcasted_iota(jnp.int32, (2 * rows, keys), 1)
+    visible = (
+        (key_pos > query_pos)
+        & (key_pos <= query_pos + rows)
+        & ((mask_ref[0] == 0) | (key_pos >= rows))
+    )
     contract_last = (((1,), (1,)), ((), ()))
     contract_first = (((0,), (0,)), ((), ()))
 
@@ -114,7 +122,7 @@
         functools.partial(attention_kernel, factor),
         grid=(col_shards,),
         in_specs=[
-            whole(mask.shape),
+            pl.BlockSpec(memory_space=pltpu.SMEM),
             row_block,
             row_block,
             whole(rows_split.shape),
@@ -141,15 +149,9 @@
 def attend(query_rows, rows_split, gathered, grad_rows, is_first, low_rows, up_full, factor):
     length = query_rows.shape[0]
     group_size = HEADS // KV_HEADS
-    query_pos = lax.broadcasted_iota(jnp.int32, (group_size * length, 2 * length), 0) % length
-    key_pos = lax.broadcasted_iota(jnp.int32, (group_size * length, 2 * length), 1)
-    visible = (
-        (key_pos > query_pos)
-        & (key_pos <= query_pos + length)
-        & (jnp.logical_not(is_first) | (key_pos >= length))
-    )
+    first_flag = is_first.astype(jnp.int32).reshape(1)
     return attention_heads(
-        visible.astype(jnp.int32), query_rows, grad_rows, rows_split, gathered, low_rows, up_full,
+        first_flag, query_rows, grad_rows, rows_split, gathered, low_rows, up_full,
         factor,
     )
 

time: 149 us -> 149 us (level)
  transfers between devices with their start and end apart: 8 -> 8, of which waited for: 7 -> 7; matrix products, arithmetic and copies ran while one was open for 6% -> 5% of each run, Pallas kernels for 0% -> 0%
where the time goes in v19:
time: 149 us
  waiting for transfers between devices  72.2 us (48%)
  blocking collectives  24.5 us (16%)
  Pallas kernels  19.7 us (13%)
  between operations  14.3 us (10%)
  local copies, waits for them, and re-layouts  9.15 us (6%)
  starting transfers between devices  6.86 us (5%)
    all_gather x1, waiting for transfers between devices, project_rows(): lax.all_gather(kv_weight, ('ctx', 'dp', 'sub'), axis=0, tiled=False)  33.7 us
    ppermute x1, waiting for transfers between devices, shifted(): return lax.ppermute(value, axis, pairs)  26.6 us
    all_gather x1, blocking collectives, gather_adapters(): gathered = lax.all_gather(joined, axes, axis=0, tiled=False)  24.5 us
    pallas_call x1, Pallas kernels, attention_heads(): pl.pallas_call(functools.partial(attention_kernel, factor), grid=(col_sha...  19.7 us
    ppermute x6, waiting for transfers between devices, exchange_scatter(): lax.ppermute(send, axis, [(i, (i + shift) % size) for i in range(size)])  11.1 us
    ppermute x6, starting transfers between devices, exchange_scatter(): lax.ppermute(send, axis, [(i, (i + shift) % size) for i in range(size)])  5.48 us
  transfers between devices with their start and end apart: 8, of which 7 were waited for; matrix products, arithmetic and copies ran while one was open for 5% of the time, Pallas kernels for 0%

profile of v19, /device:TPU:0, one launch (start us, length us, event | category | flops | bytes accessed | tf_op | source)
XLA Modules:
  0.0 148.7 jit_solution(11765059969827725427)
XLA Ops:
  7.2 0.0 copy-start
  7.2 0.0 all-gather.4.cloned.1.call-start
  7.2 0.7 all-gather.4.cloned.1.call-update
  7.9 0.8 pad_maximum_fusion.2
  8.7 24.5 %all-gather = bf16[32,16,208]{2,1,0:T(8,128)(2,1)S(1)} all-gather(bf16[2,16,208]{2,1,0:T(8,128)(2,1)S(1)} %pad_maximum_fusion.2), channel_id=2, replica_groups=mesh['groups'=2,'ctx'=4,'dp'=2,'sub'=2] {'ctx','dp','sub'}, dimensions={0}, use_global_device_ids=true | all-gather | bytes 226304 | tf_op jit(solution)/shard_map/all_gather | solution.py:179
  33.3 0.2 copy.23
  33.4 0.3 reshape.45
  33.7 0.0 copy-start.3
  33.7 0.0 copy-done
  33.8 1.3 collective-permute-start
  35.1 0.1 slice.17
  35.3 0.1 copy.32
  35.3 0.8 reshape.48.up_ref
  36.1 0.3 fusion.1
  36.4 0.0 copy-done.3
  36.5 26.6 %collective-permute-done = bf16[192,2304]{1,0:T(8,128)(2,1)S(1)} collective-permute-done((bf16[192,2304]{1,0:T(8,128)(2,1)S(1)}, bf16[192,2304]{1,0:T(8,128)(2,1)S(1)}, u32[]{:S(2)}, u32[]{:S(2)}) %collective-permute-start) | collective-permute-done | bytes 884768 | tf_op jit(solution)/shard_map/ppermute | solution.py:23
  63.1 0.0 copy-start.1
  63.1 0.9 copy-done.1
  64.0 0.1 pad_maximum_fusion
  64.1 1.1 copy.24
  65.2 0.0 copy-start.2
  65.3 0.0 copy-start.4
  65.3 2.4 %copy.25 = bf16[384,4,576]{2,0,1:T(8,128)(2,1)} copy(bf16[384,4,576]{0,2,1:T(8,128)(2,1)S(1)} %bitcast.73) | data formatting | bytes 3538944 | tf_op jit(solution)/shard_map/reshape | solution.py:168
  67.7 0.0 copy-done.2
  67.7 0.0 copy-done.4
  67.7 0.3 fusion
  68.0 0.1 pad_maximum_fusion.1
  68.2 0.8 copy.27.low_ref
  69.0 33.7 %all-gather.4.cloned.1.call-done = bf16[32,576,256]{2,1,0:T(8,128)(2,1)} async-done(((bf16[2,576,256]{2,1,0:T(8,128)(2,1)}), bf16[32,576,256]{2,1,0:T(8,128)(2,1)}) %all-gather.4.cloned.1.call-update) | async-done | bytes 9437200 | tf_op jit(solution)/shard_map/all_gather | solution.py:169
  102.7 19.7 %shard_map.93 = (bf16[192,2048]{1,0:T(8,128)(2,1)}, bf16[192,2048]{1,0:T(8,128)(2,1)}, f32[2,4,16,576]{3,2,1,0:T(8,128)}, f32[2,16,1024]{2,1,0:T(8,128)}) custom-call(s32[1]{0:T(128)} %bitcast.mask_ref, bf16[192,2048]{1,0:T(8,128)(2,1)} %bitcast.84, bf16[192,2048]{1,0:T(8,128)(2,1)} %bitcast.85, bf16[4,384,576]{2,1,0:T(8,128)(2,1)} %bitcast.72, ...), custom_call_target="tpu_custom_call" | custom-call | tf_op jit(solution)/shard_map/pallas_call | solution.py:121
  122.5 0.0 copy-start.5
  122.5 1.4 reshape.49
  123.9 0.1 copy.28
  124.0 0.0 copy-done.5
  124.0 0.2 reshape.51
  124.2 0.1 copy.29
  124.3 0.1 fusion.12
  124.4 0.5 collective-permute-start.3
  124.9 1.5 collective-permute-start.2
  126.4 0.0 collective-permute-start.1
  126.4 2.4 %collective-permute-done.3 = f32[4,208,32]{1,2,0:T(8,128)S(1)} collective-permute-done((f32[4,208,32]{1,2,0:T(8,128)S(1)}, f32[4,208,32]{1,2,0:T(8,128)S(1)}, u32[]{:S(2)}, u32[]{:S(2)}) %collective-permute-start.3) | collective-permute-done | bytes 106528 | tf_op jit(solution)/shard_map/ppermute | solution.py:194
  128.8 4.4 %collective-permute-done.2 = f32[4,208,32]{1,2,0:T(8,128)S(1)} collective-permute-done((f32[4,208,32]{1,2,0:T(8,128)S(1)}, f32[4,208,32]{1,2,0:T(8,128)S(1)}, u32[]{:S(2)}, u32[]{:S(2)}) %collective-permute-start.2) | collective-permute-done | bytes 106528 | tf_op jit(solution)/shard_map/ppermute | solution.py:194
  133.2 0.0 collective-permute-done.1
  133.2 0.1 fusion.10
  133.3 2.0 %collective-permute-start.6 = (f32[208,32]{0,1:T(8,128)S(1)}, f32[208,32]{0,1:T(8,128)S(1)}, u32[]{:S(2)}, u32[]{:S(2)}) collective-permute-start(f32[208,32]{0,1:T(8,128)S(1)} %get-tuple-element.20), channel_id=1, source_target_pairs={{0,12},{4,0},{8,4},{12,8},{1,13},{5,1},{9,5},{13,9},{2,14},{6,2},{... | collective-permute-start | bytes 79880 | tf_op jit(solution)/shard_map/ppermute | solution.py:194
  135.3 0.1 collective-permute-start.5
  135.4 1.4 collective-permute-start.4
  136.9 0.4 collective-permute-done.6
  137.3 2.8 %collective-permute-done.5 = f32[208,32]{0,1:T(8,128)S(1)} collective-permute-done((f32[208,32]{0,1:T(8,128)S(1)}, f32[208,32]{0,1:T(8,128)S(1)}, u32[]{:S(2)}, u32[]{:S(2)}) %collective-permute-start.5) | collective-permute-done | bytes 26656 | tf_op jit(solution)/shard_map/ppermute | solution.py:194
  140.1 1.0 collective-permute-done.4
  141.2 0.0 copy-start.6
  141.2 0.7 slice.19
  141.9 0.0 copy-done.6
  (3 shorter events, 0.0 us)
Async XLA Ops:
  7.2 26.6 %copy-start = (bf16[1,192,2304]{2,1,0:T(8,128)(2,1)S(1)}, bf16[1,192,2304]{2,1,0:T(8,128)(2,1)}, u32[]{:S(2)}) copy-start(bf16[1,192,2304]{2,1,0:T(8,128)(2,1)} %param.6) | copy-start | bytes 2654212
  7.2 95.6 %all-gather.4.cloned.1.call-start = ((), (), s32[]{:S(2)}) async-start(), calls=%async_computation | async-start | bytes 10027008 | tf_op jit(solution)/shard_map/all_gather | solution.py:169
  33.7 2.7 %copy-start.3 = (bf16[2,16,2304]{2,1,0:T(8,128)(2,1)}, bf16[2,16,2304]{2,1,0:T(8,128)(2,1)S(1)}, u32[]{:S(2)}) copy-start(bf16[2,16,2304]{2,1,0:T(8,128)(2,1)S(1)} %reshape.45) | copy-start | bytes 442372
  33.8 29.3 %collective-permute-start = (bf16[192,2304]{1,0:T(8,128)(2,1)S(1)}, bf16[192,2304]{1,0:T(8,128)(2,1)S(1)}, u32[]{:S(2)}, u32[]{:S(2)}) collective-permute-start(bf16[192,2304]{1,0:T(8,128)(2,1)S(1)} %bitcast.76), channel_id=1, source_target_pairs={{0,4},{4,8},{8,12},{1,5},{5,9},{9,13},{2,6},{6,10},{10,14},{3,7},{... | collective-permute-start | bytes 2654216 | tf_op jit(solution)/shard_map/ppermute | solution.py:23
  63.1 0.9 copy-start.1
  65.2 2.4 %copy-start.2 = (bf16[192,2304]{1,0:T(8,128)(2,1)S(1)}, bf16[192,2304]{1,0:T(8,128)(2,1)}, u32[]{:S(2)}) copy-start(bf16[192,2304]{1,0:T(8,128)(2,1)} %copy-done.1) | copy-start | bytes 2654212
  65.3 2.4 %copy-start.4 = (bf16[2,16,2304]{2,1,0:T(8,128)(2,1)S(1)}, bf16[2,16,2304]{2,1,0:T(8,128)(2,1)}, u32[]{:S(2)}) copy-start(bf16[2,16,2304]{2,1,0:T(8,128)(2,1)} %copy-done.3) | copy-start | bytes 442372
  122.5 1.5 %copy-start.5 = (f32[2,16,1024]{2,1,0:T(8,128)S(1)}, f32[2,16,1024]{2,1,0:T(8,128)}, u32[]{:S(2)}) copy-start(f32[2,16,1024]{2,1,0:T(8,128)} %get-tuple-element.15) | copy-start | bytes 393220
  124.4 4.4 %collective-permute-start.3 = (f32[4,208,32]{1,2,0:T(8,128)S(1)}, f32[4,208,32]{1,2,0:T(8,128)S(1)}, u32[]{:S(2)}, u32[]{:S(2)}) collective-permute-start(f32[4,208,32]{1,2,0:T(8,128)S(1)} %get-tuple-element.18), channel_id=1, source_target_pairs={{0,3},{1,0},{2,1},{3,2},{4,7},{5,4},{6,5},{7,6},{8,11},{9,8},{10,9... | collective-permute-start | bytes 319496 | tf_op jit(solution)/shard_map/ppermute | solution.py:194
  124.9 8.3 %collective-permute-start.2 = (f32[4,208,32]{1,2,0:T(8,128)S(1)}, f32[4,208,32]{1,2,0:T(8,128)S(1)}, u32[]{:S(2)}, u32[]{:S(2)}) collective-permute-start(f32[4,208,32]{1,2,0:T(8,128)S(1)} %get-tuple-element.17), channel_id=1, source_target_pairs={{0,2},{1,3},{2,0},{3,1},{4,6},{5,7},{6,4},{7,5},{8,10},{9,11},{10,... | collective-permute-start | bytes 319496 | tf_op jit(solution)/shard_map/ppermute | solution.py:194
  126.4 6.8 %collective-permute-start.1 = (f32[4,208,32]{1,2,0:T(8,128)S(1)}, f32[4,208,32]{1,2,0:T(8,128)S(1)}, u32[]{:S(2)}, u32[]{:S(2)}) collective-permute-start(f32[4,208,32]{1,2,0:T(8,128)S(1)} %get-tuple-element.16), channel_id=1, source_target_pairs={{0,1},{1,2},{2,3},{3,0},{4,5},{5,6},{6,7},{7,4},{8,9},{9,10},{10,1... | collective-permute-start | bytes 319496 | tf_op jit(solution)/shard_map/ppermute | solution.py:194
  133.3 4.0 %collective-permute-start.6 = (f32[208,32]{0,1:T(8,128)S(1)}, f32[208,32]{0,1:T(8,128)S(1)}, u32[]{:S(2)}, u32[]{:S(2)}) collective-permute-start(f32[208,32]{0,1:T(8,128)S(1)} %get-tuple-element.20), channel_id=1, source_target_pairs={{0,12},{4,0},{8,4},{12,8},{1,13},{5,1},{9,5},{13,9},{2,14},{6,2},{... | collective-permute-start | bytes 79880 | tf_op jit(solution)/shard_map/ppermute | solution.py:194
  135.3 4.8 %collective-permute-start.5 = (f32[208,32]{0,1:T(8,128)S(1)}, f32[208,32]{0,1:T(8,128)S(1)}, u32[]{:S(2)}, u32[]{:S(2)}) collective-permute-start(f32[208,32]{0,1:T(8,128)S(1)} %get-tuple-element.21), channel_id=1, source_target_pairs={{0,8},{4,12},{8,0},{12,4},{1,9},{5,13},{9,1},{13,5},{2,10},{6,14},... | collective-permute-start | bytes 79880 | tf_op jit(solution)/shard_map/ppermute | solution.py:194
  135.4 5.7 %collective-permute-start.4 = (f32[208,32]{0,1:T(8,128)S(1)}, f32[208,32]{0,1:T(8,128)S(1)}, u32[]{:S(2)}, u32[]{:S(2)}) collective-permute-start(f32[208,32]{0,1:T(8,128)S(1)} %get-tuple-element.19), channel_id=1, source_target_pairs={{0,4},{4,8},{8,12},{12,0},{1,5},{5,9},{9,13},{13,1},{2,6},{6,10},{... | collective-permute-start | bytes 79880 | tf_op jit(solution)/shard_map/ppermute | solution.py:194
  141.2 0.7 copy-start.6
Sparse Core Ops, SparseCore 0:
  10.3 92.3 all-gather.3

commit v20 on v19

--- a/solution.py
+++ b/solution.py
@@ -188,10 +188,12 @@
 def exchange_scatter(blocks, axis):
     size = lax.axis_size(axis)
     me = lax.axis_index(axis)
-    total = lax.dynamic_index_in_dim(blocks, me, axis=0, keepdims=False)
+    rolled = lax.dynamic_slice_in_dim(jnp.concatenate([blocks, blocks], axis=0), me, size, axis=0)
+    total = rolled[0]
     for shift in range(1, size):
-        send = lax.dynamic_index_in_dim(blocks, (me + shift) % size, axis=0, keepdims=False)
-        total = total + lax.ppermute(send, axis, [(i, (i + shift) % size) for i in range(size)])
+        total = total + lax.ppermute(
+            rolled[shift], axis, [(i, (i + shift) % size) for i in range(size)]
+        )
     return total
 
 

time: 149 us -> 148 us (level)
  waiting for transfers between devices: 72.2 us -> 70.2 us
    ppermute x6, waiting for transfers between devices: 11.1 us -> 8.08 us  [exchange_scatter(): lax.ppermute(rolled[shift], axis, [(i, (i + shift) % size) for i in range...]
  transfers between devices with their start and end apart: 8 -> 8, of which waited for: 7 -> 8; matrix products, arithmetic and copies ran while one was open for 5% -> 5% of each run, Pallas kernels for 0% -> 0%
where the time goes in v20:
time: 148 us
  waiting for transfers between devices  70.2 us (47%)
  blocking collectives  24.5 us (17%)
  Pallas kernels  19.7 us (13%)
  between operations  14.2 us (10%)
  local copies, waits for them, and re-layouts  9.08 us (6%)
  starting transfers between devices  7.91 us (5%)
  other arithmetic  1.49 us (1%)
    all_gather x1, waiting for transfers between devices, project_rows(): lax.all_gather(kv_weight, ('ctx', 'dp', 'sub'), axis=0, tiled=False)  34.7 us
    ppermute x1, waiting for transfers between devices, shifted(): return lax.ppermute(value, axis, pairs)  26.7 us
    all_gather x1, blocking collectives, gather_adapters(): gathered = lax.all_gather(joined, axes, axis=0, tiled=False)  24.5 us
    pallas_call x1, Pallas kernels, attention_heads(): pl.pallas_call(functools.partial(attention_kernel, factor), grid=(col_sha...  19.7 us
    ppermute x6, waiting for transfers between devices, exchange_scatter(): lax.ppermute(rolled[shift], axis, [(i, (i + shift) % size) for i in range...  8.08 us
    ppermute x6, starting transfers between devices, exchange_scatter(): lax.ppermute(rolled[shift], axis, [(i, (i + shift) % size) for i in range...  6.53 us
  transfers between devices with their start and end apart: 8, of which 8 were waited for; matrix products, arithmetic and copies ran while one was open for 5% of the time, Pallas kernels for 0%

profile of v20, /device:TPU:0, one launch (start us, length us, event | category | flops | bytes accessed | tf_op | source)
XLA Modules:
  0.0 147.8 jit_solution(13611949187919213198)
XLA Ops:
  7.2 0.0 copy-start
  7.2 0.0 all-gather.4.cloned.1.call-start
  7.2 0.7 all-gather.4.cloned.1.call-update
  7.9 0.8 pad_maximum_fusion.2
  8.7 24.5 %all-gather = bf16[32,16,208]{2,1,0:T(8,128)(2,1)S(1)} all-gather(bf16[2,16,208]{2,1,0:T(8,128)(2,1)S(1)} %pad_maximum_fusion.2), channel_id=2, replica_groups=mesh['groups'=2,'ctx'=4,'dp'=2,'sub'=2] {'ctx','dp','sub'}, dimensions={0}, use_global_device_ids=true | all-gather | bytes 226304 | tf_op jit(solution)/shard_map/all_gather | solution.py:179
  33.3 0.2 copy.23
  33.4 0.3 reshape.45
  33.7 0.0 copy-done
  33.7 1.3 collective-permute-start
  35.1 0.1 slice.49
  35.2 0.1 copy.32
  35.3 0.8 reshape.48.up_ref
  36.1 0.3 fusion.1
  36.4 26.7 %collective-permute-done = bf16[192,2304]{1,0:T(8,128)(2,1)S(1)} collective-permute-done((bf16[192,2304]{1,0:T(8,128)(2,1)S(1)}, bf16[192,2304]{1,0:T(8,128)(2,1)S(1)}, u32[]{:S(2)}, u32[]{:S(2)}) %collective-permute-start) | collective-permute-done | bytes 884768 | tf_op jit(solution)/shard_map/ppermute | solution.py:23
  63.1 0.3 fusion
  63.4 0.1 pad_maximum_fusion.1
  63.6 0.8 copy.27.low_ref
  64.4 0.1 pad_maximum_fusion
  64.5 1.1 copy.24
  65.6 2.4 %copy.25 = bf16[384,4,576]{2,0,1:T(8,128)(2,1)} copy(bf16[384,4,576]{0,2,1:T(8,128)(2,1)S(1)} %bitcast.75) | data formatting | bytes 3538944 | tf_op jit(solution)/shard_map/reshape | solution.py:168
  68.0 34.7 %all-gather.4.cloned.1.call-done = bf16[32,576,256]{2,1,0:T(8,128)(2,1)} async-done(((bf16[2,576,256]{2,1,0:T(8,128)(2,1)}), bf16[32,576,256]{2,1,0:T(8,128)(2,1)}) %all-gather.4.cloned.1.call-update) | async-done | bytes 9437200 | tf_op jit(solution)/shard_map/all_gather | solution.py:169
  102.8 19.7 %shard_map.93 = (bf16[192,2048]{1,0:T(8,128)(2,1)}, bf16[192,2048]{1,0:T(8,128)(2,1)}, f32[2,4,16,576]{3,2,1,0:T(8,128)}, f32[2,16,1024]{2,1,0:T(8,128)}) custom-call(s32[1]{0:T(128)} %bitcast.mask_ref, bf16[192,2048]{1,0:T(8,128)(2,1)} %bitcast.84, bf16[192,2048]{1,0:T(8,128)(2,1)} %bitcast.85, bf16[4,384,576]{2,1,0:T(8,128)(2,1)} %bitcast.74, ...), custom_call_target="tpu_custom_call" | custom-call | tf_op jit(solution)/shard_map/pallas_call | solution.py:121
  122.5 1.1 reshape.51
  123.6 0.1 copy.29
  123.7 1.4 reshape.49
  125.0 0.1 copy.28
  125.2 0.4 fusion.5
  125.5 0.3 collective-permute-start.1
  125.9 0.6 collective-permute-start.2
  126.4 1.2 collective-permute-start.3
  127.6 2.9 %collective-permute-done.1 = f32[4,208,32]{1,2,0:T(8,128)S(1)} collective-permute-done((f32[4,208,32]{1,2,0:T(8,128)S(1)}, f32[4,208,32]{1,2,0:T(8,128)S(1)}, u32[]{:S(2)}, u32[]{:S(2)}) %collective-permute-start.1) | collective-permute-done | bytes 106528 | tf_op jit(solution)/shard_map/ppermute | solution.py:194
  130.6 1.6 %collective-permute-done.2 = f32[4,208,32]{1,2,0:T(8,128)S(1)} collective-permute-done((f32[4,208,32]{1,2,0:T(8,128)S(1)}, f32[4,208,32]{1,2,0:T(8,128)S(1)}, u32[]{:S(2)}, u32[]{:S(2)}) %collective-permute-start.2) | collective-permute-done | bytes 106528 | tf_op jit(solution)/shard_map/ppermute | solution.py:194
  132.2 0.1 collective-permute-done.3
  132.4 1.6 %collective-permute-start.4 = (f32[208,32]{0,1:T(8,128)S(1)}, f32[208,32]{0,1:T(8,128)S(1)}, u32[]{:S(2)}, u32[]{:S(2)}) collective-permute-start(f32[208,32]{0,1:T(8,128)S(1)} %get-tuple-element.19), channel_id=1, source_target_pairs={{0,4},{4,8},{8,12},{12,0},{1,5},{5,9},{9,13},{13,1},{2,6},{6,10},{... | collective-permute-start | bytes 79880 | tf_op jit(solution)/shard_map/ppermute | solution.py:194
  134.0 2.1 %collective-permute-start.5 = (f32[208,32]{0,1:T(8,128)S(1)}, f32[208,32]{0,1:T(8,128)S(1)}, u32[]{:S(2)}, u32[]{:S(2)}) collective-permute-start(f32[208,32]{0,1:T(8,128)S(1)} %get-tuple-element.20), channel_id=1, source_target_pairs={{0,8},{4,12},{8,0},{12,4},{1,9},{5,13},{9,1},{13,5},{2,10},{6,14},... | collective-permute-start | bytes 79880 | tf_op jit(solution)/shard_map/ppermute | solution.py:194
  136.1 0.7 collective-permute-start.6
  136.8 1.3 collective-permute-done.4
  138.2 1.8 %collective-permute-done.5 = f32[208,32]{0,1:T(8,128)S(1)} collective-permute-done((f32[208,32]{0,1:T(8,128)S(1)}, f32[208,32]{0,1:T(8,128)S(1)}, u32[]{:S(2)}, u32[]{:S(2)}) %collective-permute-start.5) | collective-permute-done | bytes 26656 | tf_op jit(solution)/shard_map/ppermute | solution.py:194
  139.9 0.3 collective-permute-done.6
  140.3 0.0 copy-start.1
  140.3 0.7 slice.59
  141.0 0.0 copy-done.1
  (6 shorter events, 0.1 us)
Async XLA Ops:
  7.2 26.6 %copy-start = (bf16[1,192,2304]{2,1,0:T(8,128)(2,1)S(1)}, bf16[1,192,2304]{2,1,0:T(8,128)(2,1)}, u32[]{:S(2)}) copy-start(bf16[1,192,2304]{2,1,0:T(8,128)(2,1)} %param.6) | copy-start | bytes 2654212
  7.2 95.6 %all-gather.4.cloned.1.call-start = ((), (), s32[]{:S(2)}) async-start(), calls=%async_computation | async-start | bytes 10027008 | tf_op jit(solution)/shard_map/all_gather | solution.py:169
  33.7 29.3 %collective-permute-start = (bf16[192,2304]{1,0:T(8,128)(2,1)S(1)}, bf16[192,2304]{1,0:T(8,128)(2,1)S(1)}, u32[]{:S(2)}, u32[]{:S(2)}) collective-permute-start(bf16[192,2304]{1,0:T(8,128)(2,1)S(1)} %bitcast.76), channel_id=1, source_target_pairs={{0,4},{4,8},{8,12},{1,5},{5,9},{9,13},{2,6},{6,10},{10,14},{3,7},{... | collective-permute-start | bytes 2654216 | tf_op jit(solution)/shard_map/ppermute | solution.py:23
  125.5 5.0 %collective-permute-start.1 = (f32[4,208,32]{1,2,0:T(8,128)S(1)}, f32[4,208,32]{1,2,0:T(8,128)S(1)}, u32[]{:S(2)}, u32[]{:S(2)}) collective-permute-start(f32[4,208,32]{1,2,0:T(8,128)S(1)} %get-tuple-element.16), channel_id=1, source_target_pairs={{0,1},{1,2},{2,3},{3,0},{4,5},{5,6},{6,7},{7,4},{8,9},{9,10},{10,1... | collective-permute-start | bytes 319496 | tf_op jit(solution)/shard_map/ppermute | solution.py:194
  125.9 6.3 %collective-permute-start.2 = (f32[4,208,32]{1,2,0:T(8,128)S(1)}, f32[4,208,32]{1,2,0:T(8,128)S(1)}, u32[]{:S(2)}, u32[]{:S(2)}) collective-permute-start(f32[4,208,32]{1,2,0:T(8,128)S(1)} %get-tuple-element.17), channel_id=1, source_target_pairs={{0,2},{1,3},{2,0},{3,1},{4,6},{5,7},{6,4},{7,5},{8,10},{9,11},{10,... | collective-permute-start | bytes 319496 | tf_op jit(solution)/shard_map/ppermute | solution.py:194
  126.4 5.9 %collective-permute-start.3 = (f32[4,208,32]{1,2,0:T(8,128)S(1)}, f32[4,208,32]{1,2,0:T(8,128)S(1)}, u32[]{:S(2)}, u32[]{:S(2)}) collective-permute-start(f32[4,208,32]{1,2,0:T(8,128)S(1)} %get-tuple-element.18), channel_id=1, source_target_pairs={{0,3},{1,0},{2,1},{3,2},{4,7},{5,4},{6,5},{7,6},{8,11},{9,8},{10,9... | collective-permute-start | bytes 319496 | tf_op jit(solution)/shard_map/ppermute | solution.py:194
  132.4 5.8 %collective-permute-start.4 = (f32[208,32]{0,1:T(8,128)S(1)}, f32[208,32]{0,1:T(8,128)S(1)}, u32[]{:S(2)}, u32[]{:S(2)}) collective-permute-start(f32[208,32]{0,1:T(8,128)S(1)} %get-tuple-element.19), channel_id=1, source_target_pairs={{0,4},{4,8},{8,12},{12,0},{1,5},{5,9},{9,13},{13,1},{2,6},{6,10},{... | collective-permute-start | bytes 79880 | tf_op jit(solution)/shard_map/ppermute | solution.py:194
  134.0 6.0 %collective-permute-start.5 = (f32[208,32]{0,1:T(8,128)S(1)}, f32[208,32]{0,1:T(8,128)S(1)}, u32[]{:S(2)}, u32[]{:S(2)}) collective-permute-start(f32[208,32]{0,1:T(8,128)S(1)} %get-tuple-element.20), channel_id=1, source_target_pairs={{0,8},{4,12},{8,0},{12,4},{1,9},{5,13},{9,1},{13,5},{2,10},{6,14},... | collective-permute-start | bytes 79880 | tf_op jit(solution)/shard_map/ppermute | solution.py:194
  136.1 4.2 %collective-permute-start.6 = (f32[208,32]{0,1:T(8,128)S(1)}, f32[208,32]{0,1:T(8,128)S(1)}, u32[]{:S(2)}, u32[]{:S(2)}) collective-permute-start(f32[208,32]{0,1:T(8,128)S(1)} %get-tuple-element.21), channel_id=1, source_target_pairs={{0,12},{4,0},{8,4},{12,8},{1,13},{5,1},{9,5},{13,9},{2,14},{6,2},{... | collective-permute-start | bytes 79880 | tf_op jit(solution)/shard_map/ppermute | solution.py:194
  140.3 0.7 copy-start.1
Sparse Core Ops, SparseCore 0:
  10.3 92.4 all-gather.3
